TPU v7x, 128 devices: a whole 4x4x4 slice. The times are simulated.
128 devices in a mesh: row: 8 (over z, core), col: 16 (over x, y).
Axes of the slice: x: 4, y: 4, z: 4, core: 2. Of those that a mesh axis runs over, the one named last changes fastest.
Arguments:
- image: bfloat16 [128, 512, 768], P('row', 'col'), may hold values from -6 to 6
- dw_kernel: float32 [768, 49], replicated, may hold values from -0.875 to 0.875
- ln_gain: float32 [768], replicated, may hold values from 0.25 to 1.75
- w_in: bfloat16 [768, 3072], P('col'), may hold values from -0.21875 to 0.21875
- b_in: float32 [3072], replicated, may hold values from -3 to 3
- w_out: bfloat16 [3072, 768], P('col'), may hold values from -0.109375 to 0.109375
- layer_scale: float32 [768], replicated, may hold values from 0.5 to 1.5
- cotangent: bfloat16 [128, 512, 768], P('row', 'col'), may hold values from -8 to 8
Outputs:
- out_map: bfloat16 [128, 512, 768], P('row', 'col')
- grad_image: bfloat16 [128, 512, 768], P('row', 'col')
- grad_kernel: float32 [768, 49], P(('row', 'col'))
- grad_w_in: float32 [768, 3072], P('col')
- grad_w_out: float32 [3072, 768], P('col')
- grad_b_in: float32 [3072], replicated
- grad_gain: float32 [768], replicated
- grad_scale: float32 [768], replicated
All inputs are finite; a program needn't handle non-finite values.
Results may differ from a plain program's by a relative error of at most 0.0071.
Values may be sent and summed in bfloat16 or wider, within the bound.
No kernel may reach another device: no remote copies, remote signals or barrier semaphores. Data moves between devices by JAX's collectives and lax.ppermute only.
A program may use at most 128 MiB of HBM per device.

v0:
```python
import math

import jax
import jax.numpy as jnp
from jax import lax
from jax.sharding import PartitionSpec as P

KSIZE = 7
DILATE = 2
REACH = 6


EPSILON = 1e-06
CONTRACT_ROWS = (((0,), (0,)), ((), ()))
CONTRACT_COLS = (((1,), (1,)), ((), ()))


def normal_cdf(values):
    return 0.5 * (1.0 + jax.scipy.special.erf(values * 0.7071067811865476))


def gelu_exact(values):
    return values * normal_cdf(values)


def gelu_slope(values):
    return normal_cdf(values) + values * jnp.exp(-0.5 * values * values) * 0.3989422804014327


def group_stencil(padded, tap_table, height, breadth):
    summed = jnp.zeros((tap_table.shape[0], height, breadth), jnp.float32)
    for tap_row in range(KSIZE):
        for tap_col in range(KSIZE):
            window = padded[
                :,
                DILATE * tap_row : DILATE * tap_row + height,
                DILATE * tap_col : DILATE * tap_col + breadth,
            ].astype(jnp.float32)
            summed = summed + tap_table[:, KSIZE * tap_row + tap_col][:, None, None] * window
    return summed


def group_taps(padded, gradient, height, breadth):
    columns = []
    for tap_row in range(KSIZE):
        for tap_col in range(KSIZE):
            window = padded[
                :,
                DILATE * tap_row : DILATE * tap_row + height,
                DILATE * tap_col : DILATE * tap_col + breadth,
            ].astype(jnp.float32)
            columns.append(jnp.sum(gradient * window, axis=(1, 2)))
    return jnp.stack(columns, axis=1)


def pad_groups(field):
    return jnp.pad(field, ((0, 0), (REACH, REACH), (REACH, REACH)))


def to_groups(field, row_count, col_count):
    tile_rows, tile_cols, channels = field.shape
    group_size = channels // (row_count * col_count)
    pixels = tile_rows * tile_cols
    packed = field.reshape(pixels, channels).T.reshape(row_count, col_count, group_size, pixels)
    moved = lax.all_to_all(
        packed.reshape(row_count * col_count, group_size, pixels),
        ("row", "col"),
        split_axis=0,
        concat_axis=0,
        tiled=True,
    ).reshape(row_count, col_count, group_size, pixels)
    moved = moved.reshape(row_count, col_count, group_size, tile_rows, tile_cols)
    return moved.transpose(2, 0, 3, 1, 4).reshape(
        group_size, row_count * tile_rows, col_count * tile_cols
    )


def from_groups(field, row_count, col_count, tile_rows, tile_cols):
    group_size = field.shape[0]
    pixels = tile_rows * tile_cols
    channels = group_size * row_count * col_count
    packed = field.reshape(group_size, row_count, tile_rows, col_count, tile_cols).transpose(
        1, 3, 0, 2, 4
    )
    packed = packed.reshape(row_count, col_count, group_size, pixels)
    moved = lax.all_to_all(
        packed.reshape(row_count * col_count, group_size, pixels),
        ("row", "col"),
        split_axis=0,
        concat_axis=0,
        tiled=True,
    )
    return moved.reshape(channels, pixels).T.reshape(tile_rows, tile_cols, channels)


def local(image, dw_kernel, ln_gain, w_in, b_in, w_out, layer_scale, cotangent):
    tile_rows, tile_cols, channels = image.shape
    row_count = lax.axis_size("row")
    col_count = lax.axis_size("col")
    group_count = row_count * col_count
    group_size = channels // group_count
    pixels = tile_rows * tile_cols
    scale_factor = 1.0 / math.sqrt(pixels * group_count)
    full_in, full_out = (
        lax.all_gather(w_in, "col", axis=0, tiled=True),
        lax.all_gather(w_out, "col", axis=0, tiled=True),
    )
    flipped = dw_kernel.reshape(channels, KSIZE, KSIZE)[:, ::-1, ::-1].reshape(
        channels, KSIZE * KSIZE
    )
    group_index = lax.axis_index("row") * col_count + lax.axis_index("col")
    kernel_mine = lax.dynamic_slice_in_dim(dw_kernel, group_index * group_size, group_size, 0)
    flipped_mine = lax.dynamic_slice_in_dim(flipped, group_index * group_size, group_size, 0)
    grouped = pad_groups(to_groups(image, row_count, col_count))
    height = grouped.shape[1] - 2 * REACH
    breadth = grouped.shape[2] - 2 * REACH
    conv_groups = group_stencil(grouped, kernel_mine, height, breadth).astype(jnp.bfloat16)
    conv_tile = from_groups(conv_groups, row_count, col_count, tile_rows, tile_cols)
    conv_rows = conv_tile.astype(jnp.float32).reshape(pixels, channels)
    average = jnp.mean(conv_rows, axis=1, keepdims=True)
    centered = conv_rows - average
    inverse = lax.rsqrt(jnp.mean(centered * centered, axis=1, keepdims=True) + EPSILON)
    standard = centered * inverse
    normed = (standard * ln_gain).astype(jnp.bfloat16)
    preact = jnp.dot(normed, full_in, preferred_element_type=jnp.float32) + b_in
    hidden = gelu_exact(preact).astype(jnp.bfloat16)
    mixed = jnp.dot(hidden, full_out, preferred_element_type=jnp.float32)
    out_map = (image.reshape(pixels, channels).astype(jnp.float32) + layer_scale * mixed).astype(
        jnp.bfloat16
    )
    out_map = out_map.reshape(tile_rows, tile_cols, channels)
    upstream = cotangent.reshape(pixels, channels).astype(jnp.float32)
    scale_part = jnp.sum(upstream * mixed, axis=0)
    grad_mix = (upstream * layer_scale).astype(jnp.bfloat16)
    grad_hidden = lax.dot_general(
        grad_mix, full_out, CONTRACT_COLS, preferred_element_type=jnp.float32
    )
    grad_pre = grad_hidden * gelu_slope(preact)
    bias_part = jnp.sum(grad_pre, axis=0)
    grad_pre_rounded = grad_pre.astype(jnp.bfloat16)
    grad_norm = lax.dot_general(
        grad_pre_rounded, full_in, CONTRACT_COLS, preferred_element_type=jnp.float32
    )
    picked = normed
    part_in = lax.psum_scatter(
        lax.dot_general(
            picked, grad_pre_rounded, CONTRACT_ROWS, preferred_element_type=jnp.float32
        ),
        "col",
        scatter_dimension=0,
        tiled=True,
    )
    picked = hidden
    part_out = lax.psum_scatter(
        lax.dot_general(picked, grad_mix, CONTRACT_ROWS, preferred_element_type=jnp.float32),
        "col",
        scatter_dimension=0,
        tiled=True,
    )
    summed_in, summed_out = lax.psum((part_in, part_out), "row")
    gain_part = jnp.sum(grad_norm * standard, axis=0)
    scaled = grad_norm * ln_gain
    grad_conv = (
        (
            scaled
            - jnp.mean(scaled, axis=1, keepdims=True)
            - standard * jnp.mean(scaled * standard, axis=1, keepdims=True)
        )
        * inverse
    ).astype(jnp.bfloat16)
    grad_conv = grad_conv.reshape(tile_rows, tile_cols, channels)
    grad_groups = to_groups(grad_conv, row_count, col_count)
    back_groups = group_stencil(pad_groups(grad_groups), flipped_mine, height, breadth).astype(
        jnp.bfloat16
    )
    grad_back = from_groups(back_groups, row_count, col_count, tile_rows, tile_cols)
    grad_kernel = (
        group_taps(grouped, grad_groups.astype(jnp.float32), height, breadth) * scale_factor
    )
    grad_image = (cotangent.astype(jnp.float32) + grad_back.astype(jnp.float32)).astype(
        jnp.bfloat16
    )
    scale_sum, bias_sum, gain_sum = lax.psum((scale_part, bias_part, gain_part), ("row", "col"))
    return (
        out_map,
        grad_image,
        grad_kernel,
        summed_in * scale_factor,
        summed_out * scale_factor,
        bias_sum * scale_factor,
        gain_sum * scale_factor,
        scale_sum * scale_factor,
    )


def solution(mesh):
    in_specs = (
        P("row", "col", None),
        P(),
        P(),
        P("col", None),
        P(),
        P("col", None),
        P(),
        P("row", "col", None),
    )
    out_specs = (
        P("row", "col", None),
        P("row", "col", None),
        P(("row", "col"), None),
        P("col", None),
        P("col", None),
        P(),
        P(),
        P(),
    )
    return jax.shard_map(local, mesh=mesh, in_specs=in_specs, out_specs=out_specs, check_vma=False)
```

profile of v0, /device:TPU:0, one launch (start us, length us, event | category | flops | bytes accessed | tf_op | source)
XLA Modules:
  0.0 482.0 jit_solution(17766908874292094749)
XLA Ops:
  7.9 0.7 all-gather.5.cloned.1.call-update
  8.6 1.4 copy.37
  10.1 1.2 reshape_reshape.18
  11.3 11.2 %all-to-all-start = ((bf16[128,6,512]{2,1,0:T(8,128)(2,1)}), bf16[128,6,512]{2,1,0:T(8,128)(2,1)S(1)}, u32[]{:S(2)}, u32[]{:S(2)}) async-start(bf16[128,6,512]{2,1,0:T(8,128)(2,1)} %reshape_reshape.18), calls=%async_computation | async-start | bytes 2097152 | tf_op jit(solution)/shard_map/all_to_all | solution.py:65
  23.8 22.5 %all-to-all-done = bf16[128,6,512]{2,1,0:T(8,128)(2,1)S(1)} async-done(((bf16[128,6,512]{2,1,0:T(8,128)(2,1)}), bf16[128,6,512]{2,1,0:T(8,128)(2,1)S(1)}, u32[]{:S(2)}, u32[]{:S(2)}) %all-to-all-start) | async-done | bytes 786464 | tf_op jit(solution)/shard_map/all_to_all | solution.py:65
  46.3 1.1 copy.38
  47.4 3.5 reshape_reshape.19
  50.9 2.5 copy.39
  53.4 5.4 %reshape.178 = bf16[6,128,512]{2,1,0:T(8,128)(2,1)} reshape(bf16[6,8,16,16,32]{4,3,2,1,0:T(8,128)(2,1)} %copy.39) | data formatting | bytes 1572864 | tf_op jit(solution)/shard_map/reshape | solution.py:73
  58.8 50.4 %fusion.139 = bf16[6,128,512]{2,1,0:T(8,128)(2,1)} fusion(bf16[6,128,512]{2,1,0:T(8,128)(2,1)} %reshape.178, f32[6]{0:T(128)S(1)} %get-tuple-element.194, f32[6]{0:T(128)S(1)} %get-tuple-element.141, f32[6]{0:T(128)S(1)} %get-tuple-element.142, f32[6]{0:T(128)S(1)} %get-tuple-element.143, f32[6]{0:T(128)S(1)} %get-tuple-element.144, ...), kind=kLoop, calls=%fused_computation.345 | loop fusion | flops 57802752 | bytes 1574040 | tf_op jit(solution)/shard_map/convert_element_type | solution.py:117
  109.2 4.8 reshape.179
  114.0 4.4 copy.98
  118.4 5.1 %reshape.189 = bf16[128,6,512]{2,1,0:T(8,128)(2,1)} reshape(bf16[8,16,6,16,32]{4,3,2,1,0:T(8,128)(2,1)} %copy.98) | data formatting | bytes 1572864 | tf_op jit(solution)/shard_map/reshape;reshape | solution.py:87
  123.5 24.6 %all_to_all.20 = bf16[128,6,512]{2,1,0:T(8,128)(2,1)} all-to-all(bf16[128,6,512]{2,1,0:T(8,128)(2,1)} %reshape.189), channel_id=1, replica_groups=mesh['row'=8,'col'=16] {'row','col'}, dimensions={0} | all-to-all | bytes 1572864 | tf_op jit(solution)/shard_map/all_to_all | solution.py:86
  148.1 2.4 convert_element_type.471
  150.5 3.0 copy.42
  153.5 1.5 convert_reduce_fusion
  155.0 1.7 multiply_reduce_fusion.1
  156.8 8.6 %multiply_convert_fusion = (bf16[512,3072]{1,0:T(8,128)(2,1)}, f32[512,3072]{1,0:T(8,128)}) fusion(f32[3072]{0:T(1024)S(1)} %copy-done.9, bf16[768,3072]{1,0:T(8,128)(2,1)} %all-gather.3.cloned.1.call-done, f32[768,512]{0,1:T(8,128)} %copy.42, f32[768]{0:T(1024)S(1)} %copy-done.7, f32[512]{0:T(512)S(1)} %add_rsqrt_fusion, f32[512]{0:T(512)S(1)} %broadcast_multiply_fusion.8), kind=kOutput, calls=%fused_computation.56 | convolution fusion | flops 2426929152 | bytes 15748096 | tf_op jit(solution)/shard_map/dot_general | solution.py:125
  165.4 7.4 %fusion.130 = (f32[768]{0:T(1024)S(1)}, bf16[512,768]{1,0:T(8,128)(2,1)}, bf16[512,768]{1,0:T(8,128)(2,1)S(1)}) fusion(bf16[16,32,768]{2,1,0:T(8,128)(2,1)} %param.15, f32[768]{0:T(1024)S(1)} %copy-done.10, bf16[16,32,768]{2,1,0:T(8,128)(2,1)} %param.8, bf16[512,3072]{1,0:T(8,128)(2,1)} %get-tuple-element.189, ...), kind=kOutput, calls=%fused_computation.331 | convolution fusion | flops 2419457280 | bytes 11016192 | tf_op jit(solution)/shard_map/dot_general | solution.py:127
  172.9 4.7 fusion.143
  177.6 1.7 copy-done.4
  179.2 5.5 %fusion.134 = f32[768,3072]{1,0:T(8,128)} fusion(bf16[512,3072]{1,0:T(8,128)(2,1)S(1)} %get-tuple-element.193, f32[768,512]{0,1:T(8,128)S(1)} %copy-done, f32[768]{0:T(1024)S(1)} %copy-done.7, f32[512]{0:T(512)S(1)} %add_rsqrt_fusion, f32[512]{0:T(512)S(1)} %broadcast_multiply_fusion.8), kind=kOutput, calls=%fused_computation.338 | convolution fusion | flops 2417491968 | bytes 14162944 | tf_op jit(solution)/shard_map/dot_general | solution.py:146
  185.0 8.4 %fusion.144 = f32[3072,768]{1,0:T(8,128)} fusion(bf16[512,3072]{1,0:T(8,128)(2,1)} %get-tuple-element.189, bf16[512,768]{1,0:T(8,128)(2,1)} %copy-done.11), kind=kOutput, calls=%fused_computation.459 | convolution fusion | flops 2415919104 | bytes 13369344 | tf_op jit(solution)/shard_map/dot_general | solution.py:155
  193.6 6.9 %fusion.133 = (f32[768]{0:T(1024)S(1)}, f32[512]{0:T(512)S(1)}, f32[512]{0:T(512)S(1)}, f32[512,768]{1,0:T(8,128)S(1)}) fusion(f32[768,512]{0,1:T(8,128)} %copy.42, f32[512]{0:T(512)S(1)} %add_rsqrt_fusion, f32[512]{0:T(512)S(1)} %broadcast_multiply_fusion.8, f32[768]{0:T(1024)S(1)} %copy-done.7, bf16[768,3072]{1,0:T(8,128)(2,1)} %all-gather.3.cloned.1.call-done, ...), kind=kOutput, calls=%fused_computation.337 | convolution fusion | flops 2419063040 | bytes 11024384 | tf_op jit(solution)/shard_map/dot_general | solution.py:141
  200.5 1.3 fusion.127
  201.9 2.3 copy.43
  204.2 2.2 reshape_reshape.21
  206.4 5.8 %all-to-all-start.2 = ((bf16[128,6,512]{2,1,0:T(8,128)(2,1)}), bf16[128,6,512]{2,1,0:T(8,128)(2,1)}, u32[]{:S(2)}, u32[]{:S(2)}) async-start(bf16[128,6,512]{2,1,0:T(8,128)(2,1)} %reshape_reshape.21), calls=%async_computation.2 | async-start | bytes 2097152 | tf_op jit(solution)/shard_map/all_to_all | solution.py:65
  212.3 78.4 %all-reduce.2 = (f32[3072]{0:T(1024)S(1)}, f32[768]{0:T(1024)S(1)}, f32[768]{0:T(1024)S(1)}) all-reduce(f32[3072]{0:T(1024)S(1)} %get-tuple-element.192, f32[768]{0:T(1024)S(1)} %get-tuple-element.32, f32[768]{0:T(1024)S(1)} %get-tuple-element.88), channel_id=1, replica_groups=mesh['row'=8,'col'=16] {'row','col'}, use_global_device_ids=true, to_apply=%region_58.59 | all-reduce | flops 4608 | bytes 36864 | tf_op jit(solution)/shard_map/psum | solution.py:183
  292.6 2.4 copy.44
  294.9 4.6 reshape_reshape.22
  299.6 4.4 copy.45
  304.0 5.4 %reshape.183 = bf16[6,128,512]{2,1,0:T(8,128)(2,1)} reshape(bf16[6,8,16,16,32]{4,3,2,1,0:T(8,128)(2,1)} %copy.45) | data formatting | bytes 1572864 | tf_op jit(solution)/shard_map/reshape | solution.py:73
  309.4 50.0 %fusion.138 = bf16[6,128,512]{2,1,0:T(8,128)(2,1)} fusion(bf16[6,128,512]{2,1,0:T(8,128)(2,1)} %reshape.183, f32[6]{0:T(128)S(1)} %get-tuple-element.139, f32[6]{0:T(128)S(1)} %get-tuple-element.92, f32[6]{0:T(128)S(1)} %get-tuple-element.93, f32[6]{0:T(128)S(1)} %get-tuple-element.94, f32[6]{0:T(128)S(1)} %get-tuple-element.95, ...), kind=kLoop, calls=%fused_computation.344 | loop fusion | flops 57802752 | bytes 1574040 | tf_op jit(solution)/shard_map/convert_element_type | solution.py:173
  359.4 4.8 reshape.184
  364.2 4.5 copy.99
  368.7 5.1 %reshape.190 = bf16[128,6,512]{2,1,0:T(8,128)(2,1)} reshape(bf16[8,16,6,16,32]{4,3,2,1,0:T(8,128)(2,1)} %copy.99) | data formatting | bytes 1572864 | tf_op jit(solution)/shard_map/reshape;reshape | solution.py:87
  373.8 6.5 %all-to-all-start.3 = ((bf16[128,6,512]{2,1,0:T(8,128)(2,1)}), bf16[128,6,512]{2,1,0:T(8,128)(2,1)}, u32[]{:S(2)}, u32[]{:S(2)}) async-start(bf16[128,6,512]{2,1,0:T(8,128)(2,1)} %reshape.190), calls=%async_computation.3 | async-start | bytes 2097152 | tf_op jit(solution)/shard_map/all_to_all | solution.py:86
  380.4 16.9 %fusion.124 = (f32[6]{0:T(128)S(1)}, f32[6]{0:T(128)S(1)}, f32[6]{0:T(128)S(1)}, f32[6]{0:T(128)S(1)}, f32[6]{0:T(128)S(1)}, /*index=5*/f32[6]{0:T(128)S(1)}, f3...) fusion(bf16[6,128,512]{2,1,0:T(8,128)(2,1)} %reshape.183, ...), kind=kLoop, calls=%fused_computation.321 | loop fusion | flops 21626772 | bytes 1573296 | tf_op jit(solution)/shard_map/reduce_sum | solution.py:52
  397.4 6.1 %fusion.125 = (f32[6]{0:T(128)S(1)}, f32[6]{0:T(128)S(1)}, f32[6]{0:T(128)S(1)}, f32[6]{0:T(128)S(1)}, f32[6]{0:T(128)S(1)}, /*index=5*/f32[6]{0:T(128)S(1)}, f3...) fusion(bf16[6,128,512]{2,1,0:T(8,128)(2,1)S(1)} %copy-done.3, ...), kind=kLoop, calls=%fused_computation.322 | loop fusion | flops 21626772 | bytes 1573296 | tf_op jit(solution)/shard_map/reduce_sum | solution.py:52
  403.5 4.3 fusion.123
  407.9 3.1 multiply_reduce_fusion
  416.2 1.4 reshape.188
  418.1 2.2 fusion.128
  420.3 52.2 %all-reduce.6.cloned.1.call-done = (f32[48,3072]{1,0:T(8,128)}, f32[192,768]{1,0:T(8,128)}) async-done(((f32[48,3072]{1,0:T(8,128)}, f32[192,768]{1,0:T(8,128)}), (f32[48,3072]{1,0:T(8,128)}, f32[192,768]{1,0:T(8,128)})) %all-reduce.6.cloned.1.call-update) | async-done | bytes 1179664 | tf_op jit(solution)/shard_map/psum | solution.py:160
  472.5 2.0 broadcast_multiply_fusion.1
  474.5 0.9 broadcast_multiply_fusion
  (107 shorter events, 10.3 us)
Async XLA Ops:
  7.2 149.6 %all-gather.3.cloned.1.call-start = ((), (), s32[]{:S(2)}) async-start(), calls=%async_computation.6 | async-start | bytes 5013504 | tf_op jit(solution)/shard_map/all_gather | solution.py:105
  7.9 157.5 %all-gather.5.cloned.1.call-start = ((), (), s32[]{:S(2)}) async-start(), calls=%async_computation.7 | async-start | bytes 5013504 | tf_op jit(solution)/shard_map/all_gather | solution.py:106
  11.3 11.2 %copy-start.6 = (f32[768,49]{0,1:T(8,128)S(1)}, f32[768,49]{0,1:T(8,128)}, u32[]{:S(2)}) copy-start(f32[768,49]{0,1:T(8,128)} %param.9) | copy-start | bytes 451588
  11.3 34.9 %all-to-all-start = ((bf16[128,6,512]{2,1,0:T(8,128)(2,1)}), bf16[128,6,512]{2,1,0:T(8,128)(2,1)S(1)}, u32[]{:S(2)}, u32[]{:S(2)}) async-start(bf16[128,6,512]{2,1,0:T(8,128)(2,1)} %reshape_reshape.18), calls=%async_computation | async-start | bytes 2097152 | tf_op jit(solution)/shard_map/all_to_all | solution.py:65
  22.5 385.3 %reduce-scatter.3.cloned.1.call-start = ((), (), s32[]{:S(2)}) async-start(), calls=%async_computation.8 | async-start | bytes 10027008 | tf_op jit(solution)/shard_map/reduce_scatter | solution.py:145
  153.5 3.3 copy-start.7
  153.5 3.3 copy-start.9
  156.7 8.6 %copy-start.10 = (f32[768]{0:T(1024)S(1)}, f32[768]{0:T(1024)}, u32[]{:S(2)}) copy-start(f32[768]{0:T(1024)} %param.14) | copy-start | bytes 9220
  165.4 7.5 %copy-start.8 = (bf16[3072,768]{1,0:T(8,128)(2,1)S(1)}, bf16[3072,768]{1,0:T(8,128)(2,1)}, u32[]{:S(2)}) copy-start(bf16[3072,768]{1,0:T(8,128)(2,1)} %all-gather.5.cloned.1.call-done) | copy-start | bytes 14155780
  165.4 7.5 %copy-start.12 = (f32[512,3072]{1,0:T(8,128)S(1)}, f32[512,3072]{1,0:T(8,128)}, u32[]{:S(2)}) copy-start(f32[512,3072]{1,0:T(8,128)} %get-tuple-element.190) | copy-start | bytes 18874372
  172.8 4.7 copy-start.11
  172.8 6.4 %copy-start = (f32[768,512]{0,1:T(8,128)S(1)}, f32[768,512]{0,1:T(8,128)}, u32[]{:S(2)}) copy-start(f32[768,512]{0,1:T(8,128)} %copy.42) | copy-start | bytes 4718596
  177.6 1.7 copy-start.4
  184.7 223.1 %reduce-scatter.5.cloned.1.call-start = ((), (), s32[]{:S(2)}) async-start(), calls=%async_computation.9 | async-start | bytes 10027008 | tf_op jit(solution)/shard_map/reduce_scatter | solution.py:154
  193.6 7.0 %copy-start.1 = (f32[768,512]{0,1:T(8,128)S(1)}, f32[768,512]{0,1:T(8,128)}, u32[]{:S(2)}) copy-start(f32[768,512]{0,1:T(8,128)} %copy.42) | copy-start | bytes 4718596
  206.4 86.2 %all-to-all-start.2 = ((bf16[128,6,512]{2,1,0:T(8,128)(2,1)}), bf16[128,6,512]{2,1,0:T(8,128)(2,1)}, u32[]{:S(2)}, u32[]{:S(2)}) async-start(bf16[128,6,512]{2,1,0:T(8,128)(2,1)} %reshape_reshape.21), calls=%async_computation.2 | async-start | bytes 2097152 | tf_op jit(solution)/shard_map/all_to_all | solution.py:65
  373.8 42.4 %all-to-all-start.3 = ((bf16[128,6,512]{2,1,0:T(8,128)(2,1)}), bf16[128,6,512]{2,1,0:T(8,128)(2,1)}, u32[]{:S(2)}, u32[]{:S(2)}) async-start(bf16[128,6,512]{2,1,0:T(8,128)(2,1)} %reshape.190), calls=%async_computation.3 | async-start | bytes 2097152 | tf_op jit(solution)/shard_map/all_to_all | solution.py:86
  380.4 92.1 %all-reduce.6.cloned.1.call-start = ((), (), s32[]{:S(2)}) async-start(), calls=%async_computation.10 | async-start | bytes 2359296 | tf_op jit(solution)/shard_map/psum | solution.py:160
  380.4 17.0 %copy-start.2 = (bf16[6,128,512]{2,1,0:T(8,128)(2,1)S(1)}, bf16[6,128,512]{2,1,0:T(8,128)(2,1)}, u32[]{:S(2)}) copy-start(bf16[6,128,512]{2,1,0:T(8,128)(2,1)} %reshape.178) | copy-start | bytes 2359300
  380.4 16.9 %copy-start.3 = (bf16[6,128,512]{2,1,0:T(8,128)(2,1)S(1)}, bf16[6,128,512]{2,1,0:T(8,128)(2,1)}, u32[]{:S(2)}) copy-start(bf16[6,128,512]{2,1,0:T(8,128)(2,1)} %reshape.183) | copy-start | bytes 2359300
  472.5 2.0 copy-start.5
Sparse Core Ops, SparseCore 0:
  10.2 61.8 all-gather.2
  74.3 53.3 all-gather.4
  184.8 91.9 reduce-scatter.2
  280.1 87.1 reduce-scatter.4
  408.0 64.4 all-reduce.5
where the time goes:
time: 488 us; the launch traced here: 482 us
  other arithmetic  143 us (29%)
  blocking collectives  103 us (21%)
  local copies, waits for them, and re-layouts  80.4 us (16%)
  waiting for transfers between devices  76.1 us (16%)
  matrix products  41.5 us (9%)
  starting transfers between devices  23.9 us (5%)
  between operations  14.3 us (3%)
    psum x1, blocking collectives, local(): lax.psum((scale_part, bias_part, gain_part), ('row', 'col'))  78.4 us
    psum x1, waiting for transfers between devices, local(): summed_in, summed_out = lax.psum((part_in, part_out), 'row')  52.2 us
    convert_element_type x1, other arithmetic, local(): group_stencil(grouped, kernel_mine, height, breadth).astype(jnp.bfloat16)  50.4 us
    convert_element_type x1, other arithmetic, local(): group_stencil(pad_groups(grad_groups), flipped_mine, height, breadth)  50 us
    reduce_sum x4, other arithmetic, group_taps(): columns.append(jnp.sum(gradient * window, axis=(1, 2)))  30.5 us
    all_to_all x1, blocking collectives, from_groups(): lax.all_to_all(packed.reshape(row_count * col_count, group_size, pixels),...  24.6 us
    all_to_all x2, waiting for transfers between devices, to_groups(): lax.all_to_all(packed.reshape(row_count * col_count, group_size, pixels),...  22.5 us
    another operation x4, local copies, waits for them, and re-layouts, from_groups(): packed.reshape(row_count * col_count, group_size, pixels)  19.2 us
  transfers between devices with their start and end apart: 8, of which 2 were waited for; matrix products, arithmetic and copies ran while one was open for 50% of the time, Pallas kernels for 0%

commit v1 on v0

v1 whole, which is shorter than its diff:
```python
import math

import jax
import jax.numpy as jnp
from jax import lax
from jax.sharding import PartitionSpec as P

KSIZE = 7
DILATE = 2
REACH = 6


EPSILON = 1e-06
CONTRACT_ROWS = (((0,), (0,)), ((), ()))
CONTRACT_COLS = (((1,), (1,)), ((), ()))


def normal_cdf(values):
    return 0.5 * (1.0 + jax.scipy.special.erf(values * 0.7071067811865476))


def gelu_exact(values):
    return values * normal_cdf(values)


def gelu_slope(values):
    return normal_cdf(values) + values * jnp.exp(-0.5 * values * values) * 0.3989422804014327


def shift_pairs(count, step):
    if step > 0:
        return [(i, i + 1) for i in range(count - 1)]
    return [(i + 1, i) for i in range(count - 1)]


def add_halo(field):
    row_count = lax.axis_size("row")
    col_count = lax.axis_size("col")
    left = lax.ppermute(field[:, -REACH:, :], "col", shift_pairs(col_count, 1))
    right = lax.ppermute(field[:, :REACH, :], "col", shift_pairs(col_count, -1))
    wide = jnp.concatenate([left, field, right], axis=1)
    top = lax.ppermute(wide[-REACH:], "row", shift_pairs(row_count, 1))
    bottom = lax.ppermute(wide[:REACH], "row", shift_pairs(row_count, -1))
    return jnp.concatenate([top, wide, bottom], axis=0)


def tile_stencil(padded, tap_table, height, breadth):
    summed = jnp.zeros((height, breadth, tap_table.shape[0]), jnp.float32)
    for tap_row in range(KSIZE):
        for tap_col in range(KSIZE):
            window = padded[
                DILATE * tap_row : DILATE * tap_row + height,
                DILATE * tap_col : DILATE * tap_col + breadth,
                :,
            ].astype(jnp.float32)
            summed = summed + tap_table[:, KSIZE * tap_row + tap_col] * window
    return summed


def tile_taps(padded, gradient, height, breadth):
    columns = []
    for tap_row in range(KSIZE):
        for tap_col in range(KSIZE):
            window = padded[
                DILATE * tap_row : DILATE * tap_row + height,
                DILATE * tap_col : DILATE * tap_col + breadth,
                :,
            ].astype(jnp.float32)
            columns.append(jnp.sum(gradient * window, axis=(0, 1)))
    return jnp.stack(columns, axis=1)


def local(image, dw_kernel, ln_gain, w_in, b_in, w_out, layer_scale, cotangent):
    tile_rows, tile_cols, channels = image.shape
    row_count = lax.axis_size("row")
    col_count = lax.axis_size("col")
    group_count = row_count * col_count
    group_size = channels // group_count
    pixels = tile_rows * tile_cols
    scale_factor = 1.0 / math.sqrt(pixels * group_count)
    full_in, full_out = (
        lax.all_gather(w_in, "col", axis=0, tiled=True),
        lax.all_gather(w_out, "col", axis=0, tiled=True),
    )
    flipped = dw_kernel.reshape(channels, KSIZE, KSIZE)[:, ::-1, ::-1].reshape(
        channels, KSIZE * KSIZE
    )
    group_index = lax.axis_index("row") * col_count + lax.axis_index("col")
    padded = add_halo(image)
    conv_tile = tile_stencil(padded, dw_kernel, tile_rows, tile_cols).astype(jnp.bfloat16)
    conv_rows = conv_tile.astype(jnp.float32).reshape(pixels, channels)
    average = jnp.mean(conv_rows, axis=1, keepdims=True)
    centered = conv_rows - average
    inverse = lax.rsqrt(jnp.mean(centered * centered, axis=1, keepdims=True) + EPSILON)
    standard = centered * inverse
    normed = (standard * ln_gain).astype(jnp.bfloat16)
    preact = jnp.dot(normed, full_in, preferred_element_type=jnp.float32) + b_in
    hidden = gelu_exact(preact).astype(jnp.bfloat16)
    mixed = jnp.dot(hidden, full_out, preferred_element_type=jnp.float32)
    out_map = (image.reshape(pixels, channels).astype(jnp.float32) + layer_scale * mixed).astype(
        jnp.bfloat16
    )
    out_map = out_map.reshape(tile_rows, tile_cols, channels)
    upstream = cotangent.reshape(pixels, channels).astype(jnp.float32)
    scale_part = jnp.sum(upstream * mixed, axis=0)
    grad_mix = (upstream * layer_scale).astype(jnp.bfloat16)
    grad_hidden = lax.dot_general(
        grad_mix, full_out, CONTRACT_COLS, preferred_element_type=jnp.float32
    )
    grad_pre = grad_hidden * gelu_slope(preact)
    bias_part = jnp.sum(grad_pre, axis=0)
    grad_pre_rounded = grad_pre.astype(jnp.bfloat16)
    grad_norm = lax.dot_general(
        grad_pre_rounded, full_in, CONTRACT_COLS, preferred_element_type=jnp.float32
    )
    part_in = lax.psum_scatter(
        lax.dot_general(
            normed, grad_pre_rounded, CONTRACT_ROWS, preferred_element_type=jnp.float32
        ),
        "col",
        scatter_dimension=0,
        tiled=True,
    )
    part_out = lax.psum_scatter(
        lax.dot_general(hidden, grad_mix, CONTRACT_ROWS, preferred_element_type=jnp.float32),
        "col",
        scatter_dimension=0,
        tiled=True,
    )
    summed_in, summed_out = lax.psum((part_in, part_out), "row")
    gain_part = jnp.sum(grad_norm * standard, axis=0)
    scaled = grad_norm * ln_gain
    grad_conv = (
        (
            scaled
            - jnp.mean(scaled, axis=1, keepdims=True)
            - standard * jnp.mean(scaled * standard, axis=1, keepdims=True)
        )
        * inverse
    ).astype(jnp.bfloat16)
    grad_conv = grad_conv.reshape(tile_rows, tile_cols, channels)
    grad_padded = add_halo(grad_conv)
    grad_back = tile_stencil(grad_padded, flipped, tile_rows, tile_cols).astype(jnp.bfloat16)
    kernel_part = tile_taps(padded, grad_conv.astype(jnp.float32), tile_rows, tile_cols)
    grad_image = (cotangent.astype(jnp.float32) + grad_back.astype(jnp.float32)).astype(
        jnp.bfloat16
    )
    scale_sum, bias_sum, gain_sum, kernel_sum = lax.psum(
        (scale_part, bias_part, gain_part, kernel_part), ("row", "col")
    )
    grad_kernel = (
        lax.dynamic_slice_in_dim(kernel_sum, group_index * group_size, group_size, 0)
        * scale_factor
    )
    return (
        out_map,
        grad_image,
        grad_kernel,
        summed_in * scale_factor,
        summed_out * scale_factor,
        bias_sum * scale_factor,
        gain_sum * scale_factor,
        scale_sum * scale_factor,
    )


def solution(mesh):
    in_specs = (
        P("row", "col", None),
        P(),
        P(),
        P("col", None),
        P(),
        P("col", None),
        P(),
        P("row", "col", None),
    )
    out_specs = (
        P("row", "col", None),
        P("row", "col", None),
        P(("row", "col"), None),
        P("col", None),
        P("col", None),
        P(),
        P(),
        P(),
    )
    return jax.shard_map(local, mesh=mesh, in_specs=in_specs, out_specs=out_specs, check_vma=False)
```

time: 488 us -> 556 us (1.14)
  waiting for transfers between devices: 76.1 us -> 349 us
  other arithmetic: 143 us -> 55.1 us
  local copies, waits for them, and re-layouts: 80.4 us -> 13 us
  blocking collectives: 103 us -> 68.9 us
  starting transfers between devices: 23.9 us -> 15.1 us
    reduce_scatter x2, waiting for transfers between devices: 0.01 us -> 176 us  [the longest x1 90.5 us: local(): lax.psum_scatter(lax.dot_general(normed, grad_pre_rounded, CONTRACT_ROWS,...]
    convert_element_type x3 -> x1, other arithmetic: 102 us -> 2.33 us  [local(): normed = (standard * ln_gain).astype(jnp.bfloat16)]
    all_gather x1, waiting for transfers between devices: 0.01 us -> 48.6 us  [local(): lax.all_gather(w_out, 'col', axis=0, tiled=True)]
    psum x0 -> x1, waiting for transfers between devices: none -> 45.6 us  [local(): lax.psum((scale_part, bias_part, gain_part, kernel_part), ('row', 'col'))]
    another operation x58 -> x50, local copies, waits for them, and re-layouts: 35.4 us -> 4.72 us  [tile_taps(): return jnp.stack(columns, axis=1)]
    all_to_all x1 -> x0, blocking collectives: 24.6 us -> none  [from_groups(): lax.all_to_all(packed.reshape(row_count * col_count, group_size, pixels),...]
    all_to_all x3 -> x0, starting transfers between devices: 23.4 us -> none  [the longest x2 16.9 us: to_groups(): lax.all_to_all(packed.reshape(row_count * col_count, group_size, pixels),...]
    all_to_all x3 -> x0, waiting for transfers between devices: 22.5 us -> none  [the longest x2 22.5 us: to_groups(): lax.all_to_all(packed.reshape(row_count * col_count, group_size, pixels),...]
  transfers between devices with their start and end apart: 8 -> 14, of which waited for: 2 -> 9; matrix products, arithmetic and copies ran while one was open for 50% -> 12% of each run, Pallas kernels for 0% -> 0%
where the time goes in v1:
time: 556 us; the launch traced here: 555 us
  waiting for transfers between devices  349 us (63%)
  blocking collectives  68.9 us (12%)
  other arithmetic  55.1 us (10%)
  matrix products  39.1 us (7%)
  starting transfers between devices  15.1 us (3%)
  between operations  14.9 us (3%)
  local copies, waits for them, and re-layouts  13 us (2%)
    reduce_scatter x1, waiting for transfers between devices, local(): lax.psum_scatter(lax.dot_general(normed, grad_pre_rounded, CONTRACT_ROWS,...  90.5 us
    reduce_scatter x1, waiting for transfers between devices, local(): lax.psum_scatter(lax.dot_general(hidden, grad_mix, CONTRACT_ROWS, preferr...  85.6 us
    psum x1, blocking collectives, local(): lax.psum((scale_part, bias_part, gain_part, kernel_part), ('row', 'col'))  68.9 us
    psum x1, waiting for transfers between devices, local(): summed_in, summed_out = lax.psum((part_in, part_out), 'row')  48.7 us
    all_gather x1, waiting for transfers between devices, local(): lax.all_gather(w_out, 'col', axis=0, tiled=True)  48.6 us
    psum x1, waiting for transfers between devices, local(): lax.psum((scale_part, bias_part, gain_part, kernel_part), ('row', 'col'))  45.6 us
    all_gather x1, waiting for transfers between devices, local(): lax.all_gather(w_in, 'col', axis=0, tiled=True)  18.7 us
    convert_element_type x1, other arithmetic, local(): (cotangent.astype(jnp.float32) + grad_back.astype(jnp.float32)).astype(jn...  16.5 us
  transfers between devices with their start and end apart: 14, of which 9 were waited for; matrix products, arithmetic and copies ran while one was open for 12% of the time, Pallas kernels for 0%

profile of v1, /device:TPU:0, one launch (start us, length us, event | category | flops | bytes accessed | tf_op | source)
XLA Modules:
  0.0 555.0 jit_solution(15932435085616703313)
XLA Ops:
  7.2 0.7 all-gather.3.cloned.1.call-update
  8.0 0.7 all-gather.5.cloned.1.call-update
  8.7 1.1 fusion.146
  9.8 3.6 collective-permute-start
  13.4 1.3 collective-permute-start.1
  14.7 1.4 slice_reduce_fusion.96
  16.1 1.4 collective-permute-done
  17.5 4.1 collective-permute-done.1
  22.0 1.4 collective-permute-start.2
  23.4 1.3 collective-permute-start.3
  25.1 4.1 collective-permute-done.3
  29.3 1.3 maximum_maximum_fusion
  30.6 12.9 %convert_reduce_fusion = (f32[16,32]{1,0:T(8,128)S(1)}, bf16[16,32,768]{2,1,0:T(8,128)(2,1)}) fusion(bf16[22,44,768]{2,1,0:T(8,128)(2,1)S(1)} %get-tuple-element.191, f32[768]{0:T(1024)S(1)} %get-tuple-element.175, f32[768]{0:T(1024)S(1)} %get-tuple-element.128, f32[768]{0:T(1024)S(1)} %get-tuple-element.129, f32[768]{0:T(1024)S(1)} %get-tuple-element.130, ...), kind=kLoop, calls=%fused_computation.260 | loop fusion | flops 62127616 | bytes 37262336 | tf_op jit(solution)/shard_map/reduce_sum | solution.py:92
  43.6 1.6 multiply_reduce_fusion.2
  45.3 2.3 multiply_convert_fusion.2
  47.7 18.7 %all-gather.3.cloned.1.call-done = bf16[768,3072]{1,0:T(8,128)(2,1)} async-done(((bf16[48,3072]{1,0:T(8,128)(2,1)}), bf16[768,3072]{1,0:T(8,128)(2,1)}) %all-gather.3.cloned.1.call-update) | async-done | bytes 4718608 | tf_op jit(solution)/shard_map/all_gather | solution.py:82
  66.4 7.0 %multiply_convert_fusion = (bf16[512,3072]{1,0:T(8,128)(2,1)}, f32[512,3072]{1,0:T(8,128)}) fusion(f32[3072]{0:T(1024)S(1)} %copy-done.20, bf16[512,768]{1,0:T(8,128)(2,1)} %multiply_convert_fusion.2, bf16[768,3072]{1,0:T(8,128)(2,1)} %all-gather.3.cloned.1.call-done), kind=kOutput, calls=%fused_computation.56 | convolution fusion | flops 2425356288 | bytes 14954496 | tf_op jit(solution)/shard_map/dot_general | solution.py:97
  73.4 48.6 %all-gather.5.cloned.1.call-done = bf16[3072,768]{1,0:T(8,128)(2,1)} async-done(((bf16[192,768]{1,0:T(8,128)(2,1)}), bf16[3072,768]{1,0:T(8,128)(2,1)}) %all-gather.5.cloned.1.call-update) | async-done | bytes 4718608 | tf_op jit(solution)/shard_map/all_gather | solution.py:83
  122.0 8.0 %fusion.129 = (f32[768]{0:T(1024)}, bf16[512,768]{1,0:T(8,128)(2,1)}, bf16[512,768]{1,0:T(8,128)(2,1)S(1)}) fusion(bf16[16,32,768]{2,1,0:T(8,128)(2,1)} %param.15, f32[768]{0:T(1024)S(1)} %copy-done.21, bf16[16,32,768]{2,1,0:T(8,128)(2,1)} %param.8, bf16[512,3072]{1,0:T(8,128)(2,1)} %get-tuple-element.199, bf16[3072,768]{1,0:T(8,128)(2,1)} %all-gather.5.cloned.1.call-done), kind=kOutput, calls=%fused_computation.237 | convolution fusion | flops 2419457280 | bytes 11016192 | tf_op jit(solution)/shard_map/dot_general | solution.py:99
  130.0 5.3 fusion.147
  135.3 3.5 multiply_reduce_fusion
  138.8 5.1 fusion.126
  143.9 4.2 fusion.98
  148.1 3.1 fusion.108
  151.7 4.5 stack.199
  156.3 8.4 %fusion.148 = f32[3072,768]{1,0:T(8,128)} fusion(bf16[512,3072]{1,0:T(8,128)(2,1)} %get-tuple-element.199, bf16[512,768]{1,0:T(8,128)(2,1)} %copy-done.22), kind=kOutput, calls=%fused_computation.395 | convolution fusion | flops 2415919104 | bytes 13369344 | tf_op jit(solution)/shard_map/dot_general | solution.py:125
  164.8 1.1 copy-done.8
  165.8 7.0 %fusion.132 = f32[768,3072]{1,0:T(8,128)} fusion(bf16[512,768]{1,0:T(8,128)(2,1)S(1)} %copy-done.8, bf16[512,3072]{1,0:T(8,128)(2,1)} %copy-done.9), kind=kOutput, calls=%fused_computation.245 | convolution fusion | flops 2415919104 | bytes 13369344 | tf_op jit(solution)/shard_map/dot_general | solution.py:117
  172.9 0.8 copy-done.12
  174.2 3.3 collective-permute-start.4
  177.6 1.3 collective-permute-start.5
  178.9 0.7 slice_reduce_fusion.46
  179.6 0.7 slice_reduce_fusion.47
  180.3 68.9 %all-reduce = (f32[3072]{0:T(1024)S(1)}, f32[768]{0:T(1024)S(1)}, f32[768]{0:T(1024)S(1)}) all-reduce(f32[3072]{0:T(1024)S(1)} %copy-done.16, f32[768]{0:T(1024)S(1)} %copy-done.18, f32[768]{0:T(1024)S(1)} %copy-done.17), channel_id=1, replica_groups=mesh['row'=8,'col'=16] {'row','col'}, use_global_device_ids=true, to_apply=%region_59.0 | all-reduce | flops 4608 | bytes 36864 | tf_op jit(solution)/shard_map/psum | solution.py:148
  249.6 1.3 collective-permute-start.6
  250.9 1.3 collective-permute-start.7
  252.8 0.6 broadcast_multiply_fusion.2
  253.4 45.6 %all-reduce.5.cloned.1.call-done = f32[768,49]{0,1:T(8,128)} async-done(((f32[768,49]{0,1:T(8,128)}), f32[768,49]{0,1:T(8,128)}) %all-reduce.5.cloned.1.call-update) | async-done | bytes 150544 | tf_op jit(solution)/shard_map/psum | solution.py:148
  299.0 0.9 dynamic-slice_multiply_fusion
  299.9 0.7 copy.16
  300.6 0.8 copy-done.14
  301.3 2.7 maximum_maximum_fusion.1
  304.0 85.6 %reduce-scatter.5.cloned.1.call-done = f32[192,768]{1,0:T(8,128)} async-done(((f32[3072,768]{1,0:T(8,128)}), f32[192,768]{1,0:T(8,128)}) %reduce-scatter.5.cloned.1.call-update) | async-done | bytes 589840 | tf_op jit(solution)/shard_map/reduce_scatter | solution.py:124
  389.6 90.5 %reduce-scatter.3.cloned.1.call-done = f32[48,3072]{1,0:T(8,128)} async-done(((f32[768,3072]{1,0:T(8,128)}), f32[48,3072]{1,0:T(8,128)}) %reduce-scatter.3.cloned.1.call-update) | async-done | bytes 589840 | tf_op jit(solution)/shard_map/reduce_scatter | solution.py:116
  480.1 16.5 %fusion.127 = bf16[16,32,768]{2,1,0:T(8,128)(2,1)} fusion(bf16[16,32,768]{2,1,0:T(8,128)(2,1)} %param.15, bf16[22,44,768]{2,1,0:T(8,128)(2,1)S(1)} %get-tuple-element.187, f32[768]{0:T(1024)S(1)} %get-tuple-element.79, f32[768]{0:T(1024)S(1)} %get-tuple-element.80, f32[768]{0:T(1024)S(1)} %get-tuple-element.81, f32[768]{0:T(1024)S(1)} %get-tuple-element.82, ...), kind=kLoop, calls=%fused_computation.235 | loop fusion | flops 66453504 | bytes 35834880 | tf_op jit(solution)/shard_map/convert_element_type | solution.py:145
  496.6 48.7 %all-reduce.7.cloned.1.call-done = (f32[48,3072]{1,0:T(8,128)}, f32[192,768]{1,0:T(8,128)}) async-done(((f32[48,3072]{1,0:T(8,128)}, f32[192,768]{1,0:T(8,128)}), (f32[48,3072]{1,0:T(8,128)}, f32[192,768]{1,0:T(8,128)})) %all-reduce.7.cloned.1.call-update) | async-done | bytes 1179664 | tf_op jit(solution)/shard_map/psum | solution.py:130
  545.3 2.0 broadcast_multiply_fusion
  547.3 0.9 broadcast_multiply_fusion.1
  (131 shorter events, 2.8 us)
Async XLA Ops:
  7.2 14.5 %copy-start.4 = (bf16[16,32,768]{2,1,0:T(8,128)(2,1)S(1)}, bf16[16,32,768]{2,1,0:T(8,128)(2,1)}, u32[]{:S(2)}) copy-start(bf16[16,32,768]{2,1,0:T(8,128)(2,1)} %param.8) | copy-start | bytes 2359300
  7.2 59.2 %all-gather.3.cloned.1.call-start = ((), (), s32[]{:S(2)}) async-start(), calls=%async_computation.2 | async-start | bytes 5013504 | tf_op jit(solution)/shard_map/all_gather | solution.py:82
  7.9 16.8 %copy-start.11 = (f32[768,49]{0,1:T(8,128)S(1)}, f32[768,49]{0,1:T(8,128)}, u32[]{:S(2)}) copy-start(f32[768,49]{0,1:T(8,128)} %param.9) | copy-start | bytes 451588
  7.9 114.0 %all-gather.5.cloned.1.call-start = ((), (), s32[]{:S(2)}) async-start(), calls=%async_computation.3 | async-start | bytes 5013504 | tf_op jit(solution)/shard_map/all_gather | solution.py:83
  8.7 290.3 %all-reduce.5.cloned.1.call-start = ((), (), s32[]{:S(2)}) async-start(), calls=%async_computation.4 | async-start | bytes 344064 | tf_op jit(solution)/shard_map/psum | solution.py:148
  9.8 7.7 %collective-permute-start = (bf16[16,6,768]{2,1,0:T(8,128)(2,1)S(1)}, bf16[16,6,768]{2,1,0:T(8,128)(2,1)S(1)}, u32[]{:S(2)}, u32[]{:S(2)}) collective-permute-start(bf16[16,6,768]{2,1,0:T(8,128)(2,1)S(1)} %get-tuple-element.197), channel_id=1, source_target_pairs={{0,1},{1,2},{2,3},{3,4},{4,5},{5,6},{6,7},{7,8},{8,9},{9,10},{10,1... | collective-permute-start | bytes 442376 | tf_op jit(solution)/shard_map/ppermute | solution.py:39
  13.4 8.3 %collective-permute-start.1 = (bf16[16,6,768]{2,1,0:T(8,128)(2,1)S(1)}, bf16[16,6,768]{2,1,0:T(8,128)(2,1)S(1)}, u32[]{:S(2)}, u32[]{:S(2)}) collective-permute-start(bf16[16,6,768]{2,1,0:T(8,128)(2,1)S(1)} %get-tuple-element.198), channel_id=1, source_target_pairs={{1,0},{2,1},{3,2},{4,3},{5,4},{6,5},{7,6},{8,7},{9,8},{10,9},{11,1... | collective-permute-start | bytes 442376 | tf_op jit(solution)/shard_map/ppermute | solution.py:40
  22.0 7.3 %copy-start.5 = (bf16[16,32,768]{2,1,0:T(8,128)(2,1)S(1)}, bf16[16,32,768]{2,1,0:T(8,128)(2,1)}, u32[]{:S(2)}) copy-start(bf16[16,32,768]{2,1,0:T(8,128)(2,1)} %param.8) | copy-start | bytes 2359300
  22.0 3.1 collective-permute-start.2
  23.4 5.8 %collective-permute-start.3 = (bf16[6,44,768]{2,1,0:T(8,128)(2,1)S(1)}, bf16[6,44,768]{2,1,0:T(8,128)(2,1)S(1)}, u32[]{:S(2)}, u32[]{:S(2)}) collective-permute-start(bf16[6,44,768]{2,1,0:T(8,128)(2,1)S(1)} %get-tuple-element.193), channel_id=1, source_target_pairs={{16,0},{32,16},{48,32},{64,48},{80,64},{96,80},{112,96},{17,1},{33... | collective-permute-start | bytes 1216520 | tf_op jit(solution)/shard_map/ppermute | solution.py:43
  25.1 5.5 copy-start.2
  30.6 14.7 %copy-start.15 = (f32[768]{0:T(1024)S(1)}, f32[768]{0:T(1024)}, u32[]{:S(2)}) copy-start(f32[768]{0:T(1024)} %param.10) | copy-start | bytes 9220
  43.5 22.9 %copy-start.20 = (f32[3072]{0:T(1024)S(1)}, f32[3072]{0:T(1024)}, u32[]{:S(2)}) copy-start(f32[3072]{0:T(1024)} %param.12) | copy-start | bytes 36868
  47.7 74.3 %copy-start.21 = (f32[768]{0:T(1024)S(1)}, f32[768]{0:T(1024)}, u32[]{:S(2)}) copy-start(f32[768]{0:T(1024)} %param.14) | copy-start | bytes 9220
  122.0 8.0 %copy-start.19 = (bf16[3072,768]{1,0:T(8,128)(2,1)S(1)}, bf16[3072,768]{1,0:T(8,128)(2,1)}, u32[]{:S(2)}) copy-start(bf16[3072,768]{1,0:T(8,128)(2,1)} %all-gather.5.cloned.1.call-done) | copy-start | bytes 14155780
  122.0 8.0 %copy-start.23 = (f32[512,3072]{1,0:T(8,128)S(1)}, f32[512,3072]{1,0:T(8,128)}, u32[]{:S(2)}) copy-start(f32[512,3072]{1,0:T(8,128)} %get-tuple-element.200) | copy-start | bytes 18874372
  122.0 13.3 %slice-start = ((s8[4718592]{0:T(1024)(128)(4,1)}), s8[4194304]{0:T(1024)(128)(4,1)S(1)}, s32[]{:S(2)}) async-start(s8[4718592]{0:T(1024)(128)(4,1)} %bitcast.95), calls=%async_computation.8 | async-start | bytes 8388608
  130.0 5.3 copy-start.22
  130.0 5.3 copy-start.7
  130.0 5.3 slice-start.1
  135.3 3.5 copy-start.9
  143.8 4.2 copy-start
  143.9 4.2 copy-start.3
  143.9 4.2 copy-start.6
  156.3 233.3 %reduce-scatter.5.cloned.1.call-start = ((), (), s32[]{:S(2)}) async-start(), calls=%async_computation.6 | async-start | bytes 10027008 | tf_op jit(solution)/shard_map/reduce_scatter | solution.py:124
  164.7 1.1 copy-start.8
  164.7 315.4 %reduce-scatter.3.cloned.1.call-start = ((), (), s32[]{:S(2)}) async-start(), calls=%async_computation.5 | async-start | bytes 10027008 | tf_op jit(solution)/shard_map/reduce_scatter | solution.py:116
  172.8 0.9 copy-start.12
  172.8 1.4 copy-start.1
  172.8 7.5 %copy-start.16 = (f32[3072]{0:T(1024)S(1)}, f32[3072]{0:T(1024)}, u32[]{:S(2)}) copy-start(f32[3072]{0:T(1024)} %get-tuple-element.202) | copy-start | bytes 36868
  172.9 7.5 %copy-start.17 = (f32[768]{0:T(1024)S(1)}, f32[768]{0:T(1024)}, u32[]{:S(2)}) copy-start(f32[768]{0:T(1024)} %get-tuple-element.184) | copy-start | bytes 9220
  172.9 7.5 %copy-start.18 = (f32[768]{0:T(1024)S(1)}, f32[768]{0:T(1024)}, u32[]{:S(2)}) copy-start(f32[768]{0:T(1024)} %get-tuple-element.58) | copy-start | bytes 9220
  172.9 372.4 %all-reduce.7.cloned.1.call-start = ((), (), s32[]{:S(2)}) async-start(), calls=%async_computation.7 | async-start | bytes 2359296 | tf_op jit(solution)/shard_map/psum | solution.py:130
  174.2 75.0 %collective-permute-start.4 = (bf16[16,6,768]{2,1,0:T(8,128)(2,1)S(1)}, bf16[16,6,768]{2,1,0:T(8,128)(2,1)S(1)}, u32[]{:S(2)}, u32[]{:S(2)}) collective-permute-start(bf16[16,6,768]{2,1,0:T(8,128)(2,1)S(1)} %get-tuple-element.195), channel_id=1, source_target_pairs={{0,1},{1,2},{2,3},{3,4},{4,5},{5,6},{6,7},{7,8},{8,9},{9,10},{10,1... | collective-permute-start | bytes 442376 | tf_op jit(solution)/shard_map/ppermute | solution.py:39
  177.6 71.7 %collective-permute-start.5 = (bf16[16,6,768]{2,1,0:T(8,128)(2,1)S(1)}, bf16[16,6,768]{2,1,0:T(8,128)(2,1)S(1)}, u32[]{:S(2)}, u32[]{:S(2)}) collective-permute-start(bf16[16,6,768]{2,1,0:T(8,128)(2,1)S(1)} %get-tuple-element.196), channel_id=1, source_target_pairs={{1,0},{2,1},{3,2},{4,3},{5,4},{6,5},{7,6},{8,7},{9,8},{10,9},{11,1... | collective-permute-start | bytes 442376 | tf_op jit(solution)/shard_map/ppermute | solution.py:40
  249.2 51.3 %copy-start.10 = (bf16[16,6,768]{2,1,0:T(8,128)(2,1)}, bf16[16,6,768]{2,1,0:T(8,128)(2,1)S(1)}, u32[]{:S(2)}) copy-start(bf16[16,6,768]{2,1,0:T(8,128)(2,1)S(1)} %collective-permute-done.5) | copy-start | bytes 442372
  249.6 51.0 %collective-permute-start.6 = (bf16[6,44,768]{2,1,0:T(8,128)(2,1)S(1)}, bf16[6,44,768]{2,1,0:T(8,128)(2,1)S(1)}, u32[]{:S(2)}, u32[]{:S(2)}) collective-permute-start(bf16[6,44,768]{2,1,0:T(8,128)(2,1)S(1)} %get-tuple-element.188), channel_id=1, source_target_pairs={{0,16},{16,32},{32,48},{48,64},{64,80},{80,96},{96,112},{1,17},{17... | collective-permute-start | bytes 1216520 | tf_op jit(solution)/shard_map/ppermute | solution.py:42
  250.9 50.5 %collective-permute-start.7 = (bf16[6,44,768]{2,1,0:T(8,128)(2,1)S(1)}, bf16[6,44,768]{2,1,0:T(8,128)(2,1)}, u32[]{:S(2)}, u32[]{:S(2)}) collective-permute-start(bf16[6,44,768]{2,1,0:T(8,128)(2,1)S(1)} %get-tuple-element.189), channel_id=1, source_target_pairs={{16,0},{32,16},{48,32},{64,48},{80,64},{96,80},{112,96},{17,1},{33... | collective-permute-start | bytes 1216520 | tf_op jit(solution)/shard_map/ppermute | solution.py:43
  300.6 0.8 copy-start.14
  545.3 2.0 copy-start.13
Sparse Core Ops, SparseCore 0:
  10.2 56.1 all-gather.2
  68.5 53.3 all-gather.4
  156.4 142.5 all-reduce.4
  302.3 87.1 reduce-scatter.4
  392.9 87.1 reduce-scatter.2
  482.4 62.8 all-reduce.6

commit v2 on v1

--- a/solution.py
+++ b/solution.py
@@ -33,14 +33,19 @@
     return [(i + 1, i) for i in range(count - 1)]
 
 
+ROW = ("z", "core")
+COL = "col"
+EVERY = ("z", "core", "col")
+
+
 def add_halo(field):
-    row_count = lax.axis_size("row")
-    col_count = lax.axis_size("col")
-    left = lax.ppermute(field[:, -REACH:, :], "col", shift_pairs(col_count, 1))
-    right = lax.ppermute(field[:, :REACH, :], "col", shift_pairs(col_count, -1))
+    row_count = lax.axis_size(ROW)
+    col_count = lax.axis_size(COL)
+    left = lax.ppermute(field[:, -REACH:, :], COL, shift_pairs(col_count, 1))
+    right = lax.ppermute(field[:, :REACH, :], COL, shift_pairs(col_count, -1))
     wide = jnp.concatenate([left, field, right], axis=1)
-    top = lax.ppermute(wide[-REACH:], "row", shift_pairs(row_count, 1))
-    bottom = lax.ppermute(wide[:REACH], "row", shift_pairs(row_count, -1))
+    top = lax.ppermute(wide[-REACH:], ROW, shift_pairs(row_count, 1))
+    bottom = lax.ppermute(wide[:REACH], ROW, shift_pairs(row_count, -1))
     return jnp.concatenate([top, wide, bottom], axis=0)
 
 
@@ -70,22 +75,50 @@
     return jnp.stack(columns, axis=1)
 
 
+def gather_weights(w_in, w_out):
+    row_block, ff = w_in.shape
+    core = lax.axis_index("core")
+    flat_in = w_in.reshape(-1)
+    flat_out = w_out.reshape(-1)
+    mine = jnp.where(core == 0, flat_in, flat_out)
+    across = lax.all_gather(mine, COL, axis=0, tiled=False)
+    both = lax.all_gather(across, "core", axis=0, tiled=False)
+    full_in = both[0].reshape(-1, ff)
+    full_out = both[1].reshape(-1, w_out.shape[1])
+    return full_in, full_out
+
+
+def reduce_grads(part_in, part_out, small):
+    col_count = lax.axis_size(COL)
+    rows_in = part_in.shape[0] // col_count
+    block_in = part_in.reshape(col_count, -1)
+    block_out = part_out.reshape(col_count, -1)
+    stacked = jnp.stack([block_in, block_out], axis=1)
+    halves = lax.psum_scatter(stacked, "core", scatter_dimension=1, tiled=True)
+    halves = halves.reshape(col_count * rows_in, -1)
+    mine = lax.psum_scatter(halves, COL, scatter_dimension=0, tiled=True)
+    mine = lax.psum(mine, "z")
+    pair = lax.all_gather(mine, "core", axis=0, tiled=False).reshape(2, -1)
+    grad_in_block = pair[0].reshape(-1, part_in.shape[1])
+    grad_out_block = pair[1].reshape(-1, part_out.shape[1])
+    small_all = lax.psum(small, EVERY)
+    return grad_in_block, grad_out_block, small_all
+
+
 def local(image, dw_kernel, ln_gain, w_in, b_in, w_out, layer_scale, cotangent):
     tile_rows, tile_cols, channels = image.shape
-    row_count = lax.axis_size("row")
-    col_count = lax.axis_size("col")
+    hidden_units = w_in.shape[1]
+    row_count = lax.axis_size(ROW)
+    col_count = lax.axis_size(COL)
     group_count = row_count * col_count
     group_size = channels // group_count
     pixels = tile_rows * tile_cols
     scale_factor = 1.0 / math.sqrt(pixels * group_count)
-    full_in, full_out = (
-        lax.all_gather(w_in, "col", axis=0, tiled=True),
-        lax.all_gather(w_out, "col", axis=0, tiled=True),
-    )
+    full_in, full_out = gather_weights(w_in, w_out)
     flipped = dw_kernel.reshape(channels, KSIZE, KSIZE)[:, ::-1, ::-1].reshape(
         channels, KSIZE * KSIZE
     )
-    group_index = lax.axis_index("row") * col_count + lax.axis_index("col")
+    group_index = lax.axis_index(EVERY)
     padded = add_halo(image)
     conv_tile = tile_stencil(padded, dw_kernel, tile_rows, tile_cols).astype(jnp.bfloat16)
     conv_rows = conv_tile.astype(jnp.float32).reshape(pixels, channels)
@@ -113,21 +146,10 @@
     grad_norm = lax.dot_general(
         grad_pre_rounded, full_in, CONTRACT_COLS, preferred_element_type=jnp.float32
     )
-    part_in = lax.psum_scatter(
-        lax.dot_general(
-            normed, grad_pre_rounded, CONTRACT_ROWS, preferred_element_type=jnp.float32
-        ),
-        "col",
-        scatter_dimension=0,
-        tiled=True,
-    )
-    part_out = lax.psum_scatter(
-        lax.dot_general(hidden, grad_mix, CONTRACT_ROWS, preferred_element_type=jnp.float32),
-        "col",
-        scatter_dimension=0,
-        tiled=True,
-    )
-    summed_in, summed_out = lax.psum((part_in, part_out), "row")
+    part_in = lax.dot_general(
+        normed, grad_pre_rounded, CONTRACT_ROWS, preferred_element_type=jnp.float32
+    )
+    part_out = lax.dot_general(hidden, grad_mix, CONTRACT_ROWS, preferred_element_type=jnp.float32)
     gain_part = jnp.sum(grad_norm * standard, axis=0)
     scaled = grad_norm * ln_gain
     grad_conv = (
@@ -145,9 +167,15 @@
     grad_image = (cotangent.astype(jnp.float32) + grad_back.astype(jnp.float32)).astype(
         jnp.bfloat16
     )
-    scale_sum, bias_sum, gain_sum, kernel_sum = lax.psum(
-        (scale_part, bias_part, gain_part, kernel_part), ("row", "col")
-    )
+    small = jnp.concatenate(
+        [scale_part, bias_part, gain_part, kernel_part.reshape(-1)]
+    )
+    grad_in_block, grad_out_block, small_sum = reduce_grads(part_in, part_out, small)
+    scale_sum = small_sum[:channels]
+    bias_sum = small_sum[channels : channels + hidden_units]
+    gain_sum = small_sum[channels + hidden_units : 2 * channels + hidden_units]
+    kernel_sum = small_sum[2 * channels + hidden_units : 2 * channels + hidden_units + channels * KSIZE * KSIZE]
+    kernel_sum = kernel_sum.reshape(channels, KSIZE * KSIZE)
     grad_kernel = (
         lax.dynamic_slice_in_dim(kernel_sum, group_index * group_size, group_size, 0)
         * scale_factor
@@ -156,8 +184,8 @@
         out_map,
         grad_image,
         grad_kernel,
-        summed_in * scale_factor,
-        summed_out * scale_factor,
+        grad_in_block * scale_factor,
+        grad_out_block * scale_factor,
         bias_sum * scale_factor,
         gain_sum * scale_factor,
         scale_sum * scale_factor,
@@ -165,24 +193,9 @@
 
 
 def solution(mesh):
-    in_specs = (
-        P("row", "col", None),
-        P(),
-        P(),
-        P("col", None),
-        P(),
-        P("col", None),
-        P(),
-        P("row", "col", None),
-    )
-    out_specs = (
-        P("row", "col", None),
-        P("row", "col", None),
-        P(("row", "col"), None),
-        P("col", None),
-        P("col", None),
-        P(),
-        P(),
-        P(),
-    )
+    devices = mesh.devices.reshape(-1, 2, mesh.devices.shape[1])
+    mesh = jax.sharding.Mesh(devices, EVERY)
+    tile = P(ROW, COL, None)
+    in_specs = (tile, P(), P(), P(COL, None), P(), P(COL, None), P(), tile)
+    out_specs = (tile, tile, P(EVERY, None), P(COL, None), P(COL, None), P(), P(), P())
     return jax.shard_map(local, mesh=mesh, in_specs=in_specs, out_specs=out_specs, check_vma=False)

time: 556 us -> 584 us (1.050)
  blocking collectives: 68.9 us -> 0 us
  local copies, waits for them, and re-layouts: 13 us -> 71.8 us
  other arithmetic: 55.1 us -> 74.9 us
  waiting for transfers between devices: 349 us -> 366 us
    psum x1 -> x0, blocking collectives: 68.9 us -> none  [local(): lax.psum((scale_part, bias_part, gain_part, kernel_part), ('row', 'col'))]
    psum x2, waiting for transfers between devices: 94.3 us -> 162 us  [the longest x1 122 us: reduce_grads(): small_all = lax.psum(small, EVERY)]
    reduce_scatter x2, waiting for transfers between devices: 176 us -> 110 us  [the longest x1 88 us: reduce_grads(): mine = lax.psum_scatter(halves, COL, scatter_dimension=0, tiled=True)]
    another operation x0 -> x4, local copies, waits for them, and re-layouts: none -> 31.9 us  [the longest x2 21.5 us: reduce_grads(): stacked = jnp.stack([block_in, block_out], axis=1)]
    another operation x0 -> x1, other arithmetic: none -> 14.7 us  [reduce_grads(): stacked = jnp.stack([block_in, block_out], axis=1)]
    unnamed x54 -> x42, local copies, waits for them, and re-layouts: 3.47 us -> 16.7 us
    reshape x0 -> x3, local copies, waits for them, and re-layouts: none -> 11.6 us  [the longest x1 10.9 us: reduce_grads(): halves = halves.reshape(col_count * rows_in, -1)]
    all_gather x2 -> x3, waiting for transfers between devices: 67.3 us -> 78 us  [the longest x1 78 us: gather_weights(): across = lax.all_gather(mine, COL, axis=0, tiled=False)]
  transfers between devices with their start and end apart: 14 -> 15, of which waited for: 9 -> 10; matrix products, arithmetic and copies ran while one was open for 12% -> 12% of each run, Pallas kernels for 0% -> 0%
where the time goes in v2:
time: 584 us; the launch traced here: 577 us
  waiting for transfers between devices  366 us (63%)
  other arithmetic  74.9 us (13%)
  local copies, waits for them, and re-layouts  71.8 us (12%)
  matrix products  34.4 us (6%)
  between operations  15.4 us (3%)
  starting transfers between devices  14.9 us (3%)
    psum x1, waiting for transfers between devices, reduce_grads(): small_all = lax.psum(small, EVERY)  122 us
    reduce_scatter x1, waiting for transfers between devices, reduce_grads(): mine = lax.psum_scatter(halves, COL, scatter_dimension=0, tiled=True)  88 us
    all_gather x1, waiting for transfers between devices, gather_weights(): across = lax.all_gather(mine, COL, axis=0, tiled=False)  78 us
    psum x1, waiting for transfers between devices, reduce_grads(): mine = lax.psum(mine, 'z')  40 us
    reduce_scatter x1, waiting for transfers between devices, reduce_grads(): halves = lax.psum_scatter(stacked, 'core', scatter_dimension=1, tiled=True)  21.9 us
    another operation x2, local copies, waits for them, and re-layouts, reduce_grads(): stacked = jnp.stack([block_in, block_out], axis=1)  21.5 us
    convert_element_type x1, other arithmetic, local(): (cotangent.astype(jnp.float32) + grad_back.astype(jnp.float32)).astype(jn...  16.7 us
    unnamed x42, local copies, waits for them, and re-layouts  16.7 us
  transfers between devices with their start and end apart: 15, of which 10 were waited for; matrix products, arithmetic and copies ran while one was open for 12% of the time, Pallas kernels for 0%

profile of v2, /device:TPU:0, one launch (start us, length us, event | category | flops | bytes accessed | tf_op | source)
XLA Modules:
  0.0 577.4 jit_solution(2598795604007122244)
XLA Ops:
  7.2 1.4 copy.19
  8.6 1.4 copy.20
  10.1 1.7 fusion.145
  11.8 78.0 %all-gather.10.cloned.1.call-done = bf16[16,1,147456]{2,1,0:T(2,128)(2,1)} async-done(((bf16[1,1,147456]{2,1,0:T(2,128)(2,1)}), bf16[16,1,147456]{2,1,0:T(2,128)(2,1)}) %all-gather.10.cloned.1.call-update) | async-done | bytes 4718608 | tf_op jit(solution)/shard_map/all_gather | solution.py:84
  89.8 11.1 %copy.22 = bf16[16,1,147456]{2,0,1:T(8,128)(2,1)} copy(bf16[16,1,147456]{2,1,0:T(2,128)(2,1)} %all-gather.10.cloned.1.call-done) | data formatting | bytes 9437184
  101.0 1.1 copy-done.4
  102.1 3.3 collective-permute-start
  105.4 1.3 collective-permute-start.1
  107.2 2.2 collective-permute-done
  109.4 4.1 collective-permute-done.1
  113.8 1.3 collective-permute-start.2
  115.2 1.3 collective-permute-start.3
  117.7 3.6 collective-permute-done.3
  121.3 1.5 maximum_maximum_fusion
  122.7 12.9 %convert_reduce_fusion = (f32[16,32]{1,0:T(8,128)S(1)}, bf16[16,32,768]{2,1,0:T(8,128)(2,1)}) fusion(bf16[22,44,768]{2,1,0:T(8,128)(2,1)S(1)} %get-tuple-element.182, f32[768]{0:T(1024)S(1)} %get-tuple-element.167, f32[768]{0:T(1024)S(1)} %get-tuple-element.120, f32[768]{0:T(1024)S(1)} %get-tuple-element.121, f32[768]{0:T(1024)S(1)} %get-tuple-element.122, ...), kind=kLoop, calls=%fused_computation.258 | loop fusion | flops 62127616 | bytes 37262336 | tf_op jit(solution)/shard_map/reduce_sum | solution.py:125
  135.8 1.5 multiply_reduce_fusion.2
  137.3 2.3 multiply_convert_fusion.3
  139.7 6.4 %fusion.148 = (bf16[16,147456]{1,0:T(8,128)(2,1)}, bf16[16,147456]{1,0:T(8,128)(2,1)}) fusion(bf16[32,147456]{1,0:T(8,128)(2,1)} %all-gather.8.cloned.1.call-done), kind=kLoop, calls=%fused_computation.401 | loop fusion | bytes 18874368 | tf_op jit(solution)/shard_map/slice | solution.py:87
  146.0 5.3 reshape_squeeze.9
  151.3 5.2 reshape_squeeze.8
  156.6 6.7 %multiply_convert_fusion = (bf16[512,3072]{1,0:T(8,128)(2,1)S(1)}, f32[512,3072]{1,0:T(8,128)}) fusion(f32[3072]{0:T(1024)S(1)} %copy-done.18, bf16[512,768]{1,0:T(8,128)(2,1)} %bitcast.117, bf16[768,3072]{1,0:T(8,128)(2,1)} %reshape_squeeze.8), kind=kOutput, calls=%fused_computation.57 | convolution fusion | flops 2425356288 | bytes 14954496 | tf_op jit(solution)/shard_map/dot_general | solution.py:130
  163.3 3.6 fusion.129
  166.9 5.1 fusion.152
  172.0 10.7 %stack_reshape.7 = f32[16,1,147456]{2,0,1:T(8,128)} reshape(f32[3072,768]{1,0:T(8,128)} %fusion.152) | data formatting | bytes 18874368 | tf_op jit(solution)/shard_map/stack;reshape | solution.py:96
  182.8 7.5 %fusion.151 = (f32[3072]{0:T(1024)S(1)}, bf16[512,3072]{1,0:T(8,128)(2,1)S(1)}) fusion(f32[512,3072]{1,0:T(8,128)} %get-tuple-element.194, f32[3072]{0:T(1024)S(1)} %copy-done.18, bf16[512,768]{1,0:T(8,128)(2,1)} %bitcast.116, bf16[3072,768]{1,0:T(8,128)(2,1)} %reshape_squeeze.9), kind=kOutput, calls=%fused_computation.404 | convolution fusion | flops 2434790400 | bytes 14966784 | tf_op jit(solution)/shard_map/dot_general | solution.py:140
  190.3 6.4 %multiply_reduce_fusion = (f32[768]{0:T(1024)S(1)}, f32[512]{0:T(512)S(1)}, f32[512]{0:T(512)S(1)}, bf16[512,768]{1,0:T(8,128)(2,1)S(1)}, f32[512,768]{1,0:T(8,128)}) fusion(bf16[16,32,768]{2,1,0:T(8,128)(2,1)S(1)} %copy-done.8, f32[512]{0:T(512)S(1)} %rsqrt.13, f32[512]{0:T(512)S(1)} %div.17, f32[768]{0:T(1024)S(1)} %copy-done.16, ...), kind=kOutput, calls=%fused_computation.247 | convolution fusion | flops 2420242688 | bytes 11024384 | tf_op jit(solution)/shard_map/dot_general | solution.py:146
  196.7 5.1 fusion.133
  201.8 10.7 %stack_reshape.6 = f32[16,1,147456]{2,0,1:T(8,128)} reshape(f32[768,3072]{1,0:T(8,128)} %fusion.133) | data formatting | bytes 18874368 | tf_op jit(solution)/shard_map/stack;reshape | solution.py:96
  212.5 14.7 %pad_maximum_fusion = f32[16,2,147456]{2,0,1:T(8,128)} fusion(f32[16,1,147456]{2,0,1:T(8,128)} %stack_reshape.7, f32[16,1,147456]{2,0,1:T(8,128)} %stack_reshape.6), kind=kLoop, calls=%fused_computation.50 | loop fusion | flops 4718592 | bytes 37748736 | tf_op jit(solution)/shard_map/stack | solution.py:96
  227.3 6.2 %fusion.126 = (f32[768]{0:T(1024)S(1)}, f32[768]{0:T(1024)S(1)}, f32[768]{0:T(1024)S(1)}, f32[768]{0:T(1024)S(1)}, f32[768]{0:T(1024)S(1)}, /*index=5*/f32[768]{...) fusion(bf16[22,44,768]{2,1,0:T(8,128)(2,1)S(1)} %get-tuple-elem, ...), kind=kLoop, calls=%fused_computation.233 | loop fusion | flops 25152000 | bytes 17368064 | tf_op jit(solution)/shard_map/reduce_sum | solution.py:74
  233.5 4.0 fusion.98
  237.5 3.1 fusion.108
  242.8 21.9 %reduce-scatter.3.cloned.1.call-done = f32[16,1,147456]{2,0,1:T(8,128)} async-done(((f32[16,2,147456]{2,0,1:T(8,128)}), f32[16,1,147456]{2,0,1:T(8,128)}) %reduce-scatter.3.cloned.1.call-update) | async-done | bytes 9437200 | tf_op jit(solution)/shard_map/reduce_scatter | solution.py:97
  264.7 10.9 %reshape.249 = f32[768,3072]{1,0:T(8,128)} reshape(f32[16,1,147456]{2,0,1:T(8,128)} %reduce-scatter.3.cloned.1.call-done) | data formatting | bytes 18874368 | tf_op jit(solution)/shard_map/reshape | solution.py:98
  277.0 3.5 collective-permute-start.4
  280.5 1.3 collective-permute-start.5
  283.2 1.8 collective-permute-done.4
  285.0 4.1 collective-permute-done.5
  289.4 1.3 collective-permute-start.6
  290.7 1.3 collective-permute-start.7
  292.0 122.1 %all-reduce.3.cloned.1.call-done = f32[42240]{0:T(1024)} async-done(((f32[42240]{0:T(1024)}), f32[42240]{0:T(1024)}) %all-reduce.3.cloned.1.call-update) | async-done | bytes 168976 | tf_op jit(solution)/shard_map/psum | solution.py:104
  414.1 1.3 slice_multiply_fusion.3
  416.8 88.0 %reduce-scatter.5.cloned.1.call-done = f32[48,3072]{1,0:T(8,128)} async-done(((f32[768,3072]{1,0:T(8,128)}), f32[48,3072]{1,0:T(8,128)}) %reduce-scatter.5.cloned.1.call-update) | async-done | bytes 589840 | tf_op jit(solution)/shard_map/reduce_scatter | solution.py:99
  505.5 1.3 slice_multiply_fusion.2
  507.5 2.7 maximum_maximum_fusion.1
  510.2 40.0 %all-reduce.5.cloned.1.call-done = f32[1,48,3072]{2,1,0:T(8,128)} async-done(((f32[1,48,3072]{2,1,0:T(8,128)}), f32[1,48,3072]{2,1,0:T(8,128)}) %all-reduce.5.cloned.1.call-update) | async-done | bytes 589840 | tf_op jit(solution)/shard_map/psum | solution.py:100
  550.2 16.7 %fusion.128 = bf16[16,32,768]{2,1,0:T(8,128)(2,1)} fusion(bf16[16,32,768]{2,1,0:T(8,128)(2,1)} %param.15, bf16[22,44,768]{2,1,0:T(8,128)(2,1)S(1)} %get-tuple-element.178, f32[768]{0:T(1024)S(1)} %get-tuple-element.71, f32[768]{0:T(1024)S(1)} %get-tuple-element.72, f32[768]{0:T(1024)S(1)} %get-tuple-element.73, f32[768]{0:T(1024)S(1)} %get-tuple-element.74, ...), kind=kLoop, calls=%fused_computation.239 | loop fusion | flops 66453504 | bytes 35834880 | tf_op jit(solution)/shard_map/convert_element_type | solution.py:167
  567.0 2.2 slice_multiply_fusion
  (134 shorter events, 11.0 us)
Async XLA Ops:
  7.2 82.7 %all-gather.10.cloned.1.call-start = ((), (), s32[]{:S(2)}) async-start(), calls=%async_computation.8 | async-start | bytes 10027008 | tf_op jit(solution)/shard_map/all_gather | solution.py:84
  11.8 127.9 %all-gather.8.cloned.1.call-start = ((), (), s32[]{:S(2)}) async-start(), calls=%async_computation.7 | async-start | bytes 14155776 | tf_op jit(solution)/shard_map/all_gather | solution.py:85
  100.9 1.1 copy-start.4
  100.9 5.8 %copy-start.13 = (f32[768,49]{0,1:T(8,128)S(1)}, f32[768,49]{0,1:T(8,128)}, u32[]{:S(2)}) copy-start(f32[768,49]{0,1:T(8,128)} %param.9) | copy-start | bytes 451588
  100.9 163.7 %reduce-scatter.3.cloned.1.call-start = ((), (), s32[]{:S(2)}) async-start(), calls=%async_computation.3 | async-start | bytes 28311552 | tf_op jit(solution)/shard_map/reduce_scatter | solution.py:97
  102.1 7.3 %collective-permute-start = (bf16[16,6,768]{2,1,0:T(8,128)(2,1)S(1)}, bf16[16,6,768]{2,1,0:T(8,128)(2,1)S(1)}, u32[]{:S(2)}, u32[]{:S(2)}) collective-permute-start(bf16[16,6,768]{2,1,0:T(8,128)(2,1)S(1)} %get-tuple-element.189), channel_id=1, source_target_pairs={{0,1},{1,2},{2,3},{3,4},{4,5},{5,6},{6,7},{7,8},{8,9},{9,10},{10,1... | collective-permute-start | bytes 442376 | tf_op jit(solution)/shard_map/ppermute | solution.py:44
  105.4 8.1 %collective-permute-start.1 = (bf16[16,6,768]{2,1,0:T(8,128)(2,1)S(1)}, bf16[16,6,768]{2,1,0:T(8,128)(2,1)S(1)}, u32[]{:S(2)}, u32[]{:S(2)}) collective-permute-start(bf16[16,6,768]{2,1,0:T(8,128)(2,1)S(1)} %get-tuple-element.190), channel_id=1, source_target_pairs={{1,0},{2,1},{3,2},{4,3},{5,4},{6,5},{7,6},{8,7},{9,8},{10,9},{11,1... | collective-permute-start | bytes 442376 | tf_op jit(solution)/shard_map/ppermute | solution.py:45
  107.1 9.5 %copy-start.10 = (bf16[16,32,768]{2,1,0:T(8,128)(2,1)S(1)}, bf16[16,32,768]{2,1,0:T(8,128)(2,1)}, u32[]{:S(2)}) copy-start(bf16[16,32,768]{2,1,0:T(8,128)(2,1)} %param.15) | copy-start | bytes 2359300
  107.1 9.5 %copy-start.17 = (f32[768]{0:T(1024)S(1)}, f32[768]{0:T(1024)}, u32[]{:S(2)}) copy-start(f32[768]{0:T(1024)} %param.14) | copy-start | bytes 9220
  107.2 14.1 %copy-start.5 = (bf16[16,32,768]{2,1,0:T(8,128)(2,1)S(1)}, bf16[16,32,768]{2,1,0:T(8,128)(2,1)}, u32[]{:S(2)}) copy-start(bf16[16,32,768]{2,1,0:T(8,128)(2,1)} %param.8) | copy-start | bytes 2359300
  113.8 3.8 collective-permute-start.2
  115.2 6.1 %collective-permute-start.3 = (bf16[6,44,768]{2,1,0:T(8,128)(2,1)S(1)}, bf16[6,44,768]{2,1,0:T(8,128)(2,1)S(1)}, u32[]{:S(2)}, u32[]{:S(2)}) collective-permute-start(bf16[6,44,768]{2,1,0:T(8,128)(2,1)S(1)} %get-tuple-element.184), channel_id=1, source_target_pairs={{16,0},{32,16},{48,32},{64,48},{80,64},{96,80},{112,96},{17,1},{33... | collective-permute-start | bytes 1216520 | tf_op jit(solution)/shard_map/ppermute | solution.py:48
  117.6 5.1 copy-start.2
  122.7 14.6 %copy-start.16 = (f32[768]{0:T(1024)S(1)}, f32[768]{0:T(1024)}, u32[]{:S(2)}) copy-start(f32[768]{0:T(1024)} %param.10) | copy-start | bytes 9220
  151.3 5.2 copy-start.18
  156.5 6.7 %copy-start.6 = (bf16[16,32,768]{2,1,0:T(8,128)(2,1)S(1)}, bf16[16,32,768]{2,1,0:T(8,128)(2,1)}, u32[]{:S(2)}) copy-start(bf16[16,32,768]{2,1,0:T(8,128)(2,1)} %param.8) | copy-start | bytes 2359300
  156.5 6.7 %copy-start.9 = (bf16[3072,768]{1,0:T(8,128)(2,1)S(1)}, bf16[3072,768]{1,0:T(8,128)(2,1)}, u32[]{:S(2)}) copy-start(bf16[3072,768]{1,0:T(8,128)(2,1)} %reshape_squeeze.9) | copy-start | bytes 14155780
  156.5 6.7 %copy-start.11 = (bf16[16,32,768]{2,1,0:T(8,128)(2,1)S(1)}, bf16[16,32,768]{2,1,0:T(8,128)(2,1)}, u32[]{:S(2)}) copy-start(bf16[16,32,768]{2,1,0:T(8,128)(2,1)} %param.15) | copy-start | bytes 2359300
  182.7 7.5 %copy-start.8 = (bf16[16,32,768]{2,1,0:T(8,128)(2,1)S(1)}, bf16[16,32,768]{2,1,0:T(8,128)(2,1)}, u32[]{:S(2)}) copy-start(bf16[16,32,768]{2,1,0:T(8,128)(2,1)} %get-tuple-element.170) | copy-start | bytes 2359300
  227.2 186.9 %all-reduce.3.cloned.1.call-start = ((), (), s32[]{:S(2)}) async-start(), calls=%async_computation.2 | async-start | bytes 344064 | tf_op jit(solution)/shard_map/psum | solution.py:104
  233.5 4.0 copy-start
  233.5 4.0 copy-start.3
  233.5 4.0 copy-start.7
  242.7 262.1 %reduce-scatter.5.cloned.1.call-start = ((), (), s32[]{:S(2)}) async-start(), calls=%async_computation.4 | async-start | bytes 10027008 | tf_op jit(solution)/shard_map/reduce_scatter | solution.py:99
  275.5 0.9 copy-start.14
  275.5 1.4 copy-start.1
  275.6 274.6 %all-reduce.5.cloned.1.call-start = ((), (), s32[]{:S(2)}) async-start(), calls=%async_computation.5 | async-start | bytes 1179648 | tf_op jit(solution)/shard_map/psum | solution.py:100
  277.0 8.0 %collective-permute-start.4 = (bf16[16,6,768]{2,1,0:T(8,128)(2,1)S(1)}, bf16[16,6,768]{2,1,0:T(8,128)(2,1)S(1)}, u32[]{:S(2)}, u32[]{:S(2)}) collective-permute-start(bf16[16,6,768]{2,1,0:T(8,128)(2,1)S(1)} %get-tuple-element.187), channel_id=1, source_target_pairs={{0,1},{1,2},{2,3},{3,4},{4,5},{5,6},{6,7},{7,8},{8,9},{9,10},{10,1... | collective-permute-start | bytes 442376 | tf_op jit(solution)/shard_map/ppermute | solution.py:44
  280.5 8.6 %collective-permute-start.5 = (bf16[16,6,768]{2,1,0:T(8,128)(2,1)S(1)}, bf16[16,6,768]{2,1,0:T(8,128)(2,1)S(1)}, u32[]{:S(2)}, u32[]{:S(2)}) collective-permute-start(bf16[16,6,768]{2,1,0:T(8,128)(2,1)S(1)} %get-tuple-element.188), channel_id=1, source_target_pairs={{1,0},{2,1},{3,2},{4,3},{5,4},{6,5},{7,6},{8,7},{9,8},{10,9},{11,1... | collective-permute-start | bytes 442376 | tf_op jit(solution)/shard_map/ppermute | solution.py:45
  289.1 215.7 %copy-start.12 = (bf16[16,6,768]{2,1,0:T(8,128)(2,1)}, bf16[16,6,768]{2,1,0:T(8,128)(2,1)S(1)}, u32[]{:S(2)}) copy-start(bf16[16,6,768]{2,1,0:T(8,128)(2,1)S(1)} %collective-permute-done.5) | copy-start | bytes 442372
  289.4 217.4 %collective-permute-start.6 = (bf16[6,44,768]{2,1,0:T(8,128)(2,1)S(1)}, bf16[6,44,768]{2,1,0:T(8,128)(2,1)S(1)}, u32[]{:S(2)}, u32[]{:S(2)}) collective-permute-start(bf16[6,44,768]{2,1,0:T(8,128)(2,1)S(1)} %get-tuple-element.179), channel_id=1, source_target_pairs={{0,16},{16,32},{32,48},{48,64},{64,80},{80,96},{96,112},{1,17},{17... | collective-permute-start | bytes 1216520 | tf_op jit(solution)/shard_map/ppermute | solution.py:47
  290.7 216.8 %collective-permute-start.7 = (bf16[6,44,768]{2,1,0:T(8,128)(2,1)S(1)}, bf16[6,44,768]{2,1,0:T(8,128)(2,1)}, u32[]{:S(2)}, u32[]{:S(2)}) collective-permute-start(bf16[6,44,768]{2,1,0:T(8,128)(2,1)S(1)} %get-tuple-element.180), channel_id=1, source_target_pairs={{16,0},{32,16},{48,32},{64,48},{80,64},{96,80},{112,96},{17,1},{33... | collective-permute-start | bytes 1216520 | tf_op jit(solution)/shard_map/ppermute | solution.py:48
  504.8 62.2 %all-gather.6.cloned.1.call-start = ((), (), s32[]{:S(2)}) async-start(), calls=%async_computation.6 | async-start | bytes 1769472 | tf_op jit(solution)/shard_map/all_gather | solution.py:101
  506.8 0.8 copy-start.15
Sparse Core Ops, SparseCore 0:
  11.9 77.8 all-gather.9
  101.0 24.4 all-gather.7
  227.4 37.2 reduce-scatter.2
  269.8 144.2 all-reduce.2
  417.5 87.2 reduce-scatter.4
  507.0 43.1 all-reduce.4
  551.8 12.3 all-gather.5

commit v3 on v1

--- a/solution.py
+++ b/solution.py
@@ -72,6 +72,7 @@
 
 def local(image, dw_kernel, ln_gain, w_in, b_in, w_out, layer_scale, cotangent):
     tile_rows, tile_cols, channels = image.shape
+    hidden_units = w_in.shape[1]
     row_count = lax.axis_size("row")
     col_count = lax.axis_size("col")
     group_count = row_count * col_count
@@ -85,7 +86,6 @@
     flipped = dw_kernel.reshape(channels, KSIZE, KSIZE)[:, ::-1, ::-1].reshape(
         channels, KSIZE * KSIZE
     )
-    group_index = lax.axis_index("row") * col_count + lax.axis_index("col")
     padded = add_halo(image)
     conv_tile = tile_stencil(padded, dw_kernel, tile_rows, tile_cols).astype(jnp.bfloat16)
     conv_rows = conv_tile.astype(jnp.float32).reshape(pixels, channels)
@@ -113,21 +113,6 @@
     grad_norm = lax.dot_general(
         grad_pre_rounded, full_in, CONTRACT_COLS, preferred_element_type=jnp.float32
     )
-    part_in = lax.psum_scatter(
-        lax.dot_general(
-            normed, grad_pre_rounded, CONTRACT_ROWS, preferred_element_type=jnp.float32
-        ),
-        "col",
-        scatter_dimension=0,
-        tiled=True,
-    )
-    part_out = lax.psum_scatter(
-        lax.dot_general(hidden, grad_mix, CONTRACT_ROWS, preferred_element_type=jnp.float32),
-        "col",
-        scatter_dimension=0,
-        tiled=True,
-    )
-    summed_in, summed_out = lax.psum((part_in, part_out), "row")
     gain_part = jnp.sum(grad_norm * standard, axis=0)
     scaled = grad_norm * ln_gain
     grad_conv = (
@@ -145,13 +130,43 @@
     grad_image = (cotangent.astype(jnp.float32) + grad_back.astype(jnp.float32)).astype(
         jnp.bfloat16
     )
-    scale_sum, bias_sum, gain_sum, kernel_sum = lax.psum(
-        (scale_part, bias_part, gain_part, kernel_part), ("row", "col")
-    )
-    grad_kernel = (
-        lax.dynamic_slice_in_dim(kernel_sum, group_index * group_size, group_size, 0)
-        * scale_factor
-    )
+    gain_part = jnp.sum(grad_norm * standard, axis=0)
+    small = jnp.concatenate([bias_part, gain_part, scale_part])
+    small = jnp.pad(small, (0, (-small.shape[0]) % (8 * channels))).reshape(-1, channels)
+    small_rows = small.shape[0]
+    rows_out = hidden_units // col_count
+    stacked_out = jnp.concatenate(
+        [
+            lax.dot_general(
+                hidden, grad_mix, CONTRACT_ROWS, preferred_element_type=jnp.float32
+            ).reshape(col_count, rows_out, channels),
+            jnp.broadcast_to(small[None], (col_count, small_rows, channels)),
+        ],
+        axis=1,
+    ).reshape(-1, channels)
+    part_in = lax.psum_scatter(
+        lax.dot_general(
+            normed, grad_pre_rounded, CONTRACT_ROWS, preferred_element_type=jnp.float32
+        ),
+        "col",
+        scatter_dimension=0,
+        tiled=True,
+    )
+    part_out = lax.psum_scatter(stacked_out, "col", scatter_dimension=0, tiled=True)
+    summed_in, summed_out = lax.psum((part_in, part_out), "row")
+    small_sum = summed_out[rows_out:].reshape(-1)
+    summed_out = summed_out[:rows_out]
+    bias_sum = small_sum[:hidden_units]
+    gain_sum = small_sum[hidden_units : hidden_units + channels]
+    scale_sum = small_sum[hidden_units + channels : hidden_units + 2 * channels]
+    kernel_parts = lax.all_to_all(
+        kernel_part.reshape(group_count, group_size, KSIZE * KSIZE),
+        ("row", "col"),
+        split_axis=0,
+        concat_axis=0,
+        tiled=True,
+    )
+    grad_kernel = jnp.sum(kernel_parts, axis=0) * scale_factor
     return (
         out_map,
         grad_image,

time: 556 us -> 404 us (0.73)
  waiting for transfers between devices: 349 us -> 173 us
  local copies, waits for them, and re-layouts: 13 us -> 83.6 us
  blocking collectives: 68.9 us -> 0 us
  other arithmetic: 55.1 us -> 66.7 us
  starting transfers between devices: 15.1 us -> 26 us
    reduce_scatter x1, waiting for transfers between devices: 90.5 us -> 0.02 us  [local(): lax.psum_scatter(lax.dot_general(normed, grad_pre_rounded, CONTRACT_ROWS,...]
    reduce_scatter x1 -> x0, waiting for transfers between devices: 85.6 us -> none  [local(): lax.psum_scatter(lax.dot_general(hidden, grad_mix, CONTRACT_ROWS, preferr...]
    psum x1 -> x0, blocking collectives: 68.9 us -> none  [local(): lax.psum((scale_part, bias_part, gain_part, kernel_part), ('row', 'col'))]
    psum x1 -> x0, waiting for transfers between devices: 45.6 us -> none  [local(): lax.psum((scale_part, bias_part, gain_part, kernel_part), ('row', 'col'))]
    unnamed x54 -> x167, local copies, waits for them, and re-layouts: 3.47 us -> 45.6 us
    unnamed x6, waiting for transfers between devices: 1.44 us -> 39.2 us
    another operation x50 -> x51, local copies, waits for them, and re-layouts: 4.72 us -> 18.4 us  [tile_taps(): return jnp.stack(columns, axis=1)]
    all_to_all x0 -> x1, starting transfers between devices: none -> 10.8 us  [local(): lax.all_to_all(kernel_part.reshape(group_count, group_size, KSIZE * KSIZE...]
  transfers between devices with their start and end apart: 14 -> 14, of which waited for: 9 -> 8; matrix products, arithmetic and copies ran while one was open for 12% -> 40% of each run, Pallas kernels for 0% -> 0%
where the time goes in v3:
time: 404 us; the launch traced here: 402 us
  waiting for transfers between devices  173 us (43%)
  local copies, waits for them, and re-layouts  83.6 us (21%)
  other arithmetic  66.7 us (17%)
  matrix products  37.6 us (9%)
  starting transfers between devices  26 us (6%)
  between operations  15 us (4%)
    psum x1, waiting for transfers between devices, local(): summed_in, summed_out = lax.psum((part_in, part_out), 'row')  48.6 us
    all_gather x1, waiting for transfers between devices, local(): lax.all_gather(w_out, 'col', axis=0, tiled=True)  48.6 us
    unnamed x167, local copies, waits for them, and re-layouts  45.6 us
    unnamed x6, waiting for transfers between devices  39.2 us
    all_gather x1, waiting for transfers between devices, local(): lax.all_gather(w_in, 'col', axis=0, tiled=True)  18.7 us
    another operation x51, local copies, waits for them, and re-layouts, tile_taps(): return jnp.stack(columns, axis=1)  18.4 us
    convert_element_type x1, other arithmetic, local(): (cotangent.astype(jnp.float32) + grad_back.astype(jnp.float32)).astype(jn...  16.5 us
    reduce_sum x3, other arithmetic, tile_taps(): columns.append(jnp.sum(gradient * window, axis=(0, 1)))  15.8 us
  transfers between devices with their start and end apart: 14, of which 8 were waited for; matrix products, arithmetic and copies ran while one was open for 40% of the time, Pallas kernels for 0%

profile of v3, /device:TPU:0, one launch (start us, length us, event | category | flops | bytes accessed | tf_op | source)
XLA Modules:
  0.0 401.6 jit_solution(5673280507494612774)
XLA Ops:
  9.8 3.6 collective-permute-start
  16.1 1.5 collective-permute-done
  17.5 4.1 %collective-permute-done.1 = bf16[16,6,768]{2,1,0:T(8,128)(2,1)S(1)} collective-permute-done((bf16[16,6,768]{2,1,0:T(8,128)(2,1)S(1)}, bf16[16,6,768]{2,1,0:T(8,128)(2,1)S(1)}, u32[]{:S(2)}, u32[]{:S(2)}) %collective-permute-start.1) | collective-permute-done | bytes 147488 | tf_op jit(solution)/shard_map/ppermute | solution.py:40
  25.1 4.1 %collective-permute-done.3 = bf16[6,44,768]{2,1,0:T(8,128)(2,1)S(1)} collective-permute-done((bf16[6,44,768]{2,1,0:T(8,128)(2,1)S(1)}, bf16[6,44,768]{2,1,0:T(8,128)(2,1)S(1)}, u32[]{:S(2)}, u32[]{:S(2)}) %collective-permute-start.3) | collective-permute-done | bytes 405536 | tf_op jit(solution)/shard_map/ppermute | solution.py:43
  30.6 12.9 %convert_reduce_fusion = (f32[16,32]{1,0:T(8,128)S(1)}, bf16[16,32,768]{2,1,0:T(8,128)(2,1)}) fusion(bf16[22,44,768]{2,1,0:T(8,128)(2,1)S(1)} %get-tuple-element.198, f32[768]{0:T(1024)S(1)} %get-tuple-element.185, f32[768]{0:T(1024)S(1)} %get-tuple-element.138, f32[768]{0:T(1024)S(1)} %get-tuple-element.139, f32[768]{0:T(1024)S(1)} %get-tuple-element.140, ...), kind=kLoop, calls=%fused_computation.271 | loop fusion | flops 62127616 | bytes 37262336 | tf_op jit(solution)/shard_map/reduce_sum | solution.py:92
  43.6 1.6 multiply_reduce_fusion.2
  45.3 2.3 multiply_convert_fusion.3
  47.6 18.7 %all-gather.3.cloned.1.call-done = bf16[768,3072]{1,0:T(8,128)(2,1)} async-done(((bf16[48,3072]{1,0:T(8,128)(2,1)}), bf16[768,3072]{1,0:T(8,128)(2,1)}) %all-gather.3.cloned.1.call-update) | async-done | bytes 4718608 | tf_op jit(solution)/shard_map/all_gather | solution.py:83
  66.4 7.0 %fusion.8 = (bf16[3072,512]{0,1:T(8,128)(2,1)}, f32[512,3072]{1,0:T(8,128)}) fusion(f32[3072]{0:T(1024)S(1)} %copy-done.55, bf16[512,768]{1,0:T(8,128)(2,1)} %multiply_convert_fusion.3, bf16[768,3072]{1,0:T(8,128)(2,1)} %all-gather.3.cloned.1.call-done), kind=kOutput, calls=%fused_computation.64 | convolution fusion | flops 2425356288 | bytes 14954496 | tf_op jit(solution)/shard_map/dot_general | solution.py:97
  73.4 48.6 %all-gather.5.cloned.1.call-done = bf16[3072,768]{1,0:T(8,128)(2,1)} async-done(((bf16[192,768]{1,0:T(8,128)(2,1)}), bf16[3072,768]{1,0:T(8,128)(2,1)}) %all-gather.5.cloned.1.call-update) | async-done | bytes 4718608 | tf_op jit(solution)/shard_map/all_gather | solution.py:84
  122.0 8.0 %fusion.136 = (f32[768]{0:T(1024)S(1)}, bf16[512,768]{1,0:T(8,128)(2,1)}, bf16[512,768]{1,0:T(8,128)(2,1)S(1)}) fusion(bf16[16,32,768]{2,1,0:T(8,128)(2,1)} %param.15, f32[768]{0:T(1024)S(1)} %copy-done.51, bf16[16,32,768]{2,1,0:T(8,128)(2,1)} %param.8, bf16[3072,768]{1,0:T(8,128)(2,1)} %all-gather.5.cloned.1.call-done, ...), kind=kOutput, calls=%fused_computation.248 | convolution fusion | flops 2428894464 | bytes 14174208 | tf_op jit(solution)/shard_map/dot_general | solution.py:99
  130.0 4.7 %fusion.156 = (f32[3072]{0:T(1024)S(1)}, bf16[512,3072]{1,0:T(8,128)(2,1)S(1)}) fusion(f32[512,3072]{1,0:T(8,128)S(1)} %copy-done.56, f32[3072]{0:T(1024)S(1)} %copy-done.55, bf16[512,768]{1,0:T(8,128)(2,1)S(1)} %get-tuple-element.201, bf16[3072,768]{1,0:T(8,128)(2,1)S(1)} %copy-done.54), kind=kOutput, calls=%fused_computation.459 | convolution fusion | flops 2434790400 | bytes 14966784 | tf_op jit(solution)/shard_map/dot_general | solution.py:107
  134.6 1.6 copy-done.9
  136.3 5.2 %fusion.139 = f32[768,3072]{1,0:T(8,128)} fusion(bf16[512,768]{1,0:T(8,128)(2,1)S(1)} %copy-done.8, bf16[512,3072]{1,0:T(8,128)(2,1)S(1)} %get-tuple-element.208), kind=kOutput, calls=%fused_computation.256 | convolution fusion | flops 2415919104 | bytes 13369344 | tf_op jit(solution)/shard_map/dot_general | solution.py:148
  141.7 2.2 fusion.134
  143.9 7.9 %multiply_reduce_fusion = (f32[768]{0:T(1024)S(1)}, f32[512]{0:T(512)}, f32[512]{0:T(512)}, f32[512,768]{1,0:T(8,128)}) fusion(bf16[16,32,768]{2,1,0:T(8,128)(2,1)S(1)} %copy-done.7, f32[512]{0:T(512)S(1)} %rsqrt.12, f32[512]{0:T(512)S(1)} %div.15, f32[768]{0:T(1024)S(1)} %copy-done.32, bf16[768,3072]{1,0:T(8,128)(2,1)} %all-gather.3.cloned.1.call-done, ...), kind=kOutput, calls=%fused_computation.253 | convolution fusion | flops 2419456256 | bytes 10237952 | tf_op jit(solution)/shard_map/dot_general | solution.py:113
  151.8 4.6 %copy.73 = bf16[3072,512]{1,0:T(8,128)(2,1)} copy(bf16[3072,512]{0,1:T(8,128)(2,1)} %get-tuple-element.209) | data formatting | bytes 6291456 | tf_op jit(solution)/shard_map/convert_element_type | solution.py:98
  156.5 4.9 %fusion.157 = f32[16,192,768]{2,1,0:T(8,128)S(1)} fusion(bf16[16,192,512]{2,1,0:T(8,128)(2,1)} %bitcast.114, bf16[512,768,1]{1,0,2:T(8,128)(2,1)} %bitcast.115), kind=kOutput, calls=%fused_computation.460 | convolution fusion | flops 2415919104 | bytes 13369344 | tf_op jit(solution)/shard_map/dot_general | solution.py:140
  161.4 4.5 %pad_maximum_fusion = f32[16,200,768]{2,1,0:T(8,128)} fusion(f32[16,8,768]{2,1,0:T(8,128)S(1)} %broadcast_in_dim.5, f32[16,192,768]{2,1,0:T(8,128)S(1)} %fusion.157), kind=kLoop, calls=%fused_computation.50 | loop fusion | flops 2457600 | bytes 19660800 | tf_op jit(solution)/shard_map/concatenate | solution.py:138
  165.9 1.6 reshape.300
  167.5 3.5 rev.3
  171.0 1.6 reshape.301
  172.7 2.0 slice_reduce_fusion.48
  174.7 6.9 %fusion.132 = (f32[768]{0:T(1024)}, f32[768]{0:T(1024)}, f32[768]{0:T(1024)}, f32[768]{0:T(1024)}, f32[768]{0:T(1024)}, /*index=5*/f32[768]{0:T(1024)}, f32[768]...) fusion(bf16[22,44,768]{2,1,0:T(8,128)(2,1)S(1)} %get-tuple-elem, ...), kind=kLoop, calls=%fused_computation.240 | loop fusion | flops 25152000 | bytes 17368064 | tf_op jit(solution)/shard_map/reduce_sum | solution.py:69
  181.6 3.7 fusion.114
  185.7 5.2 %fusion.104 = (f32[768]{0:T(1024)S(1)}, f32[768]{0:T(1024)S(1)}, f32[768]{0:T(1024)S(1)}, f32[768]{0:T(1024)S(1)}, f32[768]{0:T(1024)S(1)}, /*index=5*/f32[768]{...) fusion(bf16[22,44,768]{2,1,0:T(8,128)(2,1)S(1)} %get-tuple-elem, ...), kind=kLoop, calls=%fused_computation.212 | loop fusion | flops 21613056 | bytes 14997504 | tf_op jit(solution)/shard_map/reduce_sum | solution.py:69
  206.4 3.3 collective-permute-start.4
  212.9 1.5 constant_dynamic-update-slice_fusion.47
  214.3 1.5 constant_dynamic-update-slice_fusion.46
  215.8 1.5 constant_dynamic-update-slice_fusion.45
  217.2 1.5 constant_dynamic-update-slice_fusion.44
  218.7 1.5 constant_dynamic-update-slice_fusion.43
  220.2 1.5 constant_dynamic-update-slice_fusion.42
  221.6 1.5 constant_dynamic-update-slice_fusion.41
  223.1 1.5 constant_dynamic-update-slice_fusion.40
  224.6 1.5 constant_dynamic-update-slice_fusion.39
  226.0 1.5 constant_dynamic-update-slice_fusion.38
  227.5 1.5 constant_dynamic-update-slice_fusion.37
  229.0 1.5 constant_dynamic-update-slice_fusion.36
  230.4 1.5 constant_dynamic-update-slice_fusion.35
  252.5 3.3 copy.71
  257.0 10.8 %all-to-all-start = ((f32[128,1,294]{2,1,0:T(1,128)}), f32[128,1,294]{2,1,0:T(1,128)S(1)}, u32[]{:S(2)}, u32[]{:S(2)}) async-start(f32[128,1,294]{2,1,0:T(1,128)} %reshape.408), calls=%async_computation | async-start | bytes 393216 | tf_op jit(solution)/shard_map/all_to_all | solution.py:162
  272.3 7.9 %all-to-all-done = f32[128,1,294]{2,1,0:T(1,128)S(1)} async-done(((f32[128,1,294]{2,1,0:T(1,128)}), f32[128,1,294]{2,1,0:T(1,128)S(1)}, u32[]{:S(2)}, u32[]{:S(2)}) %all-to-all-start) | async-done | bytes 150560 | tf_op jit(solution)/shard_map/all_to_all | solution.py:162
  283.8 2.7 maximum_maximum_fusion.1
  286.5 37.8 %reduce-scatter.7.cloned.1.call-done = f32[200,768]{1,0:T(8,128)} async-done(((f32[3200,768]{1,0:T(8,128)}), f32[200,768]{1,0:T(8,128)}) %reduce-scatter.7.cloned.1.call-update) | async-done | bytes 614416
  324.4 16.5 %fusion.133 = bf16[16,32,768]{2,1,0:T(8,128)(2,1)} fusion(bf16[16,32,768]{2,1,0:T(8,128)(2,1)} %param.15, bf16[22,44,768]{2,1,0:T(8,128)(2,1)S(1)} %get-tuple-element.194, f32[768]{0:T(1024)S(1)} %get-tuple-element.89, f32[768]{0:T(1024)S(1)} %get-tuple-element.90, f32[768]{0:T(1024)S(1)} %get-tuple-element.91, f32[768]{0:T(1024)S(1)} %get-tuple-element.92, ...), kind=kLoop, calls=%fused_computation.245 | loop fusion | flops 66453504 | bytes 35834880 | tf_op jit(solution)/shard_map/convert_element_type | solution.py:130
  340.9 48.6 %all-reduce.5.cloned.1.call-done = (f32[48,3072]{1,0:T(8,128)}, f32[200,768]{1,0:T(8,128)}) async-done(((f32[48,3072]{1,0:T(8,128)}, f32[200,768]{1,0:T(8,128)}), (f32[48,3072]{1,0:T(8,128)}, f32[200,768]{1,0:T(8,128)})) %all-reduce.5.cloned.1.call-update) | async-done | bytes 1204240 | tf_op jit(solution)/shard_map/psum | solution.py:156
  389.5 2.0 slice_multiply_fusion
  (252 shorter events, 62.3 us)
Async XLA Ops:
  7.2 14.5 %copy-start.4 = (bf16[16,32,768]{2,1,0:T(8,128)(2,1)S(1)}, bf16[16,32,768]{2,1,0:T(8,128)(2,1)}, u32[]{:S(2)}) copy-start(bf16[16,32,768]{2,1,0:T(8,128)(2,1)} %param.8) | copy-start | bytes 2359300
  7.2 59.2 %all-gather.3.cloned.1.call-start = ((), (), s32[]{:S(2)}) async-start(), calls=%async_computation.3 | async-start | bytes 5013504 | tf_op jit(solution)/shard_map/all_gather | solution.py:83
  7.9 16.8 %copy-start.11 = (f32[768,49]{0,1:T(8,128)S(1)}, f32[768,49]{0,1:T(8,128)}, u32[]{:S(2)}) copy-start(f32[768,49]{0,1:T(8,128)} %param.9) | copy-start | bytes 451588
  7.9 114.0 %all-gather.5.cloned.1.call-start = ((), (), s32[]{:S(2)}) async-start(), calls=%async_computation.4 | async-start | bytes 5013504 | tf_op jit(solution)/shard_map/all_gather | solution.py:84
  8.7 277.8 %reduce-scatter.5.cloned.1.call-start = ((), (), s32[]{:S(2)}) async-start(), calls=%async_computation.5 | async-start | bytes 10027008 | tf_op jit(solution)/shard_map/reduce_scatter | solution.py:147
  9.8 7.7 %collective-permute-start = (bf16[16,6,768]{2,1,0:T(8,128)(2,1)S(1)}, bf16[16,6,768]{2,1,0:T(8,128)(2,1)S(1)}, u32[]{:S(2)}, u32[]{:S(2)}) collective-permute-start(bf16[16,6,768]{2,1,0:T(8,128)(2,1)S(1)} %get-tuple-element.204), channel_id=1, source_target_pairs={{0,1},{1,2},{2,3},{3,4},{4,5},{5,6},{6,7},{7,8},{8,9},{9,10},{10,1... | collective-permute-start | bytes 442376 | tf_op jit(solution)/shard_map/ppermute | solution.py:39
  13.4 8.3 %collective-permute-start.1 = (bf16[16,6,768]{2,1,0:T(8,128)(2,1)S(1)}, bf16[16,6,768]{2,1,0:T(8,128)(2,1)S(1)}, u32[]{:S(2)}, u32[]{:S(2)}) collective-permute-start(bf16[16,6,768]{2,1,0:T(8,128)(2,1)S(1)} %get-tuple-element.205), channel_id=1, source_target_pairs={{1,0},{2,1},{3,2},{4,3},{5,4},{6,5},{7,6},{8,7},{9,8},{10,9},{11,1... | collective-permute-start | bytes 442376 | tf_op jit(solution)/shard_map/ppermute | solution.py:40
  22.0 3.1 collective-permute-start.2
  23.4 5.8 %collective-permute-start.3 = (bf16[6,44,768]{2,1,0:T(8,128)(2,1)S(1)}, bf16[6,44,768]{2,1,0:T(8,128)(2,1)S(1)}, u32[]{:S(2)}, u32[]{:S(2)}) collective-permute-start(bf16[6,44,768]{2,1,0:T(8,128)(2,1)S(1)} %get-tuple-element.200), channel_id=1, source_target_pairs={{16,0},{32,16},{48,32},{64,48},{80,64},{96,80},{112,96},{17,1},{33... | collective-permute-start | bytes 1216520 | tf_op jit(solution)/shard_map/ppermute | solution.py:43
  30.6 14.7 %copy-start.32 = (f32[768]{0:T(1024)S(1)}, f32[768]{0:T(1024)}, u32[]{:S(2)}) copy-start(f32[768]{0:T(1024)} %param.10) | copy-start | bytes 9220
  43.5 22.9 %copy-start.55 = (f32[3072]{0:T(1024)S(1)}, f32[3072]{0:T(1024)}, u32[]{:S(2)}) copy-start(f32[3072]{0:T(1024)} %param.12) | copy-start | bytes 36868
  47.6 74.3 %copy-start.51 = (f32[768]{0:T(1024)S(1)}, f32[768]{0:T(1024)}, u32[]{:S(2)}) copy-start(f32[768]{0:T(1024)} %param.14) | copy-start | bytes 9220
  141.5 182.8 %reduce-scatter.7.cloned.1.call-start = ((), (), s32[]{:S(2)}) async-start(), calls=%async_computation.6 | async-start | bytes 10444800
  185.7 16.0 %copy-start.31 = (f32[768]{0:T(1024)S(1)}, f32[768]{0:T(1024)}, u32[]{:S(2)}) copy-start(f32[768]{0:T(1024)} %get-tuple-element.84) | copy-start | bytes 9220
  185.7 16.1 %copy-start.30 = (f32[768]{0:T(1024)S(1)}, f32[768]{0:T(1024)}, u32[]{:S(2)}) copy-start(f32[768]{0:T(1024)} %get-tuple-element.83) | copy-start | bytes 9220
  185.7 16.2 %copy-start.29 = (f32[768]{0:T(1024)S(1)}, f32[768]{0:T(1024)}, u32[]{:S(2)}) copy-start(f32[768]{0:T(1024)} %get-tuple-element.85) | copy-start | bytes 9220
  185.7 16.4 %copy-start.28 = (f32[768]{0:T(1024)S(1)}, f32[768]{0:T(1024)}, u32[]{:S(2)}) copy-start(f32[768]{0:T(1024)} %get-tuple-element.82) | copy-start | bytes 9220
  191.0 12.5 %copy-start.47 = (f32[768]{0:T(1024)S(1)}, f32[768]{0:T(1024)}, u32[]{:S(2)}) copy-start(f32[768]{0:T(1024)} %get-tuple-element.38) | copy-start | bytes 9220
  191.0 12.7 %copy-start.46 = (f32[768]{0:T(1024)S(1)}, f32[768]{0:T(1024)}, u32[]{:S(2)}) copy-start(f32[768]{0:T(1024)} %get-tuple-element.37) | copy-start | bytes 9220
  191.0 12.8 %copy-start.45 = (f32[768]{0:T(1024)S(1)}, f32[768]{0:T(1024)}, u32[]{:S(2)}) copy-start(f32[768]{0:T(1024)} %get-tuple-element.36) | copy-start | bytes 9220
  191.0 12.9 %copy-start.44 = (f32[768]{0:T(1024)S(1)}, f32[768]{0:T(1024)}, u32[]{:S(2)}) copy-start(f32[768]{0:T(1024)} %get-tuple-element.35) | copy-start | bytes 9220
  191.1 13.1 %copy-start.43 = (f32[768]{0:T(1024)S(1)}, f32[768]{0:T(1024)}, u32[]{:S(2)}) copy-start(f32[768]{0:T(1024)} %get-tuple-element.34) | copy-start | bytes 9220
  191.1 13.2 %copy-start.42 = (f32[768]{0:T(1024)S(1)}, f32[768]{0:T(1024)}, u32[]{:S(2)}) copy-start(f32[768]{0:T(1024)} %get-tuple-element.33) | copy-start | bytes 9220
  191.1 13.3 %copy-start.41 = (f32[768]{0:T(1024)S(1)}, f32[768]{0:T(1024)}, u32[]{:S(2)}) copy-start(f32[768]{0:T(1024)} %get-tuple-element.32) | copy-start | bytes 9220
  191.1 13.5 %copy-start.40 = (f32[768]{0:T(1024)S(1)}, f32[768]{0:T(1024)}, u32[]{:S(2)}) copy-start(f32[768]{0:T(1024)} %get-tuple-element.31) | copy-start | bytes 9220
  191.1 13.6 %copy-start.39 = (f32[768]{0:T(1024)S(1)}, f32[768]{0:T(1024)}, u32[]{:S(2)}) copy-start(f32[768]{0:T(1024)} %get-tuple-element.30) | copy-start | bytes 9220
  191.1 13.8 %copy-start.38 = (f32[768]{0:T(1024)S(1)}, f32[768]{0:T(1024)}, u32[]{:S(2)}) copy-start(f32[768]{0:T(1024)} %get-tuple-element.29) | copy-start | bytes 9220
  191.1 13.9 %copy-start.37 = (f32[768]{0:T(1024)S(1)}, f32[768]{0:T(1024)}, u32[]{:S(2)}) copy-start(f32[768]{0:T(1024)} %get-tuple-element.28) | copy-start | bytes 9220
  191.1 14.0 %copy-start.36 = (f32[768]{0:T(1024)S(1)}, f32[768]{0:T(1024)}, u32[]{:S(2)}) copy-start(f32[768]{0:T(1024)} %get-tuple-element.27) | copy-start | bytes 9220
  191.1 14.2 %copy-start.35 = (f32[768]{0:T(1024)S(1)}, f32[768]{0:T(1024)}, u32[]{:S(2)}) copy-start(f32[768]{0:T(1024)} %get-tuple-element.26) | copy-start | bytes 9220
  191.2 14.3 %copy-start.34 = (f32[768]{0:T(1024)S(1)}, f32[768]{0:T(1024)}, u32[]{:S(2)}) copy-start(f32[768]{0:T(1024)} %get-tuple-element.25) | copy-start | bytes 9220
  191.9 13.7 %copy-start.1 = (bf16[512,768]{1,0:T(8,128)(2,1)S(1)}, bf16[512,768]{1,0:T(8,128)(2,1)}, u32[]{:S(2)}) copy-start(bf16[512,768]{1,0:T(8,128)(2,1)} %copy-done) | copy-start | bytes 2359300
  206.4 61.4 %collective-permute-start.4 = (bf16[16,6,768]{2,1,0:T(8,128)(2,1)}, bf16[16,6,768]{2,1,0:T(8,128)(2,1)S(1)}, u32[]{:S(2)}, u32[]{:S(2)}) collective-permute-start(bf16[16,6,768]{2,1,0:T(8,128)(2,1)} %get-tuple-element.202), channel_id=1, source_target_pairs={{0,1},{1,2},{2,3},{3,4},{4,5},{5,6},{6,7},{7,8},{8,9},{9,10},{10,1... | collective-permute-start | bytes 442376 | tf_op jit(solution)/shard_map/ppermute | solution.py:39
  209.7 58.1 %collective-permute-start.5 = (bf16[16,6,768]{2,1,0:T(8,128)(2,1)}, bf16[16,6,768]{2,1,0:T(8,128)(2,1)S(1)}, u32[]{:S(2)}, u32[]{:S(2)}) collective-permute-start(bf16[16,6,768]{2,1,0:T(8,128)(2,1)} %get-tuple-element.203), channel_id=1, source_target_pairs={{1,0},{2,1},{3,2},{4,3},{5,4},{6,5},{7,6},{8,7},{9,8},{10,9},{11,1... | collective-permute-start | bytes 442376 | tf_op jit(solution)/shard_map/ppermute | solution.py:40
  236.9 14.9 %copy-start.33 = (f32[768]{0:T(1024)S(1)}, f32[768]{0:T(1024)}, u32[]{:S(2)}) copy-start(f32[768]{0:T(1024)} %get-tuple-element.24) | copy-start | bytes 9220
  255.8 15.0 %copy-start.12 = (f32[768,49]{0,1:T(8,128)S(1)}, f32[768,49]{0,1:T(8,128)}, u32[]{:S(2)}) copy-start(f32[768,49]{0,1:T(8,128)} %reshape.301) | copy-start | bytes 451588
  257.0 23.2 %all-to-all-start = ((f32[128,1,294]{2,1,0:T(1,128)}), f32[128,1,294]{2,1,0:T(1,128)S(1)}, u32[]{:S(2)}, u32[]{:S(2)}) async-start(f32[128,1,294]{2,1,0:T(1,128)} %reshape.408), calls=%async_computation | async-start | bytes 393216 | tf_op jit(solution)/shard_map/all_to_all | solution.py:162
  267.8 121.7 %all-reduce.5.cloned.1.call-start = ((), (), s32[]{:S(2)}) async-start(), calls=%async_computation.7 | async-start | bytes 2408448 | tf_op jit(solution)/shard_map/psum | solution.py:156
  267.8 14.2 %copy-start.10 = (bf16[16,6,768]{2,1,0:T(8,128)(2,1)}, bf16[16,6,768]{2,1,0:T(8,128)(2,1)S(1)}, u32[]{:S(2)}) copy-start(bf16[16,6,768]{2,1,0:T(8,128)(2,1)S(1)} %collective-permute-done.5) | copy-start | bytes 442372
  268.2 14.8 %collective-permute-start.6 = (bf16[6,44,768]{2,1,0:T(8,128)(2,1)S(1)}, bf16[6,44,768]{2,1,0:T(8,128)(2,1)S(1)}, u32[]{:S(2)}, u32[]{:S(2)}) collective-permute-start(bf16[6,44,768]{2,1,0:T(8,128)(2,1)S(1)} %get-tuple-element.195), channel_id=1, source_target_pairs={{0,16},{16,32},{32,48},{48,64},{64,80},{80,96},{96,112},{1,17},{17... | collective-permute-start | bytes 1216520 | tf_op jit(solution)/shard_map/ppermute | solution.py:42
  269.5 14.2 %collective-permute-start.7 = (bf16[6,44,768]{2,1,0:T(8,128)(2,1)S(1)}, bf16[6,44,768]{2,1,0:T(8,128)(2,1)}, u32[]{:S(2)}, u32[]{:S(2)}) collective-permute-start(bf16[6,44,768]{2,1,0:T(8,128)(2,1)S(1)} %get-tuple-element.196), channel_id=1, source_target_pairs={{16,0},{32,16},{48,32},{64,48},{80,64},{96,80},{112,96},{17,1},{33... | collective-permute-start | bytes 1216520 | tf_op jit(solution)/shard_map/ppermute | solution.py:43
  283.0 41.4 %copy-start.15 = (f32[768]{0:T(1024)S(1)}, f32[768]{0:T(1024)}, u32[]{:S(2)}) copy-start(f32[768]{0:T(1024)} %get-tuple-element.100) | copy-start | bytes 9220
  283.0 41.4 %copy-start.16 = (f32[768]{0:T(1024)S(1)}, f32[768]{0:T(1024)}, u32[]{:S(2)}) copy-start(f32[768]{0:T(1024)} %get-tuple-element.101) | copy-start | bytes 9220
  283.0 41.4 %copy-start.17 = (f32[768]{0:T(1024)S(1)}, f32[768]{0:T(1024)}, u32[]{:S(2)}) copy-start(f32[768]{0:T(1024)} %get-tuple-element.102) | copy-start | bytes 9220
  283.0 41.4 %copy-start.18 = (f32[768]{0:T(1024)S(1)}, f32[768]{0:T(1024)}, u32[]{:S(2)}) copy-start(f32[768]{0:T(1024)} %get-tuple-element.103) | copy-start | bytes 9220
  283.0 41.4 %copy-start.19 = (f32[768]{0:T(1024)S(1)}, f32[768]{0:T(1024)}, u32[]{:S(2)}) copy-start(f32[768]{0:T(1024)} %get-tuple-element.104) | copy-start | bytes 9220
  283.0 41.4 %copy-start.20 = (f32[768]{0:T(1024)S(1)}, f32[768]{0:T(1024)}, u32[]{:S(2)}) copy-start(f32[768]{0:T(1024)} %get-tuple-element.105) | copy-start | bytes 9220
  283.0 41.4 %copy-start.21 = (f32[768]{0:T(1024)S(1)}, f32[768]{0:T(1024)}, u32[]{:S(2)}) copy-start(f32[768]{0:T(1024)} %get-tuple-element.106) | copy-start | bytes 9220
  (23 other events, 185.6 us)
Sparse Core Ops, SparseCore 0:
  10.2 56.1 all-gather.2
  68.5 53.3 all-gather.4
  141.6 89.7 reduce-scatter.4
  234.7 89.5 reduce-scatter.6
  326.6 62.7 all-reduce.4

commit v4 on v3

--- a/solution.py
+++ b/solution.py
@@ -79,10 +79,14 @@
     group_size = channels // group_count
     pixels = tile_rows * tile_cols
     scale_factor = 1.0 / math.sqrt(pixels * group_count)
-    full_in, full_out = (
-        lax.all_gather(w_in, "col", axis=0, tiled=True),
-        lax.all_gather(w_out, "col", axis=0, tiled=True),
-    )
+    full_in = lax.all_gather(w_in, "col", axis=0, tiled=True)
+    full_out = lax.all_to_all(
+        jnp.broadcast_to(w_out[None], (col_count,) + w_out.shape),
+        "col",
+        split_axis=0,
+        concat_axis=0,
+        tiled=True,
+    ).reshape(-1, channels)
     flipped = dw_kernel.reshape(channels, KSIZE, KSIZE)[:, ::-1, ::-1].reshape(
         channels, KSIZE * KSIZE
     )
@@ -152,7 +156,16 @@
         scatter_dimension=0,
         tiled=True,
     )
-    part_out = lax.psum_scatter(stacked_out, "col", scatter_dimension=0, tiled=True)
+    part_out = jnp.sum(
+        lax.all_to_all(
+            stacked_out.reshape(col_count, -1, channels),
+            "col",
+            split_axis=0,
+            concat_axis=0,
+            tiled=True,
+        ),
+        axis=0,
+    )
     summed_in, summed_out = lax.psum((part_in, part_out), "row")
     small_sum = summed_out[rows_out:].reshape(-1)
     summed_out = summed_out[:rows_out]

time: 404 us -> 530 us (1.31)
  waiting for transfers between devices: 173 us -> 294 us
  starting transfers between devices: 26 us -> 57.5 us
  local copies, waits for them, and re-layouts: 83.6 us -> 56 us
    ppermute x2, waiting for transfers between devices: 4.13 us -> 129 us  [add_halo(): right = lax.ppermute(field[:, :REACH, :], 'col', shift_pairs(col_count, -1))]
    all_to_all x0 -> x2, waiting for transfers between devices: none -> 71 us  [the longest x1 71 us: local(): lax.all_to_all(stacked_out.reshape(col_count, -1, channels), 'col', split...]
    all_gather x2 -> x1, waiting for transfers between devices: 67.3 us -> 26.9 us  [local(): full_in = lax.all_gather(w_in, 'col', axis=0, tiled=True)]
    unnamed x6 -> x3, waiting for transfers between devices: 39.2 us -> 0.71 us
    all_to_all x1, starting transfers between devices: 10.8 us -> 26.7 us  [local(): lax.all_to_all(kernel_part.reshape(group_count, group_size, KSIZE * KSIZE...]
    psum x1, waiting for transfers between devices: 48.6 us -> 62.4 us  [local(): summed_in, summed_out = lax.psum((part_in, part_out), 'row')]
    all_to_all x0 -> x2, starting transfers between devices: none -> 13.8 us  [the longest x1 7.32 us: local(): lax.all_to_all(jnp.broadcast_to(w_out[None], (col_count,) + w_out.shape),...]
    unnamed x167 -> x113, local copies, waits for them, and re-layouts: 45.6 us -> 35.2 us
  transfers between devices with their start and end apart: 14 -> 14, of which waited for: 8 -> 6; matrix products, arithmetic and copies ran while one was open for 40% -> 27% of each run, Pallas kernels for 0% -> 0%
where the time goes in v4:
time: 530 us; the launch traced here: 529 us
  waiting for transfers between devices  294 us (55%)
  other arithmetic  68.4 us (13%)
  starting transfers between devices  57.5 us (11%)
  local copies, waits for them, and re-layouts  56 us (11%)
  matrix products  38.6 us (7%)
  between operations  14.6 us (3%)
    ppermute x2, waiting for transfers between devices, add_halo(): right = lax.ppermute(field[:, :REACH, :], 'col', shift_pairs(col_count, -1))  129 us
    all_to_all x1, waiting for transfers between devices, local(): lax.all_to_all(stacked_out.reshape(col_count, -1, channels), 'col', split...  71 us
    psum x1, waiting for transfers between devices, local(): summed_in, summed_out = lax.psum((part_in, part_out), 'row')  62.4 us
    unnamed x113, local copies, waits for them, and re-layouts  35.2 us
    all_gather x1, waiting for transfers between devices, local(): full_in = lax.all_gather(w_in, 'col', axis=0, tiled=True)  26.9 us
    all_to_all x1, starting transfers between devices, local(): lax.all_to_all(kernel_part.reshape(group_count, group_size, KSIZE * KSIZE...  26.7 us
    convert_element_type x1, other arithmetic, local(): (cotangent.astype(jnp.float32) + grad_back.astype(jnp.float32)).astype(jn...  16.4 us
    reduce_sum x3, other arithmetic, tile_taps(): columns.append(jnp.sum(gradient * window, axis=(0, 1)))  13.8 us
  transfers between devices with their start and end apart: 14, of which 6 were waited for; matrix products, arithmetic and copies ran while one was open for 27% of the time, Pallas kernels for 0%

profile of v4, /device:TPU:0, one launch (start us, length us, event | category | flops | bytes accessed | tf_op | source)
XLA Modules:
  0.0 528.9 jit_solution(10756428475038992768)
XLA Ops:
  7.9 3.5 broadcast_in_dim.6
  11.5 7.3 %all-to-all-start = ((bf16[16,192,768]{2,1,0:T(8,128)(2,1)}), bf16[16,192,768]{2,1,0:T(8,128)(2,1)}, u32[]{:S(2)}, u32[]{:S(2)}) async-start(bf16[16,192,768]{2,1,0:T(8,128)(2,1)} %broadcast_in_dim.6), calls=%async_computation | async-start | bytes 9437184 | tf_op jit(solution)/shard_map/all_to_all | solution.py:83
  18.9 1.3 collective-permute-start.1
  20.2 4.6 collective-permute-start
  25.2 43.3 %collective-permute-done.1 = bf16[16,6,768]{2,1,0:T(8,128)(2,1)S(1)} collective-permute-done((bf16[16,6,768]{2,1,0:T(8,128)(2,1)S(1)}, bf16[16,6,768]{2,1,0:T(8,128)(2,1)S(1)}, u32[]{:S(2)}, u32[]{:S(2)}) %collective-permute-start.1) | collective-permute-done | bytes 147488 | tf_op jit(solution)/shard_map/ppermute | solution.py:40
  68.8 1.3 collective-permute-start.2
  70.1 1.3 collective-permute-start.3
  71.6 1.0 multiply_convert_fusion.3
  72.6 3.5 collective-permute-done.3
  76.1 1.3 maximum_maximum_fusion
  77.5 12.9 %convert_reduce_fusion = (f32[16,32]{1,0:T(8,128)S(1)}, bf16[16,32,768]{2,1,0:T(8,128)(2,1)}) fusion(bf16[22,44,768]{2,1,0:T(8,128)(2,1)S(1)} %get-tuple-element.198, f32[768]{0:T(1024)S(1)} %get-tuple-element.185, f32[768]{0:T(1024)S(1)} %get-tuple-element.138, f32[768]{0:T(1024)S(1)} %get-tuple-element.139, f32[768]{0:T(1024)S(1)} %get-tuple-element.140, ...), kind=kLoop, calls=%fused_computation.267 | loop fusion | flops 62127616 | bytes 37262336 | tf_op jit(solution)/shard_map/reduce_sum | solution.py:96
  90.5 1.5 multiply_reduce_fusion.2
  92.1 2.3 multiply_convert_fusion.4
  94.4 26.9 %all-gather.2.cloned.1.call-done = bf16[768,3072]{1,0:T(8,128)(2,1)} async-done(((bf16[48,3072]{1,0:T(8,128)(2,1)}), bf16[768,3072]{1,0:T(8,128)(2,1)}) %all-gather.2.cloned.1.call-update) | async-done | bytes 4718608 | tf_op jit(solution)/shard_map/all_gather | solution.py:82
  121.2 7.1 %fusion.8 = (bf16[3072,512]{0,1:T(8,128)(2,1)}, f32[512,3072]{1,0:T(8,128)}) fusion(f32[3072]{0:T(1024)S(1)} %copy-done.28, bf16[512,768]{1,0:T(8,128)(2,1)} %multiply_convert_fusion.4, bf16[768,3072]{1,0:T(8,128)(2,1)} %all-gather.2.cloned.1.call-done), kind=kOutput, calls=%fused_computation.64 | convolution fusion | flops 2425356288 | bytes 14954496 | tf_op jit(solution)/shard_map/dot_general | solution.py:101
  128.3 8.0 %fusion.153 = (f32[3072]{0:T(1024)}, bf16[512,3072]{1,0:T(8,128)(2,1)S(1)}) fusion(f32[512,3072]{1,0:T(8,128)} %get-tuple-element.209, f32[3072]{0:T(1024)S(1)} %copy-done.28, bf16[512,768]{1,0:T(8,128)(2,1)} %bitcast.110, bf16[3072,768]{1,0:T(8,128)(2,1)} %bitcast.2), kind=kOutput, calls=%fused_computation.455 | convolution fusion | flops 2434790400 | bytes 14966784 | tf_op jit(solution)/shard_map/dot_general | solution.py:111
  136.3 1.6 copy-done.10
  137.9 5.1 fusion.136
  143.1 7.0 %multiply_reduce_fusion = (f32[768]{0:T(1024)}, f32[512]{0:T(512)S(1)}, f32[512]{0:T(512)S(1)}, f32[512,768]{1,0:T(8,128)S(1)}) fusion(bf16[16,32,768]{2,1,0:T(8,128)(2,1)} %get-tuple-element.190, f32[512]{0:T(512)S(1)} %rsqrt.12, f32[512]{0:T(512)S(1)} %div.15, f32[768]{0:T(1024)S(1)} %copy-done.20, bf16[768,3072]{1,0:T(8,128)(2,1)} %all-gather.2.cloned.1.call-done, ...), kind=kOutput, calls=%fused_computation.247 | convolution fusion | flops 2419456256 | bytes 10237952 | tf_op jit(solution)/shard_map/dot_general | solution.py:117
  150.1 5.6 %fusion.132 = (f32[768]{0:T(1024)S(1)}, f32[768]{0:T(1024)S(1)}, f32[768]{0:T(1024)S(1)}, f32[768]{0:T(1024)S(1)}, f32[768]{0:T(1024)S(1)}, /*index=5*/f32[768]{...) fusion(bf16[22,44,768]{2,1,0:T(8,128)(2,1)S(1)} %get-tuple-elem, ...), kind=kLoop, calls=%fused_computation.240 | loop fusion | flops 25152000 | bytes 17368064 | tf_op jit(solution)/shard_map/reduce_sum | solution.py:69
  155.8 3.2 fusion.114
  159.4 5.0 fusion.104
  201.2 3.4 copy.71
  204.6 1.1 reshape.413
  205.8 26.7 %all-to-all-start.1 = ((f32[128,1,294]{2,1,0:T(1,128)}), f32[128,1,294]{2,1,0:T(1,128)S(1)}, u32[]{:S(2)}, u32[]{:S(2)}) async-start(f32[128,1,294]{2,1,0:T(1,128)} %reshape.413), calls=%async_computation.1 | async-start | bytes 393216 | tf_op jit(solution)/shard_map/all_to_all | solution.py:175
  232.5 7.5 %fusion.133 = (f32[768]{0:T(1024)S(1)}, bf16[512,768]{1,0:T(8,128)(2,1)}) fusion(bf16[16,32,768]{2,1,0:T(8,128)(2,1)S(1)} %copy-done.12, f32[768]{0:T(1024)S(1)} %copy-done.26, bf16[16,32,768]{2,1,0:T(8,128)(2,1)S(1)} %copy-done.7, bf16[3072,768]{1,0:T(8,128)(2,1)} %bitcast.2, f32[512,3072]{1,0:T(8,128)} %get-tuple-element.209, f32[3072]{0:T(1024)S(1)} %copy-done.29), kind=kOutput, calls=%fused_computation.242 | convolution fusion | flops 2428108032 | bytes 13387776 | tf_op jit(solution)/shard_map/dot_general | solution.py:103
  240.1 3.2 copy.73
  243.3 3.9 fusion.154
  247.2 4.5 pad_maximum_fusion
  252.4 6.5 %all-to-all-start.2 = ((f32[16,200,768]{2,1,0:T(8,128)}), f32[16,200,768]{2,1,0:T(8,128)}, u32[]{:S(2)}, u32[]{:S(2)}) async-start(f32[16,200,768]{2,1,0:T(8,128)} %pad_maximum_fusion), calls=%async_computation.3 | async-start | bytes 19660800 | tf_op jit(solution)/shard_map/all_to_all | solution.py:160
  258.9 1.3 collective-permute-start.5
  260.2 4.6 collective-permute-start.4
  265.3 86.0 %collective-permute-done.5 = bf16[16,6,768]{2,1,0:T(8,128)(2,1)S(1)} collective-permute-done((bf16[16,6,768]{2,1,0:T(8,128)(2,1)S(1)}, bf16[16,6,768]{2,1,0:T(8,128)(2,1)S(1)}, u32[]{:S(2)}, u32[]{:S(2)}) %collective-permute-start.5) | collective-permute-done | bytes 147488 | tf_op jit(solution)/shard_map/ppermute | solution.py:40
  351.6 1.3 collective-permute-start.6
  352.9 1.3 collective-permute-start.7
  354.2 0.7 slice_reduce_fusion.46
  354.9 0.7 slice_reduce_fusion.47
  356.1 1.1 reduce.202
  358.4 0.8 copy-done.19
  359.1 2.6 maximum_maximum_fusion.1
  361.7 71.0 %all-to-all-done.2 = f32[16,200,768]{2,1,0:T(8,128)} async-done(((f32[16,200,768]{2,1,0:T(8,128)}), f32[16,200,768]{2,1,0:T(8,128)}, u32[]{:S(2)}, u32[]{:S(2)}) %all-to-all-start.2) | async-done | bytes 9830432 | tf_op jit(solution)/shard_map/all_to_all | solution.py:160
  432.7 5.3 reduce_sum.579
  438.0 16.4 %add_convert_fusion = bf16[16,32,768]{2,1,0:T(8,128)(2,1)} fusion(bf16[16,32,768]{2,1,0:T(8,128)(2,1)} %param.15, bf16[22,44,768]{2,1,0:T(8,128)(2,1)S(1)} %get-tuple-element.194, f32[768]{0:T(1024)S(1)} %get-tuple-element.89, f32[768]{0:T(1024)S(1)} %get-tuple-element.90, f32[768]{0:T(1024)S(1)} %get-tuple-element.91, f32[768]{0:T(1024)S(1)} %get-tuple-element.92, ...), kind=kLoop, calls=%fused_computation.248 | loop fusion | flops 66453504 | bytes 35834880 | tf_op jit(solution)/shard_map/convert_element_type | solution.py:134
  454.4 62.4 %all-reduce.4.cloned.1.call-done = (f32[48,3072]{1,0:T(8,128)}, f32[200,768]{1,0:T(8,128)}) async-done(((f32[48,3072]{1,0:T(8,128)}, f32[200,768]{1,0:T(8,128)}), (f32[48,3072]{1,0:T(8,128)}, f32[200,768]{1,0:T(8,128)})) %all-reduce.4.cloned.1.call-update) | async-done | bytes 1204240 | tf_op jit(solution)/shard_map/psum | solution.py:169
  516.8 2.0 slice_multiply_fusion
  518.7 0.7 slice_multiply_fusion.1
  519.5 1.4 fusion.148
  520.9 0.9 broadcast_multiply_fusion
  (198 shorter events, 42.4 us)
Async XLA Ops:
  7.2 114.1 %all-gather.2.cloned.1.call-start = ((), (), s32[]{:S(2)}) async-start(), calls=%async_computation.4 | async-start | bytes 5013504 | tf_op jit(solution)/shard_map/all_gather | solution.py:82
  11.4 7.4 %copy-start.4 = (bf16[16,32,768]{2,1,0:T(8,128)(2,1)S(1)}, bf16[16,32,768]{2,1,0:T(8,128)(2,1)}, u32[]{:S(2)}) copy-start(bf16[16,32,768]{2,1,0:T(8,128)(2,1)} %param.8) | copy-start | bytes 2359300
  11.4 13.3 %copy-start.16 = (f32[768,49]{0,1:T(8,128)S(1)}, f32[768,49]{0,1:T(8,128)}, u32[]{:S(2)}) copy-start(f32[768,49]{0,1:T(8,128)} %param.9) | copy-start | bytes 451588
  11.5 116.9 %all-to-all-start = ((bf16[16,192,768]{2,1,0:T(8,128)(2,1)}), bf16[16,192,768]{2,1,0:T(8,128)(2,1)}, u32[]{:S(2)}, u32[]{:S(2)}) async-start(bf16[16,192,768]{2,1,0:T(8,128)(2,1)} %broadcast_in_dim.6), calls=%async_computation | async-start | bytes 9437184 | tf_op jit(solution)/shard_map/all_to_all | solution.py:83
  18.8 419.2 %reduce-scatter.2.cloned.1.call-start = ((), (), s32[]{:S(2)}) async-start(), calls=%async_computation.5 | async-start | bytes 10027008 | tf_op jit(solution)/shard_map/reduce_scatter | solution.py:151
  18.9 49.6 %collective-permute-start.1 = (bf16[16,6,768]{2,1,0:T(8,128)(2,1)S(1)}, bf16[16,6,768]{2,1,0:T(8,128)(2,1)S(1)}, u32[]{:S(2)}, u32[]{:S(2)}) collective-permute-start(bf16[16,6,768]{2,1,0:T(8,128)(2,1)S(1)} %get-tuple-element.204), channel_id=1, source_target_pairs={{1,0},{2,1},{3,2},{4,3},{5,4},{6,5},{7,6},{8,7},{9,8},{10,9},{11,1... | collective-permute-start | bytes 442376 | tf_op jit(solution)/shard_map/ppermute | solution.py:40
  20.2 48.3 %collective-permute-start = (bf16[16,6,768]{2,1,0:T(8,128)(2,1)S(1)}, bf16[16,6,768]{2,1,0:T(8,128)(2,1)S(1)}, u32[]{:S(2)}, u32[]{:S(2)}) collective-permute-start(bf16[16,6,768]{2,1,0:T(8,128)(2,1)S(1)} %get-tuple-element.203), channel_id=1, source_target_pairs={{0,1},{1,2},{2,3},{3,4},{4,5},{5,6},{6,7},{7,8},{8,9},{9,10},{10,1... | collective-permute-start | bytes 442376 | tf_op jit(solution)/shard_map/ppermute | solution.py:39
  25.1 46.4 %copy-start.11 = (bf16[16,32,768]{2,1,0:T(8,128)(2,1)S(1)}, bf16[16,32,768]{2,1,0:T(8,128)(2,1)}, u32[]{:S(2)}) copy-start(bf16[16,32,768]{2,1,0:T(8,128)(2,1)} %param.15) | copy-start | bytes 2359300
  25.1 46.4 %copy-start.25 = (f32[768]{0:T(1024)S(1)}, f32[768]{0:T(1024)}, u32[]{:S(2)}) copy-start(f32[768]{0:T(1024)} %param.14) | copy-start | bytes 9220
  25.2 50.9 %copy-start.5 = (bf16[16,32,768]{2,1,0:T(8,128)(2,1)S(1)}, bf16[16,32,768]{2,1,0:T(8,128)(2,1)}, u32[]{:S(2)}) copy-start(bf16[16,32,768]{2,1,0:T(8,128)(2,1)} %param.8) | copy-start | bytes 2359300
  68.8 3.8 collective-permute-start.2
  70.1 6.0 %collective-permute-start.3 = (bf16[6,44,768]{2,1,0:T(8,128)(2,1)S(1)}, bf16[6,44,768]{2,1,0:T(8,128)(2,1)S(1)}, u32[]{:S(2)}, u32[]{:S(2)}) collective-permute-start(bf16[6,44,768]{2,1,0:T(8,128)(2,1)S(1)} %get-tuple-element.200), channel_id=1, source_target_pairs={{16,0},{32,16},{48,32},{64,48},{80,64},{96,80},{112,96},{17,1},{33... | collective-permute-start | bytes 1216520 | tf_op jit(solution)/shard_map/ppermute | solution.py:43
  72.6 4.8 copy-start.2
  77.5 14.6 %copy-start.20 = (f32[768]{0:T(1024)S(1)}, f32[768]{0:T(1024)}, u32[]{:S(2)}) copy-start(f32[768]{0:T(1024)} %param.10) | copy-start | bytes 9220
  90.4 30.8 %copy-start.28 = (f32[3072]{0:T(1024)S(1)}, f32[3072]{0:T(1024)}, u32[]{:S(2)}) copy-start(f32[3072]{0:T(1024)} %param.12) | copy-start | bytes 36868
  128.3 9.6 %copy-start.9 = (bf16[512,768]{1,0:T(8,128)(2,1)S(1)}, bf16[512,768]{1,0:T(8,128)(2,1)}, u32[]{:S(2)}) copy-start(bf16[512,768]{1,0:T(8,128)(2,1)} %multiply_convert_fusion.4) | copy-start | bytes 2359300
  136.3 1.6 copy-start.10
  143.1 7.1 %copy-start.8 = (bf16[16,32,768]{2,1,0:T(8,128)(2,1)S(1)}, bf16[16,32,768]{2,1,0:T(8,128)(2,1)}, u32[]{:S(2)}) copy-start(bf16[16,32,768]{2,1,0:T(8,128)(2,1)} %get-tuple-element.190) | copy-start | bytes 2359300
  150.1 5.6 %copy-start.3 = (bf16[16,38,768]{2,1,0:T(8,128)(2,1)S(1)}, bf16[16,38,768]{2,1,0:T(8,128)(2,1)}, u32[]{:S(2)}) copy-start(bf16[16,38,768]{2,1,0:T(8,128)(2,1)} %copy-done.2) | copy-start | bytes 2801668
  150.1 5.6 %copy-start.6 = (bf16[16,32,768]{2,1,0:T(8,128)(2,1)S(1)}, bf16[16,32,768]{2,1,0:T(8,128)(2,1)}, u32[]{:S(2)}) copy-start(bf16[16,32,768]{2,1,0:T(8,128)(2,1)} %param.8) | copy-start | bytes 2359300
  155.8 3.3 copy-start
  164.4 3.8 copy-start.23
  164.4 4.0 copy-start.22
  164.4 4.1 copy-start.21
  201.2 31.3 %copy-start.7 = (bf16[16,32,768]{2,1,0:T(8,128)(2,1)S(1)}, bf16[16,32,768]{2,1,0:T(8,128)(2,1)}, u32[]{:S(2)}) copy-start(bf16[16,32,768]{2,1,0:T(8,128)(2,1)} %param.8) | copy-start | bytes 2359300
  201.2 31.3 %copy-start.12 = (bf16[16,32,768]{2,1,0:T(8,128)(2,1)S(1)}, bf16[16,32,768]{2,1,0:T(8,128)(2,1)}, u32[]{:S(2)}) copy-start(bf16[16,32,768]{2,1,0:T(8,128)(2,1)} %param.15) | copy-start | bytes 2359300
  201.2 31.3 %copy-start.26 = (f32[768]{0:T(1024)S(1)}, f32[768]{0:T(1024)}, u32[]{:S(2)}) copy-start(f32[768]{0:T(1024)} %param.14) | copy-start | bytes 9220
  201.2 31.3 %copy-start.29 = (f32[3072]{0:T(1024)S(1)}, f32[3072]{0:T(1024)}, u32[]{:S(2)}) copy-start(f32[3072]{0:T(1024)} %param.12) | copy-start | bytes 36868
  205.8 45.9 %all-to-all-start.1 = ((f32[128,1,294]{2,1,0:T(1,128)}), f32[128,1,294]{2,1,0:T(1,128)S(1)}, u32[]{:S(2)}, u32[]{:S(2)}) async-start(f32[128,1,294]{2,1,0:T(1,128)} %reshape.413), calls=%async_computation.1 | async-start | bytes 393216 | tf_op jit(solution)/shard_map/all_to_all | solution.py:175
  232.5 7.5 %copy-start.24 = (f32[3072]{0:T(1024)S(1)}, f32[3072]{0:T(1024)}, u32[]{:S(2)}) copy-start(f32[3072]{0:T(1024)} %get-tuple-element.206) | copy-start | bytes 36868
  232.5 7.5 %copy-start.27 = (f32[768]{0:T(1024)S(1)}, f32[768]{0:T(1024)}, u32[]{:S(2)}) copy-start(f32[768]{0:T(1024)} %get-tuple-element.66) | copy-start | bytes 9220
  251.7 7.2 %copy-start.1 = (bf16[512,768]{1,0:T(8,128)(2,1)S(1)}, bf16[512,768]{1,0:T(8,128)(2,1)}, u32[]{:S(2)}) copy-start(bf16[512,768]{1,0:T(8,128)(2,1)} %copy-done) | copy-start | bytes 2359300
  251.7 13.1 %copy-start.17 = (f32[768,49]{0,1:T(8,128)S(1)}, f32[768,49]{0,1:T(8,128)}, u32[]{:S(2)}) copy-start(f32[768,49]{0,1:T(8,128)} %param.9) | copy-start | bytes 451588
  251.7 0.7 copy-start.14
  252.4 180.4 %all-to-all-start.2 = ((f32[16,200,768]{2,1,0:T(8,128)}), f32[16,200,768]{2,1,0:T(8,128)}, u32[]{:S(2)}, u32[]{:S(2)}) async-start(f32[16,200,768]{2,1,0:T(8,128)} %pad_maximum_fusion), calls=%async_computation.3 | async-start | bytes 19660800 | tf_op jit(solution)/shard_map/all_to_all | solution.py:160
  258.8 257.9 %all-reduce.4.cloned.1.call-start = ((), (), s32[]{:S(2)}) async-start(), calls=%async_computation.6 | async-start | bytes 2408448 | tf_op jit(solution)/shard_map/psum | solution.py:169
  258.9 92.3 %collective-permute-start.5 = (bf16[16,6,768]{2,1,0:T(8,128)(2,1)S(1)}, bf16[16,6,768]{2,1,0:T(8,128)(2,1)S(1)}, u32[]{:S(2)}, u32[]{:S(2)}) collective-permute-start(bf16[16,6,768]{2,1,0:T(8,128)(2,1)S(1)} %get-tuple-element.202), channel_id=1, source_target_pairs={{1,0},{2,1},{3,2},{4,3},{5,4},{6,5},{7,6},{8,7},{9,8},{10,9},{11,1... | collective-permute-start | bytes 442376 | tf_op jit(solution)/shard_map/ppermute | solution.py:40
  260.2 91.0 %collective-permute-start.4 = (bf16[16,6,768]{2,1,0:T(8,128)(2,1)S(1)}, bf16[16,6,768]{2,1,0:T(8,128)(2,1)S(1)}, u32[]{:S(2)}, u32[]{:S(2)}) collective-permute-start(bf16[16,6,768]{2,1,0:T(8,128)(2,1)S(1)} %get-tuple-element.201), channel_id=1, source_target_pairs={{0,1},{1,2},{2,3},{3,4},{4,5},{5,6},{6,7},{7,8},{8,9},{9,10},{10,1... | collective-permute-start | bytes 442376 | tf_op jit(solution)/shard_map/ppermute | solution.py:39
  264.9 91.3 %copy-start.15 = (f32[128,1,294]{2,1,0:T(1,128)S(1)}, f32[128,1,294]{2,1,0:T(1,128)}, u32[]{:S(2)}) copy-start(f32[128,1,294]{2,1,0:T(1,128)} %copy-done.14) | copy-start | bytes 451588
  351.3 6.2 %copy-start.13 = (bf16[16,6,768]{2,1,0:T(8,128)(2,1)}, bf16[16,6,768]{2,1,0:T(8,128)(2,1)S(1)}, u32[]{:S(2)}) copy-start(bf16[16,6,768]{2,1,0:T(8,128)(2,1)S(1)} %collective-permute-done.4) | copy-start | bytes 442372
  351.6 6.8 %collective-permute-start.6 = (bf16[6,44,768]{2,1,0:T(8,128)(2,1)S(1)}, bf16[6,44,768]{2,1,0:T(8,128)(2,1)S(1)}, u32[]{:S(2)}, u32[]{:S(2)}) collective-permute-start(bf16[6,44,768]{2,1,0:T(8,128)(2,1)S(1)} %get-tuple-element.195), channel_id=1, source_target_pairs={{0,16},{16,32},{32,48},{48,64},{64,80},{80,96},{96,112},{1,17},{17... | collective-permute-start | bytes 1216520 | tf_op jit(solution)/shard_map/ppermute | solution.py:42
  352.9 6.2 %collective-permute-start.7 = (bf16[6,44,768]{2,1,0:T(8,128)(2,1)S(1)}, bf16[6,44,768]{2,1,0:T(8,128)(2,1)}, u32[]{:S(2)}, u32[]{:S(2)}) collective-permute-start(bf16[6,44,768]{2,1,0:T(8,128)(2,1)S(1)} %get-tuple-element.196), channel_id=1, source_target_pairs={{16,0},{32,16},{48,32},{64,48},{80,64},{96,80},{112,96},{17,1},{33... | collective-permute-start | bytes 1216520 | tf_op jit(solution)/shard_map/ppermute | solution.py:43
  358.4 0.8 copy-start.19
  516.8 4.2 copy-start.18
Sparse Core Ops, SparseCore 0:
  10.2 111.0 all-gather.1
  143.2 106.7 reduce-scatter.1
  438.1 78.5 all-reduce.3

commit v5 on v3

--- a/solution.py
+++ b/solution.py
@@ -33,14 +33,18 @@
     return [(i + 1, i) for i in range(count - 1)]
 
 
+ROW = ("z", "core")
+EVERY = ("z", "core", "col")
+
+
 def add_halo(field):
-    row_count = lax.axis_size("row")
+    row_count = lax.axis_size(ROW)
     col_count = lax.axis_size("col")
     left = lax.ppermute(field[:, -REACH:, :], "col", shift_pairs(col_count, 1))
     right = lax.ppermute(field[:, :REACH, :], "col", shift_pairs(col_count, -1))
     wide = jnp.concatenate([left, field, right], axis=1)
-    top = lax.ppermute(wide[-REACH:], "row", shift_pairs(row_count, 1))
-    bottom = lax.ppermute(wide[:REACH], "row", shift_pairs(row_count, -1))
+    top = lax.ppermute(wide[-REACH:], ROW, shift_pairs(row_count, 1))
+    bottom = lax.ppermute(wide[:REACH], ROW, shift_pairs(row_count, -1))
     return jnp.concatenate([top, wide, bottom], axis=0)
 
 
@@ -73,7 +77,7 @@
 def local(image, dw_kernel, ln_gain, w_in, b_in, w_out, layer_scale, cotangent):
     tile_rows, tile_cols, channels = image.shape
     hidden_units = w_in.shape[1]
-    row_count = lax.axis_size("row")
+    row_count = lax.axis_size(ROW)
     col_count = lax.axis_size("col")
     group_count = row_count * col_count
     group_size = channels // group_count
@@ -135,33 +139,33 @@
     small = jnp.pad(small, (0, (-small.shape[0]) % (8 * channels))).reshape(-1, channels)
     small_rows = small.shape[0]
     rows_out = hidden_units // col_count
-    stacked_out = jnp.concatenate(
-        [
-            lax.dot_general(
-                hidden, grad_mix, CONTRACT_ROWS, preferred_element_type=jnp.float32
-            ).reshape(col_count, rows_out, channels),
-            jnp.broadcast_to(small[None], (col_count, small_rows, channels)),
-        ],
-        axis=1,
-    ).reshape(-1, channels)
-    part_in = lax.psum_scatter(
-        lax.dot_general(
-            normed, grad_pre_rounded, CONTRACT_ROWS, preferred_element_type=jnp.float32
-        ),
-        "col",
-        scatter_dimension=0,
-        tiled=True,
+    block_in = lax.dot_general(
+        normed, grad_pre_rounded, CONTRACT_ROWS, preferred_element_type=jnp.float32
+    ).reshape(col_count, rows_out, channels)
+    block_out = lax.dot_general(
+        hidden, grad_mix, CONTRACT_ROWS, preferred_element_type=jnp.float32
+    ).reshape(col_count, rows_out, channels)
+    block_in = jnp.concatenate(
+        [block_in, jnp.zeros((col_count, small_rows, channels), jnp.float32)], axis=1
     )
-    part_out = lax.psum_scatter(stacked_out, "col", scatter_dimension=0, tiled=True)
-    summed_in, summed_out = lax.psum((part_in, part_out), "row")
-    small_sum = summed_out[rows_out:].reshape(-1)
-    summed_out = summed_out[:rows_out]
+    block_out = jnp.concatenate(
+        [block_out, jnp.broadcast_to(small[None], (col_count, small_rows, channels))], axis=1
+    )
+    stacked = jnp.stack([block_in, block_out], axis=1)
+    halves = lax.psum_scatter(stacked, "core", scatter_dimension=1, tiled=True)
+    halves = halves.reshape(-1, channels)
+    mine = lax.psum_scatter(halves, "col", scatter_dimension=0, tiled=True)
+    mine = lax.psum(mine, "z")
+    pair = lax.all_gather(mine, "core", axis=0, tiled=False)
+    summed_in = pair[0, :rows_out].reshape(-1, hidden_units)
+    summed_out = pair[1, :rows_out]
+    small_sum = pair[1, rows_out:].reshape(-1)
     bias_sum = small_sum[:hidden_units]
     gain_sum = small_sum[hidden_units : hidden_units + channels]
     scale_sum = small_sum[hidden_units + channels : hidden_units + 2 * channels]
     kernel_parts = lax.all_to_all(
         kernel_part.reshape(group_count, group_size, KSIZE * KSIZE),
-        ("row", "col"),
+        EVERY,
         split_axis=0,
         concat_axis=0,
         tiled=True,
@@ -180,24 +184,9 @@
 
 
 def solution(mesh):
-    in_specs = (
-        P("row", "col", None),
-        P(),
-        P(),
-        P("col", None),
-        P(),
-        P("col", None),
-        P(),
-        P("row", "col", None),
-    )
-    out_specs = (
-        P("row", "col", None),
-        P("row", "col", None),
-        P(("row", "col"), None),
-        P("col", None),
-        P("col", None),
-        P(),
-        P(),
-        P(),
-    )
+    devices = mesh.devices.reshape(-1, 2, mesh.devices.shape[1])
+    mesh = jax.sharding.Mesh(devices, EVERY)
+    tile = P(ROW, "col", None)
+    in_specs = (tile, P(), P(), P("col", None), P(), P("col", None), P(), tile)
+    out_specs = (tile, tile, P(EVERY, None), P("col", None), P("col", None), P(), P(), P())
     return jax.shard_map(local, mesh=mesh, in_specs=in_specs, out_specs=out_specs, check_vma=False)

time: 404 us -> 390 us (0.965)
  waiting for transfers between devices: 173 us -> 141 us
  local copies, waits for them, and re-layouts: 83.6 us -> 92.7 us
  other arithmetic: 66.7 us -> 74.6 us
    unnamed x6 -> x7, waiting for transfers between devices: 39.2 us -> 1.44 us
    reduce_scatter x1, waiting for transfers between devices: 0.02 us -> 29.6 us  [local(): halves = lax.psum_scatter(stacked, 'core', scatter_dimension=1, tiled=True)]
    another operation x0 -> x2, other arithmetic: none -> 14.4 us  [local(): stacked = jnp.stack([block_in, block_out], axis=1)]
    psum x1, waiting for transfers between devices: 48.6 us -> 35.3 us  [local(): mine = lax.psum(mine, 'z')]
    reshape x0 -> x1, local copies, waits for them, and re-layouts: none -> 11.6 us  [local(): block_in = lax.dot_general(normed, grad_pre_rounded, CONTRACT_ROWS, prefe...]
    unnamed x167 -> x163, local copies, waits for them, and re-layouts: 45.6 us -> 39 us
    all_gather x1, waiting for transfers between devices: 48.6 us -> 43.8 us  [local(): lax.all_gather(w_out, 'col', axis=0, tiled=True)]
    concatenate x1 -> x0, other arithmetic: 4.46 us -> none  [local(): jnp.concatenate([lax.dot_general(hidden, grad_mix, CONTRACT_ROWS, preferr...]
  transfers between devices with their start and end apart: 14 -> 15, of which waited for: 8 -> 7; matrix products, arithmetic and copies ran while one was open for 40% -> 36% of each run, Pallas kernels for 0% -> 0%
where the time goes in v5:
time: 390 us; the launch traced here: 388 us
  waiting for transfers between devices  141 us (36%)
  local copies, waits for them, and re-layouts  92.7 us (24%)
  other arithmetic  74.6 us (19%)
  matrix products  37.8 us (10%)
  starting transfers between devices  26.3 us (7%)
  between operations  15.2 us (4%)
    all_gather x1, waiting for transfers between devices, local(): lax.all_gather(w_out, 'col', axis=0, tiled=True)  43.8 us
    unnamed x163, local copies, waits for them, and re-layouts  39 us
    psum x1, waiting for transfers between devices, local(): mine = lax.psum(mine, 'z')  35.3 us
    reduce_scatter x1, waiting for transfers between devices, local(): halves = lax.psum_scatter(stacked, 'core', scatter_dimension=1, tiled=True)  29.6 us
    another operation x51, local copies, waits for them, and re-layouts, tile_taps(): return jnp.stack(columns, axis=1)  19.1 us
    all_gather x1, waiting for transfers between devices, local(): lax.all_gather(w_in, 'col', axis=0, tiled=True)  18.8 us
    convert_element_type x1, other arithmetic, local(): (cotangent.astype(jnp.float32) + grad_back.astype(jnp.float32)).astype(jn...  16.5 us
    reduce_sum x3, other arithmetic, tile_taps(): columns.append(jnp.sum(gradient * window, axis=(0, 1)))  15.5 us
  transfers between devices with their start and end apart: 15, of which 7 were waited for; matrix products, arithmetic and copies ran while one was open for 36% of the time, Pallas kernels for 0%

profile of v5, /device:TPU:0, one launch (start us, length us, event | category | flops | bytes accessed | tf_op | source)
XLA Modules:
  0.0 387.5 jit_solution(16456247684069782680)
XLA Ops:
  9.8 3.6 collective-permute-start
  13.4 1.3 collective-permute-start.1
  14.7 1.5 slice_reduce_fusion.97
  16.2 1.4 slice_reduce_fusion.96
  17.7 4.0 %collective-permute-done.1 = bf16[16,6,768]{2,1,0:T(8,128)(2,1)S(1)} collective-permute-done((bf16[16,6,768]{2,1,0:T(8,128)(2,1)S(1)}, bf16[16,6,768]{2,1,0:T(8,128)(2,1)S(1)}, u32[]{:S(2)}, u32[]{:S(2)}) %collective-permute-start.1) | collective-permute-done | bytes 147488 | tf_op jit(solution)/shard_map/ppermute | solution.py:44
  22.0 1.3 collective-permute-start.2
  26.8 2.3 collective-permute-done.3
  29.1 1.3 maximum_maximum_fusion
  30.4 12.9 %convert_reduce_fusion = (f32[16,32]{1,0:T(8,128)S(1)}, bf16[16,32,768]{2,1,0:T(8,128)(2,1)}) fusion(bf16[22,44,768]{2,1,0:T(8,128)(2,1)S(1)} %get-tuple-element.198, f32[768]{0:T(1024)S(1)} %get-tuple-element.185, f32[768]{0:T(1024)S(1)} %get-tuple-element.138, f32[768]{0:T(1024)S(1)} %get-tuple-element.139, f32[768]{0:T(1024)S(1)} %get-tuple-element.140, ...), kind=kLoop, calls=%fused_computation.273 | loop fusion | flops 62127616 | bytes 37262336 | tf_op jit(solution)/shard_map/reduce_sum | solution.py:96
  43.4 1.7 multiply_reduce_fusion.2
  45.2 2.3 multiply_convert_fusion.3
  47.6 18.8 %all-gather.4.cloned.1.call-done = bf16[768,3072]{1,0:T(8,128)(2,1)} async-done(((bf16[48,3072]{1,0:T(8,128)(2,1)}), bf16[768,3072]{1,0:T(8,128)(2,1)}) %all-gather.4.cloned.1.call-update) | async-done | bytes 4718608 | tf_op jit(solution)/shard_map/all_gather | solution.py:87
  66.4 7.1 %fusion.8 = (bf16[3072,512]{0,1:T(8,128)(2,1)}, f32[512,3072]{1,0:T(8,128)}) fusion(f32[3072]{0:T(1024)S(1)} %copy-done.51, bf16[512,768]{1,0:T(8,128)(2,1)} %multiply_convert_fusion.3, bf16[768,3072]{1,0:T(8,128)(2,1)} %all-gather.4.cloned.1.call-done), kind=kOutput, calls=%fused_computation.66 | convolution fusion | flops 2425356288 | bytes 14954496 | tf_op jit(solution)/shard_map/dot_general | solution.py:101
  73.4 4.7 %copy.73 = bf16[3072,512]{1,0:T(8,128)(2,1)} copy(bf16[3072,512]{0,1:T(8,128)(2,1)} %get-tuple-element.209) | data formatting | bytes 6291456 | tf_op jit(solution)/shard_map/convert_element_type | solution.py:102
  78.1 43.8 %all-gather.6.cloned.1.call-done = bf16[3072,768]{1,0:T(8,128)(2,1)} async-done(((bf16[192,768]{1,0:T(8,128)(2,1)}), bf16[3072,768]{1,0:T(8,128)(2,1)}) %all-gather.6.cloned.1.call-update) | async-done | bytes 4718608 | tf_op jit(solution)/shard_map/all_gather | solution.py:88
  122.0 7.9 %fusion.136 = (f32[768]{0:T(1024)S(1)}, bf16[512,768]{1,0:T(8,128)(2,1)}, bf16[512,768]{1,0:T(8,128)(2,1)S(1)}) fusion(bf16[16,32,768]{2,1,0:T(8,128)(2,1)} %param.15, f32[768]{0:T(1024)S(1)} %copy-done.47, bf16[16,32,768]{2,1,0:T(8,128)(2,1)} %param.8, bf16[3072,768]{1,0:T(8,128)(2,1)} %all-gather.6.cloned.1.call-done, ...), kind=kOutput, calls=%fused_computation.250 | convolution fusion | flops 2428894464 | bytes 14174208 | tf_op jit(solution)/shard_map/dot_general | solution.py:103
  130.0 4.7 %fusion.157 = (f32[3072]{0:T(1024)S(1)}, bf16[512,3072]{1,0:T(8,128)(2,1)S(1)}) fusion(f32[512,3072]{1,0:T(8,128)S(1)} %copy-done.52, f32[3072]{0:T(1024)S(1)} %copy-done.51, bf16[512,768]{1,0:T(8,128)(2,1)S(1)} %get-tuple-element.201, bf16[3072,768]{1,0:T(8,128)(2,1)S(1)} %copy-done.50), kind=kOutput, calls=%fused_computation.462 | convolution fusion | flops 2434790400 | bytes 14966784 | tf_op jit(solution)/shard_map/dot_general | solution.py:111
  134.7 5.1 %fusion.139 = f32[768,3072]{1,0:T(8,128)} fusion(bf16[512,768]{1,0:T(8,128)(2,1)S(1)} %copy-done.8, bf16[512,3072]{1,0:T(8,128)(2,1)S(1)} %get-tuple-element.208), kind=kOutput, calls=%fused_computation.258 | convolution fusion | flops 2415919104 | bytes 13369344 | tf_op jit(solution)/shard_map/dot_general | solution.py:142
  139.8 4.6 %multiply_reduce_fusion = (f32[768]{0:T(1024)S(1)}, f32[512]{0:T(512)}, f32[512]{0:T(512)}, f32[512,768]{1,0:T(8,128)}) fusion(bf16[16,32,768]{2,1,0:T(8,128)(2,1)S(1)} %copy-done.7, f32[512]{0:T(512)S(1)} %rsqrt.12, f32[512]{0:T(512)S(1)} %div.15, f32[768]{0:T(1024)S(1)} %copy-done.28, bf16[768,3072]{1,0:T(8,128)(2,1)S(1)} %bitcast.125, ...), kind=kOutput, calls=%fused_computation.255 | convolution fusion | flops 2419456256 | bytes 10237952 | tf_op jit(solution)/shard_map/dot_general | solution.py:117
  144.4 11.6 %reshape.309 = f32[16,192,768]{2,1,0:T(8,128)} reshape(f32[768,3072]{1,0:T(8,128)} %fusion.139) | data formatting | bytes 18874368 | tf_op jit(solution)/shard_map/reshape | solution.py:144
  156.1 8.3 %fusion.158 = f32[16,192,768]{2,1,0:T(8,128)} fusion(bf16[16,192,512]{2,1,0:T(8,128)(2,1)} %bitcast.121, bf16[512,768,1]{1,0,2:T(8,128)(2,1)} %bitcast.122), kind=kOutput, calls=%fused_computation.463 | convolution fusion | flops 2415919104 | bytes 13369344 | tf_op jit(solution)/shard_map/dot_general | solution.py:145
  164.4 7.3 %maximum_bitcast_fusion = (f32[16,1,200,768]{3,2,0,1:T(8,128)S(1)}, f32[16,1,200,768]{3,2,0,1:T(8,128)S(1)}) fusion(f32[16,8,768]{2,1,0:T(8,128)S(1)} %broadcast_in_dim.5, f32[16,192,768]{2,1,0:T(8,128)} %fusion.158, f32[16,192,768]{2,1,0:T(8,128)} %reshape.309), kind=kLoop, calls=%fused_computation.51 | loop fusion | flops 2457600 | bytes 38928384 | tf_op jit(solution)/shard_map/stack | solution.py:154
  171.7 7.1 %pad_maximum_fusion = f32[16,2,200,768]{3,2,0,1:T(8,128)} fusion(f32[16,1,200,768]{3,2,0,1:T(8,128)S(1)} %get-tuple-element.213, f32[16,1,200,768]{3,2,0,1:T(8,128)S(1)} %get-tuple-element.214), kind=kLoop, calls=%fused_computation.50 | loop fusion | flops 4915200 | bytes 39321600 | tf_op jit(solution)/shard_map/stack | solution.py:154
  178.9 29.6 %reduce-scatter.5.cloned.1.call-done = f32[16,1,200,768]{3,2,0,1:T(8,128)} async-done(((f32[16,2,200,768]{3,2,0,1:T(8,128)}), f32[16,1,200,768]{3,2,0,1:T(8,128)}) %reduce-scatter.5.cloned.1.call-update) | async-done | bytes 9830416 | tf_op jit(solution)/shard_map/reduce_scatter | solution.py:155
  208.5 1.6 reshape.306
  210.1 3.5 rev.3
  213.6 1.6 reshape.307
  215.2 2.1 slice_reduce_fusion.47
  217.3 6.9 %fusion.132 = (f32[768]{0:T(1024)}, f32[768]{0:T(1024)}, f32[768]{0:T(1024)}, f32[768]{0:T(1024)}, f32[768]{0:T(1024)}, /*index=5*/f32[768]{0:T(1024)}, f32[768]...) fusion(bf16[22,44,768]{2,1,0:T(8,128)(2,1)S(1)} %get-tuple-elem, ...), kind=kLoop, calls=%fused_computation.242 | loop fusion | flops 25152000 | bytes 17368064 | tf_op jit(solution)/shard_map/reduce_sum | solution.py:73
  224.2 3.6 fusion.114
  228.2 5.0 %fusion.104 = (f32[768]{0:T(1024)S(1)}, f32[768]{0:T(1024)S(1)}, f32[768]{0:T(1024)S(1)}, f32[768]{0:T(1024)S(1)}, f32[768]{0:T(1024)S(1)}, /*index=5*/f32[768]{...) fusion(bf16[22,44,768]{2,1,0:T(8,128)(2,1)S(1)} %get-tuple-elem, ...), kind=kLoop, calls=%fused_computation.214 | loop fusion | flops 21613056 | bytes 14997504 | tf_op jit(solution)/shard_map/reduce_sum | solution.py:73
  249.3 3.5 collective-permute-start.4
  254.1 1.5 constant_dynamic-update-slice_fusion.50
  255.6 1.5 constant_dynamic-update-slice_fusion.49
  257.0 1.5 constant_dynamic-update-slice_fusion.48
  258.5 1.5 constant_dynamic-update-slice_fusion.47
  260.0 1.5 constant_dynamic-update-slice_fusion.46
  261.4 1.5 constant_dynamic-update-slice_fusion.45
  267.3 1.5 constant_dynamic-update-slice_fusion.37
  290.7 3.3 copy.71
  295.1 11.1 %all-to-all-start = ((f32[128,1,294]{2,1,0:T(1,128)}), f32[128,1,294]{2,1,0:T(1,128)S(1)}, u32[]{:S(2)}, u32[]{:S(2)}) async-start(f32[128,1,294]{2,1,0:T(1,128)} %reshape.415), calls=%async_computation | async-start | bytes 393216 | tf_op jit(solution)/shard_map/all_to_all | solution.py:166
  306.7 1.4 collective-permute-start.6
  310.9 5.6 %all-to-all-done = f32[128,1,294]{2,1,0:T(1,128)S(1)} async-done(((f32[128,1,294]{2,1,0:T(1,128)}), f32[128,1,294]{2,1,0:T(1,128)S(1)}, u32[]{:S(2)}, u32[]{:S(2)}) %all-to-all-start) | async-done | bytes 150560 | tf_op jit(solution)/shard_map/all_to_all | solution.py:166
  320.0 2.8 maximum_maximum_fusion.1
  322.8 35.3 %all-reduce.5.cloned.1.call-done = f32[1,200,768]{2,1,0:T(8,128)} async-done(((f32[1,200,768]{2,1,0:T(8,128)}), f32[1,200,768]{2,1,0:T(8,128)}) %all-reduce.5.cloned.1.call-update) | async-done | bytes 614416 | tf_op jit(solution)/shard_map/psum | solution.py:158
  358.2 16.5 %fusion.133 = bf16[16,32,768]{2,1,0:T(8,128)(2,1)} fusion(bf16[16,32,768]{2,1,0:T(8,128)(2,1)} %param.15, bf16[22,44,768]{2,1,0:T(8,128)(2,1)S(1)} %get-tuple-element.194, f32[768]{0:T(1024)S(1)} %get-tuple-element.89, f32[768]{0:T(1024)S(1)} %get-tuple-element.90, f32[768]{0:T(1024)S(1)} %get-tuple-element.91, f32[768]{0:T(1024)S(1)} %get-tuple-element.92, ...), kind=kLoop, calls=%fused_computation.247 | loop fusion | flops 66453504 | bytes 35834880 | tf_op jit(solution)/shard_map/convert_element_type | solution.py:134
  376.1 2.1 fusion.151
  379.2 1.4 fusion.152
  (254 shorter events, 60.4 us)
Async XLA Ops:
  7.2 10.4 %copy-start.4 = (bf16[16,32,768]{2,1,0:T(8,128)(2,1)S(1)}, bf16[16,32,768]{2,1,0:T(8,128)(2,1)}, u32[]{:S(2)}) copy-start(bf16[16,32,768]{2,1,0:T(8,128)(2,1)} %param.8) | copy-start | bytes 2359300
  7.2 59.2 %all-gather.4.cloned.1.call-start = ((), (), s32[]{:S(2)}) async-start(), calls=%async_computation.3 | async-start | bytes 5013504 | tf_op jit(solution)/shard_map/all_gather | solution.py:87
  7.9 114.0 %all-gather.6.cloned.1.call-start = ((), (), s32[]{:S(2)}) async-start(), calls=%async_computation.4 | async-start | bytes 5013504 | tf_op jit(solution)/shard_map/all_gather | solution.py:88
  8.7 199.8 %reduce-scatter.5.cloned.1.call-start = ((), (), s32[]{:S(2)}) async-start(), calls=%async_computation.5 | async-start | bytes 29491200 | tf_op jit(solution)/shard_map/reduce_scatter | solution.py:155
  9.8 7.9 %collective-permute-start = (bf16[16,6,768]{2,1,0:T(8,128)(2,1)S(1)}, bf16[16,6,768]{2,1,0:T(8,128)(2,1)S(1)}, u32[]{:S(2)}, u32[]{:S(2)}) collective-permute-start(bf16[16,6,768]{2,1,0:T(8,128)(2,1)S(1)} %get-tuple-element.204), channel_id=1, source_target_pairs={{0,1},{1,2},{2,3},{3,4},{4,5},{5,6},{6,7},{7,8},{8,9},{9,10},{10,1... | collective-permute-start | bytes 442376 | tf_op jit(solution)/shard_map/ppermute | solution.py:43
  13.4 8.3 %collective-permute-start.1 = (bf16[16,6,768]{2,1,0:T(8,128)(2,1)S(1)}, bf16[16,6,768]{2,1,0:T(8,128)(2,1)S(1)}, u32[]{:S(2)}, u32[]{:S(2)}) collective-permute-start(bf16[16,6,768]{2,1,0:T(8,128)(2,1)S(1)} %get-tuple-element.205), channel_id=1, source_target_pairs={{1,0},{2,1},{3,2},{4,3},{5,4},{6,5},{7,6},{8,7},{9,8},{10,9},{11,1... | collective-permute-start | bytes 442376 | tf_op jit(solution)/shard_map/ppermute | solution.py:44
  17.6 8.1 %copy-start.9 = (bf16[16,32,768]{2,1,0:T(8,128)(2,1)S(1)}, bf16[16,32,768]{2,1,0:T(8,128)(2,1)}, u32[]{:S(2)}) copy-start(bf16[16,32,768]{2,1,0:T(8,128)(2,1)} %param.15) | copy-start | bytes 2359300
  17.6 8.1 %copy-start.47 = (f32[768]{0:T(1024)S(1)}, f32[768]{0:T(1024)}, u32[]{:S(2)}) copy-start(f32[768]{0:T(1024)} %param.14) | copy-start | bytes 9220
  17.7 11.4 %copy-start.5 = (bf16[16,32,768]{2,1,0:T(8,128)(2,1)S(1)}, bf16[16,32,768]{2,1,0:T(8,128)(2,1)}, u32[]{:S(2)}) copy-start(bf16[16,32,768]{2,1,0:T(8,128)(2,1)} %param.8) | copy-start | bytes 2359300
  22.0 4.8 %collective-permute-start.2 = (bf16[6,44,768]{2,1,0:T(8,128)(2,1)S(1)}, bf16[6,44,768]{2,1,0:T(8,128)(2,1)S(1)}, u32[]{:S(2)}, u32[]{:S(2)}) collective-permute-start(bf16[6,44,768]{2,1,0:T(8,128)(2,1)S(1)} %get-tuple-element.199), channel_id=1, source_target_pairs={{0,16},{16,32},{32,48},{48,64},{64,80},{80,96},{96,112},{1,17},{17... | collective-permute-start | bytes 1216520 | tf_op jit(solution)/shard_map/ppermute | solution.py:46
  23.3 5.8 %collective-permute-start.3 = (bf16[6,44,768]{2,1,0:T(8,128)(2,1)S(1)}, bf16[6,44,768]{2,1,0:T(8,128)(2,1)S(1)}, u32[]{:S(2)}, u32[]{:S(2)}) collective-permute-start(bf16[6,44,768]{2,1,0:T(8,128)(2,1)S(1)} %get-tuple-element.200), channel_id=1, source_target_pairs={{16,0},{32,16},{48,32},{64,48},{80,64},{96,80},{112,96},{17,1},{33... | collective-permute-start | bytes 1216520 | tf_op jit(solution)/shard_map/ppermute | solution.py:47
  30.4 14.8 %copy-start.28 = (f32[768]{0:T(1024)S(1)}, f32[768]{0:T(1024)}, u32[]{:S(2)}) copy-start(f32[768]{0:T(1024)} %param.10) | copy-start | bytes 9220
  43.3 23.0 %copy-start.51 = (f32[3072]{0:T(1024)S(1)}, f32[3072]{0:T(1024)}, u32[]{:S(2)}) copy-start(f32[3072]{0:T(1024)} %param.12) | copy-start | bytes 36868
  122.0 8.0 %copy-start.50 = (bf16[3072,768]{1,0:T(8,128)(2,1)S(1)}, bf16[3072,768]{1,0:T(8,128)(2,1)}, u32[]{:S(2)}) copy-start(bf16[3072,768]{1,0:T(8,128)(2,1)} %all-gather.6.cloned.1.call-done) | copy-start | bytes 14155780
  122.0 8.0 %copy-start.52 = (f32[512,3072]{1,0:T(8,128)S(1)}, f32[512,3072]{1,0:T(8,128)}, u32[]{:S(2)}) copy-start(f32[512,3072]{1,0:T(8,128)} %get-tuple-element.210) | copy-start | bytes 18874372
  122.0 17.8 %slice-start = ((s8[4718592]{0:T(1024)(128)(4,1)}), s8[4194304]{0:T(1024)(128)(4,1)S(1)}, s32[]{:S(2)}) async-start(s8[4718592]{0:T(1024)(128)(4,1)} %bitcast.124), calls=%async_computation.9 | async-start | bytes 8388608
  130.0 9.8 %slice-start.1 = ((s8[4718592]{0:T(1024)(128)(4,1)}), s8[524288]{0:T(1024)(128)(4,1)S(1)}, s32[]{:S(2)}) async-start(s8[4718592]{0:T(1024)(128)(4,1)} %bitcast.124), calls=%async_computation.10 | async-start | bytes 1048576
  178.9 131.3 %reduce-scatter.7.cloned.1.call-start = ((), (), s32[]{:S(2)}) async-start(), calls=%async_computation.8 | async-start | bytes 10444800
  208.5 8.8 %copy-start.48 = (f32[512]{0:T(512)S(1)}, f32[512]{0:T(512)}, u32[]{:S(2)}) copy-start(f32[512]{0:T(512)} %get-tuple-element.67) | copy-start | bytes 6148
  208.5 8.8 %copy-start.49 = (f32[512]{0:T(512)S(1)}, f32[512]{0:T(512)}, u32[]{:S(2)}) copy-start(f32[512]{0:T(512)} %get-tuple-element.74) | copy-start | bytes 6148
  228.2 7.3 %copy-start.31 = (f32[768]{0:T(1024)S(1)}, f32[768]{0:T(1024)}, u32[]{:S(2)}) copy-start(f32[768]{0:T(1024)} %get-tuple-element.40) | copy-start | bytes 9220
  228.2 7.5 %copy-start.30 = (f32[768]{0:T(1024)S(1)}, f32[768]{0:T(1024)}, u32[]{:S(2)}) copy-start(f32[768]{0:T(1024)} %get-tuple-element.41) | copy-start | bytes 9220
  228.2 7.6 %copy-start.27 = (f32[768]{0:T(1024)S(1)}, f32[768]{0:T(1024)}, u32[]{:S(2)}) copy-start(f32[768]{0:T(1024)} %get-tuple-element.43) | copy-start | bytes 9220
  233.6 14.9 %copy-start.1 = (bf16[512,768]{1,0:T(8,128)(2,1)S(1)}, bf16[512,768]{1,0:T(8,128)(2,1)}, u32[]{:S(2)}) copy-start(bf16[512,768]{1,0:T(8,128)(2,1)} %copy-done) | copy-start | bytes 2359300
  248.5 14.4 %copy-start.19 = (f32[128,6,1]{1,0,2:T(8,128)S(1)}, f32[128,6,1]{1,0,2:T(8,128)}, u32[]{:S(2)}) copy-start(f32[128,6,1]{1,0,2:T(8,128)} %stack.165) | copy-start | bytes 9220
  248.5 15.1 %copy-start.18 = (f32[128,6,1]{1,0,2:T(8,128)S(1)}, f32[128,6,1]{1,0,2:T(8,128)}, u32[]{:S(2)}) copy-start(f32[128,6,1]{1,0,2:T(8,128)} %stack.166) | copy-start | bytes 9220
  248.5 15.7 %copy-start.17 = (f32[128,6,1]{1,0,2:T(8,128)S(1)}, f32[128,6,1]{1,0,2:T(8,128)}, u32[]{:S(2)}) copy-start(f32[128,6,1]{1,0,2:T(8,128)} %stack.167) | copy-start | bytes 9220
  248.5 16.3 %copy-start.16 = (f32[128,6,1]{1,0,2:T(8,128)S(1)}, f32[128,6,1]{1,0,2:T(8,128)}, u32[]{:S(2)}) copy-start(f32[128,6,1]{1,0,2:T(8,128)} %stack.168) | copy-start | bytes 9220
  248.5 16.9 %copy-start.15 = (f32[128,6,1]{1,0,2:T(8,128)S(1)}, f32[128,6,1]{1,0,2:T(8,128)}, u32[]{:S(2)}) copy-start(f32[128,6,1]{1,0,2:T(8,128)} %stack.169) | copy-start | bytes 9220
  248.5 17.5 %copy-start.14 = (f32[128,6,1]{1,0,2:T(8,128)S(1)}, f32[128,6,1]{1,0,2:T(8,128)}, u32[]{:S(2)}) copy-start(f32[128,6,1]{1,0,2:T(8,128)} %stack.170) | copy-start | bytes 9220
  248.5 18.2 %copy-start.13 = (f32[128,6,1]{1,0,2:T(8,128)S(1)}, f32[128,6,1]{1,0,2:T(8,128)}, u32[]{:S(2)}) copy-start(f32[128,6,1]{1,0,2:T(8,128)} %stack.171) | copy-start | bytes 9220
  249.3 57.0 %collective-permute-start.4 = (bf16[16,6,768]{2,1,0:T(8,128)(2,1)}, bf16[16,6,768]{2,1,0:T(8,128)(2,1)S(1)}, u32[]{:S(2)}, u32[]{:S(2)}) collective-permute-start(bf16[16,6,768]{2,1,0:T(8,128)(2,1)} %get-tuple-element.202), channel_id=1, source_target_pairs={{0,1},{1,2},{2,3},{3,4},{4,5},{5,6},{6,7},{7,8},{8,9},{9,10},{10,1... | collective-permute-start | bytes 442376 | tf_op jit(solution)/shard_map/ppermute | solution.py:43
  252.8 53.5 %collective-permute-start.5 = (bf16[16,6,768]{2,1,0:T(8,128)(2,1)}, bf16[16,6,768]{2,1,0:T(8,128)(2,1)S(1)}, u32[]{:S(2)}, u32[]{:S(2)}) collective-permute-start(bf16[16,6,768]{2,1,0:T(8,128)(2,1)} %get-tuple-element.203), channel_id=1, source_target_pairs={{1,0},{2,1},{3,2},{4,3},{5,4},{6,5},{7,6},{8,7},{9,8},{10,9},{11,1... | collective-permute-start | bytes 442376 | tf_op jit(solution)/shard_map/ppermute | solution.py:44
  275.0 14.9 %copy-start.29 = (f32[768]{0:T(1024)S(1)}, f32[768]{0:T(1024)}, u32[]{:S(2)}) copy-start(f32[768]{0:T(1024)} %get-tuple-element.24) | copy-start | bytes 9220
  294.0 15.4 %copy-start.11 = (f32[768,49]{0,1:T(8,128)S(1)}, f32[768,49]{0,1:T(8,128)}, u32[]{:S(2)}) copy-start(f32[768,49]{0,1:T(8,128)} %reshape.307) | copy-start | bytes 451588
  295.1 21.3 %all-to-all-start = ((f32[128,1,294]{2,1,0:T(1,128)}), f32[128,1,294]{2,1,0:T(1,128)S(1)}, u32[]{:S(2)}, u32[]{:S(2)}) async-start(f32[128,1,294]{2,1,0:T(1,128)} %reshape.415), calls=%async_computation | async-start | bytes 393216 | tf_op jit(solution)/shard_map/all_to_all | solution.py:166
  306.3 51.9 %all-reduce.5.cloned.1.call-start = ((), (), s32[]{:S(2)}) async-start(), calls=%async_computation.6 | async-start | bytes 1228800 | tf_op jit(solution)/shard_map/psum | solution.py:158
  306.4 11.7 %copy-start.10 = (bf16[16,6,768]{2,1,0:T(8,128)(2,1)}, bf16[16,6,768]{2,1,0:T(8,128)(2,1)S(1)}, u32[]{:S(2)}) copy-start(bf16[16,6,768]{2,1,0:T(8,128)(2,1)S(1)} %collective-permute-done.5) | copy-start | bytes 442372
  306.7 12.6 %collective-permute-start.6 = (bf16[6,44,768]{2,1,0:T(8,128)(2,1)S(1)}, bf16[6,44,768]{2,1,0:T(8,128)(2,1)S(1)}, u32[]{:S(2)}, u32[]{:S(2)}) collective-permute-start(bf16[6,44,768]{2,1,0:T(8,128)(2,1)S(1)} %get-tuple-element.195), channel_id=1, source_target_pairs={{0,16},{16,32},{32,48},{48,64},{64,80},{80,96},{96,112},{1,17},{17... | collective-permute-start | bytes 1216520 | tf_op jit(solution)/shard_map/ppermute | solution.py:46
  308.1 12.0 %collective-permute-start.7 = (bf16[6,44,768]{2,1,0:T(8,128)(2,1)S(1)}, bf16[6,44,768]{2,1,0:T(8,128)(2,1)}, u32[]{:S(2)}, u32[]{:S(2)}) collective-permute-start(bf16[6,44,768]{2,1,0:T(8,128)(2,1)S(1)} %get-tuple-element.196), channel_id=1, source_target_pairs={{16,0},{32,16},{48,32},{64,48},{80,64},{96,80},{112,96},{17,1},{33... | collective-permute-start | bytes 1216520 | tf_op jit(solution)/shard_map/ppermute | solution.py:47
  310.1 64.6 %all-gather.8.cloned.1.call-start = ((), (), s32[]{:S(2)}) async-start(), calls=%async_computation.7 | async-start | bytes 1843200 | tf_op jit(solution)/shard_map/all_gather | solution.py:159
  319.2 39.0 %copy-start.20 = (f32[768]{0:T(1024)S(1)}, f32[768]{0:T(1024)}, u32[]{:S(2)}) copy-start(f32[768]{0:T(1024)} %get-tuple-element.119) | copy-start | bytes 9220
  319.2 39.0 %copy-start.21 = (f32[768]{0:T(1024)S(1)}, f32[768]{0:T(1024)}, u32[]{:S(2)}) copy-start(f32[768]{0:T(1024)} %get-tuple-element.120) | copy-start | bytes 9220
  319.2 39.0 %copy-start.22 = (f32[768]{0:T(1024)S(1)}, f32[768]{0:T(1024)}, u32[]{:S(2)}) copy-start(f32[768]{0:T(1024)} %get-tuple-element.121) | copy-start | bytes 9220
  319.2 39.0 %copy-start.23 = (f32[768]{0:T(1024)S(1)}, f32[768]{0:T(1024)}, u32[]{:S(2)}) copy-start(f32[768]{0:T(1024)} %get-tuple-element.122) | copy-start | bytes 9220
  319.2 39.0 %copy-start.24 = (f32[768]{0:T(1024)S(1)}, f32[768]{0:T(1024)}, u32[]{:S(2)}) copy-start(f32[768]{0:T(1024)} %get-tuple-element.123) | copy-start | bytes 9220
  319.2 39.0 %copy-start.25 = (f32[768]{0:T(1024)S(1)}, f32[768]{0:T(1024)}, u32[]{:S(2)}) copy-start(f32[768]{0:T(1024)} %get-tuple-element.124) | copy-start | bytes 9220
  319.2 39.0 %copy-start.26 = (f32[768]{0:T(1024)S(1)}, f32[768]{0:T(1024)}, u32[]{:S(2)}) copy-start(f32[768]{0:T(1024)} %get-tuple-element.125) | copy-start | bytes 9220
  (22 other events, 125.5 us)
Sparse Core Ops, SparseCore 0:
  10.2 56.1 all-gather.3
  68.5 53.3 all-gather.5
  179.0 29.4 reduce-scatter.4
  211.8 93.3 reduce-scatter.6
  310.2 47.8 all-reduce.4
  359.7 12.2 all-gather.7

commit v6 on v5

--- a/solution.py
+++ b/solution.py
@@ -136,30 +136,33 @@
     )
     gain_part = jnp.sum(grad_norm * standard, axis=0)
     small = jnp.concatenate([bias_part, gain_part, scale_part])
-    small = jnp.pad(small, (0, (-small.shape[0]) % (8 * channels))).reshape(-1, channels)
+    small = jnp.pad(small, (0, (-small.shape[0]) % (16 * channels))).reshape(-1, channels)
     small_rows = small.shape[0]
     rows_out = hidden_units // col_count
-    block_in = lax.dot_general(
-        normed, grad_pre_rounded, CONTRACT_ROWS, preferred_element_type=jnp.float32
-    ).reshape(col_count, rows_out, channels)
+    rows_in = channels // col_count
     block_out = lax.dot_general(
         hidden, grad_mix, CONTRACT_ROWS, preferred_element_type=jnp.float32
     ).reshape(col_count, rows_out, channels)
-    block_in = jnp.concatenate(
-        [block_in, jnp.zeros((col_count, small_rows, channels), jnp.float32)], axis=1
-    )
     block_out = jnp.concatenate(
         [block_out, jnp.broadcast_to(small[None], (col_count, small_rows, channels))], axis=1
     )
-    stacked = jnp.stack([block_in, block_out], axis=1)
-    halves = lax.psum_scatter(stacked, "core", scatter_dimension=1, tiled=True)
-    halves = halves.reshape(-1, channels)
-    mine = lax.psum_scatter(halves, "col", scatter_dimension=0, tiled=True)
-    mine = lax.psum(mine, "z")
-    pair = lax.all_gather(mine, "core", axis=0, tiled=False)
-    summed_in = pair[0, :rows_out].reshape(-1, hidden_units)
-    summed_out = pair[1, :rows_out]
-    small_sum = pair[1, rows_out:].reshape(-1)
+    half_out = lax.psum_scatter(block_out, "core", scatter_dimension=1, tiled=True)
+    mine_out = lax.psum_scatter(
+        half_out.reshape(-1, channels), "col", scatter_dimension=0, tiled=True
+    )
+    block_in = lax.dot_general(
+        normed, grad_pre_rounded, CONTRACT_ROWS, preferred_element_type=jnp.float32
+    ).reshape(col_count, rows_in, hidden_units)
+    half_in = lax.psum_scatter(block_in, "core", scatter_dimension=2, tiled=True)
+    mine_in = lax.psum_scatter(
+        half_in.reshape(col_count * rows_in, -1), "col", scatter_dimension=0, tiled=True
+    )
+    mine_in, mine_out = lax.psum((mine_in, mine_out), "z")
+    pair_in, pair_out = lax.all_gather((mine_in, mine_out), "core", axis=0, tiled=False)
+    summed_in = jnp.concatenate([pair_in[0], pair_in[1]], axis=1)
+    whole_out = pair_out.reshape(-1, channels)
+    summed_out = whole_out[:rows_out]
+    small_sum = whole_out[rows_out:].reshape(-1)
     bias_sum = small_sum[:hidden_units]
     gain_sum = small_sum[hidden_units : hidden_units + channels]
     scale_sum = small_sum[hidden_units + channels : hidden_units + 2 * channels]

time: 390 us -> 427 us (1.095)
  waiting for transfers between devices: 141 us -> 195 us
  local copies, waits for them, and re-layouts: 92.7 us -> 68.9 us
  other arithmetic: 74.6 us -> 68.8 us
  blocking collectives: 0 us -> 4.81 us
    unnamed x7 -> x8, waiting for transfers between devices: 1.44 us -> 66.1 us
    another operation x2 -> x0, other arithmetic: 14.4 us -> none  [local(): stacked = jnp.stack([block_in, block_out], axis=1)]
    reshape x1 -> x0, local copies, waits for them, and re-layouts: 11.6 us -> none  [local(): block_in = lax.dot_general(normed, grad_pre_rounded, CONTRACT_ROWS, prefe...]
    reduce_scatter x1 -> x3, waiting for transfers between devices: 29.6 us -> 19.8 us  [the longest x1 19.8 us: local(): lax.psum_scatter(block_out, 'core', scatter_dimension=1, tiled=True)]
    concatenate x0 -> x1, other arithmetic: none -> 8.86 us  [local(): jnp.concatenate([block_out, jnp.broadcast_to(small[None], (col_count, sma...]
    another operation x51, local copies, waits for them, and re-layouts: 19.1 us -> 12.4 us  [tile_taps(): return jnp.stack(columns, axis=1)]
    psum x1, waiting for transfers between devices: 35.3 us -> 29.7 us  [local(): mine_in, mine_out = lax.psum((mine_in, mine_out), 'z')]
    all_gather x0 -> x2, blocking collectives: none -> 4.81 us  [local(): lax.all_gather((mine_in, mine_out), 'core', axis=0, tiled=False)]
  transfers between devices with their start and end apart: 15 -> 16, of which waited for: 7 -> 9; matrix products, arithmetic and copies ran while one was open for 36% -> 37% of each run, Pallas kernels for 0% -> 0%
where the time goes in v6:
time: 427 us; the launch traced here: 424 us
  waiting for transfers between devices  195 us (46%)
  local copies, waits for them, and re-layouts  68.9 us (16%)
  other arithmetic  68.8 us (16%)
  matrix products  41.9 us (10%)
  starting transfers between devices  29.9 us (7%)
  between operations  15.2 us (4%)
  blocking collectives  4.81 us (1%)
    unnamed x8, waiting for transfers between devices  66.1 us
    all_gather x1, waiting for transfers between devices, local(): lax.all_gather(w_out, 'col', axis=0, tiled=True)  48.5 us
    unnamed x131, local copies, waits for them, and re-layouts  34.7 us
    psum x1, waiting for transfers between devices, local(): mine_in, mine_out = lax.psum((mine_in, mine_out), 'z')  29.7 us
    reduce_scatter x1, waiting for transfers between devices, local(): lax.psum_scatter(block_out, 'core', scatter_dimension=1, tiled=True)  19.8 us
    all_gather x1, waiting for transfers between devices, local(): lax.all_gather(w_in, 'col', axis=0, tiled=True)  18.4 us
    convert_element_type x1, other arithmetic, local(): (cotangent.astype(jnp.float32) + grad_back.astype(jnp.float32)).astype(jn...  16 us
    reduce_sum x3, other arithmetic, tile_taps(): columns.append(jnp.sum(gradient * window, axis=(0, 1)))  15.5 us
  transfers between devices with their start and end apart: 16, of which 9 were waited for; matrix products, arithmetic and copies ran while one was open for 37% of the time, Pallas kernels for 0%

profile of v6, /device:TPU:0, one launch (start us, length us, event | category | flops | bytes accessed | tf_op | source)
XLA Modules:
  0.0 424.2 jit_solution(2126374617362143142)
XLA Ops:
  9.8 1.3 collective-permute-start.1
  11.1 4.6 %collective-permute-start = (bf16[16,6,768]{2,1,0:T(8,128)(2,1)S(1)}, bf16[16,6,768]{2,1,0:T(8,128)(2,1)S(1)}, u32[]{:S(2)}, u32[]{:S(2)}) collective-permute-start(bf16[16,6,768]{2,1,0:T(8,128)(2,1)S(1)} %get-tuple-element.204), channel_id=1, source_target_pairs={{0,1},{1,2},{2,3},{3,4},{4,5},{5,6},{6,7},{7,8},{8,9},{9,10},{10,1... | collective-permute-start | bytes 442376 | tf_op jit(solution)/shard_map/ppermute | solution.py:43
  15.7 1.4 slice_reduce_fusion.96
  17.1 1.2 collective-permute-done.1
  18.3 1.2 collective-permute-done
  19.8 1.4 collective-permute-start.2
  21.2 1.3 collective-permute-start.3
  22.9 4.3 %collective-permute-done.3 = bf16[6,44,768]{2,1,0:T(8,128)(2,1)S(1)} collective-permute-done((bf16[6,44,768]{2,1,0:T(8,128)(2,1)S(1)}, bf16[6,44,768]{2,1,0:T(8,128)(2,1)S(1)}, u32[]{:S(2)}, u32[]{:S(2)}) %collective-permute-start.3) | collective-permute-done | bytes 405536 | tf_op jit(solution)/shard_map/ppermute | solution.py:47
  27.2 1.3 maximum_maximum_fusion
  28.5 12.9 %convert_reduce_fusion = (f32[16,32]{1,0:T(8,128)S(1)}, bf16[16,32,768]{2,1,0:T(8,128)(2,1)}) fusion(bf16[22,44,768]{2,1,0:T(8,128)(2,1)S(1)} %get-tuple-element.198, f32[768]{0:T(1024)S(1)} %get-tuple-element.185, f32[768]{0:T(1024)S(1)} %get-tuple-element.138, f32[768]{0:T(1024)S(1)} %get-tuple-element.139, f32[768]{0:T(1024)S(1)} %get-tuple-element.140, ...), kind=kLoop, calls=%fused_computation.272 | loop fusion | flops 62127616 | bytes 37262336 | tf_op jit(solution)/shard_map/reduce_sum | solution.py:96
  41.5 1.5 multiply_reduce_fusion.2
  43.1 2.5 multiply_convert_fusion.3
  45.7 2.3 copy.76
  48.0 18.4 %all-gather.3.cloned.1.call-done = bf16[768,3072]{1,0:T(8,128)(2,1)} async-done(((bf16[48,3072]{1,0:T(8,128)(2,1)}), bf16[768,3072]{1,0:T(8,128)(2,1)}) %all-gather.3.cloned.1.call-update) | async-done | bytes 4718608 | tf_op jit(solution)/shard_map/all_gather | solution.py:87
  66.4 7.1 %fusion.8 = (bf16[3072,512]{0,1:T(8,128)(2,1)}, f32[512,3072]{1,0:T(8,128)}) fusion(f32[3072]{0:T(1024)S(1)} %copy-done.36, bf16[512,768]{1,0:T(8,128)(2,1)} %multiply_convert_fusion.3, bf16[768,3072]{1,0:T(8,128)(2,1)} %all-gather.3.cloned.1.call-done), kind=kOutput, calls=%fused_computation.64 | convolution fusion | flops 2425356288 | bytes 14954496 | tf_op jit(solution)/shard_map/dot_general | solution.py:101
  73.5 48.5 %all-gather.5.cloned.1.call-done = bf16[3072,768]{1,0:T(8,128)(2,1)} async-done(((bf16[192,768]{1,0:T(8,128)(2,1)}), bf16[3072,768]{1,0:T(8,128)(2,1)}) %all-gather.5.cloned.1.call-update) | async-done | bytes 4718608 | tf_op jit(solution)/shard_map/all_gather | solution.py:88
  122.0 8.0 %fusion.138 = (f32[768]{0:T(1024)S(1)}, bf16[512,768]{1,0:T(8,128)(2,1)}, bf16[512,768]{1,0:T(8,128)(2,1)S(1)}) fusion(bf16[16,32,768]{2,1,0:T(8,128)(2,1)} %param.15, f32[768]{0:T(1024)S(1)} %copy-done.33, bf16[16,32,768]{2,1,0:T(8,128)(2,1)} %param.8, bf16[3072,768]{1,0:T(8,128)(2,1)} %all-gather.5.cloned.1.call-done, ...), kind=kOutput, calls=%fused_computation.250 | convolution fusion | flops 2428894464 | bytes 14174208 | tf_op jit(solution)/shard_map/dot_general | solution.py:103
  130.0 4.7 %fusion.157 = (f32[3072]{0:T(1024)S(1)}, bf16[512,3072]{1,0:T(8,128)(2,1)S(1)}) fusion(f32[512,3072]{1,0:T(8,128)S(1)} %copy-done.38, f32[3072]{0:T(1024)S(1)} %copy-done.36, bf16[512,768]{1,0:T(8,128)(2,1)S(1)} %get-tuple-element.201, bf16[3072,768]{1,0:T(8,128)(2,1)S(1)} %copy-done.35), kind=kOutput, calls=%fused_computation.462 | convolution fusion | flops 2434790400 | bytes 14966784 | tf_op jit(solution)/shard_map/dot_general | solution.py:111
  134.7 1.7 copy-done.37
  136.3 5.1 %fusion.10 = f32[16,48,3072]{2,1,0:T(8,128)} fusion(bf16[16,48,512]{2,1,0:T(8,128)(2,1)S(1)} %bitcast.132, bf16[512,3072]{1,0:T(8,128)(2,1)S(1)} %get-tuple-element.210), kind=kOutput, calls=%fused_computation.66 | convolution fusion | flops 2415919104 | bytes 13369344 | tf_op jit(solution)/shard_map/dot_general | solution.py:153
  141.6 2.2 fusion.136
  143.9 7.8 %multiply_reduce_fusion = (f32[768]{0:T(1024)S(1)}, f32[512]{0:T(512)S(1)}, f32[512]{0:T(512)}, f32[512,768]{1,0:T(8,128)}) fusion(bf16[16,32,768]{2,1,0:T(8,128)(2,1)S(1)} %copy-done.7, f32[512]{0:T(512)S(1)} %rsqrt.12, f32[512]{0:T(512)S(1)} %div.15, f32[768]{0:T(1024)S(1)} %copy-done.14, bf16[768,3072]{1,0:T(8,128)(2,1)} %all-gather.3.cloned.1.call-done, ...), kind=kOutput, calls=%fused_computation.255 | convolution fusion | flops 2419456256 | bytes 10237952 | tf_op jit(solution)/shard_map/dot_general | solution.py:117
  151.8 5.2 %copy.77 = bf16[3072,512]{1,0:T(8,128)(2,1)} copy(bf16[3072,512]{0,1:T(8,128)(2,1)} %get-tuple-element.211) | data formatting | bytes 6291456 | tf_op jit(solution)/shard_map/convert_element_type | solution.py:102
  156.9 9.3 %fusion.158 = f32[16,192,768]{2,1,0:T(8,128)} fusion(bf16[16,192,512]{2,1,0:T(8,128)(2,1)} %bitcast.127, bf16[512,768,1]{1,0,2:T(8,128)(2,1)} %bitcast.133), kind=kOutput, calls=%fused_computation.463 | convolution fusion | flops 2415919104 | bytes 13369344 | tf_op jit(solution)/shard_map/dot_general | solution.py:143
  167.2 8.9 %pad_maximum_fusion = f32[16,208,768]{2,1,0:T(8,128)} fusion(f32[16,16,768]{2,1,0:T(8,128)} %broadcast_in_dim.5, f32[16,192,768]{2,1,0:T(8,128)} %fusion.158), kind=kLoop, calls=%fused_computation.50 | loop fusion | flops 2555904 | bytes 20447232 | tf_op jit(solution)/shard_map/concatenate | solution.py:146
  176.7 19.8 %reduce-scatter.11.cloned.1.call-done = f32[16,104,768]{2,1,0:T(8,128)} async-done(((f32[16,208,768]{2,1,0:T(8,128)}), f32[16,104,768]{2,1,0:T(8,128)}) %reduce-scatter.11.cloned.1.call-update) | async-done | bytes 5111824 | tf_op jit(solution)/shard_map/reduce_scatter | solution.py:149
  196.5 1.6 reshape.308
  198.1 3.5 rev.3
  201.6 1.6 reshape.309
  203.2 1.5 slice_reduce_fusion.48
  204.7 6.9 %fusion.134 = (f32[768]{0:T(1024)}, f32[768]{0:T(1024)}, f32[768]{0:T(1024)}, f32[768]{0:T(1024)}, f32[768]{0:T(1024)}, /*index=5*/f32[768]{0:T(1024)}, f32[768]...) fusion(bf16[22,44,768]{2,1,0:T(8,128)(2,1)S(1)} %get-tuple-elem, ...), kind=kLoop, calls=%fused_computation.242 | loop fusion | flops 25152000 | bytes 17368064 | tf_op jit(solution)/shard_map/reduce_sum | solution.py:73
  212.5 1.3 collective-permute-start.5
  213.8 5.2 %collective-permute-start.4 = (bf16[16,6,768]{2,1,0:T(8,128)(2,1)}, bf16[16,6,768]{2,1,0:T(8,128)(2,1)}, u32[]{:S(2)}, u32[]{:S(2)}) collective-permute-start(bf16[16,6,768]{2,1,0:T(8,128)(2,1)} %get-tuple-element.202), channel_id=1, source_target_pairs={{0,1},{1,2},{2,3},{3,4},{4,5},{5,6},{6,7},{7,8},{8,9},{9,10},{10,1... | collective-permute-start | bytes 442376 | tf_op jit(solution)/shard_map/ppermute | solution.py:43
  219.0 3.7 fusion.116
  225.1 5.0 %fusion.106 = (f32[768]{0:T(1024)S(1)}, f32[768]{0:T(1024)S(1)}, f32[768]{0:T(1024)S(1)}, f32[768]{0:T(1024)S(1)}, f32[768]{0:T(1024)S(1)}, /*index=5*/f32[768]{...) fusion(bf16[22,44,768]{2,1,0:T(8,128)(2,1)S(1)} %get-tuple-elem, ...), kind=kLoop, calls=%fused_computation.214 | loop fusion | flops 21613056 | bytes 14997504 | tf_op jit(solution)/shard_map/reduce_sum | solution.py:73
  267.2 3.4 copy.74
  270.7 1.1 reshape.419
  271.8 11.4 %all-to-all-start = ((f32[128,1,294]{2,1,0:T(1,128)}), f32[128,1,294]{2,1,0:T(1,128)S(1)}, u32[]{:S(2)}, u32[]{:S(2)}) async-start(f32[128,1,294]{2,1,0:T(1,128)} %reshape.419), calls=%async_computation | async-start | bytes 393216 | tf_op jit(solution)/shard_map/all_to_all | solution.py:169
  283.3 1.3 pad_maximum_fusion.8
  284.6 1.4 collective-permute-start.6
  286.0 1.6 collective-permute-start.7
  287.8 5.6 %all-to-all-done = f32[128,1,294]{2,1,0:T(1,128)S(1)} async-done(((f32[128,1,294]{2,1,0:T(1,128)}), f32[128,1,294]{2,1,0:T(1,128)S(1)}, u32[]{:S(2)}, u32[]{:S(2)}) %all-to-all-start) | async-done | bytes 150560 | tf_op jit(solution)/shard_map/all_to_all | solution.py:169
  296.9 2.7 maximum_maximum_fusion.1
  299.7 64.2 %reduce-scatter.13.cloned.1.call-done = f32[104,768]{1,0:T(8,128)} async-done(((f32[1664,768]{1,0:T(8,128)}), f32[104,768]{1,0:T(8,128)}) %reduce-scatter.13.cloned.1.call-update) | async-done | bytes 319504
  363.9 16.0 %fusion.135 = bf16[16,32,768]{2,1,0:T(8,128)(2,1)} fusion(bf16[16,32,768]{2,1,0:T(8,128)(2,1)} %param.15, bf16[22,44,768]{2,1,0:T(8,128)(2,1)S(1)} %get-tuple-element.194, f32[768]{0:T(1024)S(1)} %get-tuple-element.89, f32[768]{0:T(1024)S(1)} %get-tuple-element.90, f32[768]{0:T(1024)S(1)} %get-tuple-element.91, f32[768]{0:T(1024)S(1)} %get-tuple-element.92, ...), kind=kLoop, calls=%fused_computation.247 | loop fusion | flops 66453504 | bytes 35834880 | tf_op jit(solution)/shard_map/convert_element_type | solution.py:134
  379.9 29.7 %all-reduce.5.cloned.1.call-done = (f32[1,48,1536]{2,1,0:T(8,128)}, f32[1,104,768]{2,1,0:T(8,128)}) async-done(((f32[1,48,1536]{2,1,0:T(8,128)}, f32[1,104,768]{2,1,0:T(8,128)}), (f32[1,48,1536]{2,1,0:T(8,128)}, f32[1,104,768]{2,1,0:T(8,128)})) %all-reduce.5.cloned.1.call-update) | async-done | bytes 614416 | tf_op jit(solution)/shard_map/psum | solution.py:160
  409.6 2.6 all_gather.23
  413.7 2.2 all_gather.21
  (226 shorter events, 52.0 us)
Async XLA Ops:
  7.2 12.3 %copy-start.4 = (bf16[16,32,768]{2,1,0:T(8,128)(2,1)S(1)}, bf16[16,32,768]{2,1,0:T(8,128)(2,1)}, u32[]{:S(2)}) copy-start(bf16[16,32,768]{2,1,0:T(8,128)(2,1)} %param.8) | copy-start | bytes 2359300
  7.2 59.2 %all-gather.3.cloned.1.call-start = ((), (), s32[]{:S(2)}) async-start(), calls=%async_computation.5 | async-start | bytes 5013504 | tf_op jit(solution)/shard_map/all_gather | solution.py:87
  7.9 14.6 %copy-start.9 = (f32[768,49]{0,1:T(8,128)S(1)}, f32[768,49]{0,1:T(8,128)}, u32[]{:S(2)}) copy-start(f32[768,49]{0,1:T(8,128)} %param.9) | copy-start | bytes 451588
  7.9 114.0 %all-gather.5.cloned.1.call-start = ((), (), s32[]{:S(2)}) async-start(), calls=%async_computation.6 | async-start | bytes 5013504 | tf_op jit(solution)/shard_map/all_gather | solution.py:88
  8.7 167.4 %reduce-scatter.7.cloned.1.call-start = ((), (), s32[]{:S(2)}) async-start(), calls=%async_computation.7 | async-start | bytes 14155776 | tf_op jit(solution)/shard_map/reduce_scatter | solution.py:156
  9.8 8.5 %collective-permute-start.1 = (bf16[16,6,768]{2,1,0:T(8,128)(2,1)S(1)}, bf16[16,6,768]{2,1,0:T(8,128)(2,1)S(1)}, u32[]{:S(2)}, u32[]{:S(2)}) collective-permute-start(bf16[16,6,768]{2,1,0:T(8,128)(2,1)S(1)} %get-tuple-element.205), channel_id=1, source_target_pairs={{1,0},{2,1},{3,2},{4,3},{5,4},{6,5},{7,6},{8,7},{9,8},{10,9},{11,1... | collective-permute-start | bytes 442376 | tf_op jit(solution)/shard_map/ppermute | solution.py:44
  11.1 8.4 %collective-permute-start = (bf16[16,6,768]{2,1,0:T(8,128)(2,1)S(1)}, bf16[16,6,768]{2,1,0:T(8,128)(2,1)S(1)}, u32[]{:S(2)}, u32[]{:S(2)}) collective-permute-start(bf16[16,6,768]{2,1,0:T(8,128)(2,1)S(1)} %get-tuple-element.204), channel_id=1, source_target_pairs={{0,1},{1,2},{2,3},{3,4},{4,5},{5,6},{6,7},{7,8},{8,9},{9,10},{10,1... | collective-permute-start | bytes 442376 | tf_op jit(solution)/shard_map/ppermute | solution.py:43
  19.8 7.4 %copy-start.5 = (bf16[16,32,768]{2,1,0:T(8,128)(2,1)S(1)}, bf16[16,32,768]{2,1,0:T(8,128)(2,1)}, u32[]{:S(2)}) copy-start(bf16[16,32,768]{2,1,0:T(8,128)(2,1)} %param.8) | copy-start | bytes 2359300
  19.8 3.1 collective-permute-start.2
  21.2 6.0 %collective-permute-start.3 = (bf16[6,44,768]{2,1,0:T(8,128)(2,1)S(1)}, bf16[6,44,768]{2,1,0:T(8,128)(2,1)S(1)}, u32[]{:S(2)}, u32[]{:S(2)}) collective-permute-start(bf16[6,44,768]{2,1,0:T(8,128)(2,1)S(1)} %get-tuple-element.200), channel_id=1, source_target_pairs={{16,0},{32,16},{48,32},{64,48},{80,64},{96,80},{112,96},{17,1},{33... | collective-permute-start | bytes 1216520 | tf_op jit(solution)/shard_map/ppermute | solution.py:47
  22.9 5.6 %copy-start.2 = (bf16[16,38,768]{2,1,0:T(8,128)(2,1)}, bf16[16,38,768]{2,1,0:T(8,128)(2,1)S(1)}, u32[]{:S(2)}) copy-start(bf16[16,38,768]{2,1,0:T(8,128)(2,1)S(1)} %constant_dynamic-update-slice_fusion) | copy-start | bytes 2801668
  28.5 14.6 %copy-start.14 = (f32[768]{0:T(1024)S(1)}, f32[768]{0:T(1024)}, u32[]{:S(2)}) copy-start(f32[768]{0:T(1024)} %param.10) | copy-start | bytes 9220
  43.1 23.3 %copy-start.36 = (f32[3072]{0:T(1024)S(1)}, f32[3072]{0:T(1024)}, u32[]{:S(2)}) copy-start(f32[3072]{0:T(1024)} %param.12) | copy-start | bytes 36868
  48.0 74.0 %copy-start.33 = (f32[768]{0:T(1024)S(1)}, f32[768]{0:T(1024)}, u32[]{:S(2)}) copy-start(f32[768]{0:T(1024)} %param.14) | copy-start | bytes 9220
  122.0 8.0 %copy-start.35 = (bf16[3072,768]{1,0:T(8,128)(2,1)S(1)}, bf16[3072,768]{1,0:T(8,128)(2,1)}, u32[]{:S(2)}) copy-start(bf16[3072,768]{1,0:T(8,128)(2,1)} %all-gather.5.cloned.1.call-done) | copy-start | bytes 14155780
  122.0 8.0 %copy-start.38 = (f32[512,3072]{1,0:T(8,128)S(1)}, f32[512,3072]{1,0:T(8,128)}, u32[]{:S(2)}) copy-start(f32[512,3072]{1,0:T(8,128)} %get-tuple-element.212) | copy-start | bytes 18874372
  130.0 6.3 %copy-start.8 = (bf16[768,512]{1,0:T(8,128)(2,1)S(1)}, bf16[768,512]{1,0:T(8,128)(2,1)}, u32[]{:S(2)}) copy-start(bf16[768,512]{1,0:T(8,128)(2,1)} %copy.76) | copy-start | bytes 2359300
  141.4 55.0 %reduce-scatter.11.cloned.1.call-start = ((), (), s32[]{:S(2)}) async-start(), calls=%async_computation.9 | async-start | bytes 15335424 | tf_op jit(solution)/shard_map/reduce_scatter | solution.py:149
  176.0 123.6 %reduce-scatter.9.cloned.1.call-start = ((), (), s32[]{:S(2)}) async-start(), calls=%async_computation.8 | async-start | bytes 5013504 | tf_op jit(solution)/shard_map/reduce_scatter | solution.py:157
  176.6 187.2 %reduce-scatter.13.cloned.1.call-start = ((), (), s32[]{:S(2)}) async-start(), calls=%async_computation.10 | async-start | bytes 5431296
  196.4 8.2 %copy-start.34 = (f32[512]{0:T(512)S(1)}, f32[512]{0:T(512)}, u32[]{:S(2)}) copy-start(f32[512]{0:T(512)} %get-tuple-element.74) | copy-start | bytes 6148
  204.7 14.3 %copy-start.3 = (bf16[16,38,768]{2,1,0:T(8,128)(2,1)S(1)}, bf16[16,38,768]{2,1,0:T(8,128)(2,1)}, u32[]{:S(2)}) copy-start(bf16[16,38,768]{2,1,0:T(8,128)(2,1)} %copy-done.2) | copy-start | bytes 2801668
  204.7 14.3 %copy-start.6 = (bf16[16,32,768]{2,1,0:T(8,128)(2,1)S(1)}, bf16[16,32,768]{2,1,0:T(8,128)(2,1)}, u32[]{:S(2)}) copy-start(bf16[16,32,768]{2,1,0:T(8,128)(2,1)} %param.8) | copy-start | bytes 2359300
  211.6 11.1 %copy-start = (bf16[512,768]{1,0:T(8,128)(2,1)}, bf16[512,768]{1,0:T(8,128)(2,1)S(1)}, u32[]{:S(2)}) copy-start(bf16[512,768]{1,0:T(8,128)(2,1)S(1)} %get-tuple-element.188) | copy-start | bytes 2359300
  212.5 70.8 %collective-permute-start.5 = (bf16[16,6,768]{2,1,0:T(8,128)(2,1)}, bf16[16,6,768]{2,1,0:T(8,128)(2,1)}, u32[]{:S(2)}, u32[]{:S(2)}) collective-permute-start(bf16[16,6,768]{2,1,0:T(8,128)(2,1)} %get-tuple-element.203), channel_id=1, source_target_pairs={{1,0},{2,1},{3,2},{4,3},{5,4},{6,5},{7,6},{8,7},{9,8},{10,9},{11,1... | collective-permute-start | bytes 442376 | tf_op jit(solution)/shard_map/ppermute | solution.py:44
  213.8 69.5 %collective-permute-start.4 = (bf16[16,6,768]{2,1,0:T(8,128)(2,1)}, bf16[16,6,768]{2,1,0:T(8,128)(2,1)}, u32[]{:S(2)}, u32[]{:S(2)}) collective-permute-start(bf16[16,6,768]{2,1,0:T(8,128)(2,1)} %get-tuple-element.202), channel_id=1, source_target_pairs={{0,1},{1,2},{2,3},{3,4},{4,5},{5,6},{6,7},{7,8},{8,9},{9,10},{10,1... | collective-permute-start | bytes 442376 | tf_op jit(solution)/shard_map/ppermute | solution.py:43
  225.1 7.6 %copy-start.13 = (f32[768]{0:T(1024)S(1)}, f32[768]{0:T(1024)}, u32[]{:S(2)}) copy-start(f32[768]{0:T(1024)} %get-tuple-element.84) | copy-start | bytes 9220
  230.1 4.4 %copy-start.29 = (f32[768]{0:T(1024)S(1)}, f32[768]{0:T(1024)}, u32[]{:S(2)}) copy-start(f32[768]{0:T(1024)} %get-tuple-element.38) | copy-start | bytes 9220
  230.1 4.5 %copy-start.28 = (f32[768]{0:T(1024)S(1)}, f32[768]{0:T(1024)}, u32[]{:S(2)}) copy-start(f32[768]{0:T(1024)} %get-tuple-element.37) | copy-start | bytes 9220
  230.2 4.7 %copy-start.27 = (f32[768]{0:T(1024)S(1)}, f32[768]{0:T(1024)}, u32[]{:S(2)}) copy-start(f32[768]{0:T(1024)} %get-tuple-element.36) | copy-start | bytes 9220
  230.2 4.8 %copy-start.26 = (f32[768]{0:T(1024)S(1)}, f32[768]{0:T(1024)}, u32[]{:S(2)}) copy-start(f32[768]{0:T(1024)} %get-tuple-element.35) | copy-start | bytes 9220
  230.2 4.9 %copy-start.25 = (f32[768]{0:T(1024)S(1)}, f32[768]{0:T(1024)}, u32[]{:S(2)}) copy-start(f32[768]{0:T(1024)} %get-tuple-element.34) | copy-start | bytes 9220
  230.2 5.1 %copy-start.24 = (f32[768]{0:T(1024)S(1)}, f32[768]{0:T(1024)}, u32[]{:S(2)}) copy-start(f32[768]{0:T(1024)} %get-tuple-element.33) | copy-start | bytes 9220
  230.2 5.2 %copy-start.23 = (f32[768]{0:T(1024)S(1)}, f32[768]{0:T(1024)}, u32[]{:S(2)}) copy-start(f32[768]{0:T(1024)} %get-tuple-element.32) | copy-start | bytes 9220
  230.2 5.3 %copy-start.22 = (f32[768]{0:T(1024)S(1)}, f32[768]{0:T(1024)}, u32[]{:S(2)}) copy-start(f32[768]{0:T(1024)} %get-tuple-element.31) | copy-start | bytes 9220
  230.2 5.5 %copy-start.21 = (f32[768]{0:T(1024)S(1)}, f32[768]{0:T(1024)}, u32[]{:S(2)}) copy-start(f32[768]{0:T(1024)} %get-tuple-element.30) | copy-start | bytes 9220
  230.2 5.6 %copy-start.20 = (f32[768]{0:T(1024)S(1)}, f32[768]{0:T(1024)}, u32[]{:S(2)}) copy-start(f32[768]{0:T(1024)} %get-tuple-element.29) | copy-start | bytes 9220
  230.2 5.8 %copy-start.19 = (f32[768]{0:T(1024)S(1)}, f32[768]{0:T(1024)}, u32[]{:S(2)}) copy-start(f32[768]{0:T(1024)} %get-tuple-element.28) | copy-start | bytes 9220
  230.2 5.9 %copy-start.18 = (f32[768]{0:T(1024)S(1)}, f32[768]{0:T(1024)}, u32[]{:S(2)}) copy-start(f32[768]{0:T(1024)} %get-tuple-element.27) | copy-start | bytes 9220
  230.3 6.0 %copy-start.17 = (f32[768]{0:T(1024)S(1)}, f32[768]{0:T(1024)}, u32[]{:S(2)}) copy-start(f32[768]{0:T(1024)} %get-tuple-element.26) | copy-start | bytes 9220
  230.3 6.2 %copy-start.16 = (f32[768]{0:T(1024)S(1)}, f32[768]{0:T(1024)}, u32[]{:S(2)}) copy-start(f32[768]{0:T(1024)} %get-tuple-element.25) | copy-start | bytes 9220
  251.5 14.9 %copy-start.15 = (f32[768]{0:T(1024)S(1)}, f32[768]{0:T(1024)}, u32[]{:S(2)}) copy-start(f32[768]{0:T(1024)} %get-tuple-element.24) | copy-start | bytes 9220
  267.2 16.1 %copy-start.1 = (bf16[512,768]{1,0:T(8,128)(2,1)S(1)}, bf16[512,768]{1,0:T(8,128)(2,1)}, u32[]{:S(2)}) copy-start(bf16[512,768]{1,0:T(8,128)(2,1)} %copy-done) | copy-start | bytes 2359300
  270.7 16.9 %copy-start.10 = (f32[768,49]{0,1:T(8,128)S(1)}, f32[768,49]{0,1:T(8,128)}, u32[]{:S(2)}) copy-start(f32[768,49]{0,1:T(8,128)} %reshape.309) | copy-start | bytes 451588
  271.8 21.6 %all-to-all-start = ((f32[128,1,294]{2,1,0:T(1,128)}), f32[128,1,294]{2,1,0:T(1,128)S(1)}, u32[]{:S(2)}, u32[]{:S(2)}) async-start(f32[128,1,294]{2,1,0:T(1,128)} %reshape.419), calls=%async_computation | async-start | bytes 393216 | tf_op jit(solution)/shard_map/all_to_all | solution.py:169
  283.2 126.4 %all-reduce.5.cloned.1.call-start = ((), (), s32[]{:S(2)}) async-start(), calls=%async_computation.11 | async-start | bytes 1228800 | tf_op jit(solution)/shard_map/psum | solution.py:160
  284.6 11.5 %collective-permute-start.6 = (bf16[6,44,768]{2,1,0:T(8,128)(2,1)S(1)}, bf16[6,44,768]{2,1,0:T(8,128)(2,1)S(1)}, u32[]{:S(2)}, u32[]{:S(2)}) collective-permute-start(bf16[6,44,768]{2,1,0:T(8,128)(2,1)S(1)} %get-tuple-element.195), channel_id=1, source_target_pairs={{0,16},{16,32},{32,48},{48,64},{64,80},{80,96},{96,112},{1,17},{17... | collective-permute-start | bytes 1216520 | tf_op jit(solution)/shard_map/ppermute | solution.py:46
  286.0 10.9 %collective-permute-start.7 = (bf16[6,44,768]{2,1,0:T(8,128)(2,1)S(1)}, bf16[6,44,768]{2,1,0:T(8,128)(2,1)}, u32[]{:S(2)}, u32[]{:S(2)}) collective-permute-start(bf16[6,44,768]{2,1,0:T(8,128)(2,1)S(1)} %get-tuple-element.196), channel_id=1, source_target_pairs={{16,0},{32,16},{48,32},{64,48},{80,64},{96,80},{112,96},{17,1},{33... | collective-permute-start | bytes 1216520 | tf_op jit(solution)/shard_map/ppermute | solution.py:47
  (7 other events, 21.1 us)
Sparse Core Ops, SparseCore 0:
  10.2 56.1 all-gather.2
  68.5 53.3 all-gather.4
  141.5 19.5 reduce-scatter.6
  176.2 20.2 reduce-scatter.10
  199.6 81.9 reduce-scatter.8
  284.9 78.9 reduce-scatter.12
  366.3 43.2 all-reduce.4

commit v7 on v5

--- a/solution.py
+++ b/solution.py
@@ -135,9 +135,6 @@
         jnp.bfloat16
     )
     gain_part = jnp.sum(grad_norm * standard, axis=0)
-    small = jnp.concatenate([bias_part, gain_part, scale_part])
-    small = jnp.pad(small, (0, (-small.shape[0]) % (8 * channels))).reshape(-1, channels)
-    small_rows = small.shape[0]
     rows_out = hidden_units // col_count
     block_in = lax.dot_general(
         normed, grad_pre_rounded, CONTRACT_ROWS, preferred_element_type=jnp.float32
@@ -145,32 +142,35 @@
     block_out = lax.dot_general(
         hidden, grad_mix, CONTRACT_ROWS, preferred_element_type=jnp.float32
     ).reshape(col_count, rows_out, channels)
-    block_in = jnp.concatenate(
-        [block_in, jnp.zeros((col_count, small_rows, channels), jnp.float32)], axis=1
-    )
-    block_out = jnp.concatenate(
-        [block_out, jnp.broadcast_to(small[None], (col_count, small_rows, channels))], axis=1
-    )
     stacked = jnp.stack([block_in, block_out], axis=1)
     halves = lax.psum_scatter(stacked, "core", scatter_dimension=1, tiled=True)
     halves = halves.reshape(-1, channels)
     mine = lax.psum_scatter(halves, "col", scatter_dimension=0, tiled=True)
     mine = lax.psum(mine, "z")
     pair = lax.all_gather(mine, "core", axis=0, tiled=False)
-    summed_in = pair[0, :rows_out].reshape(-1, hidden_units)
-    summed_out = pair[1, :rows_out]
-    small_sum = pair[1, rows_out:].reshape(-1)
-    bias_sum = small_sum[:hidden_units]
-    gain_sum = small_sum[hidden_units : hidden_units + channels]
-    scale_sum = small_sum[hidden_units + channels : hidden_units + 2 * channels]
-    kernel_parts = lax.all_to_all(
-        kernel_part.reshape(group_count, group_size, KSIZE * KSIZE),
+    summed_in = pair[0].reshape(-1, hidden_units)
+    summed_out = pair[1]
+    small = jnp.concatenate([bias_part, gain_part, scale_part]).reshape(group_count, -1)
+    chunk = small.shape[1]
+    kernel_cols = group_size * KSIZE * KSIZE
+    outgoing = jnp.concatenate(
+        [kernel_part.reshape(group_count, kernel_cols), small], axis=1
+    )
+    incoming = jnp.sum(
+        lax.all_to_all(outgoing, EVERY, split_axis=0, concat_axis=0, tiled=True), axis=0
+    )
+    grad_kernel = incoming[:kernel_cols].reshape(group_size, KSIZE * KSIZE) * scale_factor
+    small_mine = incoming[kernel_cols:]
+    small_sum = lax.all_to_all(
+        jnp.broadcast_to(small_mine[None], (group_count, chunk)),
         EVERY,
         split_axis=0,
         concat_axis=0,
         tiled=True,
-    )
-    grad_kernel = jnp.sum(kernel_parts, axis=0) * scale_factor
+    ).reshape(-1)
+    bias_sum = small_sum[:hidden_units]
+    gain_sum = small_sum[hidden_units : hidden_units + channels]
+    scale_sum = small_sum[hidden_units + channels : hidden_units + 2 * channels]
     return (
         out_map,
         grad_image,

time: 390 us -> 364 us (0.933)
  local copies, waits for them, and re-layouts: 92.7 us -> 42.9 us
  waiting for transfers between devices: 141 us -> 166 us
  starting transfers between devices: 26.3 us -> 34.8 us
  other arithmetic: 74.6 us -> 66.5 us
    unnamed x163 -> x133, local copies, waits for them, and re-layouts: 39 us -> 3.64 us
    another operation x51, local copies, waits for them, and re-layouts: 19.1 us -> 0.7 us  [tile_taps(): return jnp.stack(columns, axis=1)]
    another operation x0 -> x1, local copies, waits for them, and re-layouts: none -> 11.6 us  [local(): stacked = jnp.stack([block_in, block_out], axis=1)]
    reshape x1 -> x3, local copies, waits for them, and re-layouts: 11.6 us -> 0.37 us  [the longest x1 0.16 us: local(): kernel_part.reshape(group_count, kernel_cols)]
    reduce_scatter x0 -> x1, waiting for transfers between devices: none -> 11.2 us  [local(): mine = lax.psum_scatter(halves, 'col', scatter_dimension=0, tiled=True)]
    all_to_all x1 -> x2, waiting for transfers between devices: 5.6 us -> 15.6 us  [the longest x1 8.48 us: local(): lax.all_to_all(jnp.broadcast_to(small_mine[None], (group_count, chunk)),...]
    another operation x2 -> x1, other arithmetic: 14.4 us -> 6.92 us  [local(): stacked = jnp.stack([block_in, block_out], axis=1)]
    all_to_all x1 -> x2, starting transfers between devices: 11.1 us -> 16.8 us  [the longest x1 11.2 us: local(): lax.all_to_all(outgoing, EVERY, split_axis=0, concat_axis=0, tiled=True)]
  transfers between devices with their start and end apart: 15 -> 16, of which waited for: 7 -> 9; matrix products, arithmetic and copies ran while one was open for 36% -> 27% of each run, Pallas kernels for 0% -> 0%
where the time goes in v7:
time: 364 us; the launch traced here: 362 us
  waiting for transfers between devices  166 us (46%)
  other arithmetic  66.5 us (18%)
  local copies, waits for them, and re-layouts  42.9 us (12%)
  matrix products  36.4 us (10%)
  starting transfers between devices  34.8 us (10%)
  between operations  15.6 us (4%)
    all_gather x1, waiting for transfers between devices, local(): lax.all_gather(w_out, 'col', axis=0, tiled=True)  43.9 us
    psum x1, waiting for transfers between devices, local(): mine = lax.psum(mine, 'z')  40.2 us
    reduce_scatter x1, waiting for transfers between devices, local(): halves = lax.psum_scatter(stacked, 'core', scatter_dimension=1, tiled=True)  29.2 us
    all_gather x1, waiting for transfers between devices, local(): lax.all_gather(w_in, 'col', axis=0, tiled=True)  21 us
    convert_element_type x1, other arithmetic, local(): (cotangent.astype(jnp.float32) + grad_back.astype(jnp.float32)).astype(jn...  16.1 us
    reduce_sum x3, other arithmetic, tile_taps(): columns.append(jnp.sum(gradient * window, axis=(0, 1)))  15.5 us
    reduce_sum x1, other arithmetic, local(): average = jnp.mean(conv_rows, axis=1, keepdims=True)  12.9 us
    another operation x1, local copies, waits for them, and re-layouts, local(): stacked = jnp.stack([block_in, block_out], axis=1)  11.6 us
  transfers between devices with their start and end apart: 16, of which 9 were waited for; matrix products, arithmetic and copies ran while one was open for 27% of the time, Pallas kernels for 0%

profile of v7, /device:TPU:0, one launch (start us, length us, event | category | flops | bytes accessed | tf_op | source)
XLA Modules:
  0.0 362.0 jit_solution(4139507387646877638)
XLA Ops:
  9.8 1.3 collective-permute-start.1
  11.1 4.6 %collective-permute-start = (bf16[16,6,768]{2,1,0:T(8,128)(2,1)S(1)}, bf16[16,6,768]{2,1,0:T(8,128)(2,1)S(1)}, u32[]{:S(2)}, u32[]{:S(2)}) collective-permute-start(bf16[16,6,768]{2,1,0:T(8,128)(2,1)S(1)} %get-tuple-element.186), channel_id=1, source_target_pairs={{0,1},{1,2},{2,3},{3,4},{4,5},{5,6},{6,7},{7,8},{8,9},{9,10},{10,1... | collective-permute-start | bytes 442376 | tf_op jit(solution)/shard_map/ppermute | solution.py:43
  15.7 1.5 slice_reduce_fusion.97
  17.1 1.5 slice_reduce_fusion.96
  19.8 1.3 collective-permute-start.2
  21.1 1.3 collective-permute-start.3
  22.4 1.1 slice_reduce_fusion.95
  24.7 2.4 collective-permute-done.3
  27.1 1.3 maximum_maximum_fusion
  28.4 12.9 %convert_reduce_fusion = (f32[16,32]{1,0:T(8,128)S(1)}, bf16[16,32,768]{2,1,0:T(8,128)(2,1)}) fusion(bf16[22,44,768]{2,1,0:T(8,128)(2,1)S(1)} %get-tuple-element.180, f32[768]{0:T(1024)S(1)} %get-tuple-element.167, f32[768]{0:T(1024)S(1)} %get-tuple-element.120, f32[768]{0:T(1024)S(1)} %get-tuple-element.121, f32[768]{0:T(1024)S(1)} %get-tuple-element.122, ...), kind=kLoop, calls=%fused_computation.272 | loop fusion | flops 62127616 | bytes 37262336 | tf_op jit(solution)/shard_map/reduce_sum | solution.py:96
  41.4 1.5 multiply_reduce_fusion.2
  43.0 2.4 multiply_convert_fusion.3
  45.4 21.0 %all-gather.4.cloned.1.call-done = bf16[768,3072]{1,0:T(8,128)(2,1)} async-done(((bf16[48,3072]{1,0:T(8,128)(2,1)}), bf16[768,3072]{1,0:T(8,128)(2,1)}) %all-gather.4.cloned.1.call-update) | async-done | bytes 4718608 | tf_op jit(solution)/shard_map/all_gather | solution.py:87
  66.4 7.0 %fusion.8 = (bf16[3072,512]{0,1:T(8,128)(2,1)}, f32[512,3072]{1,0:T(8,128)}) fusion(f32[3072]{0:T(1024)S(1)} %copy-done.64, bf16[512,768]{1,0:T(8,128)(2,1)} %multiply_convert_fusion.3, bf16[768,3072]{1,0:T(8,128)(2,1)} %all-gather.4.cloned.1.call-done), kind=kOutput, calls=%fused_computation.64 | convolution fusion | flops 2425356288 | bytes 14954496 | tf_op jit(solution)/shard_map/dot_general | solution.py:101
  73.4 4.7 %copy.21 = bf16[3072,512]{1,0:T(8,128)(2,1)} copy(bf16[3072,512]{0,1:T(8,128)(2,1)} %get-tuple-element.193) | data formatting | bytes 6291456 | tf_op jit(solution)/shard_map/convert_element_type | solution.py:102
  78.1 43.9 %all-gather.6.cloned.1.call-done = bf16[3072,768]{1,0:T(8,128)(2,1)} async-done(((bf16[192,768]{1,0:T(8,128)(2,1)}), bf16[3072,768]{1,0:T(8,128)(2,1)}) %all-gather.6.cloned.1.call-update) | async-done | bytes 4718608 | tf_op jit(solution)/shard_map/all_gather | solution.py:88
  122.0 8.0 %fusion.136 = (f32[768]{0:T(1024)S(1)}, bf16[512,768]{1,0:T(8,128)(2,1)}, bf16[512,768]{1,0:T(8,128)(2,1)S(1)}) fusion(bf16[16,32,768]{2,1,0:T(8,128)(2,1)} %param.15, f32[768]{0:T(1024)S(1)} %copy-done.62, bf16[16,32,768]{2,1,0:T(8,128)(2,1)} %param.8, bf16[3072,768]{1,0:T(8,128)(2,1)} %all-gather.6.cloned.1.call-done, ...), kind=kOutput, calls=%fused_computation.249 | convolution fusion | flops 2428894464 | bytes 14174208 | tf_op jit(solution)/shard_map/dot_general | solution.py:103
  130.0 4.7 %fusion.155 = (f32[3072]{0:T(1024)S(1)}, bf16[512,3072]{1,0:T(8,128)(2,1)S(1)}) fusion(f32[512,3072]{1,0:T(8,128)S(1)} %copy-done.65, f32[3072]{0:T(1024)S(1)} %copy-done.64, bf16[512,768]{1,0:T(8,128)(2,1)S(1)} %get-tuple-element.183, bf16[3072,768]{1,0:T(8,128)(2,1)S(1)} %copy-done.63), kind=kOutput, calls=%fused_computation.409 | convolution fusion | flops 2434790400 | bytes 14966784 | tf_op jit(solution)/shard_map/dot_general | solution.py:111
  134.6 1.6 copy-done.9
  136.2 5.1 %fusion.139 = f32[768,3072]{1,0:T(8,128)} fusion(bf16[512,768]{1,0:T(8,128)(2,1)S(1)} %copy-done.8, bf16[512,3072]{1,0:T(8,128)(2,1)S(1)} %get-tuple-element.192), kind=kOutput, calls=%fused_computation.257 | convolution fusion | flops 2415919104 | bytes 13369344 | tf_op jit(solution)/shard_map/dot_general | solution.py:139
  141.4 11.6 %stack_reshape.4 = f32[16,1,192,768]{3,2,0,1:T(8,128)} reshape(f32[768,3072]{1,0:T(8,128)} %fusion.139) | data formatting | bytes 18874368 | tf_op jit(solution)/shard_map/stack;reshape | solution.py:145
  153.0 4.8 %convolution_bitcast_fusion = f32[16,1,192,768]{3,2,0,1:T(8,128)S(1)} fusion(bf16[16,192,512]{2,1,0:T(8,128)(2,1)} %bitcast.120, bf16[512,768,1]{1,0,2:T(8,128)(2,1)} %bitcast.121), kind=kOutput, calls=%fused_computation.65 | convolution fusion | flops 2415919104 | bytes 13369344 | tf_op jit(solution)/shard_map/dot_general | solution.py:142
  157.8 6.9 %pad_maximum_fusion = f32[16,2,192,768]{3,2,0,1:T(8,128)} fusion(f32[16,1,192,768]{3,2,0,1:T(8,128)S(1)} %convolution_bitcast_fusion, f32[16,1,192,768]{3,2,0,1:T(8,128)S(1)} %copy-done), kind=kLoop, calls=%fused_computation.50 | loop fusion | flops 4718592 | bytes 37748736 | tf_op jit(solution)/shard_map/stack | solution.py:145
  164.8 29.2 %reduce-scatter.3.cloned.1.call-done = f32[16,1,192,768]{3,2,0,1:T(8,128)} async-done(((f32[16,2,192,768]{3,2,0,1:T(8,128)}), f32[16,1,192,768]{3,2,0,1:T(8,128)}) %reduce-scatter.3.cloned.1.call-update) | async-done | bytes 9437200 | tf_op jit(solution)/shard_map/reduce_scatter | solution.py:146
  194.0 1.6 reshape.219
  195.6 3.5 rev.3
  199.1 1.6 reshape.220
  200.7 2.1 slice_reduce_fusion.48
  202.8 2.1 slice_reduce_fusion.47
  204.9 6.8 %multiply_reduce_fusion = (f32[768]{0:T(1024)S(1)}, f32[512]{0:T(512)S(1)}, f32[512]{0:T(512)S(1)}, f32[512,768]{1,0:T(8,128)S(1)}) fusion(bf16[16,32,768]{2,1,0:T(8,128)(2,1)} %get-tuple-element.170, f32[512]{0:T(512)S(1)} %rsqrt.12, f32[512]{0:T(512)S(1)} %div.15, f32[768]{0:T(1024)S(1)} %copy-done.43, ...), kind=kOutput, calls=%fused_computation.254 | convolution fusion | flops 2419456256 | bytes 10237952 | tf_op jit(solution)/shard_map/dot_general | solution.py:117
  211.7 5.6 %fusion.132 = (f32[768]{0:T(1024)}, f32[768]{0:T(1024)}, f32[768]{0:T(1024)}, f32[768]{0:T(1024)}, f32[768]{0:T(1024)}, /*index=5*/f32[768]{0:T(1024)}, f32[768]...) fusion(bf16[22,44,768]{2,1,0:T(8,128)(2,1)S(1)} %get-tuple-elem, ...), kind=kLoop, calls=%fused_computation.241 | loop fusion | flops 25152000 | bytes 17368064 | tf_op jit(solution)/shard_map/reduce_sum | solution.py:73
  219.0 1.3 collective-permute-start.5
  220.3 5.2 %collective-permute-start.4 = (bf16[16,6,768]{2,1,0:T(8,128)(2,1)}, bf16[16,6,768]{2,1,0:T(8,128)(2,1)}, u32[]{:S(2)}, u32[]{:S(2)}) collective-permute-start(bf16[16,6,768]{2,1,0:T(8,128)(2,1)} %get-tuple-element.184), channel_id=1, source_target_pairs={{0,1},{1,2},{2,3},{3,4},{4,5},{5,6},{6,7},{7,8},{8,9},{9,10},{10,1... | collective-permute-start | bytes 442376 | tf_op jit(solution)/shard_map/ppermute | solution.py:43
  225.7 5.8 %fusion.114 = (f32[768]{0:T(1024)S(1)}, f32[768]{0:T(1024)S(1)}, f32[768]{0:T(1024)S(1)}, f32[768]{0:T(1024)S(1)}, f32[768]{0:T(1024)S(1)}, /*index=5*/f32[768]{...) fusion(bf16[22,44,768]{2,1,0:T(8,128)(2,1)S(1)} %get-tuple-elem, ...), kind=kLoop, calls=%fused_computation.223 | loop fusion | flops 19257600 | bytes 8838144 | tf_op jit(solution)/shard_map/reduce_sum | solution.py:73
  231.8 4.0 %fusion.104 = (f32[768]{0:T(1024)S(1)}, f32[768]{0:T(1024)S(1)}, f32[768]{0:T(1024)S(1)}, f32[768]{0:T(1024)S(1)}, f32[768]{0:T(1024)S(1)}, /*index=5*/f32[768]{...) fusion(bf16[22,44,768]{2,1,0:T(8,128)(2,1)S(1)} %get-tuple-elem, ...), kind=kLoop, calls=%fused_computation.213 | loop fusion | flops 21613056 | bytes 14997504 | tf_op jit(solution)/shard_map/reduce_sum | solution.py:73
  238.2 11.2 %all-to-all-start = ((f32[128,1,330]{2,1,0:T(1,128)}), f32[128,1,330]{2,1,0:T(1,128)S(1)}, u32[]{:S(2)}, u32[]{:S(2)}) async-start(f32[128,1,330]{2,1,0:T(1,128)} %copy.20), calls=%async_computation | async-start | bytes 393216 | tf_op jit(solution)/shard_map/all_to_all | solution.py:160
  249.4 1.2 slice_reduce_fusion.46
  250.6 1.3 pad_maximum_fusion.8
  251.9 1.3 collective-permute-start.6
  253.3 1.3 collective-permute-start.7
  254.6 7.2 %all-to-all-done = f32[128,1,330]{2,1,0:T(1,128)S(1)} async-done(((f32[128,1,330]{2,1,0:T(1,128)}), f32[128,1,330]{2,1,0:T(1,128)S(1)}, u32[]{:S(2)}, u32[]{:S(2)}) %all-to-all-start) | async-done | bytes 168992 | tf_op jit(solution)/shard_map/all_to_all | solution.py:160
  262.7 5.6 %all-to-all-start.1 = ((f32[128,1,36]{2,1,0:T(1,128)}), f32[128,1,36]{2,1,0:T(1,128)S(1)}, u32[]{:S(2)}, u32[]{:S(2)}) async-start(f32[128,1,36]{2,1,0:T(1,128)} %broadcast_in_dim.2), calls=%async_computation.3 | async-start | bytes 131072 | tf_op jit(solution)/shard_map/all_to_all | solution.py:164
  269.2 8.5 %all-to-all-done.1 = f32[128,1,36]{2,1,0:T(1,128)S(1)} async-done(((f32[128,1,36]{2,1,0:T(1,128)}), f32[128,1,36]{2,1,0:T(1,128)S(1)}, u32[]{:S(2)}, u32[]{:S(2)}) %all-to-all-start.1) | async-done | bytes 18464 | tf_op jit(solution)/shard_map/all_to_all | solution.py:164
  279.1 11.2 %reduce-scatter.5.cloned.1.call-done = f32[192,768]{1,0:T(8,128)} async-done(((f32[3072,768]{1,0:T(8,128)}), f32[192,768]{1,0:T(8,128)}) %reduce-scatter.5.cloned.1.call-update) | async-done | bytes 589840 | tf_op jit(solution)/shard_map/reduce_scatter | solution.py:148
  292.6 2.7 maximum_maximum_fusion.1
  295.4 40.2 %all-reduce.2.cloned.1.call-done = f32[1,192,768]{2,1,0:T(8,128)} async-done(((f32[1,192,768]{2,1,0:T(8,128)}), f32[1,192,768]{2,1,0:T(8,128)}) %all-reduce.2.cloned.1.call-update) | async-done | bytes 589840 | tf_op jit(solution)/shard_map/psum | solution.py:149
  335.9 16.1 %fusion.133 = bf16[16,32,768]{2,1,0:T(8,128)(2,1)} fusion(bf16[16,32,768]{2,1,0:T(8,128)(2,1)} %param.15, bf16[22,44,768]{2,1,0:T(8,128)(2,1)S(1)} %get-tuple-element.176, f32[768]{0:T(1024)S(1)} %get-tuple-element.71, f32[768]{0:T(1024)S(1)} %get-tuple-element.72, f32[768]{0:T(1024)S(1)} %get-tuple-element.73, f32[768]{0:T(1024)S(1)} %get-tuple-element.74, ...), kind=kLoop, calls=%fused_computation.246 | loop fusion | flops 66453504 | bytes 35834880 | tf_op jit(solution)/shard_map/convert_element_type | solution.py:134
  352.0 2.1 fusion.151
  (229 shorter events, 15.3 us)
Async XLA Ops:
  7.2 59.2 %all-gather.4.cloned.1.call-start = ((), (), s32[]{:S(2)}) async-start(), calls=%async_computation.4 | async-start | bytes 5013504 | tf_op jit(solution)/shard_map/all_gather | solution.py:87
  7.9 114.0 %all-gather.6.cloned.1.call-start = ((), (), s32[]{:S(2)}) async-start(), calls=%async_computation.5 | async-start | bytes 5013504 | tf_op jit(solution)/shard_map/all_gather | solution.py:88
  8.7 185.3 %reduce-scatter.3.cloned.1.call-start = ((), (), s32[]{:S(2)}) async-start(), calls=%async_computation.6 | async-start | bytes 28311552 | tf_op jit(solution)/shard_map/reduce_scatter | solution.py:146
  9.8 8.9 %collective-permute-start.1 = (bf16[16,6,768]{2,1,0:T(8,128)(2,1)S(1)}, bf16[16,6,768]{2,1,0:T(8,128)(2,1)S(1)}, u32[]{:S(2)}, u32[]{:S(2)}) collective-permute-start(bf16[16,6,768]{2,1,0:T(8,128)(2,1)S(1)} %get-tuple-element.187), channel_id=1, source_target_pairs={{1,0},{2,1},{3,2},{4,3},{5,4},{6,5},{7,6},{8,7},{9,8},{10,9},{11,1... | collective-permute-start | bytes 442376 | tf_op jit(solution)/shard_map/ppermute | solution.py:44
  11.1 8.4 %collective-permute-start = (bf16[16,6,768]{2,1,0:T(8,128)(2,1)S(1)}, bf16[16,6,768]{2,1,0:T(8,128)(2,1)S(1)}, u32[]{:S(2)}, u32[]{:S(2)}) collective-permute-start(bf16[16,6,768]{2,1,0:T(8,128)(2,1)S(1)} %get-tuple-element.186), channel_id=1, source_target_pairs={{0,1},{1,2},{2,3},{3,4},{4,5},{5,6},{6,7},{7,8},{8,9},{9,10},{10,1... | collective-permute-start | bytes 442376 | tf_op jit(solution)/shard_map/ppermute | solution.py:43
  19.8 4.9 %collective-permute-start.2 = (bf16[6,44,768]{2,1,0:T(8,128)(2,1)S(1)}, bf16[6,44,768]{2,1,0:T(8,128)(2,1)S(1)}, u32[]{:S(2)}, u32[]{:S(2)}) collective-permute-start(bf16[6,44,768]{2,1,0:T(8,128)(2,1)S(1)} %get-tuple-element.181), channel_id=1, source_target_pairs={{0,16},{16,32},{32,48},{48,64},{64,80},{80,96},{96,112},{1,17},{17... | collective-permute-start | bytes 1216520 | tf_op jit(solution)/shard_map/ppermute | solution.py:46
  21.1 6.0 %collective-permute-start.3 = (bf16[6,44,768]{2,1,0:T(8,128)(2,1)S(1)}, bf16[6,44,768]{2,1,0:T(8,128)(2,1)S(1)}, u32[]{:S(2)}, u32[]{:S(2)}) collective-permute-start(bf16[6,44,768]{2,1,0:T(8,128)(2,1)S(1)} %get-tuple-element.182), channel_id=1, source_target_pairs={{16,0},{32,16},{48,32},{64,48},{80,64},{96,80},{112,96},{17,1},{33... | collective-permute-start | bytes 1216520 | tf_op jit(solution)/shard_map/ppermute | solution.py:47
  41.3 25.0 %copy-start.64 = (f32[3072]{0:T(1024)S(1)}, f32[3072]{0:T(1024)}, u32[]{:S(2)}) copy-start(f32[3072]{0:T(1024)} %param.12) | copy-start | bytes 36868
  164.8 125.5 %reduce-scatter.5.cloned.1.call-start = ((), (), s32[]{:S(2)}) async-start(), calls=%async_computation.7 | async-start | bytes 10027008 | tf_op jit(solution)/shard_map/reduce_scatter | solution.py:148
  219.0 31.5 %collective-permute-start.5 = (bf16[16,6,768]{2,1,0:T(8,128)(2,1)}, bf16[16,6,768]{2,1,0:T(8,128)(2,1)}, u32[]{:S(2)}, u32[]{:S(2)}) collective-permute-start(bf16[16,6,768]{2,1,0:T(8,128)(2,1)} %get-tuple-element.185), channel_id=1, source_target_pairs={{1,0},{2,1},{3,2},{4,3},{5,4},{6,5},{7,6},{8,7},{9,8},{10,9},{11,1... | collective-permute-start | bytes 442376 | tf_op jit(solution)/shard_map/ppermute | solution.py:44
  220.3 30.3 %collective-permute-start.4 = (bf16[16,6,768]{2,1,0:T(8,128)(2,1)}, bf16[16,6,768]{2,1,0:T(8,128)(2,1)}, u32[]{:S(2)}, u32[]{:S(2)}) collective-permute-start(bf16[16,6,768]{2,1,0:T(8,128)(2,1)} %get-tuple-element.184), channel_id=1, source_target_pairs={{0,1},{1,2},{2,3},{3,4},{4,5},{5,6},{6,7},{7,8},{8,9},{9,10},{10,1... | collective-permute-start | bytes 442376 | tf_op jit(solution)/shard_map/ppermute | solution.py:43
  238.2 23.6 %all-to-all-start = ((f32[128,1,330]{2,1,0:T(1,128)}), f32[128,1,330]{2,1,0:T(1,128)S(1)}, u32[]{:S(2)}, u32[]{:S(2)}) async-start(f32[128,1,330]{2,1,0:T(1,128)} %copy.20), calls=%async_computation | async-start | bytes 393216 | tf_op jit(solution)/shard_map/all_to_all | solution.py:160
  251.9 39.9 %collective-permute-start.6 = (bf16[6,44,768]{2,1,0:T(8,128)(2,1)S(1)}, bf16[6,44,768]{2,1,0:T(8,128)(2,1)S(1)}, u32[]{:S(2)}, u32[]{:S(2)}) collective-permute-start(bf16[6,44,768]{2,1,0:T(8,128)(2,1)S(1)} %get-tuple-element.177), channel_id=1, source_target_pairs={{0,16},{16,32},{32,48},{48,64},{64,80},{80,96},{96,112},{1,17},{17... | collective-permute-start | bytes 1216520 | tf_op jit(solution)/shard_map/ppermute | solution.py:46
  253.3 39.4 %collective-permute-start.7 = (bf16[6,44,768]{2,1,0:T(8,128)(2,1)S(1)}, bf16[6,44,768]{2,1,0:T(8,128)(2,1)}, u32[]{:S(2)}, u32[]{:S(2)}) collective-permute-start(bf16[6,44,768]{2,1,0:T(8,128)(2,1)S(1)} %get-tuple-element.178), channel_id=1, source_target_pairs={{16,0},{32,16},{48,32},{64,48},{80,64},{96,80},{112,96},{17,1},{33... | collective-permute-start | bytes 1216520 | tf_op jit(solution)/shard_map/ppermute | solution.py:47
  262.7 15.0 %all-to-all-start.1 = ((f32[128,1,36]{2,1,0:T(1,128)}), f32[128,1,36]{2,1,0:T(1,128)S(1)}, u32[]{:S(2)}, u32[]{:S(2)}) async-start(f32[128,1,36]{2,1,0:T(1,128)} %broadcast_in_dim.2), calls=%async_computation.3 | async-start | bytes 131072 | tf_op jit(solution)/shard_map/all_to_all | solution.py:164
  268.2 67.4 %all-reduce.2.cloned.1.call-start = ((), (), s32[]{:S(2)}) async-start(), calls=%async_computation.8 | async-start | bytes 1179648 | tf_op jit(solution)/shard_map/psum | solution.py:149
  290.3 61.7 %all-gather.8.cloned.1.call-start = ((), (), s32[]{:S(2)}) async-start(), calls=%async_computation.9 | async-start | bytes 1769472 | tf_op jit(solution)/shard_map/all_gather | solution.py:150
  291.6 44.0 %copy-start.12 = (f32[768]{0:T(1024)S(1)}, f32[768]{0:T(1024)}, u32[]{:S(2)}) copy-start(f32[768]{0:T(1024)} %get-tuple-element.77) | copy-start | bytes 9220
  291.6 44.0 %copy-start.13 = (f32[768]{0:T(1024)S(1)}, f32[768]{0:T(1024)}, u32[]{:S(2)}) copy-start(f32[768]{0:T(1024)} %get-tuple-element.78) | copy-start | bytes 9220
  291.6 44.0 %copy-start.14 = (f32[768]{0:T(1024)S(1)}, f32[768]{0:T(1024)}, u32[]{:S(2)}) copy-start(f32[768]{0:T(1024)} %get-tuple-element.79) | copy-start | bytes 9220
  291.6 44.1 %copy-start.15 = (f32[768]{0:T(1024)S(1)}, f32[768]{0:T(1024)}, u32[]{:S(2)}) copy-start(f32[768]{0:T(1024)} %get-tuple-element.80) | copy-start | bytes 9220
  291.6 44.1 %copy-start.16 = (f32[768]{0:T(1024)S(1)}, f32[768]{0:T(1024)}, u32[]{:S(2)}) copy-start(f32[768]{0:T(1024)} %get-tuple-element.81) | copy-start | bytes 9220
  291.6 44.1 %copy-start.17 = (f32[768]{0:T(1024)S(1)}, f32[768]{0:T(1024)}, u32[]{:S(2)}) copy-start(f32[768]{0:T(1024)} %get-tuple-element.82) | copy-start | bytes 9220
  291.6 44.1 %copy-start.18 = (f32[768]{0:T(1024)S(1)}, f32[768]{0:T(1024)}, u32[]{:S(2)}) copy-start(f32[768]{0:T(1024)} %get-tuple-element.83) | copy-start | bytes 9220
  291.6 44.1 %copy-start.19 = (f32[768]{0:T(1024)S(1)}, f32[768]{0:T(1024)}, u32[]{:S(2)}) copy-start(f32[768]{0:T(1024)} %get-tuple-element.84) | copy-start | bytes 9220
  291.6 44.1 %copy-start.20 = (f32[768]{0:T(1024)S(1)}, f32[768]{0:T(1024)}, u32[]{:S(2)}) copy-start(f32[768]{0:T(1024)} %get-tuple-element.85) | copy-start | bytes 9220
  291.6 44.1 %copy-start.21 = (f32[768]{0:T(1024)S(1)}, f32[768]{0:T(1024)}, u32[]{:S(2)}) copy-start(f32[768]{0:T(1024)} %get-tuple-element.86) | copy-start | bytes 9220
  291.7 44.1 %copy-start.22 = (f32[768]{0:T(1024)S(1)}, f32[768]{0:T(1024)}, u32[]{:S(2)}) copy-start(f32[768]{0:T(1024)} %get-tuple-element.87) | copy-start | bytes 9220
  291.7 44.1 %copy-start.23 = (f32[768]{0:T(1024)S(1)}, f32[768]{0:T(1024)}, u32[]{:S(2)}) copy-start(f32[768]{0:T(1024)} %get-tuple-element.88) | copy-start | bytes 9220
  291.7 44.1 %copy-start.24 = (f32[768]{0:T(1024)S(1)}, f32[768]{0:T(1024)}, u32[]{:S(2)}) copy-start(f32[768]{0:T(1024)} %get-tuple-element.89) | copy-start | bytes 9220
  291.7 44.1 %copy-start.25 = (f32[768]{0:T(1024)S(1)}, f32[768]{0:T(1024)}, u32[]{:S(2)}) copy-start(f32[768]{0:T(1024)} %get-tuple-element.90) | copy-start | bytes 9220
  291.7 44.1 %copy-start.26 = (f32[768]{0:T(1024)S(1)}, f32[768]{0:T(1024)}, u32[]{:S(2)}) copy-start(f32[768]{0:T(1024)} %get-tuple-element.91) | copy-start | bytes 9220
  291.7 44.1 %copy-start.27 = (f32[768]{0:T(1024)S(1)}, f32[768]{0:T(1024)}, u32[]{:S(2)}) copy-start(f32[768]{0:T(1024)} %get-tuple-element.92) | copy-start | bytes 9220
  291.7 44.1 %copy-start.28 = (f32[768]{0:T(1024)S(1)}, f32[768]{0:T(1024)}, u32[]{:S(2)}) copy-start(f32[768]{0:T(1024)} %get-tuple-element.93) | copy-start | bytes 9220
  291.7 44.1 %copy-start.29 = (f32[768]{0:T(1024)S(1)}, f32[768]{0:T(1024)}, u32[]{:S(2)}) copy-start(f32[768]{0:T(1024)} %get-tuple-element.94) | copy-start | bytes 9220
  291.7 44.1 %copy-start.30 = (f32[768]{0:T(1024)S(1)}, f32[768]{0:T(1024)}, u32[]{:S(2)}) copy-start(f32[768]{0:T(1024)} %get-tuple-element.95) | copy-start | bytes 9220
  291.7 44.1 %copy-start.31 = (f32[768]{0:T(1024)S(1)}, f32[768]{0:T(1024)}, u32[]{:S(2)}) copy-start(f32[768]{0:T(1024)} %get-tuple-element.96) | copy-start | bytes 9220
  291.8 44.1 %copy-start.32 = (f32[768]{0:T(1024)S(1)}, f32[768]{0:T(1024)}, u32[]{:S(2)}) copy-start(f32[768]{0:T(1024)} %get-tuple-element.97) | copy-start | bytes 9220
  291.8 44.1 %copy-start.33 = (f32[768]{0:T(1024)S(1)}, f32[768]{0:T(1024)}, u32[]{:S(2)}) copy-start(f32[768]{0:T(1024)} %get-tuple-element.98) | copy-start | bytes 9220
  291.8 44.1 %copy-start.34 = (f32[768]{0:T(1024)S(1)}, f32[768]{0:T(1024)}, u32[]{:S(2)}) copy-start(f32[768]{0:T(1024)} %get-tuple-element.99) | copy-start | bytes 9220
  291.8 44.1 %copy-start.35 = (f32[768]{0:T(1024)S(1)}, f32[768]{0:T(1024)}, u32[]{:S(2)}) copy-start(f32[768]{0:T(1024)} %get-tuple-element.100) | copy-start | bytes 9220
  291.8 44.1 %copy-start.36 = (f32[768]{0:T(1024)S(1)}, f32[768]{0:T(1024)}, u32[]{:S(2)}) copy-start(f32[768]{0:T(1024)} %get-tuple-element.101) | copy-start | bytes 9220
  291.8 44.1 %copy-start.37 = (f32[768]{0:T(1024)S(1)}, f32[768]{0:T(1024)}, u32[]{:S(2)}) copy-start(f32[768]{0:T(1024)} %get-tuple-element.102) | copy-start | bytes 9220
  291.8 44.1 %copy-start.38 = (f32[768]{0:T(1024)S(1)}, f32[768]{0:T(1024)}, u32[]{:S(2)}) copy-start(f32[768]{0:T(1024)} %get-tuple-element.103) | copy-start | bytes 9220
  291.8 44.1 %copy-start.39 = (f32[768]{0:T(1024)S(1)}, f32[768]{0:T(1024)}, u32[]{:S(2)}) copy-start(f32[768]{0:T(1024)} %get-tuple-element.104) | copy-start | bytes 9220
  291.8 44.1 %copy-start.40 = (f32[768]{0:T(1024)S(1)}, f32[768]{0:T(1024)}, u32[]{:S(2)}) copy-start(f32[768]{0:T(1024)} %get-tuple-element.105) | copy-start | bytes 9220
  291.8 44.1 %copy-start.41 = (f32[768]{0:T(1024)S(1)}, f32[768]{0:T(1024)}, u32[]{:S(2)}) copy-start(f32[768]{0:T(1024)} %get-tuple-element.106) | copy-start | bytes 9220
  291.9 44.1 %copy-start.42 = (f32[768]{0:T(1024)S(1)}, f32[768]{0:T(1024)}, u32[]{:S(2)}) copy-start(f32[768]{0:T(1024)} %get-tuple-element.107) | copy-start | bytes 9220
  (34 other events, 190.0 us)
Sparse Core Ops, SparseCore 0:
  10.2 56.1 all-gather.3
  68.5 53.3 all-gather.5
  164.9 29.0 reduce-scatter.2
  197.3 92.9 reduce-scatter.4
  292.5 43.0 all-reduce.1
  337.1 12.3 all-gather.7

commit v8 on v7

--- a/solution.py
+++ b/solution.py
@@ -144,8 +144,10 @@
     ).reshape(col_count, rows_out, channels)
     stacked = jnp.stack([block_in, block_out], axis=1)
     halves = lax.psum_scatter(stacked, "core", scatter_dimension=1, tiled=True)
-    halves = halves.reshape(-1, channels)
-    mine = lax.psum_scatter(halves, "col", scatter_dimension=0, tiled=True)
+    halves = halves.reshape(col_count, rows_out, channels)
+    mine = jnp.sum(
+        lax.all_to_all(halves, "col", split_axis=0, concat_axis=0, tiled=True), axis=0
+    )
     mine = lax.psum(mine, "z")
     pair = lax.all_gather(mine, "core", axis=0, tiled=False)
     summed_in = pair[0].reshape(-1, hidden_units)

time: 364 us -> 479 us (1.32)
  waiting for transfers between devices: 166 us -> 273 us
  blocking collectives: 0 us -> 32 us
  local copies, waits for them, and re-layouts: 42.9 us -> 29.6 us
  starting transfers between devices: 34.8 us -> 22.2 us
    ppermute x2, waiting for transfers between devices: 0.01 us -> 79.7 us  [add_halo(): right = lax.ppermute(field[:, :REACH, :], 'col', shift_pairs(col_count, -1))]
    all_to_all x2 -> x1, waiting for transfers between devices: 15.6 us -> 75.2 us  [local(): lax.all_to_all(halves, 'col', split_axis=0, concat_axis=0, tiled=True)]
    all_to_all x0 -> x2, blocking collectives: none -> 32 us  [the longest x1 18.1 us: local(): lax.all_to_all(outgoing, EVERY, split_axis=0, concat_axis=0, tiled=True)]
    reduce_scatter x1, waiting for transfers between devices: 29.2 us -> 0.01 us  [local(): halves = lax.psum_scatter(stacked, 'core', scatter_dimension=1, tiled=True)]
    all_to_all x2 -> x1, starting transfers between devices: 16.8 us -> 4.91 us  [local(): lax.all_to_all(halves, 'col', split_axis=0, concat_axis=0, tiled=True)]
    reduce_scatter x1 -> x0, waiting for transfers between devices: 11.2 us -> none  [local(): mine = lax.psum_scatter(halves, 'col', scatter_dimension=0, tiled=True)]
    psum x1, waiting for transfers between devices: 40.2 us -> 48.5 us  [local(): mine = lax.psum(mine, 'z')]
    reduce_sum x0 -> x1, other arithmetic: none -> 5.1 us  [local(): jnp.sum(lax.all_to_all(halves, 'col', split_axis=0, concat_axis=0, tiled=...]
  transfers between devices with their start and end apart: 16 -> 14, of which waited for: 9 -> 7; matrix products, arithmetic and copies ran while one was open for 27% -> 19% of each run, Pallas kernels for 0% -> 0%
where the time goes in v8:
time: 479 us; the launch traced here: 477 us
  waiting for transfers between devices  273 us (57%)
  other arithmetic  68.9 us (14%)
  matrix products  37 us (8%)
  blocking collectives  32 us (7%)
  local copies, waits for them, and re-layouts  29.6 us (6%)
  starting transfers between devices  22.2 us (5%)
  between operations  14.6 us (3%)
    ppermute x2, waiting for transfers between devices, add_halo(): right = lax.ppermute(field[:, :REACH, :], 'col', shift_pairs(col_count, -1))  79.7 us
    all_to_all x1, waiting for transfers between devices, local(): lax.all_to_all(halves, 'col', split_axis=0, concat_axis=0, tiled=True)  75.2 us
    psum x1, waiting for transfers between devices, local(): mine = lax.psum(mine, 'z')  48.5 us
    all_gather x1, waiting for transfers between devices, local(): lax.all_gather(w_out, 'col', axis=0, tiled=True)  43.9 us
    all_gather x1, waiting for transfers between devices, local(): lax.all_gather(w_in, 'col', axis=0, tiled=True)  20.9 us
    all_to_all x1, blocking collectives, local(): lax.all_to_all(outgoing, EVERY, split_axis=0, concat_axis=0, tiled=True)  18.1 us
    convert_element_type x1, other arithmetic, local(): (cotangent.astype(jnp.float32) + grad_back.astype(jnp.float32)).astype(jn...  16.5 us
    all_to_all x1, blocking collectives, local(): lax.all_to_all(jnp.broadcast_to(small_mine[None], (group_count, chunk)),...  13.9 us
  transfers between devices with their start and end apart: 14, of which 7 were waited for; matrix products, arithmetic and copies ran while one was open for 19% of the time, Pallas kernels for 0%

profile of v8, /device:TPU:0, one launch (start us, length us, event | category | flops | bytes accessed | tf_op | source)
XLA Modules:
  0.0 477.4 jit_solution(1783416956030885272)
XLA Ops:
  8.7 1.1 fusion.154
  9.8 1.3 collective-permute-start.1
  11.1 4.6 collective-permute-start
  15.7 1.5 slice_reduce_fusion.97
  17.1 1.4 slice_reduce_fusion.96
  18.7 0.8 collective-permute-done
  19.8 1.3 collective-permute-start.2
  21.1 1.3 collective-permute-start.3
  22.4 1.1 slice_reduce_fusion.95
  23.5 1.0 fusion.134
  24.6 2.5 collective-permute-done.3
  27.1 1.3 maximum_maximum_fusion
  28.4 12.9 %convert_reduce_fusion = (f32[16,32]{1,0:T(8,128)S(1)}, bf16[16,32,768]{2,1,0:T(8,128)(2,1)}) fusion(bf16[22,44,768]{2,1,0:T(8,128)(2,1)S(1)} %get-tuple-element.180, f32[768]{0:T(1024)S(1)} %get-tuple-element.167, f32[768]{0:T(1024)S(1)} %get-tuple-element.120, f32[768]{0:T(1024)S(1)} %get-tuple-element.121, f32[768]{0:T(1024)S(1)} %get-tuple-element.122, ...), kind=kLoop, calls=%fused_computation.272 | loop fusion | flops 62127616 | bytes 37262336 | tf_op jit(solution)/shard_map/reduce_sum | solution.py:96
  41.4 1.5 multiply_reduce_fusion.2
  43.0 2.4 multiply_convert_fusion.3
  45.4 20.9 %all-gather.4.cloned.1.call-done = bf16[768,3072]{1,0:T(8,128)(2,1)} async-done(((bf16[48,3072]{1,0:T(8,128)(2,1)}), bf16[768,3072]{1,0:T(8,128)(2,1)}) %all-gather.4.cloned.1.call-update) | async-done | bytes 4718608 | tf_op jit(solution)/shard_map/all_gather | solution.py:87
  66.4 7.0 %fusion.8 = (bf16[3072,512]{0,1:T(8,128)(2,1)}, f32[512,3072]{1,0:T(8,128)}) fusion(f32[3072]{0:T(1024)S(1)} %copy-done.17, bf16[512,768]{1,0:T(8,128)(2,1)} %multiply_convert_fusion.3, bf16[768,3072]{1,0:T(8,128)(2,1)} %all-gather.4.cloned.1.call-done), kind=kOutput, calls=%fused_computation.64 | convolution fusion | flops 2425356288 | bytes 14954496 | tf_op jit(solution)/shard_map/dot_general | solution.py:101
  73.4 4.7 copy.21
  78.1 43.9 %all-gather.6.cloned.1.call-done = bf16[3072,768]{1,0:T(8,128)(2,1)} async-done(((bf16[192,768]{1,0:T(8,128)(2,1)}), bf16[3072,768]{1,0:T(8,128)(2,1)}) %all-gather.6.cloned.1.call-update) | async-done | bytes 4718608 | tf_op jit(solution)/shard_map/all_gather | solution.py:88
  122.0 7.9 %fusion.136 = (f32[768]{0:T(1024)S(1)}, bf16[512,768]{1,0:T(8,128)(2,1)}, bf16[512,768]{1,0:T(8,128)(2,1)S(1)}) fusion(bf16[16,32,768]{2,1,0:T(8,128)(2,1)} %param.15, f32[768]{0:T(1024)S(1)} %copy-done.15, bf16[16,32,768]{2,1,0:T(8,128)(2,1)} %param.8, bf16[3072,768]{1,0:T(8,128)(2,1)} %all-gather.6.cloned.1.call-done, ...), kind=kOutput, calls=%fused_computation.249 | convolution fusion | flops 2428894464 | bytes 14174208 | tf_op jit(solution)/shard_map/dot_general | solution.py:103
  130.0 4.7 fusion.155
  134.6 1.6 copy-done.9
  136.2 5.1 %fusion.139 = f32[768,3072]{1,0:T(8,128)} fusion(bf16[512,768]{1,0:T(8,128)(2,1)S(1)} %copy-done.8, bf16[512,3072]{1,0:T(8,128)(2,1)S(1)} %get-tuple-element.192), kind=kOutput, calls=%fused_computation.257 | convolution fusion | flops 2415919104 | bytes 13369344 | tf_op jit(solution)/shard_map/dot_general | solution.py:139
  141.4 11.6 %stack_reshape.4 = f32[16,1,192,768]{3,2,0,1:T(8,128)} reshape(f32[768,3072]{1,0:T(8,128)} %fusion.139) | data formatting | bytes 18874368 | tf_op jit(solution)/shard_map/stack;reshape | solution.py:145
  153.0 4.8 %convolution_bitcast_fusion = f32[16,1,192,768]{3,2,0,1:T(8,128)S(1)} fusion(bf16[16,192,512]{2,1,0:T(8,128)(2,1)} %bitcast.120, bf16[512,768,1]{1,0,2:T(8,128)(2,1)} %bitcast.122), kind=kOutput, calls=%fused_computation.65 | convolution fusion | flops 2415919104 | bytes 13369344 | tf_op jit(solution)/shard_map/dot_general | solution.py:142
  157.8 6.9 %pad_maximum_fusion = f32[16,2,192,768]{3,2,0,1:T(8,128)} fusion(f32[16,1,192,768]{3,2,0,1:T(8,128)S(1)} %convolution_bitcast_fusion, f32[16,1,192,768]{3,2,0,1:T(8,128)S(1)} %copy-done), kind=kLoop, calls=%fused_computation.50 | loop fusion | flops 4718592 | bytes 37748736 | tf_op jit(solution)/shard_map/stack | solution.py:145
  164.8 7.4 %multiply_reduce_fusion = (f32[768]{0:T(1024)S(1)}, f32[512]{0:T(512)S(1)}, f32[512]{0:T(512)S(1)}, f32[512,768]{1,0:T(8,128)}) fusion(bf16[16,32,768]{2,1,0:T(8,128)(2,1)} %get-tuple-element.170, f32[512]{0:T(512)S(1)} %rsqrt.12, f32[512]{0:T(512)S(1)} %div.15, f32[768]{0:T(1024)S(1)} %copy-done.14, bf16[768,3072]{1,0:T(8,128)(2,1)} %all-gather.4.cloned.1.call-done, ...), kind=kOutput, calls=%fused_computation.254 | convolution fusion | flops 2419456256 | bytes 10237952 | tf_op jit(solution)/shard_map/dot_general | solution.py:117
  172.4 6.5 %fusion.132 = (f32[768]{0:T(1024)S(1)}, f32[768]{0:T(1024)S(1)}, f32[768]{0:T(1024)S(1)}, f32[768]{0:T(1024)S(1)}, f32[768]{0:T(1024)S(1)}, /*index=5*/f32[768]{...) fusion(bf16[22,44,768]{2,1,0:T(8,128)(2,1)S(1)} %get-tuple-elem, ...), kind=kLoop, calls=%fused_computation.241 | loop fusion | flops 25152000 | bytes 17368064 | tf_op jit(solution)/shard_map/reduce_sum | solution.py:73
  179.0 3.1 fusion.114
  182.1 4.0 fusion.104
  187.6 18.1 %all_to_all.20 = f32[128,1,330]{2,1,0:T(1,128)S(1)} all-to-all(f32[128,1,330]{2,1,0:T(1,128)S(1)} %copy.20), channel_id=1, replica_groups=mesh['z'=4,'core'=2,'col'=16] {'z','core','col'}, dimensions={0} | all-to-all | bytes 337920 | tf_op jit(solution)/shard_map/all_to_all | solution.py:162
  206.0 13.9 %all_to_all.21 = f32[128,1,36]{2,1,0:T(1,128)S(1)} all-to-all(f32[128,1,36]{2,1,0:T(1,128)S(1)} %broadcast_in_dim.2), channel_id=1, replica_groups=mesh['z'=4,'core'=2,'col'=16] {'z','core','col'}, dimensions={0} | all-to-all | bytes 36864 | tf_op jit(solution)/shard_map/all_to_all | solution.py:166
  219.9 4.9 %all-to-all-start.1 = ((f32[16,192,768]{2,1,0:T(8,128)}), f32[16,192,768]{2,1,0:T(8,128)}, u32[]{:S(2)}, u32[]{:S(2)}) async-start(f32[16,192,768]{2,1,0:T(8,128)} %bitcast.119), calls=%async_computation.2 | async-start | bytes 18874368 | tf_op jit(solution)/shard_map/all_to_all | solution.py:149
  225.4 1.3 collective-permute-start.5
  226.7 4.6 collective-permute-start.4
  231.9 0.8 slice_reduce_fusion.47
  232.7 79.7 %collective-permute-done.5 = bf16[16,6,768]{2,1,0:T(8,128)(2,1)S(1)} collective-permute-done((bf16[16,6,768]{2,1,0:T(8,128)(2,1)S(1)}, bf16[16,6,768]{2,1,0:T(8,128)(2,1)S(1)}, u32[]{:S(2)}, u32[]{:S(2)}) %collective-permute-start.5) | collective-permute-done | bytes 147488 | tf_op jit(solution)/shard_map/ppermute | solution.py:44
  312.7 1.3 collective-permute-start.6
  314.0 1.3 collective-permute-start.7
  316.5 0.8 reduce.202
  317.4 75.2 %all-to-all-done.1 = f32[16,192,768]{2,1,0:T(8,128)} async-done(((f32[16,192,768]{2,1,0:T(8,128)}), f32[16,192,768]{2,1,0:T(8,128)}, u32[]{:S(2)}, u32[]{:S(2)}) %all-to-all-start.1) | async-done | bytes 9437216 | tf_op jit(solution)/shard_map/all_to_all | solution.py:149
  392.6 5.1 %reduce_sum.579 = f32[192,768]{1,0:T(8,128)} reduce(f32[16,192,768]{2,1,0:T(8,128)} %all-to-all-done.1, f32[]{:T(128)} %constant.9.clone.1), dimensions={0}, to_apply=%region_58.0 | reduce | flops 2211840 | bytes 10027012 | tf_op jit(solution)/shard_map/reduce_sum | solution.py:148
  399.3 0.8 copy-done.13
  400.0 2.6 maximum_maximum_fusion.1
  402.6 48.5 %all-reduce.2.cloned.1.call-done = f32[1,192,768]{2,1,0:T(8,128)} async-done(((f32[1,192,768]{2,1,0:T(8,128)}), f32[1,192,768]{2,1,0:T(8,128)}) %all-reduce.2.cloned.1.call-update) | async-done | bytes 589840 | tf_op jit(solution)/shard_map/psum | solution.py:151
  451.2 16.5 %fusion.133 = bf16[16,32,768]{2,1,0:T(8,128)(2,1)} fusion(bf16[16,32,768]{2,1,0:T(8,128)(2,1)} %param.15, bf16[22,44,768]{2,1,0:T(8,128)(2,1)S(1)} %get-tuple-element.176, f32[768]{0:T(1024)S(1)} %get-tuple-element.71, f32[768]{0:T(1024)S(1)} %get-tuple-element.72, f32[768]{0:T(1024)S(1)} %get-tuple-element.73, f32[768]{0:T(1024)S(1)} %get-tuple-element.74, ...), kind=kLoop, calls=%fused_computation.246 | loop fusion | flops 66453504 | bytes 35834880 | tf_op jit(solution)/shard_map/convert_element_type | solution.py:134
  467.8 2.1 fusion.151
  469.9 1.0 mul.1651
  (133 shorter events, 8.1 us)
Async XLA Ops:
  7.2 11.4 %copy-start.5 = (bf16[16,32,768]{2,1,0:T(8,128)(2,1)S(1)}, bf16[16,32,768]{2,1,0:T(8,128)(2,1)}, u32[]{:S(2)}) copy-start(bf16[16,32,768]{2,1,0:T(8,128)(2,1)} %param.8) | copy-start | bytes 2359300
  7.2 59.2 %all-gather.4.cloned.1.call-start = ((), (), s32[]{:S(2)}) async-start(), calls=%async_computation.4 | async-start | bytes 5013504 | tf_op jit(solution)/shard_map/all_gather | solution.py:87
  7.9 114.0 %all-gather.6.cloned.1.call-start = ((), (), s32[]{:S(2)}) async-start(), calls=%async_computation.5 | async-start | bytes 5013504 | tf_op jit(solution)/shard_map/all_gather | solution.py:88
  8.7 211.2 %reduce-scatter.2.cloned.1.call-start = ((), (), s32[]{:S(2)}) async-start(), calls=%async_computation.6 | async-start | bytes 28311552 | tf_op jit(solution)/shard_map/reduce_scatter | solution.py:146
  9.8 8.9 %collective-permute-start.1 = (bf16[16,6,768]{2,1,0:T(8,128)(2,1)S(1)}, bf16[16,6,768]{2,1,0:T(8,128)(2,1)S(1)}, u32[]{:S(2)}, u32[]{:S(2)}) collective-permute-start(bf16[16,6,768]{2,1,0:T(8,128)(2,1)S(1)} %get-tuple-element.187), channel_id=1, source_target_pairs={{1,0},{2,1},{3,2},{4,3},{5,4},{6,5},{7,6},{8,7},{9,8},{10,9},{11,1... | collective-permute-start | bytes 442376 | tf_op jit(solution)/shard_map/ppermute | solution.py:44
  11.1 8.4 %collective-permute-start = (bf16[16,6,768]{2,1,0:T(8,128)(2,1)S(1)}, bf16[16,6,768]{2,1,0:T(8,128)(2,1)S(1)}, u32[]{:S(2)}, u32[]{:S(2)}) collective-permute-start(bf16[16,6,768]{2,1,0:T(8,128)(2,1)S(1)} %get-tuple-element.186), channel_id=1, source_target_pairs={{0,1},{1,2},{2,3},{3,4},{4,5},{5,6},{6,7},{7,8},{8,9},{9,10},{10,1... | collective-permute-start | bytes 442376 | tf_op jit(solution)/shard_map/ppermute | solution.py:43
  18.6 4.9 %copy-start.10 = (bf16[16,32,768]{2,1,0:T(8,128)(2,1)S(1)}, bf16[16,32,768]{2,1,0:T(8,128)(2,1)}, u32[]{:S(2)}) copy-start(bf16[16,32,768]{2,1,0:T(8,128)(2,1)} %param.15) | copy-start | bytes 2359300
  18.6 4.9 %copy-start.15 = (f32[768]{0:T(1024)S(1)}, f32[768]{0:T(1024)}, u32[]{:S(2)}) copy-start(f32[768]{0:T(1024)} %param.14) | copy-start | bytes 9220
  18.6 8.4 %copy-start.6 = (bf16[16,32,768]{2,1,0:T(8,128)(2,1)S(1)}, bf16[16,32,768]{2,1,0:T(8,128)(2,1)}, u32[]{:S(2)}) copy-start(bf16[16,32,768]{2,1,0:T(8,128)(2,1)} %param.8) | copy-start | bytes 2359300
  19.8 4.8 %collective-permute-start.2 = (bf16[6,44,768]{2,1,0:T(8,128)(2,1)S(1)}, bf16[6,44,768]{2,1,0:T(8,128)(2,1)S(1)}, u32[]{:S(2)}, u32[]{:S(2)}) collective-permute-start(bf16[6,44,768]{2,1,0:T(8,128)(2,1)S(1)} %get-tuple-element.181), channel_id=1, source_target_pairs={{0,16},{16,32},{32,48},{48,64},{64,80},{80,96},{96,112},{1,17},{17... | collective-permute-start | bytes 1216520 | tf_op jit(solution)/shard_map/ppermute | solution.py:46
  21.1 6.0 %collective-permute-start.3 = (bf16[6,44,768]{2,1,0:T(8,128)(2,1)S(1)}, bf16[6,44,768]{2,1,0:T(8,128)(2,1)S(1)}, u32[]{:S(2)}, u32[]{:S(2)}) collective-permute-start(bf16[6,44,768]{2,1,0:T(8,128)(2,1)S(1)} %get-tuple-element.182), channel_id=1, source_target_pairs={{16,0},{32,16},{48,32},{64,48},{80,64},{96,80},{112,96},{17,1},{33... | collective-permute-start | bytes 1216520 | tf_op jit(solution)/shard_map/ppermute | solution.py:47
  24.6 3.8 copy-start.3
  28.4 14.6 %copy-start.14 = (f32[768]{0:T(1024)S(1)}, f32[768]{0:T(1024)}, u32[]{:S(2)}) copy-start(f32[768]{0:T(1024)} %param.10) | copy-start | bytes 9220
  41.3 25.1 %copy-start.17 = (f32[3072]{0:T(1024)S(1)}, f32[3072]{0:T(1024)}, u32[]{:S(2)}) copy-start(f32[3072]{0:T(1024)} %param.12) | copy-start | bytes 36868
  122.0 7.9 %copy-start.16 = (bf16[3072,768]{1,0:T(8,128)(2,1)S(1)}, bf16[3072,768]{1,0:T(8,128)(2,1)}, u32[]{:S(2)}) copy-start(bf16[3072,768]{1,0:T(8,128)(2,1)} %all-gather.6.cloned.1.call-done) | copy-start | bytes 14155780
  122.0 8.0 %copy-start.18 = (f32[512,3072]{1,0:T(8,128)S(1)}, f32[512,3072]{1,0:T(8,128)}, u32[]{:S(2)}) copy-start(f32[512,3072]{1,0:T(8,128)} %get-tuple-element.194) | copy-start | bytes 18874372
  130.0 6.3 %copy-start.8 = (bf16[512,768]{1,0:T(8,128)(2,1)S(1)}, bf16[512,768]{1,0:T(8,128)(2,1)}, u32[]{:S(2)}) copy-start(bf16[512,768]{1,0:T(8,128)(2,1)} %multiply_convert_fusion.3) | copy-start | bytes 2359300
  134.6 1.6 copy-start.9
  153.0 4.9 %copy-start = (f32[16,1,192,768]{3,2,0,1:T(8,128)S(1)}, f32[16,1,192,768]{3,2,0,1:T(8,128)}, u32[]{:S(2)}) copy-start(f32[16,1,192,768]{3,2,0,1:T(8,128)} %stack_reshape.4) | copy-start | bytes 28311556
  172.4 6.6 %copy-start.4 = (bf16[16,38,768]{2,1,0:T(8,128)(2,1)S(1)}, bf16[16,38,768]{2,1,0:T(8,128)(2,1)}, u32[]{:S(2)}) copy-start(bf16[16,38,768]{2,1,0:T(8,128)(2,1)} %copy-done.3) | copy-start | bytes 2801668
  172.4 6.6 %copy-start.7 = (bf16[16,32,768]{2,1,0:T(8,128)(2,1)S(1)}, bf16[16,32,768]{2,1,0:T(8,128)(2,1)}, u32[]{:S(2)}) copy-start(bf16[16,32,768]{2,1,0:T(8,128)(2,1)} %param.8) | copy-start | bytes 2359300
  178.9 3.1 copy-start.1
  219.9 5.0 %copy-start.12 = (f32[768,49]{0,1:T(8,128)S(1)}, f32[768,49]{0,1:T(8,128)}, u32[]{:S(2)}) copy-start(f32[768,49]{0,1:T(8,128)} %param.9) | copy-start | bytes 451588
  219.9 5.4 %copy-start.2 = (bf16[512,768]{1,0:T(8,128)(2,1)S(1)}, bf16[512,768]{1,0:T(8,128)(2,1)}, u32[]{:S(2)}) copy-start(bf16[512,768]{1,0:T(8,128)(2,1)} %copy-done.1) | copy-start | bytes 2359300
  219.9 172.8 %all-to-all-start.1 = ((f32[16,192,768]{2,1,0:T(8,128)}), f32[16,192,768]{2,1,0:T(8,128)}, u32[]{:S(2)}, u32[]{:S(2)}) async-start(f32[16,192,768]{2,1,0:T(8,128)} %bitcast.119), calls=%async_computation.2 | async-start | bytes 18874368 | tf_op jit(solution)/shard_map/all_to_all | solution.py:149
  224.8 226.4 %all-reduce.2.cloned.1.call-start = ((), (), s32[]{:S(2)}) async-start(), calls=%async_computation.7 | async-start | bytes 1179648 | tf_op jit(solution)/shard_map/psum | solution.py:151
  225.4 87.0 %collective-permute-start.5 = (bf16[16,6,768]{2,1,0:T(8,128)(2,1)S(1)}, bf16[16,6,768]{2,1,0:T(8,128)(2,1)S(1)}, u32[]{:S(2)}, u32[]{:S(2)}) collective-permute-start(bf16[16,6,768]{2,1,0:T(8,128)(2,1)S(1)} %get-tuple-element.185), channel_id=1, source_target_pairs={{1,0},{2,1},{3,2},{4,3},{5,4},{6,5},{7,6},{8,7},{9,8},{10,9},{11,1... | collective-permute-start | bytes 442376 | tf_op jit(solution)/shard_map/ppermute | solution.py:44
  226.7 85.7 %collective-permute-start.4 = (bf16[16,6,768]{2,1,0:T(8,128)(2,1)S(1)}, bf16[16,6,768]{2,1,0:T(8,128)(2,1)S(1)}, u32[]{:S(2)}, u32[]{:S(2)}) collective-permute-start(bf16[16,6,768]{2,1,0:T(8,128)(2,1)S(1)} %get-tuple-element.184), channel_id=1, source_target_pairs={{0,1},{1,2},{2,3},{3,4},{4,5},{5,6},{6,7},{7,8},{8,9},{9,10},{10,1... | collective-permute-start | bytes 442376 | tf_op jit(solution)/shard_map/ppermute | solution.py:43
  312.4 85.3 %copy-start.11 = (bf16[16,6,768]{2,1,0:T(8,128)(2,1)}, bf16[16,6,768]{2,1,0:T(8,128)(2,1)S(1)}, u32[]{:S(2)}) copy-start(bf16[16,6,768]{2,1,0:T(8,128)(2,1)S(1)} %collective-permute-done.4) | copy-start | bytes 442372
  312.7 86.5 %collective-permute-start.6 = (bf16[6,44,768]{2,1,0:T(8,128)(2,1)S(1)}, bf16[6,44,768]{2,1,0:T(8,128)(2,1)S(1)}, u32[]{:S(2)}, u32[]{:S(2)}) collective-permute-start(bf16[6,44,768]{2,1,0:T(8,128)(2,1)S(1)} %get-tuple-element.177), channel_id=1, source_target_pairs={{0,16},{16,32},{32,48},{48,64},{64,80},{80,96},{96,112},{1,17},{17... | collective-permute-start | bytes 1216520 | tf_op jit(solution)/shard_map/ppermute | solution.py:46
  314.0 86.0 %collective-permute-start.7 = (bf16[6,44,768]{2,1,0:T(8,128)(2,1)S(1)}, bf16[6,44,768]{2,1,0:T(8,128)(2,1)}, u32[]{:S(2)}, u32[]{:S(2)}) collective-permute-start(bf16[6,44,768]{2,1,0:T(8,128)(2,1)S(1)} %get-tuple-element.178), channel_id=1, source_target_pairs={{16,0},{32,16},{48,32},{64,48},{80,64},{96,80},{112,96},{17,1},{33... | collective-permute-start | bytes 1216520 | tf_op jit(solution)/shard_map/ppermute | solution.py:47
  397.8 70.0 %all-gather.8.cloned.1.call-start = ((), (), s32[]{:S(2)}) async-start(), calls=%async_computation.8 | async-start | bytes 1769472 | tf_op jit(solution)/shard_map/all_gather | solution.py:152
  399.3 0.8 copy-start.13
Sparse Core Ops, SparseCore 0:
  10.2 56.1 all-gather.3
  68.5 53.3 all-gather.5
  164.9 29.0 reduce-scatter.1
  397.9 53.2 all-reduce.1
  452.7 12.3 all-gather.7

commit v9 on v7

--- a/solution.py
+++ b/solution.py
@@ -142,8 +142,10 @@
     block_out = lax.dot_general(
         hidden, grad_mix, CONTRACT_ROWS, preferred_element_type=jnp.float32
     ).reshape(col_count, rows_out, channels)
-    stacked = jnp.stack([block_in, block_out], axis=1)
-    halves = lax.psum_scatter(stacked, "core", scatter_dimension=1, tiled=True)
+    first_core = lax.axis_index("core") == 0
+    sent = jnp.where(first_core, block_out, block_in)
+    kept = jnp.where(first_core, block_in, block_out)
+    halves = kept + lax.ppermute(sent, "core", [(0, 1), (1, 0)])
     halves = halves.reshape(-1, channels)
     mine = lax.psum_scatter(halves, "col", scatter_dimension=0, tiled=True)
     mine = lax.psum(mine, "z")

time: 364 us -> 362 us (level)
  waiting for transfers between devices: 166 us -> 149 us
  matrix products: 36.4 us -> 43.2 us
    reduce_scatter x1 -> x0, waiting for transfers between devices: 29.2 us -> none  [local(): halves = lax.psum_scatter(stacked, 'core', scatter_dimension=1, tiled=True)]
    ppermute x0 -> x1, waiting for transfers between devices: none -> 14.6 us  [local(): halves = kept + lax.ppermute(sent, 'core', [(0, 1), (1, 0)])]
    another operation x1 -> x0, local copies, waits for them, and re-layouts: 11.6 us -> none  [local(): stacked = jnp.stack([block_in, block_out], axis=1)]
    reshape x0 -> x1, local copies, waits for them, and re-layouts: none -> 11.6 us  [local(): block_in = lax.dot_general(normed, grad_pre_rounded, CONTRACT_ROWS, prefe...]
    add x0 -> x1, other arithmetic: none -> 7.34 us  [local(): halves = kept + lax.ppermute(sent, 'core', [(0, 1), (1, 0)])]
    another operation x1 -> x0, other arithmetic: 6.92 us -> none  [local(): stacked = jnp.stack([block_in, block_out], axis=1)]
    dot_general x1, matrix products: 4.84 us -> 11.4 us  [local(): lax.dot_general(hidden, grad_mix, CONTRACT_ROWS, preferred_element_type=j...]
    all_gather x1, waiting for transfers between devices: 43.9 us -> 48.5 us  [local(): lax.all_gather(w_out, 'col', axis=0, tiled=True)]
where the time goes in v9:
time: 362 us; the launch traced here: 360 us
  waiting for transfers between devices  149 us (41%)
  other arithmetic  69 us (19%)
  local copies, waits for them, and re-layouts  45.6 us (13%)
  matrix products  43.2 us (12%)
  starting transfers between devices  38 us (10%)
  between operations  15.6 us (4%)
    all_gather x1, waiting for transfers between devices, local(): lax.all_gather(w_out, 'col', axis=0, tiled=True)  48.5 us
    psum x1, waiting for transfers between devices, local(): mine = lax.psum(mine, 'z')  40.2 us
    all_gather x1, waiting for transfers between devices, local(): lax.all_gather(w_in, 'col', axis=0, tiled=True)  18.1 us
    convert_element_type x1, other arithmetic, local(): (cotangent.astype(jnp.float32) + grad_back.astype(jnp.float32)).astype(jn...  15.8 us
    reduce_sum x3, other arithmetic, tile_taps(): columns.append(jnp.sum(gradient * window, axis=(0, 1)))  15.5 us
    ppermute x1, waiting for transfers between devices, local(): halves = kept + lax.ppermute(sent, 'core', [(0, 1), (1, 0)])  14.6 us
    reduce_sum x1, other arithmetic, local(): average = jnp.mean(conv_rows, axis=1, keepdims=True)  12.9 us
    all_to_all x1, starting transfers between devices, local(): lax.all_to_all(outgoing, EVERY, split_axis=0, concat_axis=0, tiled=True)  12 us
  transfers between devices with their start and end apart: 16, of which 9 were waited for; matrix products, arithmetic and copies ran while one was open for 27% of the time, Pallas kernels for 0%

profile of v9, /device:TPU:0, one launch (start us, length us, event | category | flops | bytes accessed | tf_op | source)
XLA Modules:
  0.0 359.9 jit_solution(18321101001025846073)
XLA Ops:
  9.8 1.3 collective-permute-start.1
  11.1 4.6 %collective-permute-start = (bf16[16,6,768]{2,1,0:T(8,128)(2,1)S(1)}, bf16[16,6,768]{2,1,0:T(8,128)(2,1)S(1)}, u32[]{:S(2)}, u32[]{:S(2)}) collective-permute-start(bf16[16,6,768]{2,1,0:T(8,128)(2,1)S(1)} %get-tuple-element.186), channel_id=1, source_target_pairs={{0,1},{1,2},{2,3},{3,4},{4,5},{5,6},{6,7},{7,8},{8,9},{9,10},{10,1... | collective-permute-start | bytes 442376 | tf_op jit(solution)/shard_map/ppermute | solution.py:43
  15.7 1.4 slice_reduce_fusion.97
  17.1 2.0 slice_reduce_fusion.96
  19.5 1.3 pad_maximum_fusion.10
  20.7 1.3 collective-permute-start.2
  22.0 1.3 collective-permute-start.3
  23.3 1.8 slice_reduce_fusion.95
  28.3 2.8 maximum_maximum_fusion
  31.4 12.9 %convert_reduce_fusion = (f32[16,32]{1,0:T(8,128)S(1)}, bf16[16,32,768]{2,1,0:T(8,128)(2,1)}) fusion(bf16[22,44,768]{2,1,0:T(8,128)(2,1)S(1)} %get-tuple-element.180, f32[768]{0:T(1024)S(1)} %copy-done.85, f32[768]{0:T(1024)S(1)} %get-tuple-element.120, f32[768]{0:T(1024)S(1)} %get-tuple-element.121, f32[768]{0:T(1024)S(1)} %get-tuple-element.122, ...), kind=kLoop, calls=%fused_computation.272 | loop fusion | flops 62127616 | bytes 37262336 | tf_op jit(solution)/shard_map/reduce_sum | solution.py:96
  44.4 1.5 multiply_reduce_fusion.2
  45.9 2.3 multiply_convert_fusion.3
  48.3 18.1 %all-gather.4.cloned.1.call-done = bf16[768,3072]{1,0:T(8,128)(2,1)} async-done(((bf16[48,3072]{1,0:T(8,128)(2,1)}), bf16[768,3072]{1,0:T(8,128)(2,1)}) %all-gather.4.cloned.1.call-update) | async-done | bytes 4718608 | tf_op jit(solution)/shard_map/all_gather | solution.py:87
  66.4 7.1 %fusion.8 = (bf16[3072,512]{0,1:T(8,128)(2,1)}, f32[512,3072]{1,0:T(8,128)}) fusion(f32[3072]{0:T(1024)S(1)} %copy-done.89, bf16[512,768]{1,0:T(8,128)(2,1)} %multiply_convert_fusion.3, bf16[768,3072]{1,0:T(8,128)(2,1)} %all-gather.4.cloned.1.call-done), kind=kOutput, calls=%fused_computation.64 | convolution fusion | flops 2425356288 | bytes 14954496 | tf_op jit(solution)/shard_map/dot_general | solution.py:101
  73.5 48.5 %all-gather.6.cloned.1.call-done = bf16[3072,768]{1,0:T(8,128)(2,1)} async-done(((bf16[192,768]{1,0:T(8,128)(2,1)}), bf16[3072,768]{1,0:T(8,128)(2,1)}) %all-gather.6.cloned.1.call-update) | async-done | bytes 4718608 | tf_op jit(solution)/shard_map/all_gather | solution.py:88
  122.0 8.0 %fusion.136 = (f32[768]{0:T(1024)S(1)}, bf16[512,768]{1,0:T(8,128)(2,1)}, bf16[512,768]{1,0:T(8,128)(2,1)S(1)}) fusion(bf16[16,32,768]{2,1,0:T(8,128)(2,1)} %param.15, f32[768]{0:T(1024)S(1)} %copy-done.87, bf16[16,32,768]{2,1,0:T(8,128)(2,1)} %param.8, bf16[3072,768]{1,0:T(8,128)(2,1)} %all-gather.6.cloned.1.call-done, ...), kind=kOutput, calls=%fused_computation.249 | convolution fusion | flops 2428894464 | bytes 14174208 | tf_op jit(solution)/shard_map/dot_general | solution.py:103
  130.0 4.7 %fusion.155 = (f32[3072]{0:T(1024)S(1)}, bf16[512,3072]{1,0:T(8,128)(2,1)S(1)}) fusion(f32[512,3072]{1,0:T(8,128)S(1)} %copy-done.90, f32[3072]{0:T(1024)S(1)} %copy-done.89, bf16[512,768]{1,0:T(8,128)(2,1)S(1)} %get-tuple-element.183, bf16[3072,768]{1,0:T(8,128)(2,1)S(1)} %copy-done.88), kind=kOutput, calls=%fused_computation.409 | convolution fusion | flops 2434790400 | bytes 14966784 | tf_op jit(solution)/shard_map/dot_general | solution.py:111
  134.6 1.6 copy-done.9
  136.3 5.1 %fusion.139 = f32[768,3072]{1,0:T(8,128)} fusion(bf16[512,768]{1,0:T(8,128)(2,1)S(1)} %copy-done.8, bf16[512,3072]{1,0:T(8,128)(2,1)S(1)} %get-tuple-element.192), kind=kOutput, calls=%fused_computation.257 | convolution fusion | flops 2415919104 | bytes 13369344 | tf_op jit(solution)/shard_map/dot_general | solution.py:139
  141.4 11.6 %reshape.223 = f32[16,192,768]{2,1,0:T(8,128)} reshape(f32[768,3072]{1,0:T(8,128)} %fusion.139) | data formatting | bytes 18874368 | tf_op jit(solution)/shard_map/reshape | solution.py:141
  153.0 4.7 %copy.21 = bf16[3072,512]{1,0:T(8,128)(2,1)} copy(bf16[3072,512]{0,1:T(8,128)(2,1)} %get-tuple-element.193) | data formatting | bytes 6291456 | tf_op jit(solution)/shard_map/convert_element_type | solution.py:102
  157.7 11.4 %broadcast_select_fusion = (f32[16,192,768]{2,1,0:T(8,128)}, f32[16,192,768]{2,1,0:T(8,128)}) fusion(f32[16,192,768]{2,1,0:T(8,128)} %reshape.223, pred[]{:T(512)S(6)} %eq.3, bf16[16,192,512]{2,1,0:T(8,128)(2,1)} %bitcast.120, bf16[512,768,1]{1,0,2:T(8,128)(2,1)} %bitcast.121), kind=kOutput, calls=%fused_computation.65 | convolution fusion | flops 2418278400 | bytes 32243712 | tf_op jit(solution)/shard_map/dot_general | solution.py:142
  169.1 2.5 collective-permute-start.8
  171.5 14.6 %collective-permute-done.8 = f32[16,192,768]{2,1,0:T(8,128)} collective-permute-done((f32[16,192,768]{2,1,0:T(8,128)}, f32[16,192,768]{2,1,0:T(8,128)}, u32[]{:S(2)}, u32[]{:S(2)}) %collective-permute-start.8) | collective-permute-done | bytes 9437216 | tf_op jit(solution)/shard_map/ppermute | solution.py:148
  186.2 7.3 %select_add_fusion = f32[16,192,768]{2,1,0:T(8,128)} fusion(f32[16,192,768]{2,1,0:T(8,128)} %collective-permute-done.8, f32[16,192,768]{2,1,0:T(8,128)S(1)} %bitcast.114, f32[16,192,768]{2,1,0:T(8,128)} %get-tuple-element.196, pred[]{:T(512)S(6)} %eq.3), kind=kLoop, calls=%fused_computation.51 | loop fusion | flops 4718592 | bytes 37748736 | tf_op jit(solution)/shard_map/add | solution.py:148
  193.5 1.6 reshape.218
  195.1 3.5 rev.3
  198.7 1.6 reshape.219
  200.3 2.1 slice_reduce_fusion.48
  202.3 2.0 slice_reduce_fusion.47
  204.4 6.9 %multiply_reduce_fusion = (f32[768]{0:T(1024)S(1)}, f32[512]{0:T(512)S(1)}, f32[512]{0:T(512)S(1)}, f32[512,768]{1,0:T(8,128)S(1)}) fusion(bf16[16,32,768]{2,1,0:T(8,128)(2,1)} %get-tuple-element.170, f32[512]{0:T(512)S(1)} %rsqrt.12, f32[512]{0:T(512)S(1)} %div.15, f32[768]{0:T(1024)S(1)} %copy-done.45, ...), kind=kOutput, calls=%fused_computation.254 | convolution fusion | flops 2419456256 | bytes 10237952 | tf_op jit(solution)/shard_map/dot_general | solution.py:117
  211.3 5.7 %fusion.132 = (f32[768]{0:T(1024)}, f32[768]{0:T(1024)}, f32[768]{0:T(1024)}, f32[768]{0:T(1024)}, f32[768]{0:T(1024)}, /*index=5*/f32[768]{0:T(1024)}, f32[768]...) fusion(bf16[22,44,768]{2,1,0:T(8,128)(2,1)S(1)} %get-tuple-elem, ...), kind=kLoop, calls=%fused_computation.241 | loop fusion | flops 25152000 | bytes 17368064 | tf_op jit(solution)/shard_map/reduce_sum | solution.py:73
  218.6 1.3 collective-permute-start.5
  219.9 5.2 %collective-permute-start.4 = (bf16[16,6,768]{2,1,0:T(8,128)(2,1)}, bf16[16,6,768]{2,1,0:T(8,128)(2,1)}, u32[]{:S(2)}, u32[]{:S(2)}) collective-permute-start(bf16[16,6,768]{2,1,0:T(8,128)(2,1)} %get-tuple-element.184), channel_id=1, source_target_pairs={{0,1},{1,2},{2,3},{3,4},{4,5},{5,6},{6,7},{7,8},{8,9},{9,10},{10,1... | collective-permute-start | bytes 442376 | tf_op jit(solution)/shard_map/ppermute | solution.py:43
  225.3 5.9 %fusion.114 = (f32[768]{0:T(1024)S(1)}, f32[768]{0:T(1024)S(1)}, f32[768]{0:T(1024)S(1)}, f32[768]{0:T(1024)S(1)}, f32[768]{0:T(1024)S(1)}, /*index=5*/f32[768]{...) fusion(bf16[22,44,768]{2,1,0:T(8,128)(2,1)S(1)} %get-tuple-elem, ...), kind=kLoop, calls=%fused_computation.223 | loop fusion | flops 19257600 | bytes 8838144 | tf_op jit(solution)/shard_map/reduce_sum | solution.py:73
  231.4 4.0 %fusion.104 = (f32[768]{0:T(1024)S(1)}, f32[768]{0:T(1024)S(1)}, f32[768]{0:T(1024)S(1)}, f32[768]{0:T(1024)S(1)}, f32[768]{0:T(1024)S(1)}, /*index=5*/f32[768]{...) fusion(bf16[22,44,768]{2,1,0:T(8,128)(2,1)S(1)} %get-tuple-elem, ...), kind=kLoop, calls=%fused_computation.213 | loop fusion | flops 21613056 | bytes 14997504 | tf_op jit(solution)/shard_map/reduce_sum | solution.py:73
  237.8 12.0 %all-to-all-start = ((f32[128,1,330]{2,1,0:T(1,128)}), f32[128,1,330]{2,1,0:T(1,128)S(1)}, u32[]{:S(2)}, u32[]{:S(2)}) async-start(f32[128,1,330]{2,1,0:T(1,128)} %copy.20), calls=%async_computation | async-start | bytes 393216 | tf_op jit(solution)/shard_map/all_to_all | solution.py:162
  251.0 1.3 pad_maximum_fusion.7
  252.3 1.3 collective-permute-start.6
  253.7 1.3 collective-permute-start.7
  255.0 6.9 %all-to-all-done = f32[128,1,330]{2,1,0:T(1,128)S(1)} async-done(((f32[128,1,330]{2,1,0:T(1,128)}), f32[128,1,330]{2,1,0:T(1,128)S(1)}, u32[]{:S(2)}, u32[]{:S(2)}) %all-to-all-start) | async-done | bytes 168992 | tf_op jit(solution)/shard_map/all_to_all | solution.py:162
  262.8 5.7 %all-to-all-start.1 = ((f32[128,1,36]{2,1,0:T(1,128)}), f32[128,1,36]{2,1,0:T(1,128)S(1)}, u32[]{:S(2)}, u32[]{:S(2)}) async-start(f32[128,1,36]{2,1,0:T(1,128)} %broadcast_in_dim.2), calls=%async_computation.2 | async-start | bytes 131072 | tf_op jit(solution)/shard_map/all_to_all | solution.py:166
  269.3 8.7 %all-to-all-done.1 = f32[128,1,36]{2,1,0:T(1,128)S(1)} async-done(((f32[128,1,36]{2,1,0:T(1,128)}), f32[128,1,36]{2,1,0:T(1,128)S(1)}, u32[]{:S(2)}, u32[]{:S(2)}) %all-to-all-start.1) | async-done | bytes 18464 | tf_op jit(solution)/shard_map/all_to_all | solution.py:166
  279.4 9.4 %reduce-scatter.2.cloned.1.call-done = f32[192,768]{1,0:T(8,128)} async-done(((f32[3072,768]{1,0:T(8,128)}), f32[192,768]{1,0:T(8,128)}) %reduce-scatter.2.cloned.1.call-update) | async-done | bytes 589840 | tf_op jit(solution)/shard_map/reduce_scatter | solution.py:150
  291.2 2.7 maximum_maximum_fusion.1
  293.9 40.2 %all-reduce.2.cloned.1.call-done = f32[1,192,768]{2,1,0:T(8,128)} async-done(((f32[1,192,768]{2,1,0:T(8,128)}), f32[1,192,768]{2,1,0:T(8,128)}) %all-reduce.2.cloned.1.call-update) | async-done | bytes 589840 | tf_op jit(solution)/shard_map/psum | solution.py:151
  334.4 15.8 %fusion.133 = bf16[16,32,768]{2,1,0:T(8,128)(2,1)} fusion(bf16[16,32,768]{2,1,0:T(8,128)(2,1)} %param.15, bf16[22,44,768]{2,1,0:T(8,128)(2,1)S(1)} %get-tuple-element.176, f32[768]{0:T(1024)S(1)} %get-tuple-element.71, f32[768]{0:T(1024)S(1)} %get-tuple-element.72, f32[768]{0:T(1024)S(1)} %get-tuple-element.73, f32[768]{0:T(1024)S(1)} %get-tuple-element.74, ...), kind=kLoop, calls=%fused_computation.246 | loop fusion | flops 66453504 | bytes 35834880 | tf_op jit(solution)/shard_map/convert_element_type | solution.py:134
  350.3 2.1 fusion.151
  (285 shorter events, 17.3 us)
Async XLA Ops:
  7.2 59.2 %all-gather.4.cloned.1.call-start = ((), (), s32[]{:S(2)}) async-start(), calls=%async_computation.3 | async-start | bytes 5013504 | tf_op jit(solution)/shard_map/all_gather | solution.py:87
  7.9 114.0 %all-gather.6.cloned.1.call-start = ((), (), s32[]{:S(2)}) async-start(), calls=%async_computation.4 | async-start | bytes 5013504 | tf_op jit(solution)/shard_map/all_gather | solution.py:88
  8.7 280.2 %reduce-scatter.2.cloned.1.call-start = ((), (), s32[]{:S(2)}) async-start(), calls=%async_computation.5 | async-start | bytes 10027008 | tf_op jit(solution)/shard_map/reduce_scatter | solution.py:150
  9.8 9.4 %collective-permute-start.1 = (bf16[16,6,768]{2,1,0:T(8,128)(2,1)S(1)}, bf16[16,6,768]{2,1,0:T(8,128)(2,1)S(1)}, u32[]{:S(2)}, u32[]{:S(2)}) collective-permute-start(bf16[16,6,768]{2,1,0:T(8,128)(2,1)S(1)} %get-tuple-element.187), channel_id=1, source_target_pairs={{1,0},{2,1},{3,2},{4,3},{5,4},{6,5},{7,6},{8,7},{9,8},{10,9},{11,1... | collective-permute-start | bytes 442376 | tf_op jit(solution)/shard_map/ppermute | solution.py:44
  11.1 8.4 %collective-permute-start = (bf16[16,6,768]{2,1,0:T(8,128)(2,1)S(1)}, bf16[16,6,768]{2,1,0:T(8,128)(2,1)S(1)}, u32[]{:S(2)}, u32[]{:S(2)}) collective-permute-start(bf16[16,6,768]{2,1,0:T(8,128)(2,1)S(1)} %get-tuple-element.186), channel_id=1, source_target_pairs={{0,1},{1,2},{2,3},{3,4},{4,5},{5,6},{6,7},{7,8},{8,9},{9,10},{10,1... | collective-permute-start | bytes 442376 | tf_op jit(solution)/shard_map/ppermute | solution.py:43
  20.7 5.7 %collective-permute-start.2 = (bf16[6,44,768]{2,1,0:T(8,128)(2,1)}, bf16[6,44,768]{2,1,0:T(8,128)(2,1)S(1)}, u32[]{:S(2)}, u32[]{:S(2)}) collective-permute-start(bf16[6,44,768]{2,1,0:T(8,128)(2,1)} %get-tuple-element.181), channel_id=1, source_target_pairs={{0,16},{16,32},{32,48},{48,64},{64,80},{80,96},{96,112},{1,17},{17... | collective-permute-start | bytes 1216520 | tf_op jit(solution)/shard_map/ppermute | solution.py:46
  22.0 6.3 %collective-permute-start.3 = (bf16[6,44,768]{2,1,0:T(8,128)(2,1)}, bf16[6,44,768]{2,1,0:T(8,128)(2,1)}, u32[]{:S(2)}, u32[]{:S(2)}) collective-permute-start(bf16[6,44,768]{2,1,0:T(8,128)(2,1)} %get-tuple-element.182), channel_id=1, source_target_pairs={{16,0},{32,16},{48,32},{64,48},{80,64},{96,80},{112,96},{17,1},{33... | collective-permute-start | bytes 1216520 | tf_op jit(solution)/shard_map/ppermute | solution.py:47
  48.3 73.7 %copy-start.87 = (f32[768]{0:T(1024)S(1)}, f32[768]{0:T(1024)}, u32[]{:S(2)}) copy-start(f32[768]{0:T(1024)} %param.14) | copy-start | bytes 9220
  169.1 17.1 %collective-permute-start.8 = (f32[16,192,768]{2,1,0:T(8,128)}, f32[16,192,768]{2,1,0:T(8,128)}, u32[]{:S(2)}, u32[]{:S(2)}) collective-permute-start(f32[16,192,768]{2,1,0:T(8,128)} %get-tuple-element.195), channel_id=1, source_target_pairs={{0,16},{16,0},{1,17},{17,1},{2,18},{18,2},{3,19},{19,3},{4,20},{20... | collective-permute-start | bytes 28311560 | tf_op jit(solution)/shard_map/ppermute | solution.py:148
  218.6 32.3 %collective-permute-start.5 = (bf16[16,6,768]{2,1,0:T(8,128)(2,1)}, bf16[16,6,768]{2,1,0:T(8,128)(2,1)}, u32[]{:S(2)}, u32[]{:S(2)}) collective-permute-start(bf16[16,6,768]{2,1,0:T(8,128)(2,1)} %get-tuple-element.185), channel_id=1, source_target_pairs={{1,0},{2,1},{3,2},{4,3},{5,4},{6,5},{7,6},{8,7},{9,8},{10,9},{11,1... | collective-permute-start | bytes 442376 | tf_op jit(solution)/shard_map/ppermute | solution.py:44
  219.9 31.1 %collective-permute-start.4 = (bf16[16,6,768]{2,1,0:T(8,128)(2,1)}, bf16[16,6,768]{2,1,0:T(8,128)(2,1)}, u32[]{:S(2)}, u32[]{:S(2)}) collective-permute-start(bf16[16,6,768]{2,1,0:T(8,128)(2,1)} %get-tuple-element.184), channel_id=1, source_target_pairs={{0,1},{1,2},{2,3},{3,4},{4,5},{5,6},{6,7},{7,8},{8,9},{9,10},{10,1... | collective-permute-start | bytes 442376 | tf_op jit(solution)/shard_map/ppermute | solution.py:43
  237.8 24.1 %all-to-all-start = ((f32[128,1,330]{2,1,0:T(1,128)}), f32[128,1,330]{2,1,0:T(1,128)S(1)}, u32[]{:S(2)}, u32[]{:S(2)}) async-start(f32[128,1,330]{2,1,0:T(1,128)} %copy.20), calls=%async_computation | async-start | bytes 393216 | tf_op jit(solution)/shard_map/all_to_all | solution.py:162
  252.3 38.1 %collective-permute-start.6 = (bf16[6,44,768]{2,1,0:T(8,128)(2,1)S(1)}, bf16[6,44,768]{2,1,0:T(8,128)(2,1)S(1)}, u32[]{:S(2)}, u32[]{:S(2)}) collective-permute-start(bf16[6,44,768]{2,1,0:T(8,128)(2,1)S(1)} %get-tuple-element.177), channel_id=1, source_target_pairs={{0,16},{16,32},{32,48},{48,64},{64,80},{80,96},{96,112},{1,17},{17... | collective-permute-start | bytes 1216520 | tf_op jit(solution)/shard_map/ppermute | solution.py:46
  253.7 37.5 %collective-permute-start.7 = (bf16[6,44,768]{2,1,0:T(8,128)(2,1)S(1)}, bf16[6,44,768]{2,1,0:T(8,128)(2,1)}, u32[]{:S(2)}, u32[]{:S(2)}) collective-permute-start(bf16[6,44,768]{2,1,0:T(8,128)(2,1)S(1)} %get-tuple-element.178), channel_id=1, source_target_pairs={{16,0},{32,16},{48,32},{64,48},{80,64},{96,80},{112,96},{17,1},{33... | collective-permute-start | bytes 1216520 | tf_op jit(solution)/shard_map/ppermute | solution.py:47
  262.8 15.2 %all-to-all-start.1 = ((f32[128,1,36]{2,1,0:T(1,128)}), f32[128,1,36]{2,1,0:T(1,128)S(1)}, u32[]{:S(2)}, u32[]{:S(2)}) async-start(f32[128,1,36]{2,1,0:T(1,128)} %broadcast_in_dim.2), calls=%async_computation.2 | async-start | bytes 131072 | tf_op jit(solution)/shard_map/all_to_all | solution.py:166
  268.6 65.5 %all-reduce.2.cloned.1.call-start = ((), (), s32[]{:S(2)}) async-start(), calls=%async_computation.6 | async-start | bytes 1179648 | tf_op jit(solution)/shard_map/psum | solution.py:151
  288.8 61.4 %all-gather.8.cloned.1.call-start = ((), (), s32[]{:S(2)}) async-start(), calls=%async_computation.7 | async-start | bytes 1769472 | tf_op jit(solution)/shard_map/all_gather | solution.py:152
  290.1 44.0 %copy-start.14 = (f32[768]{0:T(1024)S(1)}, f32[768]{0:T(1024)}, u32[]{:S(2)}) copy-start(f32[768]{0:T(1024)} %get-tuple-element.77) | copy-start | bytes 9220
  290.1 44.0 %copy-start.15 = (f32[768]{0:T(1024)S(1)}, f32[768]{0:T(1024)}, u32[]{:S(2)}) copy-start(f32[768]{0:T(1024)} %get-tuple-element.78) | copy-start | bytes 9220
  290.1 44.0 %copy-start.16 = (f32[768]{0:T(1024)S(1)}, f32[768]{0:T(1024)}, u32[]{:S(2)}) copy-start(f32[768]{0:T(1024)} %get-tuple-element.79) | copy-start | bytes 9220
  290.1 44.0 %copy-start.17 = (f32[768]{0:T(1024)S(1)}, f32[768]{0:T(1024)}, u32[]{:S(2)}) copy-start(f32[768]{0:T(1024)} %get-tuple-element.80) | copy-start | bytes 9220
  290.1 44.0 %copy-start.18 = (f32[768]{0:T(1024)S(1)}, f32[768]{0:T(1024)}, u32[]{:S(2)}) copy-start(f32[768]{0:T(1024)} %get-tuple-element.81) | copy-start | bytes 9220
  290.1 44.0 %copy-start.19 = (f32[768]{0:T(1024)S(1)}, f32[768]{0:T(1024)}, u32[]{:S(2)}) copy-start(f32[768]{0:T(1024)} %get-tuple-element.82) | copy-start | bytes 9220
  290.1 44.0 %copy-start.20 = (f32[768]{0:T(1024)S(1)}, f32[768]{0:T(1024)}, u32[]{:S(2)}) copy-start(f32[768]{0:T(1024)} %get-tuple-element.83) | copy-start | bytes 9220
  290.1 44.0 %copy-start.21 = (f32[768]{0:T(1024)S(1)}, f32[768]{0:T(1024)}, u32[]{:S(2)}) copy-start(f32[768]{0:T(1024)} %get-tuple-element.84) | copy-start | bytes 9220
  290.1 44.0 %copy-start.22 = (f32[768]{0:T(1024)S(1)}, f32[768]{0:T(1024)}, u32[]{:S(2)}) copy-start(f32[768]{0:T(1024)} %get-tuple-element.85) | copy-start | bytes 9220
  290.2 44.0 %copy-start.23 = (f32[768]{0:T(1024)S(1)}, f32[768]{0:T(1024)}, u32[]{:S(2)}) copy-start(f32[768]{0:T(1024)} %get-tuple-element.86) | copy-start | bytes 9220
  290.2 44.0 %copy-start.24 = (f32[768]{0:T(1024)S(1)}, f32[768]{0:T(1024)}, u32[]{:S(2)}) copy-start(f32[768]{0:T(1024)} %get-tuple-element.87) | copy-start | bytes 9220
  290.2 44.0 %copy-start.25 = (f32[768]{0:T(1024)S(1)}, f32[768]{0:T(1024)}, u32[]{:S(2)}) copy-start(f32[768]{0:T(1024)} %get-tuple-element.88) | copy-start | bytes 9220
  290.2 44.0 %copy-start.26 = (f32[768]{0:T(1024)S(1)}, f32[768]{0:T(1024)}, u32[]{:S(2)}) copy-start(f32[768]{0:T(1024)} %get-tuple-element.89) | copy-start | bytes 9220
  290.2 44.0 %copy-start.27 = (f32[768]{0:T(1024)S(1)}, f32[768]{0:T(1024)}, u32[]{:S(2)}) copy-start(f32[768]{0:T(1024)} %get-tuple-element.90) | copy-start | bytes 9220
  290.2 44.0 %copy-start.28 = (f32[768]{0:T(1024)S(1)}, f32[768]{0:T(1024)}, u32[]{:S(2)}) copy-start(f32[768]{0:T(1024)} %get-tuple-element.91) | copy-start | bytes 9220
  290.2 44.0 %copy-start.29 = (f32[768]{0:T(1024)S(1)}, f32[768]{0:T(1024)}, u32[]{:S(2)}) copy-start(f32[768]{0:T(1024)} %get-tuple-element.92) | copy-start | bytes 9220
  290.2 44.0 %copy-start.30 = (f32[768]{0:T(1024)S(1)}, f32[768]{0:T(1024)}, u32[]{:S(2)}) copy-start(f32[768]{0:T(1024)} %get-tuple-element.93) | copy-start | bytes 9220
  290.2 44.0 %copy-start.31 = (f32[768]{0:T(1024)S(1)}, f32[768]{0:T(1024)}, u32[]{:S(2)}) copy-start(f32[768]{0:T(1024)} %get-tuple-element.94) | copy-start | bytes 9220
  290.2 44.0 %copy-start.32 = (f32[768]{0:T(1024)S(1)}, f32[768]{0:T(1024)}, u32[]{:S(2)}) copy-start(f32[768]{0:T(1024)} %get-tuple-element.95) | copy-start | bytes 9220
  290.3 44.0 %copy-start.33 = (f32[768]{0:T(1024)S(1)}, f32[768]{0:T(1024)}, u32[]{:S(2)}) copy-start(f32[768]{0:T(1024)} %get-tuple-element.96) | copy-start | bytes 9220
  290.3 44.0 %copy-start.34 = (f32[768]{0:T(1024)S(1)}, f32[768]{0:T(1024)}, u32[]{:S(2)}) copy-start(f32[768]{0:T(1024)} %get-tuple-element.97) | copy-start | bytes 9220
  290.3 44.0 %copy-start.35 = (f32[768]{0:T(1024)S(1)}, f32[768]{0:T(1024)}, u32[]{:S(2)}) copy-start(f32[768]{0:T(1024)} %get-tuple-element.98) | copy-start | bytes 9220
  290.3 44.0 %copy-start.36 = (f32[768]{0:T(1024)S(1)}, f32[768]{0:T(1024)}, u32[]{:S(2)}) copy-start(f32[768]{0:T(1024)} %get-tuple-element.99) | copy-start | bytes 9220
  290.3 44.0 %copy-start.37 = (f32[768]{0:T(1024)S(1)}, f32[768]{0:T(1024)}, u32[]{:S(2)}) copy-start(f32[768]{0:T(1024)} %get-tuple-element.100) | copy-start | bytes 9220
  290.3 44.0 %copy-start.38 = (f32[768]{0:T(1024)S(1)}, f32[768]{0:T(1024)}, u32[]{:S(2)}) copy-start(f32[768]{0:T(1024)} %get-tuple-element.101) | copy-start | bytes 9220
  290.3 44.0 %copy-start.39 = (f32[768]{0:T(1024)S(1)}, f32[768]{0:T(1024)}, u32[]{:S(2)}) copy-start(f32[768]{0:T(1024)} %get-tuple-element.102) | copy-start | bytes 9220
  290.3 44.0 %copy-start.40 = (f32[768]{0:T(1024)S(1)}, f32[768]{0:T(1024)}, u32[]{:S(2)}) copy-start(f32[768]{0:T(1024)} %get-tuple-element.103) | copy-start | bytes 9220
  290.3 44.0 %copy-start.41 = (f32[768]{0:T(1024)S(1)}, f32[768]{0:T(1024)}, u32[]{:S(2)}) copy-start(f32[768]{0:T(1024)} %get-tuple-element.104) | copy-start | bytes 9220
  290.3 44.0 %copy-start.42 = (f32[768]{0:T(1024)S(1)}, f32[768]{0:T(1024)}, u32[]{:S(2)}) copy-start(f32[768]{0:T(1024)} %get-tuple-element.105) | copy-start | bytes 9220
  290.4 44.0 %copy-start.43 = (f32[768]{0:T(1024)S(1)}, f32[768]{0:T(1024)}, u32[]{:S(2)}) copy-start(f32[768]{0:T(1024)} %get-tuple-element.106) | copy-start | bytes 9220
  290.4 44.0 %copy-start.44 = (f32[768]{0:T(1024)S(1)}, f32[768]{0:T(1024)}, u32[]{:S(2)}) copy-start(f32[768]{0:T(1024)} %get-tuple-element.107) | copy-start | bytes 9220
  (62 other events, 409.7 us)
Sparse Core Ops, SparseCore 0:
  10.2 56.1 all-gather.3
  68.5 53.3 all-gather.5
  193.7 95.1 reduce-scatter.1
  291.0 43.0 all-reduce.1
  335.6 12.3 all-gather.7

commit v10 on v9

--- a/solution.py
+++ b/solution.py
@@ -148,8 +148,14 @@
     halves = kept + lax.ppermute(sent, "core", [(0, 1), (1, 0)])
     halves = halves.reshape(-1, channels)
     mine = lax.psum_scatter(halves, "col", scatter_dimension=0, tiled=True)
-    mine = lax.psum(mine, "z")
-    pair = lax.all_gather(mine, "core", axis=0, tiled=False)
+    depth = lax.axis_size("z")
+    total = mine
+    for step in range(1, depth):
+        total = total + lax.ppermute(
+            mine, "z", [(i, (i + step) % depth) for i in range(depth)]
+        )
+    other = lax.ppermute(total, "core", [(0, 1), (1, 0)])
+    pair = jnp.where(first_core, jnp.stack([total, other]), jnp.stack([other, total]))
     summed_in = pair[0].reshape(-1, hidden_units)
     summed_out = pair[1]
     small = jnp.concatenate([bias_part, gain_part, scale_part]).reshape(group_count, -1)

time: 362 us -> 346 us (0.956)
  waiting for transfers between devices: 149 us -> 130 us
  starting transfers between devices: 38 us -> 42.9 us
    psum x1 -> x0, waiting for transfers between devices: 40.2 us -> none  [local(): mine = lax.psum(mine, 'z')]
    ppermute x0 -> x4, waiting for transfers between devices: none -> 22.1 us  [the longest x3 22.1 us: local(): lax.ppermute(mine, 'z', [(i, (i + step) % depth) for i in range(depth)])]
    ppermute x0 -> x4, starting transfers between devices: none -> 4.66 us  [the longest x3 4.57 us: local(): lax.ppermute(mine, 'z', [(i, (i + step) % depth) for i in range(depth)])]
  transfers between devices with their start and end apart: 16 -> 18, of which waited for: 9 -> 10; matrix products, arithmetic and copies ran while one was open for 27% -> 28% of each run, Pallas kernels for 0% -> 0%
where the time goes in v10:
time: 346 us; the launch traced here: 343 us
  waiting for transfers between devices  130 us (38%)
  other arithmetic  66.6 us (19%)
  local copies, waits for them, and re-layouts  45 us (13%)
  matrix products  43.2 us (12%)
  starting transfers between devices  42.9 us (12%)
  between operations  15.6 us (5%)
    all_gather x1, waiting for transfers between devices, local(): lax.all_gather(w_out, 'col', axis=0, tiled=True)  48.5 us
    ppermute x3, waiting for transfers between devices, local(): lax.ppermute(mine, 'z', [(i, (i + step) % depth) for i in range(depth)])  22.1 us
    all_gather x1, waiting for transfers between devices, local(): lax.all_gather(w_in, 'col', axis=0, tiled=True)  18.1 us
    reduce_sum x3, other arithmetic, tile_taps(): columns.append(jnp.sum(gradient * window, axis=(0, 1)))  15.6 us
    convert_element_type x1, other arithmetic, local(): (cotangent.astype(jnp.float32) + grad_back.astype(jnp.float32)).astype(jn...  14.7 us
    ppermute x1, waiting for transfers between devices, local(): halves = kept + lax.ppermute(sent, 'core', [(0, 1), (1, 0)])  14.6 us
    reduce_sum x1, other arithmetic, local(): average = jnp.mean(conv_rows, axis=1, keepdims=True)  12.9 us
    all_to_all x1, starting transfers between devices, local(): lax.all_to_all(outgoing, EVERY, split_axis=0, concat_axis=0, tiled=True)  12 us
  transfers between devices with their start and end apart: 18, of which 10 were waited for; matrix products, arithmetic and copies ran while one was open for 28% of the time, Pallas kernels for 0%

profile of v10, /device:TPU:0, one launch (start us, length us, event | category | flops | bytes accessed | tf_op | source)
XLA Modules:
  0.0 343.2 jit_solution(17861997575289620793)
XLA Ops:
  9.8 1.3 collective-permute-start.1
  11.1 4.6 %collective-permute-start = (bf16[16,6,768]{2,1,0:T(8,128)(2,1)S(1)}, bf16[16,6,768]{2,1,0:T(8,128)(2,1)S(1)}, u32[]{:S(2)}, u32[]{:S(2)}) collective-permute-start(bf16[16,6,768]{2,1,0:T(8,128)(2,1)S(1)} %get-tuple-element.186), channel_id=1, source_target_pairs={{0,1},{1,2},{2,3},{3,4},{4,5},{5,6},{6,7},{7,8},{8,9},{9,10},{10,1... | collective-permute-start | bytes 442376 | tf_op jit(solution)/shard_map/ppermute | solution.py:43
  15.7 1.4 slice_reduce_fusion.97
  17.1 2.0 slice_reduce_fusion.96
  20.7 1.3 collective-permute-start.2
  22.0 1.3 collective-permute-start.3
  23.3 1.8 slice_reduce_fusion.95
  28.3 2.8 maximum_maximum_fusion
  31.4 12.9 %convert_reduce_fusion = (f32[16,32]{1,0:T(8,128)S(1)}, bf16[16,32,768]{2,1,0:T(8,128)(2,1)}) fusion(bf16[22,44,768]{2,1,0:T(8,128)(2,1)S(1)} %get-tuple-element.180, f32[768]{0:T(1024)S(1)} %copy-done.86, f32[768]{0:T(1024)S(1)} %get-tuple-element.120, f32[768]{0:T(1024)S(1)} %get-tuple-element.121, f32[768]{0:T(1024)S(1)} %get-tuple-element.122, ...), kind=kLoop, calls=%fused_computation.273 | loop fusion | flops 62127616 | bytes 37262336 | tf_op jit(solution)/shard_map/reduce_sum | solution.py:96
  44.4 1.5 multiply_reduce_fusion.2
  45.9 2.3 multiply_convert_fusion.3
  48.3 18.1 %all-gather.3.cloned.1.call-done = bf16[768,3072]{1,0:T(8,128)(2,1)} async-done(((bf16[48,3072]{1,0:T(8,128)(2,1)}), bf16[768,3072]{1,0:T(8,128)(2,1)}) %all-gather.3.cloned.1.call-update) | async-done | bytes 4718608 | tf_op jit(solution)/shard_map/all_gather | solution.py:87
  66.4 7.1 %fusion.8 = (bf16[3072,512]{0,1:T(8,128)(2,1)}, f32[512,3072]{1,0:T(8,128)}) fusion(f32[3072]{0:T(1024)S(1)} %copy-done.90, bf16[512,768]{1,0:T(8,128)(2,1)} %multiply_convert_fusion.3, bf16[768,3072]{1,0:T(8,128)(2,1)} %all-gather.3.cloned.1.call-done), kind=kOutput, calls=%fused_computation.64 | convolution fusion | flops 2425356288 | bytes 14954496 | tf_op jit(solution)/shard_map/dot_general | solution.py:101
  73.5 48.5 %all-gather.5.cloned.1.call-done = bf16[3072,768]{1,0:T(8,128)(2,1)} async-done(((bf16[192,768]{1,0:T(8,128)(2,1)}), bf16[3072,768]{1,0:T(8,128)(2,1)}) %all-gather.5.cloned.1.call-update) | async-done | bytes 4718608 | tf_op jit(solution)/shard_map/all_gather | solution.py:88
  122.0 8.0 %fusion.136 = (f32[768]{0:T(1024)S(1)}, bf16[512,768]{1,0:T(8,128)(2,1)}, bf16[512,768]{1,0:T(8,128)(2,1)S(1)}) fusion(bf16[16,32,768]{2,1,0:T(8,128)(2,1)} %param.15, f32[768]{0:T(1024)S(1)} %copy-done.88, bf16[16,32,768]{2,1,0:T(8,128)(2,1)} %param.8, bf16[3072,768]{1,0:T(8,128)(2,1)} %all-gather.5.cloned.1.call-done, ...), kind=kOutput, calls=%fused_computation.249 | convolution fusion | flops 2428894464 | bytes 14174208 | tf_op jit(solution)/shard_map/dot_general | solution.py:103
  130.0 4.7 %fusion.155 = (f32[3072]{0:T(1024)S(1)}, bf16[512,3072]{1,0:T(8,128)(2,1)S(1)}) fusion(f32[512,3072]{1,0:T(8,128)S(1)} %copy-done.91, f32[3072]{0:T(1024)S(1)} %copy-done.90, bf16[512,768]{1,0:T(8,128)(2,1)S(1)} %get-tuple-element.183, bf16[3072,768]{1,0:T(8,128)(2,1)S(1)} %copy-done.89), kind=kOutput, calls=%fused_computation.411 | convolution fusion | flops 2434790400 | bytes 14966784 | tf_op jit(solution)/shard_map/dot_general | solution.py:111
  134.6 1.6 copy-done.9
  136.3 5.1 %fusion.139 = f32[768,3072]{1,0:T(8,128)} fusion(bf16[512,768]{1,0:T(8,128)(2,1)S(1)} %copy-done.8, bf16[512,3072]{1,0:T(8,128)(2,1)S(1)} %get-tuple-element.192), kind=kOutput, calls=%fused_computation.257 | convolution fusion | flops 2415919104 | bytes 13369344 | tf_op jit(solution)/shard_map/dot_general | solution.py:139
  141.4 11.6 %reshape.223 = f32[16,192,768]{2,1,0:T(8,128)} reshape(f32[768,3072]{1,0:T(8,128)} %fusion.139) | data formatting | bytes 18874368 | tf_op jit(solution)/shard_map/reshape | solution.py:141
  153.0 4.7 %copy.21 = bf16[3072,512]{1,0:T(8,128)(2,1)} copy(bf16[3072,512]{0,1:T(8,128)(2,1)} %get-tuple-element.193) | data formatting | bytes 6291456 | tf_op jit(solution)/shard_map/convert_element_type | solution.py:102
  157.7 11.4 %broadcast_select_fusion = (f32[16,192,768]{2,1,0:T(8,128)}, f32[16,192,768]{2,1,0:T(8,128)}) fusion(f32[16,192,768]{2,1,0:T(8,128)} %reshape.223, pred[]{:T(512)S(6)} %eq.3, bf16[16,192,512]{2,1,0:T(8,128)(2,1)} %bitcast.121, bf16[512,768,1]{1,0,2:T(8,128)(2,1)} %bitcast.122), kind=kOutput, calls=%fused_computation.65 | convolution fusion | flops 2418278400 | bytes 32243712 | tf_op jit(solution)/shard_map/dot_general | solution.py:142
  169.1 2.5 collective-permute-start.8
  171.5 14.6 %collective-permute-done.8 = f32[16,192,768]{2,1,0:T(8,128)} collective-permute-done((f32[16,192,768]{2,1,0:T(8,128)}, f32[16,192,768]{2,1,0:T(8,128)}, u32[]{:S(2)}, u32[]{:S(2)}) %collective-permute-start.8) | collective-permute-done | bytes 9437216 | tf_op jit(solution)/shard_map/ppermute | solution.py:148
  186.2 7.3 %select_add_fusion = f32[16,192,768]{2,1,0:T(8,128)} fusion(f32[16,192,768]{2,1,0:T(8,128)} %collective-permute-done.8, f32[16,192,768]{2,1,0:T(8,128)S(1)} %bitcast.115, f32[16,192,768]{2,1,0:T(8,128)} %get-tuple-element.196, pred[]{:T(512)S(6)} %eq.3), kind=kLoop, calls=%fused_computation.51 | loop fusion | flops 4718592 | bytes 37748736 | tf_op jit(solution)/shard_map/add | solution.py:148
  193.5 1.6 reshape.218
  195.1 3.5 %rev.3 = f32[768,7,7]{0,2,1:T(8,128)} reverse(f32[768,7,7]{0,2,1:T(8,128)} %reshape.218), dimensions={1,2} | reverse | bytes 301056 | tf_op jit(solution)/shard_map/rev | solution.py:90
  198.7 1.6 reshape.219
  200.3 2.1 slice_reduce_fusion.48
  202.4 2.1 slice_reduce_fusion.47
  204.5 6.9 %multiply_reduce_fusion = (f32[768]{0:T(1024)S(1)}, f32[512]{0:T(512)S(1)}, f32[512]{0:T(512)S(1)}, f32[512,768]{1,0:T(8,128)S(1)}) fusion(bf16[16,32,768]{2,1,0:T(8,128)(2,1)} %get-tuple-element.170, f32[512]{0:T(512)S(1)} %rsqrt.12, f32[512]{0:T(512)S(1)} %div.15, f32[768]{0:T(1024)S(1)} %copy-done.46, ...), kind=kOutput, calls=%fused_computation.254 | convolution fusion | flops 2419456256 | bytes 10237952 | tf_op jit(solution)/shard_map/dot_general | solution.py:117
  211.4 5.7 %fusion.132 = (f32[768]{0:T(1024)}, f32[768]{0:T(1024)}, f32[768]{0:T(1024)}, f32[768]{0:T(1024)}, f32[768]{0:T(1024)}, /*index=5*/f32[768]{0:T(1024)}, f32[768]...) fusion(bf16[22,44,768]{2,1,0:T(8,128)(2,1)S(1)} %get-tuple-elem, ...), kind=kLoop, calls=%fused_computation.241 | loop fusion | flops 25152000 | bytes 17368064 | tf_op jit(solution)/shard_map/reduce_sum | solution.py:73
  218.7 1.3 collective-permute-start.5
  220.0 5.2 %collective-permute-start.4 = (bf16[16,6,768]{2,1,0:T(8,128)(2,1)}, bf16[16,6,768]{2,1,0:T(8,128)(2,1)}, u32[]{:S(2)}, u32[]{:S(2)}) collective-permute-start(bf16[16,6,768]{2,1,0:T(8,128)(2,1)} %get-tuple-element.184), channel_id=1, source_target_pairs={{0,1},{1,2},{2,3},{3,4},{4,5},{5,6},{6,7},{7,8},{8,9},{9,10},{10,1... | collective-permute-start | bytes 442376 | tf_op jit(solution)/shard_map/ppermute | solution.py:43
  225.4 5.9 %fusion.114 = (f32[768]{0:T(1024)S(1)}, f32[768]{0:T(1024)S(1)}, f32[768]{0:T(1024)S(1)}, f32[768]{0:T(1024)S(1)}, f32[768]{0:T(1024)S(1)}, /*index=5*/f32[768]{...) fusion(bf16[22,44,768]{2,1,0:T(8,128)(2,1)S(1)} %get-tuple-elem, ...), kind=kLoop, calls=%fused_computation.223 | loop fusion | flops 19257600 | bytes 8838144 | tf_op jit(solution)/shard_map/reduce_sum | solution.py:73
  231.6 4.0 %fusion.104 = (f32[768]{0:T(1024)S(1)}, f32[768]{0:T(1024)S(1)}, f32[768]{0:T(1024)S(1)}, f32[768]{0:T(1024)S(1)}, f32[768]{0:T(1024)S(1)}, /*index=5*/f32[768]{...) fusion(bf16[22,44,768]{2,1,0:T(8,128)(2,1)S(1)} %get-tuple-elem, ...), kind=kLoop, calls=%fused_computation.213 | loop fusion | flops 21613056 | bytes 14997504 | tf_op jit(solution)/shard_map/reduce_sum | solution.py:73
  238.0 12.0 %all-to-all-start = ((f32[128,1,330]{2,1,0:T(1,128)}), f32[128,1,330]{2,1,0:T(1,128)S(1)}, u32[]{:S(2)}, u32[]{:S(2)}) async-start(f32[128,1,330]{2,1,0:T(1,128)} %copy.20), calls=%async_computation | async-start | bytes 393216 | tf_op jit(solution)/shard_map/all_to_all | solution.py:168
  251.2 1.3 pad_maximum_fusion.7
  252.5 1.4 collective-permute-start.6
  253.8 1.3 collective-permute-start.7
  255.1 6.6 %all-to-all-done = f32[128,1,330]{2,1,0:T(1,128)S(1)} async-done(((f32[128,1,330]{2,1,0:T(1,128)}), f32[128,1,330]{2,1,0:T(1,128)S(1)}, u32[]{:S(2)}, u32[]{:S(2)}) %all-to-all-start) | async-done | bytes 168992 | tf_op jit(solution)/shard_map/all_to_all | solution.py:168
  262.7 6.0 %all-to-all-start.1 = ((f32[128,1,36]{2,1,0:T(1,128)}), f32[128,1,36]{2,1,0:T(1,128)S(1)}, u32[]{:S(2)}, u32[]{:S(2)}) async-start(f32[128,1,36]{2,1,0:T(1,128)} %broadcast_in_dim.2), calls=%async_computation.2 | async-start | bytes 131072 | tf_op jit(solution)/shard_map/all_to_all | solution.py:172
  269.4 8.8 %all-to-all-done.1 = f32[128,1,36]{2,1,0:T(1,128)S(1)} async-done(((f32[128,1,36]{2,1,0:T(1,128)}), f32[128,1,36]{2,1,0:T(1,128)S(1)}, u32[]{:S(2)}, u32[]{:S(2)}) %all-to-all-start.1) | async-done | bytes 18464 | tf_op jit(solution)/shard_map/all_to_all | solution.py:172
  279.6 9.2 %reduce-scatter.2.cloned.1.call-done = f32[192,768]{1,0:T(8,128)} async-done(((f32[3072,768]{1,0:T(8,128)}), f32[192,768]{1,0:T(8,128)}) %reduce-scatter.2.cloned.1.call-update) | async-done | bytes 589840 | tf_op jit(solution)/shard_map/reduce_scatter | solution.py:150
  288.8 2.9 collective-permute-start.11
  294.6 2.4 maximum_maximum_fusion.1
  297.3 18.5 %collective-permute-done.11 = f32[192,768]{1,0:T(8,128)S(1)} collective-permute-done((f32[192,768]{1,0:T(8,128)}, f32[192,768]{1,0:T(8,128)S(1)}, u32[]{:S(2)}, u32[]{:S(2)}) %collective-permute-start.11) | collective-permute-done | bytes 589856 | tf_op jit(solution)/shard_map/ppermute | solution.py:154
  315.8 3.6 %collective-permute-done.9 = f32[192,768]{1,0:T(8,128)S(1)} collective-permute-done((f32[192,768]{1,0:T(8,128)}, f32[192,768]{1,0:T(8,128)S(1)}, u32[]{:S(2)}, u32[]{:S(2)}) %collective-permute-start.9) | collective-permute-done | bytes 589856 | tf_op jit(solution)/shard_map/ppermute | solution.py:154
  320.0 14.7 %fusion.133 = bf16[16,32,768]{2,1,0:T(8,128)(2,1)} fusion(bf16[16,32,768]{2,1,0:T(8,128)(2,1)S(1)} %copy-done.11, bf16[22,44,768]{2,1,0:T(8,128)(2,1)S(1)} %get-tuple-element.176, f32[768]{0:T(1024)S(1)} %get-tuple-element.71, f32[768]{0:T(1024)S(1)} %get-tuple-element.72, f32[768]{0:T(1024)S(1)} %get-tuple-element.73, f32[768]{0:T(1024)S(1)} %get-tuple-element.74, ...), kind=kLoop, calls=%fused_computation.246 | loop fusion | flops 66453504 | bytes 35834880 | tf_op jit(solution)/shard_map/convert_element_type | solution.py:134
  (291 shorter events, 20.5 us)
Async XLA Ops:
  7.2 59.2 %all-gather.3.cloned.1.call-start = ((), (), s32[]{:S(2)}) async-start(), calls=%async_computation.3 | async-start | bytes 5013504 | tf_op jit(solution)/shard_map/all_gather | solution.py:87
  7.9 114.0 %all-gather.5.cloned.1.call-start = ((), (), s32[]{:S(2)}) async-start(), calls=%async_computation.4 | async-start | bytes 5013504 | tf_op jit(solution)/shard_map/all_gather | solution.py:88
  8.7 280.1 %reduce-scatter.2.cloned.1.call-start = ((), (), s32[]{:S(2)}) async-start(), calls=%async_computation.5 | async-start | bytes 10027008 | tf_op jit(solution)/shard_map/reduce_scatter | solution.py:150
  9.8 9.4 %collective-permute-start.1 = (bf16[16,6,768]{2,1,0:T(8,128)(2,1)S(1)}, bf16[16,6,768]{2,1,0:T(8,128)(2,1)S(1)}, u32[]{:S(2)}, u32[]{:S(2)}) collective-permute-start(bf16[16,6,768]{2,1,0:T(8,128)(2,1)S(1)} %get-tuple-element.187), channel_id=1, source_target_pairs={{1,0},{2,1},{3,2},{4,3},{5,4},{6,5},{7,6},{8,7},{9,8},{10,9},{11,1... | collective-permute-start | bytes 442376 | tf_op jit(solution)/shard_map/ppermute | solution.py:44
  11.1 8.4 %collective-permute-start = (bf16[16,6,768]{2,1,0:T(8,128)(2,1)S(1)}, bf16[16,6,768]{2,1,0:T(8,128)(2,1)S(1)}, u32[]{:S(2)}, u32[]{:S(2)}) collective-permute-start(bf16[16,6,768]{2,1,0:T(8,128)(2,1)S(1)} %get-tuple-element.186), channel_id=1, source_target_pairs={{0,1},{1,2},{2,3},{3,4},{4,5},{5,6},{6,7},{7,8},{8,9},{9,10},{10,1... | collective-permute-start | bytes 442376 | tf_op jit(solution)/shard_map/ppermute | solution.py:43
  20.7 5.7 %collective-permute-start.2 = (bf16[6,44,768]{2,1,0:T(8,128)(2,1)}, bf16[6,44,768]{2,1,0:T(8,128)(2,1)S(1)}, u32[]{:S(2)}, u32[]{:S(2)}) collective-permute-start(bf16[6,44,768]{2,1,0:T(8,128)(2,1)} %get-tuple-element.181), channel_id=1, source_target_pairs={{0,16},{16,32},{32,48},{48,64},{64,80},{80,96},{96,112},{1,17},{17... | collective-permute-start | bytes 1216520 | tf_op jit(solution)/shard_map/ppermute | solution.py:46
  22.0 6.3 %collective-permute-start.3 = (bf16[6,44,768]{2,1,0:T(8,128)(2,1)}, bf16[6,44,768]{2,1,0:T(8,128)(2,1)}, u32[]{:S(2)}, u32[]{:S(2)}) collective-permute-start(bf16[6,44,768]{2,1,0:T(8,128)(2,1)} %get-tuple-element.182), channel_id=1, source_target_pairs={{16,0},{32,16},{48,32},{64,48},{80,64},{96,80},{112,96},{17,1},{33... | collective-permute-start | bytes 1216520 | tf_op jit(solution)/shard_map/ppermute | solution.py:47
  48.3 73.7 %copy-start.88 = (f32[768]{0:T(1024)S(1)}, f32[768]{0:T(1024)}, u32[]{:S(2)}) copy-start(f32[768]{0:T(1024)} %param.14) | copy-start | bytes 9220
  157.6 28.5 %slice-start = ((s8[9437184]{0:T(1024)(128)(4,1)}), s8[4194304]{0:T(1024)(128)(4,1)S(1)}, s32[]{:S(2)}) async-start(s8[9437184]{0:T(1024)(128)(4,1)} %bitcast.114), calls=%async_computation.6 | async-start | bytes 8388608
  157.6 28.5 %slice-start.1 = ((s8[9437184]{0:T(1024)(128)(4,1)}), s8[4194304]{0:T(1024)(128)(4,1)S(1)}, s32[]{:S(2)}) async-start(s8[9437184]{0:T(1024)(128)(4,1)} %bitcast.114), calls=%async_computation.7 | async-start | bytes 8388608
  157.6 28.5 %slice-start.2 = ((s8[9437184]{0:T(1024)(128)(4,1)}), s8[1048576]{0:T(1024)(128)(4,1)S(1)}, s32[]{:S(2)}) async-start(s8[9437184]{0:T(1024)(128)(4,1)} %bitcast.114), calls=%async_computation.8 | async-start | bytes 2097152
  169.1 17.1 %collective-permute-start.8 = (f32[16,192,768]{2,1,0:T(8,128)}, f32[16,192,768]{2,1,0:T(8,128)}, u32[]{:S(2)}, u32[]{:S(2)}) collective-permute-start(f32[16,192,768]{2,1,0:T(8,128)} %get-tuple-element.195), channel_id=1, source_target_pairs={{0,16},{16,0},{1,17},{17,1},{2,18},{18,2},{3,19},{19,3},{4,20},{20... | collective-permute-start | bytes 28311560 | tf_op jit(solution)/shard_map/ppermute | solution.py:148
  218.7 32.4 %collective-permute-start.5 = (bf16[16,6,768]{2,1,0:T(8,128)(2,1)}, bf16[16,6,768]{2,1,0:T(8,128)(2,1)}, u32[]{:S(2)}, u32[]{:S(2)}) collective-permute-start(bf16[16,6,768]{2,1,0:T(8,128)(2,1)} %get-tuple-element.185), channel_id=1, source_target_pairs={{1,0},{2,1},{3,2},{4,3},{5,4},{6,5},{7,6},{8,7},{9,8},{10,9},{11,1... | collective-permute-start | bytes 442376 | tf_op jit(solution)/shard_map/ppermute | solution.py:44
  220.0 31.1 %collective-permute-start.4 = (bf16[16,6,768]{2,1,0:T(8,128)(2,1)}, bf16[16,6,768]{2,1,0:T(8,128)(2,1)}, u32[]{:S(2)}, u32[]{:S(2)}) collective-permute-start(bf16[16,6,768]{2,1,0:T(8,128)(2,1)} %get-tuple-element.184), channel_id=1, source_target_pairs={{0,1},{1,2},{2,3},{3,4},{4,5},{5,6},{6,7},{7,8},{8,9},{9,10},{10,1... | collective-permute-start | bytes 442376 | tf_op jit(solution)/shard_map/ppermute | solution.py:43
  238.0 23.8 %all-to-all-start = ((f32[128,1,330]{2,1,0:T(1,128)}), f32[128,1,330]{2,1,0:T(1,128)S(1)}, u32[]{:S(2)}, u32[]{:S(2)}) async-start(f32[128,1,330]{2,1,0:T(1,128)} %copy.20), calls=%async_computation | async-start | bytes 393216 | tf_op jit(solution)/shard_map/all_to_all | solution.py:168
  252.5 42.1 %collective-permute-start.6 = (bf16[6,44,768]{2,1,0:T(8,128)(2,1)S(1)}, bf16[6,44,768]{2,1,0:T(8,128)(2,1)S(1)}, u32[]{:S(2)}, u32[]{:S(2)}) collective-permute-start(bf16[6,44,768]{2,1,0:T(8,128)(2,1)S(1)} %get-tuple-element.177), channel_id=1, source_target_pairs={{0,16},{16,32},{32,48},{48,64},{64,80},{80,96},{96,112},{1,17},{17... | collective-permute-start | bytes 1216520 | tf_op jit(solution)/shard_map/ppermute | solution.py:46
  253.8 40.7 %collective-permute-start.7 = (bf16[6,44,768]{2,1,0:T(8,128)(2,1)S(1)}, bf16[6,44,768]{2,1,0:T(8,128)(2,1)S(1)}, u32[]{:S(2)}, u32[]{:S(2)}) collective-permute-start(bf16[6,44,768]{2,1,0:T(8,128)(2,1)S(1)} %get-tuple-element.178), channel_id=1, source_target_pairs={{16,0},{32,16},{48,32},{64,48},{80,64},{96,80},{112,96},{17,1},{33... | collective-permute-start | bytes 1216520 | tf_op jit(solution)/shard_map/ppermute | solution.py:47
  262.7 15.5 %all-to-all-start.1 = ((f32[128,1,36]{2,1,0:T(1,128)}), f32[128,1,36]{2,1,0:T(1,128)S(1)}, u32[]{:S(2)}, u32[]{:S(2)}) async-start(f32[128,1,36]{2,1,0:T(1,128)} %broadcast_in_dim.2), calls=%async_computation.2 | async-start | bytes 131072 | tf_op jit(solution)/shard_map/all_to_all | solution.py:172
  288.8 27.0 %collective-permute-start.11 = (f32[192,768]{1,0:T(8,128)}, f32[192,768]{1,0:T(8,128)S(1)}, u32[]{:S(2)}, u32[]{:S(2)}) collective-permute-start(f32[192,768]{1,0:T(8,128)} %reduce-scatter.2.cloned.1.call-done), channel_id=1, source_target_pairs={{0,96},{32,0},{64,32},{96,64},{1,97},{33,1},{65,33},{97,65},{2,98}... | collective-permute-start | bytes 1769480 | tf_op jit(solution)/shard_map/ppermute | solution.py:154
  291.7 24.1 %collective-permute-start.10 = (f32[192,768]{1,0:T(8,128)}, f32[192,768]{1,0:T(8,128)S(1)}, u32[]{:S(2)}, u32[]{:S(2)}) collective-permute-start(f32[192,768]{1,0:T(8,128)} %reduce-scatter.2.cloned.1.call-done), channel_id=1, source_target_pairs={{0,64},{32,96},{64,0},{96,32},{1,65},{33,97},{65,1},{97,33},{2,66}... | collective-permute-start | bytes 1769480 | tf_op jit(solution)/shard_map/ppermute | solution.py:154
  292.4 27.0 %collective-permute-start.9 = (f32[192,768]{1,0:T(8,128)}, f32[192,768]{1,0:T(8,128)S(1)}, u32[]{:S(2)}, u32[]{:S(2)}) collective-permute-start(f32[192,768]{1,0:T(8,128)} %reduce-scatter.2.cloned.1.call-done), channel_id=1, source_target_pairs={{0,32},{32,64},{64,96},{96,0},{1,33},{33,65},{65,97},{97,1},{2,34}... | collective-permute-start | bytes 1769480 | tf_op jit(solution)/shard_map/ppermute | solution.py:154
  294.6 24.8 %copy-start.13 = (f32[192,768]{1,0:T(8,128)S(1)}, f32[192,768]{1,0:T(8,128)}, u32[]{:S(2)}) copy-start(f32[192,768]{1,0:T(8,128)} %reduce-scatter.2.cloned.1.call-done) | copy-start | bytes 1769476
  297.0 22.6 %copy-start.11 = (bf16[16,32,768]{2,1,0:T(8,128)(2,1)S(1)}, bf16[16,32,768]{2,1,0:T(8,128)(2,1)}, u32[]{:S(2)}) copy-start(bf16[16,32,768]{2,1,0:T(8,128)(2,1)} %param.15) | copy-start | bytes 2359300
  297.0 22.6 %copy-start.15 = (f32[768]{0:T(1024)S(1)}, f32[768]{0:T(1024)}, u32[]{:S(2)}) copy-start(f32[768]{0:T(1024)} %get-tuple-element.77) | copy-start | bytes 9220
  297.0 22.6 %copy-start.16 = (f32[768]{0:T(1024)S(1)}, f32[768]{0:T(1024)}, u32[]{:S(2)}) copy-start(f32[768]{0:T(1024)} %get-tuple-element.78) | copy-start | bytes 9220
  297.0 22.6 %copy-start.17 = (f32[768]{0:T(1024)S(1)}, f32[768]{0:T(1024)}, u32[]{:S(2)}) copy-start(f32[768]{0:T(1024)} %get-tuple-element.79) | copy-start | bytes 9220
  297.0 22.6 %copy-start.18 = (f32[768]{0:T(1024)S(1)}, f32[768]{0:T(1024)}, u32[]{:S(2)}) copy-start(f32[768]{0:T(1024)} %get-tuple-element.80) | copy-start | bytes 9220
  297.0 22.6 %copy-start.19 = (f32[768]{0:T(1024)S(1)}, f32[768]{0:T(1024)}, u32[]{:S(2)}) copy-start(f32[768]{0:T(1024)} %get-tuple-element.81) | copy-start | bytes 9220
  297.1 22.6 %copy-start.20 = (f32[768]{0:T(1024)S(1)}, f32[768]{0:T(1024)}, u32[]{:S(2)}) copy-start(f32[768]{0:T(1024)} %get-tuple-element.82) | copy-start | bytes 9220
  297.1 22.6 %copy-start.21 = (f32[768]{0:T(1024)S(1)}, f32[768]{0:T(1024)}, u32[]{:S(2)}) copy-start(f32[768]{0:T(1024)} %get-tuple-element.83) | copy-start | bytes 9220
  297.1 22.6 %copy-start.22 = (f32[768]{0:T(1024)S(1)}, f32[768]{0:T(1024)}, u32[]{:S(2)}) copy-start(f32[768]{0:T(1024)} %get-tuple-element.84) | copy-start | bytes 9220
  297.1 22.6 %copy-start.23 = (f32[768]{0:T(1024)S(1)}, f32[768]{0:T(1024)}, u32[]{:S(2)}) copy-start(f32[768]{0:T(1024)} %get-tuple-element.85) | copy-start | bytes 9220
  297.1 22.6 %copy-start.24 = (f32[768]{0:T(1024)S(1)}, f32[768]{0:T(1024)}, u32[]{:S(2)}) copy-start(f32[768]{0:T(1024)} %get-tuple-element.86) | copy-start | bytes 9220
  297.1 22.6 %copy-start.25 = (f32[768]{0:T(1024)S(1)}, f32[768]{0:T(1024)}, u32[]{:S(2)}) copy-start(f32[768]{0:T(1024)} %get-tuple-element.87) | copy-start | bytes 9220
  297.1 22.6 %copy-start.26 = (f32[768]{0:T(1024)S(1)}, f32[768]{0:T(1024)}, u32[]{:S(2)}) copy-start(f32[768]{0:T(1024)} %get-tuple-element.88) | copy-start | bytes 9220
  297.1 22.6 %copy-start.27 = (f32[768]{0:T(1024)S(1)}, f32[768]{0:T(1024)}, u32[]{:S(2)}) copy-start(f32[768]{0:T(1024)} %get-tuple-element.89) | copy-start | bytes 9220
  297.1 22.6 %copy-start.28 = (f32[768]{0:T(1024)S(1)}, f32[768]{0:T(1024)}, u32[]{:S(2)}) copy-start(f32[768]{0:T(1024)} %get-tuple-element.90) | copy-start | bytes 9220
  297.1 22.6 %copy-start.29 = (f32[768]{0:T(1024)S(1)}, f32[768]{0:T(1024)}, u32[]{:S(2)}) copy-start(f32[768]{0:T(1024)} %get-tuple-element.91) | copy-start | bytes 9220
  297.2 22.6 %copy-start.30 = (f32[768]{0:T(1024)S(1)}, f32[768]{0:T(1024)}, u32[]{:S(2)}) copy-start(f32[768]{0:T(1024)} %get-tuple-element.92) | copy-start | bytes 9220
  297.2 22.6 %copy-start.31 = (f32[768]{0:T(1024)S(1)}, f32[768]{0:T(1024)}, u32[]{:S(2)}) copy-start(f32[768]{0:T(1024)} %get-tuple-element.93) | copy-start | bytes 9220
  297.2 22.6 %copy-start.32 = (f32[768]{0:T(1024)S(1)}, f32[768]{0:T(1024)}, u32[]{:S(2)}) copy-start(f32[768]{0:T(1024)} %get-tuple-element.94) | copy-start | bytes 9220
  297.2 22.6 %copy-start.33 = (f32[768]{0:T(1024)S(1)}, f32[768]{0:T(1024)}, u32[]{:S(2)}) copy-start(f32[768]{0:T(1024)} %get-tuple-element.95) | copy-start | bytes 9220
  297.2 22.6 %copy-start.34 = (f32[768]{0:T(1024)S(1)}, f32[768]{0:T(1024)}, u32[]{:S(2)}) copy-start(f32[768]{0:T(1024)} %get-tuple-element.96) | copy-start | bytes 9220
  297.2 22.6 %copy-start.35 = (f32[768]{0:T(1024)S(1)}, f32[768]{0:T(1024)}, u32[]{:S(2)}) copy-start(f32[768]{0:T(1024)} %get-tuple-element.97) | copy-start | bytes 9220
  297.2 22.6 %copy-start.36 = (f32[768]{0:T(1024)S(1)}, f32[768]{0:T(1024)}, u32[]{:S(2)}) copy-start(f32[768]{0:T(1024)} %get-tuple-element.98) | copy-start | bytes 9220
  297.2 22.6 %copy-start.37 = (f32[768]{0:T(1024)S(1)}, f32[768]{0:T(1024)}, u32[]{:S(2)}) copy-start(f32[768]{0:T(1024)} %get-tuple-element.99) | copy-start | bytes 9220
  297.2 22.6 %copy-start.38 = (f32[768]{0:T(1024)S(1)}, f32[768]{0:T(1024)}, u32[]{:S(2)}) copy-start(f32[768]{0:T(1024)} %get-tuple-element.100) | copy-start | bytes 9220
  319.5 15.2 %collective-permute-start.12 = (f32[192,768]{1,0:T(8,128)S(1)}, f32[192,768]{1,0:T(8,128)S(1)}, u32[]{:S(2)}, u32[]{:S(2)}) collective-permute-start(f32[192,768]{1,0:T(8,128)S(1)} %add_add_fusion), channel_id=1, source_target_pairs={{0,16},{16,0},{1,17},{17,1},{2,18},{18,2},{3,19},{19,3},{4,20},{20... | collective-permute-start | bytes 1769480 | tf_op jit(solution)/shard_map/ppermute | solution.py:157
  (65 other events, 481.9 us)
Sparse Core Ops, SparseCore 0:
  10.2 56.1 all-gather.2
  68.5 53.3 all-gather.4
  193.7 95.0 reduce-scatter.1

commit v11 on v10

--- a/solution.py
+++ b/solution.py
@@ -148,6 +148,7 @@
     halves = kept + lax.ppermute(sent, "core", [(0, 1), (1, 0)])
     halves = halves.reshape(-1, channels)
     mine = lax.psum_scatter(halves, "col", scatter_dimension=0, tiled=True)
+    grad_image, mine = lax.optimization_barrier((grad_image, mine))
     depth = lax.axis_size("z")
     total = mine
     for step in range(1, depth):

time: 346 us -> 345 us (level)
  blocking collectives: 0 us -> 20.7 us
  starting transfers between devices: 42.9 us -> 31.9 us
  local copies, waits for them, and re-layouts: 45 us -> 38.8 us
    reduce_scatter x1, waiting for transfers between devices: 9.19 us -> 31.4 us  [local(): mine = lax.psum_scatter(halves, 'col', scatter_dimension=0, tiled=True)]
    ppermute x3, waiting for transfers between devices: 22.1 us -> 0.01 us  [local(): lax.ppermute(mine, 'z', [(i, (i + step) % depth) for i in range(depth)])]
    all_to_all x0 -> x1, blocking collectives: none -> 20.7 us  [local(): lax.all_to_all(outgoing, EVERY, split_axis=0, concat_axis=0, tiled=True)]
    all_to_all x1 -> x0, starting transfers between devices: 12 us -> none  [local(): lax.all_to_all(outgoing, EVERY, split_axis=0, concat_axis=0, tiled=True)]
    ppermute x2, waiting for transfers between devices: 0.01 us -> 6.84 us  [add_halo(): right = lax.ppermute(field[:, :REACH, :], 'col', shift_pairs(col_count, -1))]
    all_to_all x1 -> x0, waiting for transfers between devices: 6.64 us -> none  [local(): lax.all_to_all(outgoing, EVERY, split_axis=0, concat_axis=0, tiled=True)]
    ppermute x2, waiting for transfers between devices: 0.23 us -> 6.49 us  [add_halo(): left = lax.ppermute(field[:, -REACH:, :], 'col', shift_pairs(col_count, 1))]
    all_gather x1, waiting for transfers between devices: 48.5 us -> 43.9 us  [local(): lax.all_gather(w_out, 'col', axis=0, tiled=True)]
  transfers between devices with their start and end apart: 18 -> 17, of which waited for: 10 -> 9; matrix products, arithmetic and copies ran while one was open for 28% -> 27% of each run, Pallas kernels for 0% -> 0%
where the time goes in v11:
time: 345 us; the launch traced here: 343 us
  waiting for transfers between devices  128 us (37%)
  other arithmetic  64.4 us (19%)
  matrix products  44.4 us (13%)
  local copies, waits for them, and re-layouts  38.8 us (11%)
  starting transfers between devices  31.9 us (9%)
  blocking collectives  20.7 us (6%)
  between operations  15.1 us (4%)
    all_gather x1, waiting for transfers between devices, local(): lax.all_gather(w_out, 'col', axis=0, tiled=True)  43.9 us
    reduce_scatter x1, waiting for transfers between devices, local(): mine = lax.psum_scatter(halves, 'col', scatter_dimension=0, tiled=True)  31.4 us
    all_to_all x1, blocking collectives, local(): lax.all_to_all(outgoing, EVERY, split_axis=0, concat_axis=0, tiled=True)  20.7 us
    all_gather x1, waiting for transfers between devices, local(): lax.all_gather(w_in, 'col', axis=0, tiled=True)  16.1 us
    reduce_sum x3, other arithmetic, tile_taps(): columns.append(jnp.sum(gradient * window, axis=(0, 1)))  15.5 us
    ppermute x1, waiting for transfers between devices, local(): halves = kept + lax.ppermute(sent, 'core', [(0, 1), (1, 0)])  14.6 us
    convert_element_type x1, other arithmetic, local(): (cotangent.astype(jnp.float32) + grad_back.astype(jnp.float32)).astype(jn...  13.4 us
    reduce_sum x1, other arithmetic, local(): average = jnp.mean(conv_rows, axis=1, keepdims=True)  12.9 us
  transfers between devices with their start and end apart: 17, of which 9 were waited for; matrix products, arithmetic and copies ran while one was open for 27% of the time, Pallas kernels for 0%

profile of v11, /device:TPU:0, one launch (start us, length us, event | category | flops | bytes accessed | tf_op | source)
XLA Modules:
  0.0 343.4 jit_solution(15111497546170850726)
XLA Ops:
  9.8 3.6 %collective-permute-start = (bf16[16,6,768]{2,1,0:T(8,128)(2,1)S(1)}, bf16[16,6,768]{2,1,0:T(8,128)(2,1)S(1)}, u32[]{:S(2)}, u32[]{:S(2)}) collective-permute-start(bf16[16,6,768]{2,1,0:T(8,128)(2,1)S(1)} %get-tuple-element.190), channel_id=1, source_target_pairs={{0,1},{1,2},{2,3},{3,4},{4,5},{5,6},{6,7},{7,8},{8,9},{9,10},{10,1... | collective-permute-start | bytes 442376 | tf_op jit(solution)/shard_map/ppermute | solution.py:43
  13.4 1.3 collective-permute-start.1
  14.7 1.4 slice_reduce_fusion.97
  16.1 2.1 slice_reduce_fusion.96
  18.3 3.4 collective-permute-done.1
  21.7 1.2 pad_maximum_fusion.10
  22.9 1.3 collective-permute-start.2
  24.2 1.3 collective-permute-start.3
  25.5 1.7 slice_reduce_fusion.95
  30.3 2.7 maximum_maximum_fusion
  33.4 12.9 %convert_reduce_fusion = (f32[16,32]{1,0:T(8,128)S(1)}, bf16[16,32,768]{2,1,0:T(8,128)(2,1)}) fusion(bf16[22,44,768]{2,1,0:T(8,128)(2,1)S(1)} %get-tuple-element.184, f32[768]{0:T(1024)S(1)} %copy-done.46, f32[768]{0:T(1024)S(1)} %get-tuple-element.124, f32[768]{0:T(1024)S(1)} %get-tuple-element.125, f32[768]{0:T(1024)S(1)} %get-tuple-element.126, ...), kind=kLoop, calls=%fused_computation.273 | loop fusion | flops 62127616 | bytes 37262336 | tf_op jit(solution)/shard_map/reduce_sum | solution.py:96
  46.3 1.5 multiply_reduce_fusion.2
  47.9 2.3 multiply_convert_fusion.3
  50.2 16.1 %all-gather.3.cloned.1.call-done = bf16[768,3072]{1,0:T(8,128)(2,1)} async-done(((bf16[48,3072]{1,0:T(8,128)(2,1)}), bf16[768,3072]{1,0:T(8,128)(2,1)}) %all-gather.3.cloned.1.call-update) | async-done | bytes 4718608 | tf_op jit(solution)/shard_map/all_gather | solution.py:87
  66.4 7.1 %fusion.8 = (bf16[3072,512]{0,1:T(8,128)(2,1)}, f32[512,3072]{1,0:T(8,128)}) fusion(f32[3072]{0:T(1024)S(1)} %copy-done.53, bf16[512,768]{1,0:T(8,128)(2,1)} %multiply_convert_fusion.3, bf16[768,3072]{1,0:T(8,128)(2,1)} %all-gather.3.cloned.1.call-done), kind=kOutput, calls=%fused_computation.64 | convolution fusion | flops 2425356288 | bytes 14954496 | tf_op jit(solution)/shard_map/dot_general | solution.py:101
  73.4 4.7 %copy.19 = bf16[3072,512]{1,0:T(8,128)(2,1)} copy(bf16[3072,512]{0,1:T(8,128)(2,1)} %get-tuple-element.195) | data formatting | bytes 6291456 | tf_op jit(solution)/shard_map/convert_element_type | solution.py:102
  78.1 43.9 %all-gather.5.cloned.1.call-done = bf16[3072,768]{1,0:T(8,128)(2,1)} async-done(((bf16[192,768]{1,0:T(8,128)(2,1)}), bf16[3072,768]{1,0:T(8,128)(2,1)}) %all-gather.5.cloned.1.call-update) | async-done | bytes 4718608 | tf_op jit(solution)/shard_map/all_gather | solution.py:88
  122.0 8.6 %fusion.136 = (f32[768]{0:T(1024)}, bf16[512,768]{1,0:T(8,128)(2,1)}, bf16[512,768]{1,0:T(8,128)(2,1)S(1)}) fusion(bf16[16,32,768]{2,1,0:T(8,128)(2,1)} %param.15, f32[768]{0:T(1024)S(1)} %copy-done.49, bf16[16,32,768]{2,1,0:T(8,128)(2,1)} %param.8, bf16[3072,768]{1,0:T(8,128)(2,1)} %all-gather.5.cloned.1.call-done, f32[512,3072]{1,0:T(8,128)} %get-tuple-element.196, ...), kind=kOutput, calls=%fused_computation.249 | convolution fusion | flops 2428894464 | bytes 14174208 | tf_op jit(solution)/shard_map/dot_general | solution.py:103
  130.5 5.3 %fusion.155 = (f32[3072]{0:T(1024)}, bf16[512,3072]{1,0:T(8,128)(2,1)S(1)}) fusion(f32[512,3072]{1,0:T(8,128)S(1)} %copy-done.54, f32[3072]{0:T(1024)S(1)} %copy-done.53, bf16[512,768]{1,0:T(8,128)(2,1)S(1)} %get-tuple-element.187, bf16[3072,768]{1,0:T(8,128)(2,1)S(1)} %copy-done.52), kind=kOutput, calls=%fused_computation.411 | convolution fusion | flops 2434790400 | bytes 14966784 | tf_op jit(solution)/shard_map/dot_general | solution.py:111
  135.8 1.6 copy-done.7
  137.4 5.1 %fusion.139 = f32[768,3072]{1,0:T(8,128)} fusion(bf16[512,768]{1,0:T(8,128)(2,1)S(1)} %copy-done.6, bf16[512,3072]{1,0:T(8,128)(2,1)S(1)} %get-tuple-element.200), kind=kOutput, calls=%fused_computation.257 | convolution fusion | flops 2415919104 | bytes 13369344 | tf_op jit(solution)/shard_map/dot_general | solution.py:139
  142.5 11.6 %reshape.221 = f32[16,192,768]{2,1,0:T(8,128)} reshape(f32[768,3072]{1,0:T(8,128)} %fusion.139) | data formatting | bytes 18874368 | tf_op jit(solution)/shard_map/reshape | solution.py:141
  154.2 11.4 %broadcast_select_fusion = (f32[16,192,768]{2,1,0:T(8,128)}, f32[16,192,768]{2,1,0:T(8,128)}) fusion(f32[16,192,768]{2,1,0:T(8,128)} %reshape.221, pred[]{:T(512)S(6)} %eq.3, bf16[16,192,512]{2,1,0:T(8,128)(2,1)} %bitcast.121, bf16[512,768,1]{1,0,2:T(8,128)(2,1)} %bitcast.122), kind=kOutput, calls=%fused_computation.65 | convolution fusion | flops 2418278400 | bytes 32243712 | tf_op jit(solution)/shard_map/dot_general | solution.py:142
  165.6 2.5 collective-permute-start.8
  168.0 14.6 %collective-permute-done.8 = f32[16,192,768]{2,1,0:T(8,128)} collective-permute-done((f32[16,192,768]{2,1,0:T(8,128)}, f32[16,192,768]{2,1,0:T(8,128)}, u32[]{:S(2)}, u32[]{:S(2)}) %collective-permute-start.8) | collective-permute-done | bytes 9437216 | tf_op jit(solution)/shard_map/ppermute | solution.py:148
  182.7 7.3 %select_add_fusion = f32[16,192,768]{2,1,0:T(8,128)} fusion(f32[16,192,768]{2,1,0:T(8,128)} %collective-permute-done.8, f32[16,192,768]{2,1,0:T(8,128)S(1)} %bitcast.115, f32[16,192,768]{2,1,0:T(8,128)} %get-tuple-element.198, pred[]{:T(512)S(6)} %eq.3), kind=kLoop, calls=%fused_computation.51 | loop fusion | flops 4718592 | bytes 37748736 | tf_op jit(solution)/shard_map/add | solution.py:148
  190.0 1.6 reshape.218
  191.6 3.5 %rev.3 = f32[768,7,7]{0,2,1:T(8,128)} reverse(f32[768,7,7]{0,2,1:T(8,128)} %reshape.218), dimensions={1,2} | reverse | bytes 301056 | tf_op jit(solution)/shard_map/rev | solution.py:90
  195.2 1.6 reshape.219
  196.8 1.5 slice_reduce_fusion.48
  198.2 7.0 %multiply_reduce_fusion = (f32[768]{0:T(1024)}, f32[512]{0:T(512)S(1)}, f32[512]{0:T(512)S(1)}, f32[512,768]{1,0:T(8,128)S(1)}) fusion(bf16[16,32,768]{2,1,0:T(8,128)(2,1)} %get-tuple-element.174, f32[512]{0:T(512)S(1)} %rsqrt.12, f32[512]{0:T(512)S(1)} %div.15, f32[768]{0:T(1024)S(1)} %copy-done.14, bf16[768,3072]{1,0:T(8,128)(2,1)} %all-gather.3.cloned.1.call-done, ...), kind=kOutput, calls=%fused_computation.254 | convolution fusion | flops 2419456256 | bytes 10237952 | tf_op jit(solution)/shard_map/dot_general | solution.py:117
  205.3 5.6 %fusion.132 = (f32[768]{0:T(1024)}, f32[768]{0:T(1024)}, f32[768]{0:T(1024)}, f32[768]{0:T(1024)}, f32[768]{0:T(1024)}, /*index=5*/f32[768]{0:T(1024)}, f32[768]...) fusion(bf16[22,44,768]{2,1,0:T(8,128)(2,1)S(1)} %get-tuple-elem, ...), kind=kLoop, calls=%fused_computation.241 | loop fusion | flops 25152000 | bytes 17368064 | tf_op jit(solution)/shard_map/reduce_sum | solution.py:73
  210.9 3.3 collective-permute-start.4
  214.3 1.3 collective-permute-start.5
  215.9 6.5 %collective-permute-done.4 = bf16[16,6,768]{2,1,0:T(8,128)(2,1)S(1)} collective-permute-done((bf16[16,6,768]{2,1,0:T(8,128)(2,1)S(1)}, bf16[16,6,768]{2,1,0:T(8,128)(2,1)S(1)}, u32[]{:S(2)}, u32[]{:S(2)}) %collective-permute-start.4) | collective-permute-done | bytes 147488 | tf_op jit(solution)/shard_map/ppermute | solution.py:43
  222.4 3.5 %collective-permute-done.5 = bf16[16,6,768]{2,1,0:T(8,128)(2,1)S(1)} collective-permute-done((bf16[16,6,768]{2,1,0:T(8,128)(2,1)S(1)}, bf16[16,6,768]{2,1,0:T(8,128)(2,1)S(1)}, u32[]{:S(2)}, u32[]{:S(2)}) %collective-permute-start.5) | collective-permute-done | bytes 147488 | tf_op jit(solution)/shard_map/ppermute | solution.py:44
  226.1 5.8 %collective-permute-start.6 = (bf16[6,44,768]{2,1,0:T(8,128)(2,1)S(1)}, bf16[6,44,768]{2,1,0:T(8,128)(2,1)S(1)}, u32[]{:S(2)}, u32[]{:S(2)}) collective-permute-start(bf16[6,44,768]{2,1,0:T(8,128)(2,1)S(1)} %get-tuple-element.181), channel_id=1, source_target_pairs={{0,16},{16,32},{32,48},{48,64},{64,80},{80,96},{96,112},{1,17},{17... | collective-permute-start | bytes 1216520 | tf_op jit(solution)/shard_map/ppermute | solution.py:46
  232.0 1.3 collective-permute-start.7
  233.3 4.2 %fusion.104 = (f32[768]{0:T(1024)S(1)}, f32[768]{0:T(1024)S(1)}, f32[768]{0:T(1024)S(1)}, f32[768]{0:T(1024)S(1)}, f32[768]{0:T(1024)S(1)}, /*index=5*/f32[768]{...) fusion(bf16[22,44,768]{2,1,0:T(8,128)(2,1)S(1)} %get-tuple-elem, ...), kind=kLoop, calls=%fused_computation.213 | loop fusion | flops 21613056 | bytes 14997504 | tf_op jit(solution)/shard_map/reduce_sum | solution.py:73
  237.5 1.3 maximum_maximum_fusion.1
  238.9 13.4 %fusion.133 = bf16[16,32,768]{2,1,0:T(8,128)(2,1)} fusion(bf16[16,32,768]{2,1,0:T(8,128)(2,1)S(1)} %copy-done.9, bf16[22,44,768]{2,1,0:T(8,128)(2,1)S(1)} %get-tuple-element.180, f32[768]{0:T(1024)S(1)} %get-tuple-element.75, f32[768]{0:T(1024)S(1)} %get-tuple-element.76, f32[768]{0:T(1024)S(1)} %get-tuple-element.77, f32[768]{0:T(1024)S(1)} %get-tuple-element.78, ...), kind=kLoop, calls=%fused_computation.246 | loop fusion | flops 66453504 | bytes 35834880 | tf_op jit(solution)/shard_map/convert_element_type | solution.py:134
  252.3 31.4 %reduce-scatter.2.cloned.1.call-done = f32[192,768]{1,0:T(8,128)} async-done(((f32[3072,768]{1,0:T(8,128)}), f32[192,768]{1,0:T(8,128)}) %reduce-scatter.2.cloned.1.call-update) | async-done | bytes 589840 | tf_op jit(solution)/shard_map/reduce_scatter | solution.py:150
  283.7 3.0 collective-permute-start.11
  288.4 5.7 %fusion.114 = (f32[768]{0:T(1024)S(1)}, f32[768]{0:T(1024)S(1)}, f32[768]{0:T(1024)S(1)}, f32[768]{0:T(1024)S(1)}, f32[768]{0:T(1024)S(1)}, /*index=5*/f32[768]{...) fusion(bf16[22,44,768]{2,1,0:T(8,128)(2,1)S(1)} %get-tuple-elem, ...), kind=kLoop, calls=%fused_computation.223 | loop fusion | flops 19257600 | bytes 8838144 | tf_op jit(solution)/shard_map/reduce_sum | solution.py:73
  295.9 20.7 %all_to_all.15 = f32[128,1,330]{2,1,0:T(1,128)S(1)} all-to-all(f32[128,1,330]{2,1,0:T(1,128)S(1)} %copy.21), channel_id=1, replica_groups=mesh['z'=4,'core'=2,'col'=16] {'z','core','col'}, dimensions={0} | all-to-all | bytes 337920 | tf_op jit(solution)/shard_map/all_to_all | solution.py:169
  317.5 5.3 %all-to-all-start.1 = ((f32[128,1,36]{2,1,0:T(1,128)}), f32[128,1,36]{2,1,0:T(1,128)S(1)}, u32[]{:S(2)}, u32[]{:S(2)}) async-start(f32[128,1,36]{2,1,0:T(1,128)} %broadcast_in_dim.2), calls=%async_computation.2 | async-start | bytes 131072 | tf_op jit(solution)/shard_map/all_to_all | solution.py:173
  322.9 1.6 add_add_fusion
  325.2 7.1 %all-to-all-done.1 = f32[128,1,36]{2,1,0:T(1,128)S(1)} async-done(((f32[128,1,36]{2,1,0:T(1,128)}), f32[128,1,36]{2,1,0:T(1,128)S(1)}, u32[]{:S(2)}, u32[]{:S(2)}) %all-to-all-start.1) | async-done | bytes 18464 | tf_op jit(solution)/shard_map/all_to_all | solution.py:173
  (216 shorter events, 15.7 us)
Async XLA Ops:
  7.2 11.0 %copy-start.3 = (bf16[16,32,768]{2,1,0:T(8,128)(2,1)S(1)}, bf16[16,32,768]{2,1,0:T(8,128)(2,1)}, u32[]{:S(2)}) copy-start(bf16[16,32,768]{2,1,0:T(8,128)(2,1)} %param.8) | copy-start | bytes 2359300
  7.2 59.2 %all-gather.3.cloned.1.call-start = ((), (), s32[]{:S(2)}) async-start(), calls=%async_computation.3 | async-start | bytes 5013504 | tf_op jit(solution)/shard_map/all_gather | solution.py:87
  7.9 114.0 %all-gather.5.cloned.1.call-start = ((), (), s32[]{:S(2)}) async-start(), calls=%async_computation.4 | async-start | bytes 5013504 | tf_op jit(solution)/shard_map/all_gather | solution.py:88
  8.7 275.0 %reduce-scatter.2.cloned.1.call-start = ((), (), s32[]{:S(2)}) async-start(), calls=%async_computation.5 | async-start | bytes 10027008 | tf_op jit(solution)/shard_map/reduce_scatter | solution.py:150
  9.8 8.5 %collective-permute-start = (bf16[16,6,768]{2,1,0:T(8,128)(2,1)S(1)}, bf16[16,6,768]{2,1,0:T(8,128)(2,1)S(1)}, u32[]{:S(2)}, u32[]{:S(2)}) collective-permute-start(bf16[16,6,768]{2,1,0:T(8,128)(2,1)S(1)} %get-tuple-element.190), channel_id=1, source_target_pairs={{0,1},{1,2},{2,3},{3,4},{4,5},{5,6},{6,7},{7,8},{8,9},{9,10},{10,1... | collective-permute-start | bytes 442376 | tf_op jit(solution)/shard_map/ppermute | solution.py:43
  13.4 8.3 %collective-permute-start.1 = (bf16[16,6,768]{2,1,0:T(8,128)(2,1)S(1)}, bf16[16,6,768]{2,1,0:T(8,128)(2,1)S(1)}, u32[]{:S(2)}, u32[]{:S(2)}) collective-permute-start(bf16[16,6,768]{2,1,0:T(8,128)(2,1)S(1)} %get-tuple-element.191), channel_id=1, source_target_pairs={{1,0},{2,1},{3,2},{4,3},{5,4},{6,5},{7,6},{8,7},{9,8},{10,9},{11,1... | collective-permute-start | bytes 442376 | tf_op jit(solution)/shard_map/ppermute | solution.py:44
  18.2 9.0 %copy-start.8 = (bf16[16,32,768]{2,1,0:T(8,128)(2,1)S(1)}, bf16[16,32,768]{2,1,0:T(8,128)(2,1)}, u32[]{:S(2)}) copy-start(bf16[16,32,768]{2,1,0:T(8,128)(2,1)} %param.15) | copy-start | bytes 2359300
  18.2 9.0 %copy-start.48 = (f32[768]{0:T(1024)S(1)}, f32[768]{0:T(1024)}, u32[]{:S(2)}) copy-start(f32[768]{0:T(1024)} %param.14) | copy-start | bytes 9220
  21.7 6.6 %copy-start.10 = (bf16[16,6,768]{2,1,0:T(8,128)(2,1)}, bf16[16,6,768]{2,1,0:T(8,128)(2,1)S(1)}, u32[]{:S(2)}) copy-start(bf16[16,6,768]{2,1,0:T(8,128)(2,1)S(1)} %collective-permute-done.1) | copy-start | bytes 442372
  22.9 5.6 %collective-permute-start.2 = (bf16[6,44,768]{2,1,0:T(8,128)(2,1)}, bf16[6,44,768]{2,1,0:T(8,128)(2,1)S(1)}, u32[]{:S(2)}, u32[]{:S(2)}) collective-permute-start(bf16[6,44,768]{2,1,0:T(8,128)(2,1)} %get-tuple-element.185), channel_id=1, source_target_pairs={{0,16},{16,32},{32,48},{48,64},{64,80},{80,96},{96,112},{1,17},{17... | collective-permute-start | bytes 1216520 | tf_op jit(solution)/shard_map/ppermute | solution.py:46
  24.2 6.2 %collective-permute-start.3 = (bf16[6,44,768]{2,1,0:T(8,128)(2,1)}, bf16[6,44,768]{2,1,0:T(8,128)(2,1)}, u32[]{:S(2)}, u32[]{:S(2)}) collective-permute-start(bf16[6,44,768]{2,1,0:T(8,128)(2,1)} %get-tuple-element.186), channel_id=1, source_target_pairs={{16,0},{32,16},{48,32},{64,48},{80,64},{96,80},{112,96},{17,1},{33... | collective-permute-start | bytes 1216520 | tf_op jit(solution)/shard_map/ppermute | solution.py:47
  28.2 4.9 %copy-start.4 = (bf16[16,32,768]{2,1,0:T(8,128)(2,1)S(1)}, bf16[16,32,768]{2,1,0:T(8,128)(2,1)}, u32[]{:S(2)}) copy-start(bf16[16,32,768]{2,1,0:T(8,128)(2,1)} %param.8) | copy-start | bytes 2359300
  33.3 14.6 %copy-start.14 = (f32[768]{0:T(1024)S(1)}, f32[768]{0:T(1024)}, u32[]{:S(2)}) copy-start(f32[768]{0:T(1024)} %param.10) | copy-start | bytes 9220
  46.2 20.1 %copy-start.53 = (f32[3072]{0:T(1024)S(1)}, f32[3072]{0:T(1024)}, u32[]{:S(2)}) copy-start(f32[3072]{0:T(1024)} %param.12) | copy-start | bytes 36868
  73.4 48.5 %copy-start.49 = (f32[768]{0:T(1024)S(1)}, f32[768]{0:T(1024)}, u32[]{:S(2)}) copy-start(f32[768]{0:T(1024)} %param.14) | copy-start | bytes 9220
  122.0 8.6 %copy-start.52 = (bf16[3072,768]{1,0:T(8,128)(2,1)S(1)}, bf16[3072,768]{1,0:T(8,128)(2,1)}, u32[]{:S(2)}) copy-start(bf16[3072,768]{1,0:T(8,128)(2,1)} %all-gather.5.cloned.1.call-done) | copy-start | bytes 14155780
  122.0 8.6 %copy-start.54 = (f32[512,3072]{1,0:T(8,128)S(1)}, f32[512,3072]{1,0:T(8,128)}, u32[]{:S(2)}) copy-start(f32[512,3072]{1,0:T(8,128)} %get-tuple-element.196) | copy-start | bytes 18874372
  130.5 6.9 %copy-start.6 = (bf16[512,768]{1,0:T(8,128)(2,1)S(1)}, bf16[512,768]{1,0:T(8,128)(2,1)}, u32[]{:S(2)}) copy-start(bf16[512,768]{1,0:T(8,128)(2,1)} %multiply_convert_fusion.3) | copy-start | bytes 2359300
  154.1 28.5 %slice-start = ((s8[9437184]{0:T(1024)(128)(4,1)}), s8[4194304]{0:T(1024)(128)(4,1)S(1)}, s32[]{:S(2)}) async-start(s8[9437184]{0:T(1024)(128)(4,1)} %bitcast.114), calls=%async_computation.6 | async-start | bytes 8388608
  154.1 28.5 %slice-start.1 = ((s8[9437184]{0:T(1024)(128)(4,1)}), s8[4194304]{0:T(1024)(128)(4,1)S(1)}, s32[]{:S(2)}) async-start(s8[9437184]{0:T(1024)(128)(4,1)} %bitcast.114), calls=%async_computation.7 | async-start | bytes 8388608
  154.1 28.5 %slice-start.2 = ((s8[9437184]{0:T(1024)(128)(4,1)}), s8[1048576]{0:T(1024)(128)(4,1)S(1)}, s32[]{:S(2)}) async-start(s8[9437184]{0:T(1024)(128)(4,1)} %bitcast.114), calls=%async_computation.8 | async-start | bytes 2097152
  165.6 17.1 %collective-permute-start.8 = (f32[16,192,768]{2,1,0:T(8,128)}, f32[16,192,768]{2,1,0:T(8,128)}, u32[]{:S(2)}, u32[]{:S(2)}) collective-permute-start(f32[16,192,768]{2,1,0:T(8,128)} %get-tuple-element.197), channel_id=1, source_target_pairs={{0,16},{16,0},{1,17},{17,1},{2,18},{18,2},{3,19},{19,3},{4,20},{20... | collective-permute-start | bytes 28311560 | tf_op jit(solution)/shard_map/ppermute | solution.py:148
  198.2 7.1 %copy-start.5 = (bf16[16,32,768]{2,1,0:T(8,128)(2,1)S(1)}, bf16[16,32,768]{2,1,0:T(8,128)(2,1)}, u32[]{:S(2)}) copy-start(bf16[16,32,768]{2,1,0:T(8,128)(2,1)} %get-tuple-element.174) | copy-start | bytes 2359300
  205.3 10.3 %copy-start.11 = (f32[768,49]{0,1:T(8,128)S(1)}, f32[768,49]{0,1:T(8,128)}, u32[]{:S(2)}) copy-start(f32[768,49]{0,1:T(8,128)} %reshape.219) | copy-start | bytes 451588
  210.9 28.0 %copy-start = (bf16[512,768]{1,0:T(8,128)(2,1)}, bf16[512,768]{1,0:T(8,128)(2,1)S(1)}, u32[]{:S(2)}) copy-start(bf16[512,768]{1,0:T(8,128)(2,1)S(1)} %get-tuple-element.172) | copy-start | bytes 2359300
  210.9 11.4 %collective-permute-start.4 = (bf16[16,6,768]{2,1,0:T(8,128)(2,1)S(1)}, bf16[16,6,768]{2,1,0:T(8,128)(2,1)S(1)}, u32[]{:S(2)}, u32[]{:S(2)}) collective-permute-start(bf16[16,6,768]{2,1,0:T(8,128)(2,1)S(1)} %get-tuple-element.188), channel_id=1, source_target_pairs={{0,1},{1,2},{2,3},{3,4},{4,5},{5,6},{6,7},{7,8},{8,9},{9,10},{10,1... | collective-permute-start | bytes 442376 | tf_op jit(solution)/shard_map/ppermute | solution.py:43
  214.3 11.5 %collective-permute-start.5 = (bf16[16,6,768]{2,1,0:T(8,128)(2,1)S(1)}, bf16[16,6,768]{2,1,0:T(8,128)(2,1)S(1)}, u32[]{:S(2)}, u32[]{:S(2)}) collective-permute-start(bf16[16,6,768]{2,1,0:T(8,128)(2,1)S(1)} %get-tuple-element.189), channel_id=1, source_target_pairs={{1,0},{2,1},{3,2},{4,3},{5,4},{6,5},{7,6},{8,7},{9,8},{10,9},{11,1... | collective-permute-start | bytes 442376 | tf_op jit(solution)/shard_map/ppermute | solution.py:44
  226.1 11.4 %collective-permute-start.6 = (bf16[6,44,768]{2,1,0:T(8,128)(2,1)S(1)}, bf16[6,44,768]{2,1,0:T(8,128)(2,1)S(1)}, u32[]{:S(2)}, u32[]{:S(2)}) collective-permute-start(bf16[6,44,768]{2,1,0:T(8,128)(2,1)S(1)} %get-tuple-element.181), channel_id=1, source_target_pairs={{0,16},{16,32},{32,48},{48,64},{64,80},{80,96},{96,112},{1,17},{17... | collective-permute-start | bytes 1216520 | tf_op jit(solution)/shard_map/ppermute | solution.py:46
  232.0 5.5 %collective-permute-start.7 = (bf16[6,44,768]{2,1,0:T(8,128)(2,1)S(1)}, bf16[6,44,768]{2,1,0:T(8,128)(2,1)S(1)}, u32[]{:S(2)}, u32[]{:S(2)}) collective-permute-start(bf16[6,44,768]{2,1,0:T(8,128)(2,1)S(1)} %get-tuple-element.182), channel_id=1, source_target_pairs={{16,0},{32,16},{48,32},{64,48},{80,64},{96,80},{112,96},{17,1},{33... | collective-permute-start | bytes 1216520 | tf_op jit(solution)/shard_map/ppermute | solution.py:47
  283.6 10.5 %copy-start.24 = (f32[768]{0:T(1024)S(1)}, f32[768]{0:T(1024)}, u32[]{:S(2)}) copy-start(f32[768]{0:T(1024)} %get-tuple-element.12) | copy-start | bytes 9220
  283.6 10.5 %copy-start.23 = (f32[768]{0:T(1024)S(1)}, f32[768]{0:T(1024)}, u32[]{:S(2)}) copy-start(f32[768]{0:T(1024)} %get-tuple-element.13) | copy-start | bytes 9220
  283.6 10.5 %copy-start.22 = (f32[768]{0:T(1024)S(1)}, f32[768]{0:T(1024)}, u32[]{:S(2)}) copy-start(f32[768]{0:T(1024)} %get-tuple-element.14) | copy-start | bytes 9220
  283.6 10.5 %copy-start.21 = (f32[768]{0:T(1024)S(1)}, f32[768]{0:T(1024)}, u32[]{:S(2)}) copy-start(f32[768]{0:T(1024)} %get-tuple-element.15) | copy-start | bytes 9220
  283.6 10.5 %copy-start.20 = (f32[768]{0:T(1024)S(1)}, f32[768]{0:T(1024)}, u32[]{:S(2)}) copy-start(f32[768]{0:T(1024)} %get-tuple-element.16) | copy-start | bytes 9220
  283.6 10.6 %copy-start.19 = (f32[768]{0:T(1024)S(1)}, f32[768]{0:T(1024)}, u32[]{:S(2)}) copy-start(f32[768]{0:T(1024)} %get-tuple-element.17) | copy-start | bytes 9220
  283.6 10.6 %copy-start.18 = (f32[768]{0:T(1024)S(1)}, f32[768]{0:T(1024)}, u32[]{:S(2)}) copy-start(f32[768]{0:T(1024)} %get-tuple-element.18) | copy-start | bytes 9220
  283.6 10.6 %copy-start.17 = (f32[768]{0:T(1024)S(1)}, f32[768]{0:T(1024)}, u32[]{:S(2)}) copy-start(f32[768]{0:T(1024)} %get-tuple-element.19) | copy-start | bytes 9220
  283.7 10.6 %copy-start.16 = (f32[768]{0:T(1024)S(1)}, f32[768]{0:T(1024)}, u32[]{:S(2)}) copy-start(f32[768]{0:T(1024)} %get-tuple-element.20) | copy-start | bytes 9220
  283.7 10.6 %copy-start.15 = (f32[768]{0:T(1024)S(1)}, f32[768]{0:T(1024)}, u32[]{:S(2)}) copy-start(f32[768]{0:T(1024)} %get-tuple-element.21) | copy-start | bytes 9220
  283.7 11.1 %copy-start.47 = (f32[3072]{0:T(1024)S(1)}, f32[3072]{0:T(1024)}, u32[]{:S(2)}) copy-start(f32[3072]{0:T(1024)} %get-tuple-element.199) | copy-start | bytes 36868
  283.7 11.1 %copy-start.50 = (f32[768]{0:T(1024)S(1)}, f32[768]{0:T(1024)}, u32[]{:S(2)}) copy-start(f32[768]{0:T(1024)} %get-tuple-element.175) | copy-start | bytes 9220
  283.7 11.1 %copy-start.51 = (f32[768]{0:T(1024)S(1)}, f32[768]{0:T(1024)}, u32[]{:S(2)}) copy-start(f32[768]{0:T(1024)} %get-tuple-element.54) | copy-start | bytes 9220
  283.7 39.2 %collective-permute-start.11 = (f32[192,768]{1,0:T(8,128)}, f32[192,768]{1,0:T(8,128)}, u32[]{:S(2)}, u32[]{:S(2)}) collective-permute-start(f32[192,768]{1,0:T(8,128)} %reduce-scatter.2.cloned.1.call-done), channel_id=1, source_target_pairs={{0,96},{32,0},{64,32},{96,64},{1,97},{33,1},{65,33},{97,65},{2,98}... | collective-permute-start | bytes 1769480 | tf_op jit(solution)/shard_map/ppermute | solution.py:155
  286.8 36.1 %collective-permute-start.10 = (f32[192,768]{1,0:T(8,128)}, f32[192,768]{1,0:T(8,128)}, u32[]{:S(2)}, u32[]{:S(2)}) collective-permute-start(f32[192,768]{1,0:T(8,128)} %reduce-scatter.2.cloned.1.call-done), channel_id=1, source_target_pairs={{0,64},{32,96},{64,0},{96,32},{1,65},{33,97},{65,1},{97,33},{2,66}... | collective-permute-start | bytes 1769480 | tf_op jit(solution)/shard_map/ppermute | solution.py:155
  287.4 35.5 %collective-permute-start.9 = (f32[192,768]{1,0:T(8,128)}, f32[192,768]{1,0:T(8,128)}, u32[]{:S(2)}, u32[]{:S(2)}) collective-permute-start(f32[192,768]{1,0:T(8,128)} %reduce-scatter.2.cloned.1.call-done), channel_id=1, source_target_pairs={{0,32},{32,64},{64,96},{96,0},{1,33},{33,65},{65,97},{97,1},{2,34}... | collective-permute-start | bytes 1769480 | tf_op jit(solution)/shard_map/ppermute | solution.py:155
  294.9 28.0 %copy-start.12 = (f32[192,768]{1,0:T(8,128)S(1)}, f32[192,768]{1,0:T(8,128)}, u32[]{:S(2)}) copy-start(f32[192,768]{1,0:T(8,128)} %reduce-scatter.2.cloned.1.call-done) | copy-start | bytes 1769476
  317.5 14.8 %all-to-all-start.1 = ((f32[128,1,36]{2,1,0:T(1,128)}), f32[128,1,36]{2,1,0:T(1,128)S(1)}, u32[]{:S(2)}, u32[]{:S(2)}) async-start(f32[128,1,36]{2,1,0:T(1,128)} %broadcast_in_dim.2), calls=%async_computation.2 | async-start | bytes 131072 | tf_op jit(solution)/shard_map/all_to_all | solution.py:173
  324.5 10.5 %collective-permute-start.12 = (f32[192,768]{1,0:T(8,128)S(1)}, f32[192,768]{1,0:T(8,128)S(1)}, u32[]{:S(2)}, u32[]{:S(2)}) collective-permute-start(f32[192,768]{1,0:T(8,128)S(1)} %add_add_fusion), channel_id=1, source_target_pairs={{0,16},{16,0},{1,17},{17,1},{2,18},{18,2},{3,19},{19,3},{4,20},{20... | collective-permute-start | bytes 1769480 | tf_op jit(solution)/shard_map/ppermute | solution.py:158
  (27 other events, 114.3 us)
Sparse Core Ops, SparseCore 0:
  10.2 56.1 all-gather.2
  68.5 53.3 all-gather.4
  190.2 93.4 reduce-scatter.1
